TPU v7x, 32 devices: a whole 2x2x4 slice. The times are simulated.
32 devices in a mesh: bin: 2 (over y), row: 4 (over x, core), col: 4 (over z).
Axes of the slice: x: 2, y: 2, z: 4, core: 2. Of those that a mesh axis runs over, the one named last changes fastest.
Arguments:
- snapshots: bfloat16 [4096, 16, 64], P('row', 'bin', 'col'), may hold values from -6 to 6
- focus_in: bfloat16 [16, 4096, 128], P('bin', 'row'), may hold values from -0.09375 to 0.09375
- focus_out: bfloat16 [16, 4096, 128], P('bin', 'row'), may hold values from -0.5 to 0.5
- start_basis: float32 [4096, 128], replicated, may hold values from -6 to 6
Outputs:
- covariance: float32 [4096, 4096], P('col', 'row')
- basis_out: float32 [4096, 128], P(('row', 'col'))
All inputs are finite; a program needn't handle non-finite values.
Results may differ from a plain program's by a relative error of at most 0.0045.
Values may be sent and summed in bfloat16 or wider, within the bound.
No kernel may reach another device: no remote copies, remote signals or barrier semaphores. Data moves between devices by JAX's collectives and lax.ppermute only.
A program may use at most 128 MiB of HBM per device.

v0:
```python
import math

import jax
import jax.numpy as jnp
from jax import lax
from jax.sharding import PartitionSpec as P

ITERS = 2


def shards(snapshots, focus_in, focus_out, start_basis):
    rows_here, bins_here, snaps_here = snapshots.shape
    bin_count = lax.axis_size("bin")
    row_count = lax.axis_size("row")
    col_count = lax.axis_size("col")
    col_here = lax.axis_index("col")
    row_here = lax.axis_index("row")
    partial_proj = jnp.einsum(
        "mbs,bmr->brs", snapshots, focus_in, preferred_element_type=jnp.float32
    )
    projected = lax.psum(partial_proj, "row").astype(jnp.bfloat16)
    lifted = jnp.einsum("bmr,brs->mbs", focus_out, projected, preferred_element_type=jnp.float32)
    focused = (snapshots.astype(jnp.float32) + lifted).astype(jnp.bfloat16)
    columns = bins_here * snaps_here
    local_rows = focused.reshape(rows_here, columns)
    all_rows = lax.all_gather(local_rows, "row", axis=0, tiled=True)
    array_size = all_rows.shape[0]
    col_block = array_size // col_count
    scaling = 1.0 / (columns * col_count * bin_count)
    piece = lax.all_gather(all_rows, "col", axis=1, tiled=True)
    left_rows = lax.dynamic_slice_in_dim(piece, col_here * col_block, col_block, 0)
    right_rows = lax.dynamic_slice_in_dim(piece, row_here * rows_here, rows_here, 0)
    bin_block = lax.dot_general(
        left_rows, right_rows, (((1,), (1,)), ((), ())), preferred_element_type=jnp.float32
    )
    share_rows = lax.psum_scatter(bin_block, "bin", scatter_dimension=0, tiled=True)
    tile_block = lax.all_gather(share_rows, "bin", axis=0, tiled=True)
    covariance = tile_block * scaling
    basis_now = start_basis
    for sweep_index in range(ITERS):
        col_rows = lax.dynamic_slice_in_dim(basis_now, col_here * col_block, col_block, 0)
        partial_image = lax.dot_general(
            covariance,
            col_rows,
            (((0,), (0,)), ((), ())),
            precision=lax.Precision.HIGHEST,
            preferred_element_type=jnp.float32,
        )
        row_sums = lax.psum(partial_image, "col")
        full_image = lax.all_gather(row_sums, "row", axis=0, tiled=True)
        gram_matrix = jnp.dot(
            full_image.T,
            full_image,
            precision=lax.Precision.HIGHEST,
            preferred_element_type=jnp.float32,
        )
        lower_factor = jnp.linalg.cholesky(gram_matrix)
        basis_now = jax.scipy.linalg.solve_triangular(lower_factor, full_image.T, lower=True).T
    out_rows = array_size // (row_count * col_count)
    mine_start = (row_here * col_count + col_here) * out_rows
    basis_out = lax.dynamic_slice_in_dim(basis_now, mine_start, out_rows, 0) * math.sqrt(array_size)
    return (covariance, basis_out)


def solution(mesh):
    in_specs = (P("row", "bin", "col"), P("bin", "row", None), P("bin", "row", None), P())
    out_specs = (P("col", "row"), P(("row", "col"), None))
    return jax.shard_map(shards, mesh=mesh, in_specs=in_specs, out_specs=out_specs, check_vma=False)
```

profile of v0, /device:TPU:0, one launch (start us, length us, event | category | flops | bytes accessed | tf_op | source)
XLA Modules:
  0.0 470.6 jit_solution(1303326926260951757)
XLA Ops:
  7.2 0.0 copy-start
  7.2 0.0 all-gather.6.cloned.1.call-start
  7.2 2.2 fusion.27
  9.4 13.4 %psum.21 = bf16[8,128,16]{1,2,0:T(8,128)(2,1)S(1)} all-reduce(f32[8,128,16]{1,2,0:T(8,128)S(1)} %fusion.27), channel_id=1, replica_groups=mesh['bin'=2,'row'=4,'col'=4] {'row'}, use_global_device_ids=true, to_apply=%region_0.0 | all-reduce | flops 16384 | bytes 98304 | tf_op jit(solution)/shard_map/psum | solution.py:21
  22.9 1.4 fusion.5
  24.3 0.0 all-gather.6.cloned.1.call-update
  24.3 0.0 all-gather.8.cloned.1.call-start
  24.3 17.1 %all-gather.6.cloned.1.call-done = bf16[4096,128]{0,1:T(8,128)(2,1)} async-done(((bf16[1024,128]{0,1:T(8,128)(2,1)}), bf16[4096,128]{0,1:T(8,128)(2,1)}) %all-gather.6.cloned.1.call-update) | async-done | bytes 1048592 | tf_op jit(solution)/shard_map/all_gather | solution.py:26
  41.5 0.0 all-gather.8.cloned.1.call-update
  41.5 0.0 reduce-scatter.2.cloned.1.call-start
  41.5 82.3 %all-gather.8.cloned.1.call-done = bf16[4096,512]{0,1:T(8,128)(2,1)} async-done(((bf16[4096,128]{0,1:T(8,128)(2,1)}), bf16[4096,512]{0,1:T(8,128)(2,1)}) %all-gather.8.cloned.1.call-update) | async-done | bytes 4194320 | tf_op jit(solution)/shard_map/all_gather | solution.py:30
  123.8 5.0 %fusion.6 = f32[1024,1024]{1,0:T(8,128)} fusion(bf16[4096,512]{0,1:T(8,128)(2,1)} %all-gather.8.cloned.1.call-done, s32[]{:T(128)S(6)} %select_n.15, s32[]{:T(128)S(6)} %select_n.14), kind=kOutput, calls=%fused_computation.8 | convolution fusion | flops 1073741824 | bytes 6291464 | tf_op jit(solution)/shard_map/dot_general | solution.py:33
  128.8 0.0 reduce-scatter.2.cloned.1.call-update
  128.8 0.0 all-gather.10.cloned.1.call-start
  128.9 52.8 %reduce-scatter.2.cloned.1.call-done = f32[512,1024]{1,0:T(8,128)} async-done(((f32[1024,1024]{1,0:T(8,128)}), f32[512,1024]{1,0:T(8,128)}) %reduce-scatter.2.cloned.1.call-update) | async-done | bytes 2097168 | tf_op jit(solution)/shard_map/reduce_scatter | solution.py:36
  181.7 0.0 all-gather.10.cloned.1.call-update
  181.7 0.0 all-reduce.3.cloned.1.call-start
  181.8 58.1 %all-gather.10.cloned.1.call-done = f32[1024,1024]{1,0:T(8,128)} async-done(((f32[512,1024]{1,0:T(8,128)}), f32[1024,1024]{1,0:T(8,128)}) %all-gather.10.cloned.1.call-update) | async-done | bytes 4194320 | tf_op jit(solution)/shard_map/all_gather | solution.py:37
  239.9 2.6 broadcast_multiply_fusion
  242.5 2.0 copy-done.1
  244.5 8.5 %fusion.11 = f32[1024,128]{1,0:T(8,128)} fusion(f32[1024,1024]{1,0:T(8,128)S(1)} %broadcast_multiply_fusion, f32[4096,128]{1,0:T(8,128)} %param.10, s32[]{:T(128)S(6)} %select_n.14), kind=kOutput, calls=%fused_computation.13 | convolution fusion | flops 1610612736 | bytes 5242884 | tf_op jit(solution)/shard_map/dot_general | solution.py:42
  253.0 0.0 all-reduce.3.cloned.1.call-update
  253.0 0.0 all-gather.12.cloned.1.call-start
  253.1 38.7 %all-reduce.3.cloned.1.call-done = f32[1024,128]{1,0:T(8,128)} async-done(((f32[1024,128]{1,0:T(8,128)}), f32[1024,128]{1,0:T(8,128)}) %all-reduce.3.cloned.1.call-update) | async-done | bytes 524304 | tf_op jit(solution)/shard_map/psum | solution.py:49
  291.8 0.0 all-gather.12.cloned.1.call-update
  291.8 0.3 all-reduce.5.cloned.1.call-start
  292.1 23.5 %all-gather.12.cloned.1.call-done = f32[4096,128]{1,0:T(8,128)} async-done(((f32[1024,128]{1,0:T(8,128)}), f32[4096,128]{1,0:T(8,128)}) %all-gather.12.cloned.1.call-update) | async-done | bytes 2097168 | tf_op jit(solution)/shard_map/all_gather | solution.py:50
  315.6 5.7 %fusion.25 = f32[128,128]{1,0:T(8,128)S(1)} fusion(f32[4096,128]{1,0:T(8,128)} %all-gather.12.cloned.1.call-done), kind=kOutput, calls=%fused_computation.37 | convolution fusion | flops 805306368 | bytes 2162688 | tf_op jit(solution)/shard_map/dot_general | solution.py:51
  321.3 0.1 copy.6
  321.4 11.7 %cholesky.44 = f32[128,128]{1,0:T(8,128)S(1)} custom-call(f32[128,128]{1,0:T(8,128)S(1)} %fusion.18), custom_call_target="Cholesky" | custom-call | tf_op jit(solution)/shard_map/jit(cholesky)/cholesky | solution.py:57
  333.2 0.6 compare_reduce_fusion.1
  333.8 0.7 fusion.13
  334.5 9.8 %custom-call.6 = f32[1,128,128]{1,2,0:T(8,128)S(1)} custom-call(f32[1,128,128]{2,1,0:T(8,128)S(1)} %fusion.13), custom_call_target="InvertDiagBlocksLowerTriangular" | custom-call | tf_op jit(solution)/shard_map/jit(_solve_triangular)/triangular_solve | solution.py:58
  344.3 3.7 fusion.2
  348.0 20.0 %fusion.9 = f32[1024,128]{1,0:T(8,128)} fusion(f32[1024,1024]{1,0:T(8,128)S(1)} %copy-done.2, f32[128,4096]{1,0:T(8,128)S(1)} %fusion.2, s32[]{:T(128)S(6)} %select_n.14), kind=kOutput, calls=%fused_computation.11 | convolution fusion | flops 1610612736 | bytes 5242884 | tf_op jit(solution)/shard_map/dot_general | solution.py:42
  368.0 0.0 all-reduce.5.cloned.1.call-update
  368.0 0.0 all-gather.14.cloned.1.call-start
  368.0 38.6 %all-reduce.5.cloned.1.call-done = f32[1024,128]{1,0:T(8,128)} async-done(((f32[1024,128]{1,0:T(8,128)}), f32[1024,128]{1,0:T(8,128)}) %all-reduce.5.cloned.1.call-update) | async-done | bytes 524304 | tf_op jit(solution)/shard_map/psum | solution.py:49
  406.7 0.0 all-gather.14.cloned.1.call-update
  406.7 23.9 %all-gather.14.cloned.1.call-done = f32[4096,128]{1,0:T(8,128)} async-done(((f32[1024,128]{1,0:T(8,128)}), f32[4096,128]{1,0:T(8,128)}) %all-gather.14.cloned.1.call-update) | async-done | bytes 2097168 | tf_op jit(solution)/shard_map/all_gather | solution.py:50
  430.6 5.7 %fusion.26 = f32[128,128]{1,0:T(8,128)S(1)} fusion(f32[4096,128]{1,0:T(8,128)} %all-gather.14.cloned.1.call-done), kind=kOutput, calls=%fused_computation.38 | convolution fusion | flops 805306368 | bytes 2162688 | tf_op jit(solution)/shard_map/dot_general | solution.py:51
  436.3 0.1 copy.7
  436.4 11.7 %cholesky.55 = f32[128,128]{1,0:T(8,128)S(1)} custom-call(f32[128,128]{1,0:T(8,128)S(1)} %fusion.16), custom_call_target="Cholesky" | custom-call | tf_op jit(solution)/shard_map/jit(cholesky)/cholesky | solution.py:57
  448.2 0.6 compare_reduce_fusion
  448.8 0.7 fusion.14
  449.5 9.8 %custom-call.7 = f32[1,128,128]{1,2,0:T(8,128)S(1)} custom-call(f32[1,128,128]{2,1,0:T(8,128)S(1)} %fusion.14), custom_call_target="InvertDiagBlocksLowerTriangular" | custom-call | tf_op jit(solution)/shard_map/jit(_solve_triangular)/triangular_solve | solution.py:58
  459.3 3.5 fusion
  462.9 0.8 copy.8
  (11 shorter events, 0.1 us)
Async XLA Ops:
  7.2 15.7 %copy-start = (bf16[8,1024,128]{2,1,0:T(8,128)(2,1)S(1)}, bf16[8,1024,128]{2,1,0:T(8,128)(2,1)}, u32[]{:S(2)}) copy-start(bf16[8,1024,128]{2,1,0:T(8,128)(2,1)} %param.9) | copy-start | bytes 6291460
  7.2 15.7 %copy-start.3 = (bf16[1024,8,16]{0,2,1:T(8,128)(2,1)S(1)}, bf16[1024,8,16]{0,2,1:T(8,128)(2,1)}, u32[]{:S(2)}) copy-start(bf16[1024,8,16]{0,2,1:T(8,128)(2,1)} %param.7) | copy-start | bytes 786436
  7.2 34.3 %all-gather.6.cloned.1.call-start = ((), (), s32[]{:S(2)}) async-start(), calls=%async_computation.1 | async-start | bytes 1310720 | tf_op jit(solution)/shard_map/all_gather | solution.py:26
  24.3 99.5 %all-gather.8.cloned.1.call-start = ((), (), s32[]{:S(2)}) async-start(), calls=%async_computation.2 | async-start | bytes 5242880 | tf_op jit(solution)/shard_map/all_gather | solution.py:30
  41.5 140.2 %reduce-scatter.2.cloned.1.call-start = ((), (), s32[]{:S(2)}) async-start(), calls=%async_computation.3 | async-start | bytes 6291456 | tf_op jit(solution)/shard_map/reduce_scatter | solution.py:36
  128.8 111.0 %all-gather.10.cloned.1.call-start = ((), (), s32[]{:S(2)}) async-start(), calls=%async_computation.4 | async-start | bytes 6291456 | tf_op jit(solution)/shard_map/all_gather | solution.py:37
  181.7 110.1 %all-reduce.3.cloned.1.call-start = ((), (), s32[]{:S(2)}) async-start(), calls=%async_computation.5 | async-start | bytes 1048576 | tf_op jit(solution)/shard_map/psum | solution.py:49
  242.5 2.0 copy-start.1
  253.0 62.6 %all-gather.12.cloned.1.call-start = ((), (), s32[]{:S(2)}) async-start(), calls=%async_computation.6 | async-start | bytes 2621440 | tf_op jit(solution)/shard_map/all_gather | solution.py:50
  291.8 114.8 %all-reduce.5.cloned.1.call-start = ((), (), s32[]{:S(2)}) async-start(), calls=%async_computation.7 | async-start | bytes 1048576 | tf_op jit(solution)/shard_map/psum | solution.py:49
  344.3 3.7 copy-start.2
  368.0 62.7 %all-gather.14.cloned.1.call-start = ((), (), s32[]{:S(2)}) async-start(), calls=%async_computation.8 | async-start | bytes 2621440 | tf_op jit(solution)/shard_map/all_gather | solution.py:50
Sparse Core Ops, SparseCore 0:
  24.4 17.0 all-gather.5
  43.0 80.7 all-gather.7
  129.0 52.6 reduce-scatter.1
  183.1 56.7 all-gather.9
  253.2 38.6 all-reduce.2
  293.2 22.3 all-gather.11
  368.1 38.5 all-reduce.4
  408.2 22.3 all-gather.13
where the time goes:
time: 472 us; the launch traced here: 471 us
  waiting for transfers between devices  335 us (71%)
  matrix products  55.6 us (12%)
  other arithmetic  48.4 us (10%)
  between operations  14.5 us (3%)
  blocking collectives  13.4 us (3%)
    all_gather x1, waiting for transfers between devices, shards(): piece = lax.all_gather(all_rows, 'col', axis=1, tiled=True)  82.3 us
    psum x2, waiting for transfers between devices, shards(): row_sums = lax.psum(partial_image, 'col')  77.4 us
    all_gather x1, waiting for transfers between devices, shards(): tile_block = lax.all_gather(share_rows, 'bin', axis=0, tiled=True)  58.1 us
    reduce_scatter x1, waiting for transfers between devices, shards(): lax.psum_scatter(bin_block, 'bin', scatter_dimension=0, tiled=True)  52.8 us
    all_gather x2, waiting for transfers between devices, shards(): full_image = lax.all_gather(row_sums, 'row', axis=0, tiled=True)  47.4 us
    dot_general x2, matrix products, shards(): lax.dot_general(covariance, col_rows, (((0,), (0,)), ((), ())), precision...  28.5 us
    another operation x6, other arithmetic, shards(): lower_factor = jnp.linalg.cholesky(gram_matrix)  24.8 us
    another operation x4, other arithmetic, shards(): jax.scipy.linalg.solve_triangular(lower_factor, full_image.T, lower=True)  20.9 us
  transfers between devices with their start and end apart: 8, of which 8 were waited for; matrix products, arithmetic and copies ran while one was open for 0% of the time, Pallas kernels for 0%

commit v1 on v0

v1 whole, which is shorter than its diff:
```python
import math

import jax
import jax.numpy as jnp
from jax import lax
from jax.sharding import PartitionSpec as P

ITERS = 2


def _transpose_pairs(row_count, col_count):
    return [
        (i * col_count + j, j * row_count + i)
        for i in range(row_count)
        for j in range(col_count)
        if i != j
    ]


def _qr_step(image, gram_axis):
    gram_part = jnp.dot(
        image.T, image, precision=lax.Precision.HIGHEST, preferred_element_type=jnp.float32
    )
    gram_matrix = lax.psum(gram_part, gram_axis)
    lower_factor = jnp.linalg.cholesky(gram_matrix)
    return jax.scipy.linalg.solve_triangular(lower_factor, image.T, lower=True).T


def shards(snapshots, focus_in, focus_out, start_basis):
    rows_here, bins_here, snaps_here = snapshots.shape
    bin_count = lax.axis_size("bin")
    row_count = lax.axis_size("row")
    col_count = lax.axis_size("col")
    col_here = lax.axis_index("col")
    row_here = lax.axis_index("row")
    partial_proj = jnp.einsum(
        "mbs,bmr->brs", snapshots, focus_in, preferred_element_type=jnp.float32
    )
    projected = lax.psum(partial_proj, "row").astype(jnp.bfloat16)
    lifted = jnp.einsum("bmr,brs->mbs", focus_out, projected, preferred_element_type=jnp.float32)
    focused = (snapshots.astype(jnp.float32) + lifted).astype(jnp.bfloat16)
    columns = bins_here * snaps_here
    local_rows = focused.reshape(rows_here, columns)
    array_size = rows_here * row_count
    col_block = array_size // col_count
    scaling = 1.0 / (columns * col_count * bin_count)

    right_rows = lax.all_gather(local_rows, ("bin", "col"), axis=0, tiled=False)
    if row_count == col_count:
        swapped = lax.ppermute(local_rows, ("row", "col"), _transpose_pairs(row_count, col_count))
        swapped = jnp.where(row_here == col_here, local_rows, swapped)
        left_rows = lax.all_gather(swapped, ("bin", "row"), axis=0, tiled=False)
    else:
        every_row = lax.all_gather(right_rows, "row", axis=1, tiled=True)
        left_rows = lax.dynamic_slice_in_dim(every_row, col_here * col_block, col_block, 1)
    covariance = lax.dot_general(
        left_rows, right_rows, (((0, 2), (0, 2)), ((), ())), preferred_element_type=jnp.float32
    ) * scaling

    basis_rows = lax.dynamic_slice_in_dim(start_basis, row_here * rows_here, rows_here, 0)
    on_rows = True
    for sweep_index in range(ITERS):
        if on_rows:
            partial_image = jnp.dot(
                covariance, basis_rows, precision=lax.Precision.HIGHEST,
                preferred_element_type=jnp.float32,
            )
            image = lax.psum(partial_image, "row")
            basis_rows = _qr_step(image, "col")
        else:
            partial_image = lax.dot_general(
                covariance, basis_rows, (((0,), (0,)), ((), ())),
                precision=lax.Precision.HIGHEST, preferred_element_type=jnp.float32,
            )
            image = lax.psum(partial_image, "col")
            basis_rows = _qr_step(image, "row")
        on_rows = not on_rows
    if not on_rows:
        swapped = lax.ppermute(basis_rows, ("row", "col"), _transpose_pairs(row_count, col_count))
        basis_rows = jnp.where(row_here == col_here, basis_rows, swapped)
    out_rows = array_size // (row_count * col_count)
    basis_out = lax.dynamic_slice_in_dim(basis_rows, col_here * out_rows, out_rows, 0) * math.sqrt(array_size)
    return (covariance, basis_out)


def solution(mesh):
    in_specs = (P("row", "bin", "col"), P("bin", "row", None), P("bin", "row", None), P())
    out_specs = (P("col", "row"), P(("row", "col"), None))
    return jax.shard_map(shards, mesh=mesh, in_specs=in_specs, out_specs=out_specs, check_vma=False)
```

time: 472 us -> 344 us (0.73)
  waiting for transfers between devices: 335 us -> 226 us
  matrix products: 55.6 us -> 31.6 us
  local copies, waits for them, and re-layouts: 2.96 us -> 9.52 us
    all_gather x5 -> x2, waiting for transfers between devices: 205 us -> 89.1 us  [the longest x1 47.2 us: shards(): right_rows = lax.all_gather(local_rows, ('bin', 'col'), axis=0, tiled=False)]
    psum x2 -> x4, waiting for transfers between devices: 77.4 us -> 136 us  [the longest x2 65.8 us: _qr_step(): gram_matrix = lax.psum(gram_part, gram_axis)]
    reduce_scatter x1 -> x0, waiting for transfers between devices: 52.8 us -> none  [shards(): lax.psum_scatter(bin_block, 'bin', scatter_dimension=0, tiled=True)]
    dot_general x5, matrix products: 44.8 us -> 25.4 us  [the longest x1 9.89 us: shards(): lax.dot_general(covariance, basis_rows, (((0,), (0,)), ((), ())), precisi...]
  transfers between devices with their start and end apart: 8 -> 7, of which waited for: 8 -> 6; matrix products, arithmetic and copies ran while one was open for 0% -> 1% of each run, Pallas kernels for 0% -> 0%
where the time goes in v1:
time: 344 us
  waiting for transfers between devices  226 us (66%)
  other arithmetic  48.2 us (14%)
  matrix products  31.6 us (9%)
  between operations  14.3 us (4%)
  blocking collectives  13.4 us (4%)
  local copies, waits for them, and re-layouts  9.52 us (3%)
    psum x2, waiting for transfers between devices, _qr_step(): gram_matrix = lax.psum(gram_part, gram_axis)  65.8 us
    all_gather x1, waiting for transfers between devices, shards(): right_rows = lax.all_gather(local_rows, ('bin', 'col'), axis=0, tiled=False)  47.2 us
    all_gather x1, waiting for transfers between devices, shards(): left_rows = lax.all_gather(swapped, ('bin', 'row'), axis=0, tiled=False)  42 us
    psum x1, waiting for transfers between devices, shards(): image = lax.psum(partial_image, 'col')  38.5 us
    psum x1, waiting for transfers between devices, shards(): image = lax.psum(partial_image, 'row')  32 us
    another operation x6, other arithmetic, _qr_step(): lower_factor = jnp.linalg.cholesky(gram_matrix)  24.8 us
    another operation x4, other arithmetic, _qr_step(): jax.scipy.linalg.solve_triangular(lower_factor, image.T, lower=True)  20.9 us
    psum x1, blocking collectives, shards(): projected = lax.psum(partial_proj, 'row').astype(jnp.bfloat16)  13.4 us
  transfers between devices with their start and end apart: 7, of which 6 were waited for; matrix products, arithmetic and copies ran while one was open for 1% of the time, Pallas kernels for 0%

profile of v1, /device:TPU:0, one launch (start us, length us, event | category | flops | bytes accessed | tf_op | source)
XLA Modules:
  0.0 343.7 jit_solution(17615606288194781556)
XLA Ops:
  7.2 0.0 copy-start
  7.2 0.0 all-gather.6.cloned.1.call-start
  7.2 2.2 fusion.21
  9.4 13.4 %psum.35 = bf16[8,128,16]{1,2,0:T(8,128)(2,1)S(1)} all-reduce(f32[8,128,16]{1,2,0:T(8,128)S(1)} %fusion.21), channel_id=1, replica_groups=mesh['bin'=2,'row'=4,'col'=4] {'row'}, use_global_device_ids=true, to_apply=%region_0.0 | all-reduce | flops 16384 | bytes 98304 | tf_op jit(solution)/shard_map/psum | solution.py:39
  22.9 0.6 fusion.1
  23.6 0.7 collective-permute-start
  24.3 0.8 broadcast_select_fusion
  25.0 0.0 all-gather.6.cloned.1.call-update
  25.0 0.0 all-gather.4.cloned.1.call-start
  25.1 0.8 copy.14
  25.9 0.0 all-gather.4.cloned.1.call-update
  25.9 0.0 all-reduce.5.cloned.1.call-start
  26.0 42.0 %all-gather.6.cloned.1.call-done = bf16[8192,128]{0,1:T(8,128)(2,1)} async-done(((bf16[1024,128]{0,1:T(8,128)(2,1)}), bf16[8192,128]{0,1:T(8,128)(2,1)}) %all-gather.6.cloned.1.call-update) | async-done | bytes 2097168 | tf_op jit(solution)/shard_map/all_gather | solution.py:52
  68.0 4.1 %copy.13 = bf16[8192,128]{1,0:T(8,128)(2,1)} copy(bf16[8192,128]{0,1:T(8,128)(2,1)} %all-gather.6.cloned.1.call-done) | data formatting | bytes 4194304 | tf_op jit(solution)/shard_map/all_gather | solution.py:52
  72.0 47.2 %all-gather.4.cloned.1.call-done = bf16[8,1024,128]{2,1,0:T(8,128)(2,1)} async-done(((bf16[1,1024,128]{2,1,0:T(8,128)(2,1)}), bf16[8,1024,128]{2,1,0:T(8,128)(2,1)}) %all-gather.4.cloned.1.call-update) | async-done | bytes 2097168 | tf_op jit(solution)/shard_map/all_gather | solution.py:48
  119.2 4.6 %bitcast_multiply_fusion = f32[1024,1024]{1,0:T(8,128)S(1)} fusion(bf16[8,1024,128]{2,1,0:T(8,128)(2,1)} %bitcast.53, bf16[8,1024,128]{2,1,0:T(8,128)(2,1)} %all-gather.4.cloned.1.call-done), kind=kOutput, calls=%fused_computation | convolution fusion | flops 2148532224 | bytes 8388608 | tf_op jit(solution)/shard_map/dot_general | solution.py:56
  123.8 0.0 copy-start.1
  123.8 2.0 copy-done.1
  125.8 5.3 %fusion.6 = f32[1024,128]{1,0:T(8,128)} fusion(f32[1024,1024]{1,0:T(8,128)S(1)} %bitcast_multiply_fusion, f32[4096,128]{1,0:T(8,128)} %param.10, s32[]{:T(128)S(6)} %select_n.19), kind=kOutput, calls=%fused_computation.8 | convolution fusion | flops 1610612736 | bytes 5242884 | tf_op jit(solution)/shard_map/dot_general | solution.py:64
  131.1 0.0 all-reduce.5.cloned.1.call-update
  131.1 0.0 all-reduce.7.cloned.1.call-start
  131.2 32.0 %all-reduce.5.cloned.1.call-done = f32[1024,128]{1,0:T(8,128)} async-done(((f32[1024,128]{1,0:T(8,128)}), f32[1024,128]{1,0:T(8,128)}) %all-reduce.5.cloned.1.call-update) | async-done | bytes 524304 | tf_op jit(solution)/shard_map/psum | solution.py:68
  163.2 2.8 fusion.18
  166.0 0.0 all-reduce.7.cloned.1.call-update
  166.0 0.2 all-reduce.9.cloned.1.call-start
  166.3 34.3 %all-reduce.7.cloned.1.call-done = f32[128,128]{0,1:T(8,128)} async-done(((f32[128,128]{0,1:T(8,128)}), f32[128,128]{0,1:T(8,128)}) %all-reduce.7.cloned.1.call-update) | async-done | bytes 65552 | tf_op jit(solution)/shard_map/psum | solution.py:24
  200.6 0.9 copy.16
  201.5 0.9 fusion.13
  202.4 11.7 %cholesky.44 = f32[128,128]{1,0:T(8,128)S(1)} custom-call(f32[128,128]{1,0:T(8,128)S(1)} %fusion.13), custom_call_target="Cholesky" | custom-call | tf_op jit(solution)/shard_map/jit(cholesky)/cholesky | solution.py:25
  214.2 0.6 compare_reduce_fusion.1
  214.8 0.7 fusion.8
  215.5 9.8 %custom-call.6 = f32[1,128,128]{1,2,0:T(8,128)S(1)} custom-call(f32[1,128,128]{2,1,0:T(8,128)S(1)} %fusion.8), custom_call_target="InvertDiagBlocksLowerTriangular" | custom-call | tf_op jit(solution)/shard_map/jit(_solve_triangular)/triangular_solve | solution.py:26
  225.3 1.7 fusion.4
  227.0 9.9 %fusion.19 = f32[1024,128]{1,0:T(8,128)} fusion(f32[1024,1024]{1,0:T(8,128)} %copy-done.1, f32[128,1024]{1,0:T(8,128)S(1)} %fusion.4), kind=kOutput, calls=%fused_computation.32 | convolution fusion | flops 1610612736 | bytes 5242880 | tf_op jit(solution)/shard_map/dot_general | solution.py:71
  236.9 0.0 all-reduce.9.cloned.1.call-update
  236.9 0.0 all-reduce.11.cloned.1.call-start
  236.9 38.5 %all-reduce.9.cloned.1.call-done = f32[1024,128]{1,0:T(8,128)} async-done(((f32[1024,128]{1,0:T(8,128)}), f32[1024,128]{1,0:T(8,128)}) %all-reduce.9.cloned.1.call-update) | async-done | bytes 524304 | tf_op jit(solution)/shard_map/psum | solution.py:75
  275.4 2.8 fusion.20
  278.2 0.0 all-reduce.11.cloned.1.call-update
  278.2 31.5 %all-reduce.11.cloned.1.call-done = f32[128,128]{0,1:T(8,128)} async-done(((f32[128,128]{0,1:T(8,128)}), f32[128,128]{0,1:T(8,128)}) %all-reduce.11.cloned.1.call-update) | async-done | bytes 65552 | tf_op jit(solution)/shard_map/psum | solution.py:24
  309.7 0.9 copy.18
  310.7 0.9 fusion.11
  311.5 11.7 %cholesky.55 = f32[128,128]{1,0:T(8,128)S(1)} custom-call(f32[128,128]{1,0:T(8,128)S(1)} %fusion.11), custom_call_target="Cholesky" | custom-call | tf_op jit(solution)/shard_map/jit(cholesky)/cholesky | solution.py:25
  323.3 0.6 compare_reduce_fusion
  323.9 0.7 fusion.9
  324.6 9.8 %custom-call.7 = f32[1,128,128]{1,2,0:T(8,128)S(1)} custom-call(f32[1,128,128]{2,1,0:T(8,128)S(1)} %fusion.9), custom_call_target="InvertDiagBlocksLowerTriangular" | custom-call | tf_op jit(solution)/shard_map/jit(_solve_triangular)/triangular_solve | solution.py:26
  334.4 1.7 fusion.2
  336.1 0.8 copy.19
  (7 shorter events, 0.1 us)
Async XLA Ops:
  7.2 15.7 %copy-start = (bf16[8,1024,128]{2,1,0:T(8,128)(2,1)S(1)}, bf16[8,1024,128]{2,1,0:T(8,128)(2,1)}, u32[]{:S(2)}) copy-start(bf16[8,1024,128]{2,1,0:T(8,128)(2,1)} %param.9) | copy-start | bytes 6291460
  7.2 15.7 %copy-start.2 = (bf16[1024,8,16]{0,2,1:T(8,128)(2,1)S(1)}, bf16[1024,8,16]{0,2,1:T(8,128)(2,1)}, u32[]{:S(2)}) copy-start(bf16[1024,8,16]{0,2,1:T(8,128)(2,1)} %param.7) | copy-start | bytes 786436
  7.2 60.8 %all-gather.6.cloned.1.call-start = ((), (), s32[]{:S(2)}) async-start(), calls=%async_computation.5 | async-start | bytes 2359296 | tf_op jit(solution)/shard_map/all_gather | solution.py:52
  23.6 0.7 collective-permute-start
  25.0 94.2 %all-gather.4.cloned.1.call-start = ((), (), s32[]{:S(2)}) async-start(), calls=%async_computation | async-start | bytes 2359296 | tf_op jit(solution)/shard_map/all_gather | solution.py:48
  25.9 137.3 %all-reduce.5.cloned.1.call-start = ((), (), s32[]{:S(2)}) async-start(), calls=%async_computation.1 | async-start | bytes 1048576 | tf_op jit(solution)/shard_map/psum | solution.py:68
  123.8 2.0 copy-start.1
  131.1 69.5 %all-reduce.7.cloned.1.call-start = ((), (), s32[]{:S(2)}) async-start(), calls=%async_computation.2 | async-start | bytes 131072 | tf_op jit(solution)/shard_map/psum | solution.py:24
  166.0 109.3 %all-reduce.9.cloned.1.call-start = ((), (), s32[]{:S(2)}) async-start(), calls=%async_computation.3 | async-start | bytes 1048576 | tf_op jit(solution)/shard_map/psum | solution.py:75
  236.9 72.9 %all-reduce.11.cloned.1.call-start = ((), (), s32[]{:S(2)}) async-start(), calls=%async_computation.4 | async-start | bytes 131072 | tf_op jit(solution)/shard_map/psum | solution.py:24
Sparse Core Ops, SparseCore 0:
  25.2 42.7 all-gather.5
  70.1 49.0 all-gather.3
  131.2 31.9 all-reduce.4
  166.2 34.3 all-reduce.6
  237.0 38.3 all-reduce.8
  278.4 31.3 all-reduce.10

commit v2 on v1

--- a/solution.py
+++ b/solution.py
@@ -17,11 +17,40 @@
     ]
 
 
+def _butterfly_sum(x, axis):
+    count = lax.axis_size(axis)
+    if count & (count - 1):
+        return lax.psum(x, axis)
+    step = 1
+    while step < count:
+        x = x + lax.ppermute(x, axis, [(i, i ^ step) for i in range(count)])
+        step *= 2
+    return x
+
+
+def _butterfly_gather(x, axes):
+    x = x[None]
+    for axis in axes:
+        count = lax.axis_size(axis)
+        if count & (count - 1):
+            x = lax.all_gather(x, axis, axis=0, tiled=False)
+            x = x.reshape((-1,) + x.shape[2:])
+            continue
+        here = lax.axis_index(axis)
+        step = 1
+        while step < count:
+            other = lax.ppermute(x, axis, [(i, i ^ step) for i in range(count)])
+            low = (here & step) == 0
+            x = jnp.where(low, jnp.concatenate([x, other], 0), jnp.concatenate([other, x], 0))
+            step *= 2
+    return x
+
+
 def _qr_step(image, gram_axis):
     gram_part = jnp.dot(
         image.T, image, precision=lax.Precision.HIGHEST, preferred_element_type=jnp.float32
     )
-    gram_matrix = lax.psum(gram_part, gram_axis)
+    gram_matrix = _butterfly_sum(gram_part, gram_axis)
     lower_factor = jnp.linalg.cholesky(gram_matrix)
     return jax.scipy.linalg.solve_triangular(lower_factor, image.T, lower=True).T
 
@@ -36,7 +65,7 @@
     partial_proj = jnp.einsum(
         "mbs,bmr->brs", snapshots, focus_in, preferred_element_type=jnp.float32
     )
-    projected = lax.psum(partial_proj, "row").astype(jnp.bfloat16)
+    projected = _butterfly_sum(partial_proj, "row").astype(jnp.bfloat16)
     lifted = jnp.einsum("bmr,brs->mbs", focus_out, projected, preferred_element_type=jnp.float32)
     focused = (snapshots.astype(jnp.float32) + lifted).astype(jnp.bfloat16)
     columns = bins_here * snaps_here
@@ -45,11 +74,11 @@
     col_block = array_size // col_count
     scaling = 1.0 / (columns * col_count * bin_count)
 
-    right_rows = lax.all_gather(local_rows, ("bin", "col"), axis=0, tiled=False)
+    right_rows = _butterfly_gather(local_rows, ("bin", "col"))
     if row_count == col_count:
         swapped = lax.ppermute(local_rows, ("row", "col"), _transpose_pairs(row_count, col_count))
         swapped = jnp.where(row_here == col_here, local_rows, swapped)
-        left_rows = lax.all_gather(swapped, ("bin", "row"), axis=0, tiled=False)
+        left_rows = _butterfly_gather(swapped, ("bin", "row"))
     else:
         every_row = lax.all_gather(right_rows, "row", axis=1, tiled=True)
         left_rows = lax.dynamic_slice_in_dim(every_row, col_here * col_block, col_block, 1)
@@ -65,14 +94,14 @@
                 covariance, basis_rows, precision=lax.Precision.HIGHEST,
                 preferred_element_type=jnp.float32,
             )
-            image = lax.psum(partial_image, "row")
+            image = _butterfly_sum(partial_image, "row")
             basis_rows = _qr_step(image, "col")
         else:
             partial_image = lax.dot_general(
                 covariance, basis_rows, (((0,), (0,)), ((), ())),
                 precision=lax.Precision.HIGHEST, preferred_element_type=jnp.float32,
             )
-            image = lax.psum(partial_image, "col")
+            image = _butterfly_sum(partial_image, "col")
             basis_rows = _qr_step(image, "row")
         on_rows = not on_rows
     if not on_rows:

time: 344 us -> 227 us (0.66)
  waiting for transfers between devices: 226 us -> 122 us
  starting transfers between devices: 1.11 us -> 25.3 us
  between operations: 14.3 us -> 0.89 us
  blocking collectives: 13.4 us -> 0 us
  local copies, waits for them, and re-layouts: 9.52 us -> 1.3 us
  matrix products: 31.6 us -> 24.8 us
  other arithmetic: 48.2 us -> 51.8 us
    psum x4 -> x0, waiting for transfers between devices: 136 us -> none  [the longest x2 65.8 us: _qr_step(): gram_matrix = lax.psum(gram_part, gram_axis)]
    ppermute x0 -> x16, waiting for transfers between devices: none -> 122 us  [the longest x10 64.1 us: _butterfly_sum(): x = x + lax.ppermute(x, axis, [(i, i ^ step) for i in range(count)])]
    all_gather x2 -> x0, waiting for transfers between devices: 89.1 us -> none  [the longest x1 47.2 us: shards(): right_rows = lax.all_gather(local_rows, ('bin', 'col'), axis=0, tiled=False)]
    ppermute x0 -> x16, starting transfers between devices: none -> 24.6 us  [the longest x6 16.7 us: _butterfly_gather(): other = lax.ppermute(x, axis, [(i, i ^ step) for i in range(count)])]
    psum x1 -> x0, blocking collectives: 13.4 us -> none  [shards(): projected = lax.psum(partial_proj, 'row').astype(jnp.bfloat16)]
    select_n x1 -> x4, other arithmetic: 0.75 us -> 5.85 us  [_butterfly_gather(): jnp.where(low, jnp.concatenate([x, other], 0), jnp.concatenate([other, x]...]
    all_gather x1 -> x0, local copies, waits for them, and re-layouts: 4.06 us -> none  [shards(): left_rows = lax.all_gather(swapped, ('bin', 'row'), axis=0, tiled=False)]
    dot_general x2, matrix products: 5.66 us -> 2.03 us  [_qr_step(): jnp.dot(image.T, image, precision=lax.Precision.HIGHEST, preferred_elemen...]
  transfers between devices with their start and end apart: 7 -> 17, of which waited for: 6 -> 14; matrix products, arithmetic and copies ran while one was open for 1% -> 3% of each run, Pallas kernels for 0% -> 0%
where the time goes in v2:
time: 227 us
  waiting for transfers between devices  122 us (54%)
  other arithmetic  51.8 us (23%)
  starting transfers between devices  25.3 us (11%)
  matrix products  24.8 us (11%)
    ppermute x10, waiting for transfers between devices, _butterfly_sum(): x = x + lax.ppermute(x, axis, [(i, i ^ step) for i in range(count)])  64.1 us
    ppermute x6, waiting for transfers between devices, _butterfly_gather(): other = lax.ppermute(x, axis, [(i, i ^ step) for i in range(count)])  58.4 us
    another operation x6, other arithmetic, _qr_step(): lower_factor = jnp.linalg.cholesky(gram_matrix)  24.8 us
    another operation x4, other arithmetic, _qr_step(): jax.scipy.linalg.solve_triangular(lower_factor, image.T, lower=True)  21 us
    ppermute x6, starting transfers between devices, _butterfly_gather(): other = lax.ppermute(x, axis, [(i, i ^ step) for i in range(count)])  16.7 us
    dot_general x1, matrix products, shards(): lax.dot_general(covariance, basis_rows, (((0,), (0,)), ((), ())), precisi...  8.48 us
    ppermute x10, starting transfers between devices, _butterfly_sum(): x = x + lax.ppermute(x, axis, [(i, i ^ step) for i in range(count)])  7.9 us
    select_n x4, other arithmetic, _butterfly_gather(): jnp.where(low, jnp.concatenate([x, other], 0), jnp.concatenate([other, x]...  5.85 us
  transfers between devices with their start and end apart: 17, of which 14 were waited for; matrix products, arithmetic and copies ran while one was open for 3% of the time, Pallas kernels for 0%

profile of v2, /device:TPU:0, one launch (start us, length us, event | category | flops | bytes accessed | tf_op | source)
XLA Modules:
  0.0 226.6 jit_solution(15521732650220855266)
XLA Ops:
  0.7 2.2 fusion.37
  2.9 0.6 collective-permute-start
  3.4 0.9 collective-permute-done
  4.3 2.9 %collective-permute-start.1 = (f32[8,128,16]{1,2,0:T(8,128)S(1)}, f32[8,128,16]{1,2,0:T(8,128)S(1)}, u32[]{:S(2)}, u32[]{:S(2)}) collective-permute-start(f32[8,128,16]{1,2,0:T(8,128)S(1)} %add.48), channel_id=1, source_target_pairs={{0,8},{4,12},{8,0},{12,4},{1,9},{5,13},{9,1},{13,5},{2,10},{6,14},... | collective-permute-start | bytes 196616 | tf_op jit(solution)/shard_map/ppermute | solution.py:26
  7.2 2.4 %collective-permute-done.1 = f32[8,128,16]{1,2,0:T(8,128)S(1)} collective-permute-done((f32[8,128,16]{1,2,0:T(8,128)S(1)}, f32[8,128,16]{1,2,0:T(8,128)S(1)}, u32[]{:S(2)}, u32[]{:S(2)}) %collective-permute-start.1) | collective-permute-done | bytes 65568 | tf_op jit(solution)/shard_map/ppermute | solution.py:26
  9.6 0.7 fusion.13
  10.3 0.2 copy.7
  10.5 0.7 collective-permute-start.2
  11.2 0.2 copy.9
  11.4 1.9 collective-permute-start.6
  13.3 0.2 collective-permute-start.3
  13.6 4.7 %collective-permute-done.6 = bf16[1,1024,128]{2,1,0:T(8,128)(2,1)S(1)} collective-permute-done((bf16[1,1024,128]{2,1,0:T(8,128)(2,1)S(1)}, bf16[1,1024,128]{2,1,0:T(8,128)(2,1)S(1)}, u32[]{:S(2)}, u32[]{:S(2)}) %collective-permute-start.6) | collective-permute-done | bytes 262176 | tf_op jit(solution)/shard_map/ppermute | solution.py:42
  18.4 5.2 %collective-permute-start.7 = (bf16[2,1024,128]{2,1,0:T(8,128)(2,1)S(1)}, bf16[2,1024,128]{2,1,0:T(8,128)(2,1)}, u32[]{:S(2)}, u32[]{:S(2)}) collective-permute-start(bf16[2,1024,128]{2,1,0:T(8,128)(2,1)S(1)} %maximum_select_fusion.7), channel_id=1, source_target_pairs={{0,1},{1,0},{2,3},{3,2},{4,5},{5,4},{6,7},{7,6},{8,9},{9,8},{10,11... | collective-permute-start | bytes 1572872 | tf_op jit(solution)/shard_map/ppermute | solution.py:42
  23.5 0.5 collective-permute-done.3
  24.0 1.1 maximum_select_fusion.6
  25.1 2.5 %collective-permute-start.4 = (bf16[2,1024,128]{2,1,0:T(8,128)(2,1)S(1)}, bf16[2,1024,128]{2,1,0:T(8,128)(2,1)}, u32[]{:S(2)}, u32[]{:S(2)}) collective-permute-start(bf16[2,1024,128]{2,1,0:T(8,128)(2,1)S(1)} %maximum_select_fusion.6), channel_id=1, source_target_pairs={{0,4},{4,0},{8,12},{12,8},{1,5},{5,1},{9,13},{13,9},{2,6},{6,2},{1... | collective-permute-start | bytes 1572872 | tf_op jit(solution)/shard_map/ppermute | solution.py:42
  27.6 10.1 %collective-permute-done.7 = bf16[2,1024,128]{2,1,0:T(8,128)(2,1)} collective-permute-done((bf16[2,1024,128]{2,1,0:T(8,128)(2,1)S(1)}, bf16[2,1024,128]{2,1,0:T(8,128)(2,1)}, u32[]{:S(2)}, u32[]{:S(2)}) %collective-permute-start.7) | collective-permute-done | bytes 524320 | tf_op jit(solution)/shard_map/ppermute | solution.py:42
  37.7 2.3 %maximum_select_fusion.5 = bf16[4,1024,128]{2,1,0:T(8,128)(2,1)} fusion(bf16[2,1024,128]{2,1,0:T(8,128)(2,1)} %collective-permute-done.7, bf16[2,1024,128]{2,1,0:T(8,128)(2,1)S(1)} %maximum_select_fusion.7, pred[]{:T(512)S(6)} %eq.24), kind=kLoop, calls=%fused_computation.19 | loop fusion | flops 1572864 | bytes 2097153 | tf_op jit(solution)/shard_map/jit(_where)/select_n | solution.py:44
  40.0 6.9 %collective-permute-start.8 = (bf16[4,1024,128]{2,1,0:T(8,128)(2,1)}, bf16[4,1024,128]{2,1,0:T(8,128)(2,1)}, u32[]{:S(2)}, u32[]{:S(2)}) collective-permute-start(bf16[4,1024,128]{2,1,0:T(8,128)(2,1)} %maximum_select_fusion.5), channel_id=1, source_target_pairs={{0,2},{1,3},{2,0},{3,1},{4,6},{5,7},{6,4},{7,5},{8,10},{9,11},{10,... | collective-permute-start | bytes 3145736 | tf_op jit(solution)/shard_map/ppermute | solution.py:42
  46.9 2.3 %maximum_select_fusion.4 = bf16[4,1024,128]{2,1,0:T(8,128)(2,1)} fusion(bf16[2,1024,128]{2,1,0:T(8,128)(2,1)} %collective-permute-done.4, bf16[2,1024,128]{2,1,0:T(8,128)(2,1)S(1)} %maximum_select_fusion.6, pred[]{:T(512)S(6)} %eq.20), kind=kLoop, calls=%fused_computation.18 | loop fusion | flops 1572864 | bytes 2097153 | tf_op jit(solution)/shard_map/jit(_where)/select_n | solution.py:44
  49.3 43.1 %collective-permute-done.8 = bf16[4,1024,128]{2,1,0:T(8,128)(2,1)} collective-permute-done((bf16[4,1024,128]{2,1,0:T(8,128)(2,1)}, bf16[4,1024,128]{2,1,0:T(8,128)(2,1)}, u32[]{:S(2)}, u32[]{:S(2)}) %collective-permute-start.8) | collective-permute-done | bytes 1048608 | tf_op jit(solution)/shard_map/ppermute | solution.py:42
  92.4 5.3 %bitcast_multiply_fusion = f32[1024,1024]{1,0:T(8,128)S(1)} fusion(bf16[4,1024,128]{2,1,0:T(8,128)(2,1)S(1)} %collective-permute-done.5, bf16[4,1024,128]{2,1,0:T(8,128)(2,1)} %maximum_select_fusion.4, bf16[4,1024,128]{2,1,0:T(8,128)(2,1)} %collective-permute-done.8, bf16[4,1024,128]{2,1,0:T(8,128)(2,1)} %maximum_select_fusion.5, pred[]{:T(512)S(6)} %eq.23, ...), kind=kOutput, calls=%fused_computation | convolution fusion | flops 2154823680 | bytes 8388610 | tf_op jit(solution)/shard_map/dot_general | solution.py:85
  97.7 4.9 %fusion.18 = f32[1024,128]{1,0:T(8,128)S(1)} fusion(f32[1024,1024]{1,0:T(8,128)S(1)} %bitcast_multiply_fusion, f32[4096,128]{1,0:T(8,128)} %param.10, s32[]{:T(128)S(6)} %select_n.70), kind=kOutput, calls=%fused_computation.26 | convolution fusion | flops 1610612736 | bytes 5242884 | tf_op jit(solution)/shard_map/dot_general | solution.py:93
  102.7 1.8 collective-permute-done.9
  104.7 14.0 %collective-permute-done.10 = f32[1024,128]{1,0:T(8,128)S(1)} collective-permute-done((f32[1024,128]{1,0:T(8,128)S(1)}, f32[1024,128]{1,0:T(8,128)S(1)}, u32[]{:S(2)}, u32[]{:S(2)}) %collective-permute-start.10) | collective-permute-done | bytes 524320 | tf_op jit(solution)/shard_map/ppermute | solution.py:26
  118.6 1.0 fusion.24
  119.7 4.3 %collective-permute-done.11 = f32[128,128]{0,1:T(8,128)S(1)} collective-permute-done((f32[128,128]{0,1:T(8,128)S(1)}, f32[128,128]{0,1:T(8,128)S(1)}, u32[]{:S(2)}, u32[]{:S(2)}) %collective-permute-start.11) | collective-permute-done | bytes 65568 | tf_op jit(solution)/shard_map/ppermute | solution.py:26
  124.0 1.3 collective-permute-start.12
  125.3 4.4 %collective-permute-done.12 = f32[128,128]{0,1:T(8,128)S(1)} collective-permute-done((f32[128,128]{0,1:T(8,128)S(1)}, f32[128,128]{0,1:T(8,128)S(1)}, u32[]{:S(2)}, u32[]{:S(2)}) %collective-permute-start.12) | collective-permute-done | bytes 65568 | tf_op jit(solution)/shard_map/ppermute | solution.py:26
  129.8 11.7 %cholesky.44 = f32[128,128]{1,0:T(8,128)S(1)} custom-call(f32[128,128]{1,0:T(8,128)S(1)} %fusion.31), custom_call_target="Cholesky" | custom-call | tf_op jit(solution)/shard_map/jit(cholesky)/cholesky | solution.py:54
  141.5 0.6 compare_reduce_fusion.1
  142.2 0.7 fusion.26
  142.8 9.8 %custom-call.6 = f32[1,128,128]{1,2,0:T(8,128)S(1)} custom-call(f32[1,128,128]{2,1,0:T(8,128)S(1)} %fusion.26), custom_call_target="InvertDiagBlocksLowerTriangular" | custom-call | tf_op jit(solution)/shard_map/jit(_solve_triangular)/triangular_solve | solution.py:55
  152.7 0.6 fusion.16
  153.3 8.5 %fusion.36 = f32[1024,128]{1,0:T(8,128)S(1)} fusion(f32[1024,1024]{1,0:T(8,128)} %copy-done.1, f32[128,1024]{1,0:T(8,128)S(1)} %fusion.16), kind=kOutput, calls=%fused_computation.56 | convolution fusion | flops 1610612736 | bytes 5242880 | tf_op jit(solution)/shard_map/dot_general | solution.py:100
  161.9 11.1 %collective-permute-done.13 = f32[1024,128]{1,0:T(8,128)S(1)} collective-permute-done((f32[1024,128]{1,0:T(8,128)S(1)}, f32[1024,128]{1,0:T(8,128)S(1)}, u32[]{:S(2)}, u32[]{:S(2)}) %collective-permute-start.13) | collective-permute-done | bytes 524320 | tf_op jit(solution)/shard_map/ppermute | solution.py:26
  173.0 1.9 collective-permute-start.14
  174.9 20.6 %collective-permute-done.14 = f32[1024,128]{1,0:T(8,128)S(1)} collective-permute-done((f32[1024,128]{1,0:T(8,128)S(1)}, f32[1024,128]{1,0:T(8,128)S(1)}, u32[]{:S(2)}, u32[]{:S(2)}) %collective-permute-start.14) | collective-permute-done | bytes 524320 | tf_op jit(solution)/shard_map/ppermute | solution.py:26
  195.5 1.0 fusion.21
  196.6 1.2 collective-permute-done.15
  197.8 0.9 collective-permute-start.16
  198.7 3.4 %collective-permute-done.16 = f32[128,128]{0,1:T(8,128)S(1)} collective-permute-done((f32[128,128]{0,1:T(8,128)S(1)}, f32[128,128]{0,1:T(8,128)S(1)}, u32[]{:S(2)}, u32[]{:S(2)}) %collective-permute-start.16) | collective-permute-done | bytes 65568 | tf_op jit(solution)/shard_map/ppermute | solution.py:26
  202.3 11.7 %cholesky.55 = f32[128,128]{1,0:T(8,128)S(1)} custom-call(f32[128,128]{1,0:T(8,128)S(1)} %fusion.29), custom_call_target="Cholesky" | custom-call | tf_op jit(solution)/shard_map/jit(cholesky)/cholesky | solution.py:54
  214.0 0.6 compare_reduce_fusion
  214.7 0.7 fusion.27
  215.3 9.8 %custom-call.7 = f32[1,128,128]{1,2,0:T(8,128)S(1)} custom-call(f32[1,128,128]{2,1,0:T(8,128)S(1)} %fusion.27), custom_call_target="InvertDiagBlocksLowerTriangular" | custom-call | tf_op jit(solution)/shard_map/jit(_solve_triangular)/triangular_solve | solution.py:55
  225.1 0.6 fusion.14
  225.8 0.8 copy.17
  (31 shorter events, 1.0 us)
Async XLA Ops:
  0.6 9.0 %copy-start = (bf16[8,1024,128]{2,1,0:T(8,128)(2,1)S(1)}, bf16[8,1024,128]{2,1,0:T(8,128)(2,1)}, u32[]{:S(2)}) copy-start(bf16[8,1024,128]{2,1,0:T(8,128)(2,1)} %param.9) | copy-start | bytes 6291460
  0.6 9.0 %copy-start.2 = (bf16[1024,8,16]{0,2,1:T(8,128)(2,1)S(1)}, bf16[1024,8,16]{0,2,1:T(8,128)(2,1)}, u32[]{:S(2)}) copy-start(bf16[1024,8,16]{0,2,1:T(8,128)(2,1)} %param.7) | copy-start | bytes 786436
  2.9 1.5 collective-permute-start
  4.3 5.3 %collective-permute-start.1 = (f32[8,128,16]{1,2,0:T(8,128)S(1)}, f32[8,128,16]{1,2,0:T(8,128)S(1)}, u32[]{:S(2)}, u32[]{:S(2)}) collective-permute-start(f32[8,128,16]{1,2,0:T(8,128)S(1)} %add.48), channel_id=1, source_target_pairs={{0,8},{4,12},{8,0},{12,4},{1,9},{5,13},{9,1},{13,5},{2,10},{6,14},... | collective-permute-start | bytes 196616 | tf_op jit(solution)/shard_map/ppermute | solution.py:26
  10.5 2.8 %collective-permute-start.2 = (bf16[1024,128]{1,0:T(8,128)(2,1)S(1)}, bf16[1024,128]{1,0:T(8,128)(2,1)S(1)}, u32[]{:S(2)}, u32[]{:S(2)}) collective-permute-start(bf16[1024,128]{1,0:T(8,128)(2,1)S(1)} %copy.7), channel_id=1, source_target_pairs={{1,4},{2,8},{3,12},{4,1},{6,9},{7,13},{8,2},{9,6},{11,14},{12,3},{... | collective-permute-start | bytes 786440 | tf_op jit(solution)/shard_map/ppermute | solution.py:79
  11.4 6.9 %collective-permute-start.6 = (bf16[1,1024,128]{2,1,0:T(8,128)(2,1)S(1)}, bf16[1,1024,128]{2,1,0:T(8,128)(2,1)S(1)}, u32[]{:S(2)}, u32[]{:S(2)}) collective-permute-start(bf16[1,1024,128]{2,1,0:T(8,128)(2,1)S(1)} %copy.9), channel_id=1, source_target_pairs={{0,16},{16,0},{1,17},{17,1},{2,18},{18,2},{3,19},{19,3},{4,20},{20... | collective-permute-start | bytes 786440 | tf_op jit(solution)/shard_map/ppermute | solution.py:42
  13.3 10.7 %collective-permute-start.3 = (bf16[1,1024,128]{2,1,0:T(8,128)(2,1)S(1)}, bf16[1,1024,128]{2,1,0:T(8,128)(2,1)}, u32[]{:S(2)}, u32[]{:S(2)}) collective-permute-start(bf16[1,1024,128]{2,1,0:T(8,128)(2,1)S(1)} %select_bitcast_fusion), channel_id=1, source_target_pairs={{0,16},{16,0},{1,17},{17,1},{2,18},{18,2},{3,19},{19,3},{4,20},{20... | collective-permute-start | bytes 786440 | tf_op jit(solution)/shard_map/ppermute | solution.py:42
  18.4 19.3 %collective-permute-start.7 = (bf16[2,1024,128]{2,1,0:T(8,128)(2,1)S(1)}, bf16[2,1024,128]{2,1,0:T(8,128)(2,1)}, u32[]{:S(2)}, u32[]{:S(2)}) collective-permute-start(bf16[2,1024,128]{2,1,0:T(8,128)(2,1)S(1)} %maximum_select_fusion.7), channel_id=1, source_target_pairs={{0,1},{1,0},{2,3},{3,2},{4,5},{5,4},{6,7},{7,6},{8,9},{9,8},{10,11... | collective-permute-start | bytes 1572872 | tf_op jit(solution)/shard_map/ppermute | solution.py:42
  25.1 21.8 %collective-permute-start.4 = (bf16[2,1024,128]{2,1,0:T(8,128)(2,1)S(1)}, bf16[2,1024,128]{2,1,0:T(8,128)(2,1)}, u32[]{:S(2)}, u32[]{:S(2)}) collective-permute-start(bf16[2,1024,128]{2,1,0:T(8,128)(2,1)S(1)} %maximum_select_fusion.6), channel_id=1, source_target_pairs={{0,4},{4,0},{8,12},{12,8},{1,5},{5,1},{9,13},{13,9},{2,6},{6,2},{1... | collective-permute-start | bytes 1572872 | tf_op jit(solution)/shard_map/ppermute | solution.py:42
  40.0 52.3 %collective-permute-start.8 = (bf16[4,1024,128]{2,1,0:T(8,128)(2,1)}, bf16[4,1024,128]{2,1,0:T(8,128)(2,1)}, u32[]{:S(2)}, u32[]{:S(2)}) collective-permute-start(bf16[4,1024,128]{2,1,0:T(8,128)(2,1)} %maximum_select_fusion.5), channel_id=1, source_target_pairs={{0,2},{1,3},{2,0},{3,1},{4,6},{5,7},{6,4},{7,5},{8,10},{9,11},{10,... | collective-permute-start | bytes 3145736 | tf_op jit(solution)/shard_map/ppermute | solution.py:42
  49.3 43.1 %collective-permute-start.5 = (bf16[4,1024,128]{2,1,0:T(8,128)(2,1)}, bf16[4,1024,128]{2,1,0:T(8,128)(2,1)S(1)}, u32[]{:S(2)}, u32[]{:S(2)}) collective-permute-start(bf16[4,1024,128]{2,1,0:T(8,128)(2,1)} %maximum_select_fusion.4), channel_id=1, source_target_pairs={{0,8},{4,12},{8,0},{12,4},{1,9},{5,13},{9,1},{13,5},{2,10},{6,14},... | collective-permute-start | bytes 3145736 | tf_op jit(solution)/shard_map/ppermute | solution.py:42
  97.7 4.9 %copy-start.1 = (f32[1024,1024]{1,0:T(8,128)}, f32[1024,1024]{1,0:T(8,128)S(1)}, u32[]{:S(2)}) copy-start(f32[1024,1024]{1,0:T(8,128)S(1)} %bitcast_multiply_fusion) | copy-start | bytes 12582916
  102.6 2.0 collective-permute-start.9
  104.6 14.0 %collective-permute-start.10 = (f32[1024,128]{1,0:T(8,128)S(1)}, f32[1024,128]{1,0:T(8,128)S(1)}, u32[]{:S(2)}, u32[]{:S(2)}) collective-permute-start(f32[1024,128]{1,0:T(8,128)S(1)} %add.52), channel_id=1, source_target_pairs={{0,8},{4,12},{8,0},{12,4},{1,9},{5,13},{9,1},{13,5},{2,10},{6,14},... | collective-permute-start | bytes 1572872 | tf_op jit(solution)/shard_map/ppermute | solution.py:26
  119.7 4.3 %collective-permute-start.11 = (f32[128,128]{0,1:T(8,128)S(1)}, f32[128,128]{0,1:T(8,128)S(1)}, u32[]{:S(2)}, u32[]{:S(2)}) collective-permute-start(f32[128,128]{0,1:T(8,128)S(1)} %fusion.24), channel_id=1, source_target_pairs={{0,1},{1,0},{2,3},{3,2},{4,5},{5,4},{6,7},{7,6},{8,9},{9,8},{10,11... | collective-permute-start | bytes 196616 | tf_op jit(solution)/shard_map/ppermute | solution.py:26
  124.0 5.7 %collective-permute-start.12 = (f32[128,128]{0,1:T(8,128)S(1)}, f32[128,128]{0,1:T(8,128)S(1)}, u32[]{:S(2)}, u32[]{:S(2)}) collective-permute-start(f32[128,128]{0,1:T(8,128)S(1)} %add.54), channel_id=1, source_target_pairs={{0,2},{1,3},{2,0},{3,1},{4,6},{5,7},{6,4},{7,5},{8,10},{9,11},{10,... | collective-permute-start | bytes 196616 | tf_op jit(solution)/shard_map/ppermute | solution.py:26
  161.8 11.1 %collective-permute-start.13 = (f32[1024,128]{1,0:T(8,128)S(1)}, f32[1024,128]{1,0:T(8,128)S(1)}, u32[]{:S(2)}, u32[]{:S(2)}) collective-permute-start(f32[1024,128]{1,0:T(8,128)S(1)} %fusion.36), channel_id=1, source_target_pairs={{0,1},{1,0},{2,3},{3,2},{4,5},{5,4},{6,7},{7,6},{8,9},{9,8},{10,11... | collective-permute-start | bytes 1572872 | tf_op jit(solution)/shard_map/ppermute | solution.py:26
  173.0 22.4 %collective-permute-start.14 = (f32[1024,128]{1,0:T(8,128)S(1)}, f32[1024,128]{1,0:T(8,128)S(1)}, u32[]{:S(2)}, u32[]{:S(2)}) collective-permute-start(f32[1024,128]{1,0:T(8,128)S(1)} %add.56), channel_id=1, source_target_pairs={{0,2},{1,3},{2,0},{3,1},{4,6},{5,7},{6,4},{7,5},{8,10},{9,11},{10,... | collective-permute-start | bytes 1572872 | tf_op jit(solution)/shard_map/ppermute | solution.py:26
  196.5 1.3 collective-permute-start.15
  197.8 4.3 %collective-permute-start.16 = (f32[128,128]{0,1:T(8,128)S(1)}, f32[128,128]{0,1:T(8,128)S(1)}, u32[]{:S(2)}, u32[]{:S(2)}) collective-permute-start(f32[128,128]{0,1:T(8,128)S(1)} %add.58), channel_id=1, source_target_pairs={{0,8},{4,12},{8,0},{12,4},{1,9},{5,13},{9,1},{13,5},{2,10},{6,14},... | collective-permute-start | bytes 196616 | tf_op jit(solution)/shard_map/ppermute | solution.py:26

commit v3 on v2

--- a/solution.py
+++ b/solution.py
@@ -28,6 +28,15 @@
     return x
 
 
+def _bits(count, far_first):
+    steps = []
+    step = 1
+    while step < count:
+        steps.append(step)
+        step *= 2
+    return steps[::-1] if far_first else steps
+
+
 def _butterfly_gather(x, axes):
     x = x[None]
     for axis in axes:
@@ -37,12 +46,29 @@
             x = x.reshape((-1,) + x.shape[2:])
             continue
         here = lax.axis_index(axis)
-        step = 1
-        while step < count:
+        for step in _bits(count, True):
             other = lax.ppermute(x, axis, [(i, i ^ step) for i in range(count)])
             low = (here & step) == 0
             x = jnp.where(low, jnp.concatenate([x, other], 0), jnp.concatenate([other, x], 0))
-            step *= 2
+    return x
+
+
+def _halving_sum(x, axis):
+    count = lax.axis_size(axis)
+    if count & (count - 1) or x.shape[0] % count:
+        return _butterfly_sum(x, axis)
+    here = lax.axis_index(axis)
+    steps = _bits(count, False)
+    for step in steps:
+        half = x.shape[0] // 2
+        low = (here & step) == 0
+        keep = jnp.where(low, x[:half], x[half:])
+        give = jnp.where(low, x[half:], x[:half])
+        x = keep + lax.ppermute(give, axis, [(i, i ^ step) for i in range(count)])
+    for step in steps[::-1]:
+        low = (here & step) == 0
+        other = lax.ppermute(x, axis, [(i, i ^ step) for i in range(count)])
+        x = jnp.where(low, jnp.concatenate([x, other], 0), jnp.concatenate([other, x], 0))
     return x
 
 
@@ -101,7 +127,7 @@
                 covariance, basis_rows, (((0,), (0,)), ((), ())),
                 precision=lax.Precision.HIGHEST, preferred_element_type=jnp.float32,
             )
-            image = _butterfly_sum(partial_image, "col")
+            image = _halving_sum(partial_image, "col")
             basis_rows = _qr_step(image, "row")
         on_rows = not on_rows
     if not on_rows:

time: 227 us -> 213 us (0.938)
  waiting for transfers between devices: 122 us -> 107 us
    ppermute x10 -> x8, waiting for transfers between devices: 64.1 us -> 33.7 us  [_butterfly_sum(): x = x + lax.ppermute(x, axis, [(i, i ^ step) for i in range(count)])]
    ppermute x0 -> x4, waiting for transfers between devices: none -> 29.2 us  [the longest x2 16.1 us: _halving_sum(): x = keep + lax.ppermute(give, axis, [(i, i ^ step) for i in range(count)])]
    ppermute x6, waiting for transfers between devices: 58.4 us -> 44 us  [_butterfly_gather(): other = lax.ppermute(x, axis, [(i, i ^ step) for i in range(count)])]
    ppermute x6, starting transfers between devices: 16.7 us -> 20.1 us  [_butterfly_gather(): other = lax.ppermute(x, axis, [(i, i ^ step) for i in range(count)])]
    ppermute x10 -> x8, starting transfers between devices: 7.9 us -> 4.7 us  [_butterfly_sum(): x = x + lax.ppermute(x, axis, [(i, i ^ step) for i in range(count)])]
  transfers between devices with their start and end apart: 17 -> 19, of which waited for: 14 -> 15; matrix products, arithmetic and copies ran while one was open for 3% -> 3% of each run, Pallas kernels for 0% -> 0%
where the time goes in v3:
time: 213 us
  waiting for transfers between devices  107 us (50%)
  other arithmetic  52 us (24%)
  starting transfers between devices  26.8 us (13%)
  matrix products  24.8 us (12%)
    ppermute x6, waiting for transfers between devices, _butterfly_gather(): other = lax.ppermute(x, axis, [(i, i ^ step) for i in range(count)])  44 us
    ppermute x8, waiting for transfers between devices, _butterfly_sum(): x = x + lax.ppermute(x, axis, [(i, i ^ step) for i in range(count)])  33.7 us
    another operation x6, other arithmetic, _qr_step(): lower_factor = jnp.linalg.cholesky(gram_matrix)  24.8 us
    another operation x4, other arithmetic, _qr_step(): jax.scipy.linalg.solve_triangular(lower_factor, image.T, lower=True)  21 us
    ppermute x6, starting transfers between devices, _butterfly_gather(): other = lax.ppermute(x, axis, [(i, i ^ step) for i in range(count)])  20.1 us
    ppermute x2, waiting for transfers between devices, _halving_sum(): x = keep + lax.ppermute(give, axis, [(i, i ^ step) for i in range(count)])  16.1 us
    ppermute x2, waiting for transfers between devices, _halving_sum(): other = lax.ppermute(x, axis, [(i, i ^ step) for i in range(count)])  13.1 us
    dot_general x1, matrix products, shards(): lax.dot_general(covariance, basis_rows, (((0,), (0,)), ((), ())), precisi...  8.48 us
  transfers between devices with their start and end apart: 19, of which 15 were waited for; matrix products, arithmetic and copies ran while one was open for 3% of the time, Pallas kernels for 0%

profile of v3, /device:TPU:0, one launch (start us, length us, event | category | flops | bytes accessed | tf_op | source)
XLA Modules:
  0.0 212.6 jit_solution(2018617891465267406)
XLA Ops:
  0.7 2.2 %fusion.39 = f32[8,128,16]{1,2,0:T(8,128)S(1)} fusion(bf16[1024,8,16]{0,2,1:T(8,128)(2,1)} %param.7, bf16[8,1024,128]{2,1,0:T(8,128)(2,1)} %param.8), kind=kOutput, calls=%fused_computation.65 | convolution fusion | flops 33554432 | bytes 2424832 | tf_op jit(solution)/shard_map/mbs,bmr->brs/dot_general | solution.py:91
  2.9 0.6 collective-permute-start
  3.4 0.9 collective-permute-done
  4.3 2.9 %collective-permute-start.1 = (f32[8,128,16]{1,2,0:T(8,128)S(1)}, f32[8,128,16]{1,2,0:T(8,128)S(1)}, u32[]{:S(2)}, u32[]{:S(2)}) collective-permute-start(f32[8,128,16]{1,2,0:T(8,128)S(1)} %add.48), channel_id=1, source_target_pairs={{0,8},{4,12},{8,0},{12,4},{1,9},{5,13},{9,1},{13,5},{2,10},{6,14},... | collective-permute-start | bytes 196616 | tf_op jit(solution)/shard_map/ppermute | solution.py:26
  7.2 2.4 %collective-permute-done.1 = f32[8,128,16]{1,2,0:T(8,128)S(1)} collective-permute-done((f32[8,128,16]{1,2,0:T(8,128)S(1)}, f32[8,128,16]{1,2,0:T(8,128)S(1)}, u32[]{:S(2)}, u32[]{:S(2)}) %collective-permute-start.1) | collective-permute-done | bytes 65568 | tf_op jit(solution)/shard_map/ppermute | solution.py:26
  9.6 0.7 fusion.13
  10.3 0.2 copy.7
  10.5 1.4 collective-permute-start.2
  11.9 0.2 copy.9
  12.0 1.9 collective-permute-start.6
  14.0 0.2 collective-permute-start.3
  14.2 5.4 %collective-permute-done.6 = bf16[1,1024,128]{2,1,0:T(8,128)(2,1)S(1)} collective-permute-done((bf16[1,1024,128]{2,1,0:T(8,128)(2,1)S(1)}, bf16[1,1024,128]{2,1,0:T(8,128)(2,1)S(1)}, u32[]{:S(2)}, u32[]{:S(2)}) %collective-permute-start.6) | collective-permute-done | bytes 262176 | tf_op jit(solution)/shard_map/ppermute | solution.py:50
  19.7 11.0 %collective-permute-start.7 = (bf16[2,1024,128]{2,1,0:T(8,128)(2,1)S(1)}, bf16[2,1024,128]{2,1,0:T(8,128)(2,1)}, u32[]{:S(2)}, u32[]{:S(2)}) collective-permute-start(bf16[2,1024,128]{2,1,0:T(8,128)(2,1)S(1)} %maximum_select_fusion.7), channel_id=1, source_target_pairs={{0,2},{1,3},{2,0},{3,1},{4,6},{5,7},{6,4},{7,5},{8,10},{9,11},{10,... | collective-permute-start | bytes 1572872 | tf_op jit(solution)/shard_map/ppermute | solution.py:50
  30.7 1.1 maximum_select_fusion.6
  31.8 6.9 %collective-permute-start.4 = (bf16[2,1024,128]{2,1,0:T(8,128)(2,1)S(1)}, bf16[2,1024,128]{2,1,0:T(8,128)(2,1)}, u32[]{:S(2)}, u32[]{:S(2)}) collective-permute-start(bf16[2,1024,128]{2,1,0:T(8,128)(2,1)S(1)} %maximum_select_fusion.6), channel_id=1, source_target_pairs={{0,8},{4,12},{8,0},{12,4},{1,9},{5,13},{9,1},{13,5},{2,10},{6,14},... | collective-permute-start | bytes 1572872 | tf_op jit(solution)/shard_map/ppermute | solution.py:50
  38.7 15.5 %collective-permute-done.7 = bf16[2,1024,128]{2,1,0:T(8,128)(2,1)} collective-permute-done((bf16[2,1024,128]{2,1,0:T(8,128)(2,1)S(1)}, bf16[2,1024,128]{2,1,0:T(8,128)(2,1)}, u32[]{:S(2)}, u32[]{:S(2)}) %collective-permute-start.7) | collective-permute-done | bytes 524320 | tf_op jit(solution)/shard_map/ppermute | solution.py:50
  54.2 2.3 %maximum_select_fusion.5 = bf16[4,1024,128]{2,1,0:T(8,128)(2,1)} fusion(bf16[2,1024,128]{2,1,0:T(8,128)(2,1)} %collective-permute-done.7, bf16[2,1024,128]{2,1,0:T(8,128)(2,1)S(1)} %maximum_select_fusion.7, pred[]{:T(512)S(6)} %eq.28), kind=kLoop, calls=%fused_computation.19 | loop fusion | flops 1572864 | bytes 2097153 | tf_op jit(solution)/shard_map/jit(_where)/select_n | solution.py:52
  56.6 2.3 %maximum_select_fusion.4 = bf16[4,1024,128]{2,1,0:T(8,128)(2,1)} fusion(bf16[2,1024,128]{2,1,0:T(8,128)(2,1)} %collective-permute-done.4, bf16[2,1024,128]{2,1,0:T(8,128)(2,1)S(1)} %maximum_select_fusion.6, pred[]{:T(512)S(6)} %eq.24), kind=kLoop, calls=%fused_computation.18 | loop fusion | flops 1572864 | bytes 2097153 | tf_op jit(solution)/shard_map/jit(_where)/select_n | solution.py:52
  59.0 23.0 %collective-permute-done.8 = bf16[4,1024,128]{2,1,0:T(8,128)(2,1)} collective-permute-done((bf16[4,1024,128]{2,1,0:T(8,128)(2,1)}, bf16[4,1024,128]{2,1,0:T(8,128)(2,1)}, u32[]{:S(2)}, u32[]{:S(2)}) %collective-permute-start.8) | collective-permute-done | bytes 1048608 | tf_op jit(solution)/shard_map/ppermute | solution.py:50
  82.1 5.3 %bitcast_multiply_fusion = f32[1024,1024]{1,0:T(8,128)S(1)} fusion(bf16[4,1024,128]{2,1,0:T(8,128)(2,1)S(1)} %collective-permute-done.5, bf16[4,1024,128]{2,1,0:T(8,128)(2,1)} %maximum_select_fusion.4, bf16[4,1024,128]{2,1,0:T(8,128)(2,1)} %collective-permute-done.8, bf16[4,1024,128]{2,1,0:T(8,128)(2,1)} %maximum_select_fusion.5, pred[]{:T(512)S(6)} %eq.27, ...), kind=kOutput, calls=%fused_computation | convolution fusion | flops 2154823680 | bytes 8388610 | tf_op jit(solution)/shard_map/dot_general | solution.py:111
  87.4 4.9 %fusion.18 = f32[1024,128]{1,0:T(8,128)S(1)} fusion(f32[1024,1024]{1,0:T(8,128)S(1)} %bitcast_multiply_fusion, f32[4096,128]{1,0:T(8,128)} %param.10, s32[]{:T(128)S(6)} %select_n.112), kind=kOutput, calls=%fused_computation.27 | convolution fusion | flops 1610612736 | bytes 5242884 | tf_op jit(solution)/shard_map/dot_general | solution.py:119
  92.4 1.9 collective-permute-done.9
  94.4 14.0 %collective-permute-done.10 = f32[1024,128]{1,0:T(8,128)S(1)} collective-permute-done((f32[1024,128]{1,0:T(8,128)S(1)}, f32[1024,128]{1,0:T(8,128)S(1)}, u32[]{:S(2)}, u32[]{:S(2)}) %collective-permute-start.10) | collective-permute-done | bytes 524320 | tf_op jit(solution)/shard_map/ppermute | solution.py:26
  108.4 1.0 fusion.24
  109.4 0.3 collective-permute-start.11
  109.7 4.0 %collective-permute-done.11 = f32[128,128]{0,1:T(8,128)S(1)} collective-permute-done((f32[128,128]{0,1:T(8,128)S(1)}, f32[128,128]{0,1:T(8,128)S(1)}, u32[]{:S(2)}, u32[]{:S(2)}) %collective-permute-start.11) | collective-permute-done | bytes 65568 | tf_op jit(solution)/shard_map/ppermute | solution.py:26
  113.7 0.6 collective-permute-start.12
  114.3 5.0 %collective-permute-done.12 = f32[128,128]{0,1:T(8,128)S(1)} collective-permute-done((f32[128,128]{0,1:T(8,128)S(1)}, f32[128,128]{0,1:T(8,128)S(1)}, u32[]{:S(2)}, u32[]{:S(2)}) %collective-permute-start.12) | collective-permute-done | bytes 65568 | tf_op jit(solution)/shard_map/ppermute | solution.py:26
  119.5 11.7 %cholesky.44 = f32[128,128]{1,0:T(8,128)S(1)} custom-call(f32[128,128]{1,0:T(8,128)S(1)} %fusion.31), custom_call_target="Cholesky" | custom-call | tf_op jit(solution)/shard_map/jit(cholesky)/cholesky | solution.py:80
  131.2 0.6 compare_reduce_fusion.1
  131.9 0.7 fusion.26
  132.6 9.9 %custom-call.6 = f32[1,128,128]{1,2,0:T(8,128)S(1)} custom-call(f32[1,128,128]{2,1,0:T(8,128)S(1)} %fusion.26), custom_call_target="InvertDiagBlocksLowerTriangular" | custom-call | tf_op jit(solution)/shard_map/jit(_solve_triangular)/triangular_solve | solution.py:81
  142.5 0.6 fusion.16
  143.1 8.5 %fusion.38 = f32[1024,128]{1,0:T(8,128)S(1)} fusion(f32[1024,1024]{1,0:T(8,128)} %copy-done.1, f32[128,1024]{1,0:T(8,128)S(1)} %fusion.16), kind=kOutput, calls=%fused_computation.64 | convolution fusion | flops 1610612736 | bytes 5242880 | tf_op jit(solution)/shard_map/dot_general | solution.py:126
  151.7 6.8 %collective-permute-done.13 = f32[512,128]{1,0:T(8,128)S(1)} collective-permute-done((f32[512,128]{1,0:T(8,128)S(1)}, f32[512,128]{1,0:T(8,128)S(1)}, u32[]{:S(2)}, u32[]{:S(2)}) %collective-permute-start.13) | collective-permute-done | bytes 262176 | tf_op jit(solution)/shard_map/ppermute | solution.py:67
  158.6 0.4 collective-permute-start.14
  159.0 9.3 %collective-permute-done.14 = f32[256,128]{1,0:T(8,128)S(1)} collective-permute-done((f32[256,128]{1,0:T(8,128)S(1)}, f32[256,128]{1,0:T(8,128)S(1)}, u32[]{:S(2)}, u32[]{:S(2)}) %collective-permute-start.14) | collective-permute-done | bytes 131104 | tf_op jit(solution)/shard_map/ppermute | solution.py:67
  168.4 6.7 %collective-permute-done.15 = f32[256,128]{1,0:T(8,128)S(1)} collective-permute-done((f32[256,128]{1,0:T(8,128)S(1)}, f32[256,128]{1,0:T(8,128)S(1)}, u32[]{:S(2)}, u32[]{:S(2)}) %collective-permute-start.15) | collective-permute-done | bytes 131104 | tf_op jit(solution)/shard_map/ppermute | solution.py:70
  175.2 6.4 %collective-permute-done.16 = f32[512,128]{1,0:T(8,128)S(1)} collective-permute-done((f32[512,128]{1,0:T(8,128)S(1)}, f32[512,128]{1,0:T(8,128)S(1)}, u32[]{:S(2)}, u32[]{:S(2)}) %collective-permute-start.16) | collective-permute-done | bytes 262176 | tf_op jit(solution)/shard_map/ppermute | solution.py:70
  181.5 1.0 fusion.20
  182.6 1.2 collective-permute-done.17
  184.0 4.3 %collective-permute-done.18 = f32[128,128]{0,1:T(8,128)S(1)} collective-permute-done((f32[128,128]{0,1:T(8,128)S(1)}, f32[128,128]{0,1:T(8,128)S(1)}, u32[]{:S(2)}, u32[]{:S(2)}) %collective-permute-start.18) | collective-permute-done | bytes 65568 | tf_op jit(solution)/shard_map/ppermute | solution.py:26
  188.3 11.7 %cholesky.55 = f32[128,128]{1,0:T(8,128)S(1)} custom-call(f32[128,128]{1,0:T(8,128)S(1)} %fusion.29), custom_call_target="Cholesky" | custom-call | tf_op jit(solution)/shard_map/jit(cholesky)/cholesky | solution.py:80
  200.1 0.6 compare_reduce_fusion
  200.7 0.7 fusion.27
  201.4 9.8 %custom-call.7 = f32[1,128,128]{1,2,0:T(8,128)S(1)} custom-call(f32[1,128,128]{2,1,0:T(8,128)S(1)} %fusion.27), custom_call_target="InvertDiagBlocksLowerTriangular" | custom-call | tf_op jit(solution)/shard_map/jit(_solve_triangular)/triangular_solve | solution.py:81
  211.2 0.6 fusion.14
  211.9 0.8 copy.17
  (39 shorter events, 1.3 us)
Async XLA Ops:
  0.6 9.0 %copy-start = (bf16[8,1024,128]{2,1,0:T(8,128)(2,1)S(1)}, bf16[8,1024,128]{2,1,0:T(8,128)(2,1)}, u32[]{:S(2)}) copy-start(bf16[8,1024,128]{2,1,0:T(8,128)(2,1)} %param.9) | copy-start | bytes 6291460
  0.6 9.0 %copy-start.2 = (bf16[1024,8,16]{0,2,1:T(8,128)(2,1)S(1)}, bf16[1024,8,16]{0,2,1:T(8,128)(2,1)}, u32[]{:S(2)}) copy-start(bf16[1024,8,16]{0,2,1:T(8,128)(2,1)} %param.7) | copy-start | bytes 786436
  2.9 1.5 collective-permute-start
  4.3 5.3 %collective-permute-start.1 = (f32[8,128,16]{1,2,0:T(8,128)S(1)}, f32[8,128,16]{1,2,0:T(8,128)S(1)}, u32[]{:S(2)}, u32[]{:S(2)}) collective-permute-start(f32[8,128,16]{1,2,0:T(8,128)S(1)} %add.48), channel_id=1, source_target_pairs={{0,8},{4,12},{8,0},{12,4},{1,9},{5,13},{9,1},{13,5},{2,10},{6,14},... | collective-permute-start | bytes 196616 | tf_op jit(solution)/shard_map/ppermute | solution.py:26
  10.5 3.5 %collective-permute-start.2 = (bf16[1024,128]{1,0:T(8,128)(2,1)S(1)}, bf16[1024,128]{1,0:T(8,128)(2,1)}, u32[]{:S(2)}, u32[]{:S(2)}) collective-permute-start(bf16[1024,128]{1,0:T(8,128)(2,1)S(1)} %copy.7), channel_id=1, source_target_pairs={{1,4},{2,8},{3,12},{4,1},{6,9},{7,13},{8,2},{9,6},{11,14},{12,3},{... | collective-permute-start | bytes 786440 | tf_op jit(solution)/shard_map/ppermute | solution.py:105
  12.0 7.6 %collective-permute-start.6 = (bf16[1,1024,128]{2,1,0:T(8,128)(2,1)S(1)}, bf16[1,1024,128]{2,1,0:T(8,128)(2,1)S(1)}, u32[]{:S(2)}, u32[]{:S(2)}) collective-permute-start(bf16[1,1024,128]{2,1,0:T(8,128)(2,1)S(1)} %copy.9), channel_id=1, source_target_pairs={{0,16},{16,0},{1,17},{17,1},{2,18},{18,2},{3,19},{19,3},{4,20},{20... | collective-permute-start | bytes 786440 | tf_op jit(solution)/shard_map/ppermute | solution.py:50
  14.0 16.7 %collective-permute-start.3 = (bf16[1,1024,128]{2,1,0:T(8,128)(2,1)S(1)}, bf16[1,1024,128]{2,1,0:T(8,128)(2,1)}, u32[]{:S(2)}, u32[]{:S(2)}) collective-permute-start(bf16[1,1024,128]{2,1,0:T(8,128)(2,1)S(1)} %select_bitcast_fusion), channel_id=1, source_target_pairs={{0,16},{16,0},{1,17},{17,1},{2,18},{18,2},{3,19},{19,3},{4,20},{20... | collective-permute-start | bytes 786440 | tf_op jit(solution)/shard_map/ppermute | solution.py:50
  19.7 34.5 %collective-permute-start.7 = (bf16[2,1024,128]{2,1,0:T(8,128)(2,1)S(1)}, bf16[2,1024,128]{2,1,0:T(8,128)(2,1)}, u32[]{:S(2)}, u32[]{:S(2)}) collective-permute-start(bf16[2,1024,128]{2,1,0:T(8,128)(2,1)S(1)} %maximum_select_fusion.7), channel_id=1, source_target_pairs={{0,2},{1,3},{2,0},{3,1},{4,6},{5,7},{6,4},{7,5},{8,10},{9,11},{10,... | collective-permute-start | bytes 1572872 | tf_op jit(solution)/shard_map/ppermute | solution.py:50
  31.8 24.8 %collective-permute-start.4 = (bf16[2,1024,128]{2,1,0:T(8,128)(2,1)S(1)}, bf16[2,1024,128]{2,1,0:T(8,128)(2,1)}, u32[]{:S(2)}, u32[]{:S(2)}) collective-permute-start(bf16[2,1024,128]{2,1,0:T(8,128)(2,1)S(1)} %maximum_select_fusion.6), channel_id=1, source_target_pairs={{0,8},{4,12},{8,0},{12,4},{1,9},{5,13},{9,1},{13,5},{2,10},{6,14},... | collective-permute-start | bytes 1572872 | tf_op jit(solution)/shard_map/ppermute | solution.py:50
  56.6 25.5 %collective-permute-start.8 = (bf16[4,1024,128]{2,1,0:T(8,128)(2,1)}, bf16[4,1024,128]{2,1,0:T(8,128)(2,1)}, u32[]{:S(2)}, u32[]{:S(2)}) collective-permute-start(bf16[4,1024,128]{2,1,0:T(8,128)(2,1)} %maximum_select_fusion.5), channel_id=1, source_target_pairs={{0,1},{1,0},{2,3},{3,2},{4,5},{5,4},{6,7},{7,6},{8,9},{9,8},{10,11... | collective-permute-start | bytes 3145736 | tf_op jit(solution)/shard_map/ppermute | solution.py:50
  58.9 23.2 %collective-permute-start.5 = (bf16[4,1024,128]{2,1,0:T(8,128)(2,1)}, bf16[4,1024,128]{2,1,0:T(8,128)(2,1)S(1)}, u32[]{:S(2)}, u32[]{:S(2)}) collective-permute-start(bf16[4,1024,128]{2,1,0:T(8,128)(2,1)} %maximum_select_fusion.4), channel_id=1, source_target_pairs={{0,4},{4,0},{8,12},{12,8},{1,5},{5,1},{9,13},{13,9},{2,6},{6,2},{1... | collective-permute-start | bytes 3145736 | tf_op jit(solution)/shard_map/ppermute | solution.py:50
  87.4 4.9 %copy-start.1 = (f32[1024,1024]{1,0:T(8,128)}, f32[1024,1024]{1,0:T(8,128)S(1)}, u32[]{:S(2)}) copy-start(f32[1024,1024]{1,0:T(8,128)S(1)} %bitcast_multiply_fusion) | copy-start | bytes 12582916
  92.3 2.0 collective-permute-start.9
  94.3 14.0 %collective-permute-start.10 = (f32[1024,128]{1,0:T(8,128)S(1)}, f32[1024,128]{1,0:T(8,128)S(1)}, u32[]{:S(2)}, u32[]{:S(2)}) collective-permute-start(f32[1024,128]{1,0:T(8,128)S(1)} %add.52), channel_id=1, source_target_pairs={{0,8},{4,12},{8,0},{12,4},{1,9},{5,13},{9,1},{13,5},{2,10},{6,14},... | collective-permute-start | bytes 1572872 | tf_op jit(solution)/shard_map/ppermute | solution.py:26
  109.4 4.3 %collective-permute-start.11 = (f32[128,128]{0,1:T(8,128)S(1)}, f32[128,128]{0,1:T(8,128)S(1)}, u32[]{:S(2)}, u32[]{:S(2)}) collective-permute-start(f32[128,128]{0,1:T(8,128)S(1)} %fusion.24), channel_id=1, source_target_pairs={{0,1},{1,0},{2,3},{3,2},{4,5},{5,4},{6,7},{7,6},{8,9},{9,8},{10,11... | collective-permute-start | bytes 196616 | tf_op jit(solution)/shard_map/ppermute | solution.py:26
  113.7 5.7 %collective-permute-start.12 = (f32[128,128]{0,1:T(8,128)S(1)}, f32[128,128]{0,1:T(8,128)S(1)}, u32[]{:S(2)}, u32[]{:S(2)}) collective-permute-start(f32[128,128]{0,1:T(8,128)S(1)} %add.54), channel_id=1, source_target_pairs={{0,2},{1,3},{2,0},{3,1},{4,6},{5,7},{6,4},{7,5},{8,10},{9,11},{10,... | collective-permute-start | bytes 196616 | tf_op jit(solution)/shard_map/ppermute | solution.py:26
  151.6 6.9 %collective-permute-start.13 = (f32[512,128]{1,0:T(8,128)S(1)}, f32[512,128]{1,0:T(8,128)S(1)}, u32[]{:S(2)}, u32[]{:S(2)}) collective-permute-start(f32[512,128]{1,0:T(8,128)S(1)} %slice_select_fusion), channel_id=1, source_target_pairs={{0,1},{1,0},{2,3},{3,2},{4,5},{5,4},{6,7},{7,6},{8,9},{9,8},{10,11... | collective-permute-start | bytes 786440 | tf_op jit(solution)/shard_map/ppermute | solution.py:67
  158.6 9.7 %collective-permute-start.14 = (f32[256,128]{1,0:T(8,128)S(1)}, f32[256,128]{1,0:T(8,128)S(1)}, u32[]{:S(2)}, u32[]{:S(2)}) collective-permute-start(f32[256,128]{1,0:T(8,128)S(1)} %slice_select_fusion.1), channel_id=1, source_target_pairs={{0,2},{1,3},{2,0},{3,1},{4,6},{5,7},{6,4},{7,5},{8,10},{9,11},{10,... | collective-permute-start | bytes 393224 | tf_op jit(solution)/shard_map/ppermute | solution.py:67
  168.3 6.8 %collective-permute-start.15 = (f32[256,128]{1,0:T(8,128)S(1)}, f32[256,128]{1,0:T(8,128)S(1)}, u32[]{:S(2)}, u32[]{:S(2)}) collective-permute-start(f32[256,128]{1,0:T(8,128)S(1)} %select_add_fusion.1), channel_id=1, source_target_pairs={{0,2},{1,3},{2,0},{3,1},{4,6},{5,7},{6,4},{7,5},{8,10},{9,11},{10,... | collective-permute-start | bytes 393224 | tf_op jit(solution)/shard_map/ppermute | solution.py:70
  175.1 6.4 %collective-permute-start.16 = (f32[512,128]{1,0:T(8,128)S(1)}, f32[512,128]{1,0:T(8,128)S(1)}, u32[]{:S(2)}, u32[]{:S(2)}) collective-permute-start(f32[512,128]{1,0:T(8,128)S(1)} %maximum_select_fusion.11), channel_id=1, source_target_pairs={{0,1},{1,0},{2,3},{3,2},{4,5},{5,4},{6,7},{7,6},{8,9},{9,8},{10,11... | collective-permute-start | bytes 786440 | tf_op jit(solution)/shard_map/ppermute | solution.py:70
  182.6 1.3 collective-permute-start.17
  183.9 4.3 %collective-permute-start.18 = (f32[128,128]{0,1:T(8,128)S(1)}, f32[128,128]{0,1:T(8,128)S(1)}, u32[]{:S(2)}, u32[]{:S(2)}) collective-permute-start(f32[128,128]{0,1:T(8,128)S(1)} %add.58), channel_id=1, source_target_pairs={{0,8},{4,12},{8,0},{12,4},{1,9},{5,13},{9,1},{13,5},{2,10},{6,14},... | collective-permute-start | bytes 196616 | tf_op jit(solution)/shard_map/ppermute | solution.py:26

commit v4 on v3

--- a/solution.py
+++ b/solution.py
@@ -37,20 +37,33 @@
     return steps[::-1] if far_first else steps
 
 
-def _butterfly_gather(x, axes):
+def _plan(axes):
+    steps = []
+    for axis in axes:
+        steps += [(axis, step) for step in _bits(lax.axis_size(axis), True)]
+    return steps
+
+
+def _butterfly_gather(x, plan):
     x = x[None]
-    for axis in axes:
+    for axis, step in plan:
         count = lax.axis_size(axis)
-        if count & (count - 1):
-            x = lax.all_gather(x, axis, axis=0, tiled=False)
-            x = x.reshape((-1,) + x.shape[2:])
-            continue
         here = lax.axis_index(axis)
-        for step in _bits(count, True):
-            other = lax.ppermute(x, axis, [(i, i ^ step) for i in range(count)])
-            low = (here & step) == 0
-            x = jnp.where(low, jnp.concatenate([x, other], 0), jnp.concatenate([other, x], 0))
+        other = lax.ppermute(x, axis, [(i, i ^ step) for i in range(count)])
+        low = (here & step) == 0
+        x = jnp.where(low, jnp.concatenate([x, other], 0), jnp.concatenate([other, x], 0))
     return x
+
+
+def _keys(plan, rename):
+    keys = []
+    for index in range(2 ** len(plan)):
+        key = {}
+        for bit, (axis, step) in enumerate(plan):
+            name = rename.get(axis, axis)
+            key[name] = key.get(name, 0) + (step if index >> bit & 1 else 0)
+        keys.append(tuple(sorted(key.items())))
+    return keys
 
 
 def _halving_sum(x, axis):
@@ -100,12 +113,19 @@
     col_block = array_size // col_count
     scaling = 1.0 / (columns * col_count * bin_count)
 
-    right_rows = _butterfly_gather(local_rows, ("bin", "col"))
-    if row_count == col_count:
+    power_of_two = all(n & (n - 1) == 0 for n in (bin_count, row_count, col_count))
+    if row_count == col_count and power_of_two:
+        right_plan = _plan(("col", "bin"))
+        left_plan = _plan(("bin", "row"))
+        right_rows = _butterfly_gather(local_rows, right_plan)
         swapped = lax.ppermute(local_rows, ("row", "col"), _transpose_pairs(row_count, col_count))
         swapped = jnp.where(row_here == col_here, local_rows, swapped)
-        left_rows = _butterfly_gather(swapped, ("bin", "row"))
+        left_rows = _butterfly_gather(swapped, left_plan)
+        left_keys = _keys(left_plan, {"row": "col"})
+        order = [left_keys.index(key) for key in _keys(right_plan, {})]
+        left_rows = jnp.stack([left_rows[j] for j in order])
     else:
+        right_rows = lax.all_gather(local_rows, ("bin", "col"), axis=0, tiled=False)
         every_row = lax.all_gather(right_rows, "row", axis=1, tiled=True)
         left_rows = lax.dynamic_slice_in_dim(every_row, col_here * col_block, col_block, 1)
     covariance = lax.dot_general(

time: 213 us -> 222 us (1.042)
  starting transfers between devices: 26.8 us -> 41.6 us
  waiting for transfers between devices: 107 us -> 102 us
  matrix products: 24.8 us -> 21.9 us
    ppermute x8, starting transfers between devices: 4.7 us -> 13.2 us  [_butterfly_sum(): x = x + lax.ppermute(x, axis, [(i, i ^ step) for i in range(count)])]
    ppermute x8, waiting for transfers between devices: 33.7 us -> 28.9 us  [_butterfly_sum(): x = x + lax.ppermute(x, axis, [(i, i ^ step) for i in range(count)])]
    ppermute x6, waiting for transfers between devices: 44 us -> 47.4 us  [_butterfly_gather(): other = lax.ppermute(x, axis, [(i, i ^ step) for i in range(count)])]
    ppermute x2, starting transfers between devices: 0.45 us -> 3.86 us  [_halving_sum(): x = keep + lax.ppermute(give, axis, [(i, i ^ step) for i in range(count)])]
    ppermute x6, starting transfers between devices: 20.1 us -> 23.3 us  [_butterfly_gather(): other = lax.ppermute(x, axis, [(i, i ^ step) for i in range(count)])]
    ppermute x2, waiting for transfers between devices: 16.1 us -> 13 us  [_halving_sum(): x = keep + lax.ppermute(give, axis, [(i, i ^ step) for i in range(count)])]
    dot_general x1, matrix products: 5.3 us -> 2.37 us  [shards(): lax.dot_general(left_rows, right_rows, (((0, 2), (0, 2)), ((), ())), pref...]
    select_n x4 -> x5, other arithmetic: 5.86 us -> 7.39 us  [_butterfly_gather(): jnp.where(low, jnp.concatenate([x, other], 0), jnp.concatenate([other, x]...]
  transfers between devices with their start and end apart: 19 -> 19, of which waited for: 15 -> 17; matrix products, arithmetic and copies ran while one was open for 3% -> 3% of each run, Pallas kernels for 0% -> 0%
where the time goes in v4:
time: 222 us
  waiting for transfers between devices  102 us (46%)
  other arithmetic  53.6 us (24%)
  starting transfers between devices  41.6 us (19%)
  matrix products  21.9 us (10%)
    ppermute x6, waiting for transfers between devices, _butterfly_gather(): other = lax.ppermute(x, axis, [(i, i ^ step) for i in range(count)])  47.4 us
    ppermute x8, waiting for transfers between devices, _butterfly_sum(): x = x + lax.ppermute(x, axis, [(i, i ^ step) for i in range(count)])  28.9 us
    another operation x6, other arithmetic, _qr_step(): lower_factor = jnp.linalg.cholesky(gram_matrix)  24.9 us
    ppermute x6, starting transfers between devices, _butterfly_gather(): other = lax.ppermute(x, axis, [(i, i ^ step) for i in range(count)])  23.3 us
    another operation x4, other arithmetic, _qr_step(): jax.scipy.linalg.solve_triangular(lower_factor, image.T, lower=True)  20.9 us
    ppermute x8, starting transfers between devices, _butterfly_sum(): x = x + lax.ppermute(x, axis, [(i, i ^ step) for i in range(count)])  13.2 us
    ppermute x2, waiting for transfers between devices, _halving_sum(): other = lax.ppermute(x, axis, [(i, i ^ step) for i in range(count)])  13.1 us
    ppermute x2, waiting for transfers between devices, _halving_sum(): x = keep + lax.ppermute(give, axis, [(i, i ^ step) for i in range(count)])  13 us
  transfers between devices with their start and end apart: 19, of which 17 were waited for; matrix products, arithmetic and copies ran while one was open for 3% of the time, Pallas kernels for 0%

profile of v4, /device:TPU:0, one launch (start us, length us, event | category | flops | bytes accessed | tf_op | source)
XLA Modules:
  0.0 222.1 jit_solution(8171295345179074603)
XLA Ops:
  0.7 2.2 fusion.33
  3.4 0.9 collective-permute-done
  4.3 2.9 %collective-permute-start.1 = (f32[8,128,16]{1,2,0:T(8,128)S(1)}, f32[8,128,16]{1,2,0:T(8,128)S(1)}, u32[]{:S(2)}, u32[]{:S(2)}) collective-permute-start(f32[8,128,16]{1,2,0:T(8,128)S(1)} %add.48), channel_id=1, source_target_pairs={{0,8},{4,12},{8,0},{12,4},{1,9},{5,13},{9,1},{13,5},{2,10},{6,14},... | collective-permute-start | bytes 196616 | tf_op jit(solution)/shard_map/ppermute | solution.py:26
  7.2 2.4 %collective-permute-done.1 = f32[8,128,16]{1,2,0:T(8,128)S(1)} collective-permute-done((f32[8,128,16]{1,2,0:T(8,128)S(1)}, f32[8,128,16]{1,2,0:T(8,128)S(1)}, u32[]{:S(2)}, u32[]{:S(2)}) %collective-permute-start.1) | collective-permute-done | bytes 65568 | tf_op jit(solution)/shard_map/ppermute | solution.py:26
  9.6 0.7 fusion.7
  10.5 0.7 collective-permute-start.2
  11.2 1.9 collective-permute-start.3
  13.2 4.5 %collective-permute-done.3 = bf16[1,1024,128]{2,1,0:T(8,128)(2,1)S(1)} collective-permute-done((bf16[1,1024,128]{2,1,0:T(8,128)(2,1)S(1)}, bf16[1,1024,128]{2,1,0:T(8,128)(2,1)S(1)}, u32[]{:S(2)}, u32[]{:S(2)}) %collective-permute-start.3) | collective-permute-done | bytes 262176 | tf_op jit(solution)/shard_map/ppermute | solution.py:52
  17.8 18.7 %collective-permute-start.4 = (bf16[2,1024,128]{2,1,0:T(8,128)(2,1)S(1)}, bf16[2,1024,128]{2,1,0:T(8,128)(2,1)}, u32[]{:S(2)}, u32[]{:S(2)}) collective-permute-start(bf16[2,1024,128]{2,1,0:T(8,128)(2,1)S(1)} %maximum_select_fusion.5), channel_id=1, source_target_pairs={{0,8},{4,12},{8,0},{12,4},{1,9},{5,13},{9,1},{13,5},{2,10},{6,14},... | collective-permute-start | bytes 1572872 | tf_op jit(solution)/shard_map/ppermute | solution.py:52
  36.7 0.9 collective-permute-start.6
  37.6 6.2 %collective-permute-done.4 = bf16[2,1024,128]{2,1,0:T(8,128)(2,1)} collective-permute-done((bf16[2,1024,128]{2,1,0:T(8,128)(2,1)S(1)}, bf16[2,1024,128]{2,1,0:T(8,128)(2,1)}, u32[]{:S(2)}, u32[]{:S(2)}) %collective-permute-start.4) | collective-permute-done | bytes 524320 | tf_op jit(solution)/shard_map/ppermute | solution.py:52
  43.8 1.8 maximum_select_fusion.3
  45.7 3.4 %collective-permute-done.6 = bf16[1,1024,128]{2,1,0:T(8,128)(2,1)} collective-permute-done((bf16[1,1024,128]{2,1,0:T(8,128)(2,1)S(1)}, bf16[1,1024,128]{2,1,0:T(8,128)(2,1)}, u32[]{:S(2)}, u32[]{:S(2)}) %collective-permute-start.6) | collective-permute-done | bytes 262176 | tf_op jit(solution)/shard_map/ppermute | solution.py:52
  49.0 1.9 maximum_select_fusion.6
  50.9 13.5 %collective-permute-done.7 = bf16[2,1024,128]{2,1,0:T(8,128)(2,1)} collective-permute-done((bf16[2,1024,128]{2,1,0:T(8,128)(2,1)}, bf16[2,1024,128]{2,1,0:T(8,128)(2,1)}, u32[]{:S(2)}, u32[]{:S(2)}) %collective-permute-start.7) | collective-permute-done | bytes 524320 | tf_op jit(solution)/shard_map/ppermute | solution.py:52
  64.5 1.8 maximum_select_fusion.4
  66.2 1.6 collective-permute-start.8
  67.8 1.9 maximum_select_fusion
  70.0 19.9 %collective-permute-done.8 = bf16[4,1024,128]{2,1,0:T(8,128)(2,1)S(1)} collective-permute-done((bf16[4,1024,128]{2,1,0:T(8,128)(2,1)S(1)}, bf16[4,1024,128]{2,1,0:T(8,128)(2,1)S(1)}, u32[]{:S(2)}, u32[]{:S(2)}) %collective-permute-start.8) | collective-permute-done | bytes 1048608 | tf_op jit(solution)/shard_map/ppermute | solution.py:52
  89.9 2.4 %bitcast_multiply_fusion = f32[1024,1024]{1,0:T(8,128)S(1)} fusion(bf16[8,1024,128]{2,1,0:T(8,128)(2,1)S(1)} %slice_dynamic-update-slice_fusion, bf16[4,1024,128]{2,1,0:T(8,128)(2,1)S(1)} %collective-permute-done.8, bf16[4,1024,128]{2,1,0:T(8,128)(2,1)S(1)} %maximum_select_fusion.4, pred[]{:T(512)S(6)} %eq.25), kind=kOutput, calls=%fused_computation | convolution fusion | flops 2151677952 | bytes 8388609 | tf_op jit(solution)/shard_map/dot_general | solution.py:131
  92.3 4.9 %fusion.12 = f32[1024,128]{1,0:T(8,128)S(1)} fusion(f32[1024,1024]{1,0:T(8,128)S(1)} %bitcast_multiply_fusion, f32[4096,128]{1,0:T(8,128)} %param.10, s32[]{:T(128)S(6)} %select_n.115), kind=kOutput, calls=%fused_computation.21 | convolution fusion | flops 1610612736 | bytes 5242884 | tf_op jit(solution)/shard_map/dot_general | solution.py:139
  97.3 1.9 collective-permute-done.9
  99.2 3.0 %collective-permute-start.10 = (f32[1024,128]{1,0:T(8,128)S(1)}, f32[1024,128]{1,0:T(8,128)S(1)}, u32[]{:S(2)}, u32[]{:S(2)}) collective-permute-start(f32[1024,128]{1,0:T(8,128)S(1)} %add.52), channel_id=1, source_target_pairs={{0,8},{4,12},{8,0},{12,4},{1,9},{5,13},{9,1},{13,5},{2,10},{6,14},... | collective-permute-start | bytes 1572872 | tf_op jit(solution)/shard_map/ppermute | solution.py:26
  102.3 12.2 %collective-permute-done.10 = f32[1024,128]{1,0:T(8,128)S(1)} collective-permute-done((f32[1024,128]{1,0:T(8,128)S(1)}, f32[1024,128]{1,0:T(8,128)S(1)}, u32[]{:S(2)}, u32[]{:S(2)}) %collective-permute-start.10) | collective-permute-done | bytes 524320 | tf_op jit(solution)/shard_map/ppermute | solution.py:26
  114.5 1.0 fusion.18
  116.1 3.7 %collective-permute-done.11 = f32[128,128]{0,1:T(8,128)S(1)} collective-permute-done((f32[128,128]{0,1:T(8,128)S(1)}, f32[128,128]{0,1:T(8,128)S(1)}, u32[]{:S(2)}, u32[]{:S(2)}) %collective-permute-start.11) | collective-permute-done | bytes 65568 | tf_op jit(solution)/shard_map/ppermute | solution.py:26
  119.8 5.6 %collective-permute-start.12 = (f32[128,128]{0,1:T(8,128)S(1)}, f32[128,128]{0,1:T(8,128)S(1)}, u32[]{:S(2)}, u32[]{:S(2)}) collective-permute-start(f32[128,128]{0,1:T(8,128)S(1)} %add.54), channel_id=1, source_target_pairs={{0,2},{1,3},{2,0},{3,1},{4,6},{5,7},{6,4},{7,5},{8,10},{9,11},{10,... | collective-permute-start | bytes 196616 | tf_op jit(solution)/shard_map/ppermute | solution.py:26
  125.5 2.6 %collective-permute-done.12 = f32[128,128]{0,1:T(8,128)S(1)} collective-permute-done((f32[128,128]{0,1:T(8,128)S(1)}, f32[128,128]{0,1:T(8,128)S(1)}, u32[]{:S(2)}, u32[]{:S(2)}) %collective-permute-start.12) | collective-permute-done | bytes 65568 | tf_op jit(solution)/shard_map/ppermute | solution.py:26
  128.2 11.9 %cholesky.44 = f32[128,128]{1,0:T(8,128)S(1)} custom-call(f32[128,128]{1,0:T(8,128)S(1)} %fusion.25), custom_call_target="Cholesky" | custom-call | tf_op jit(solution)/shard_map/jit(cholesky)/cholesky | solution.py:93
  140.1 0.6 compare_reduce_fusion.1
  140.7 0.7 fusion.20
  141.4 9.8 %custom-call.6 = f32[1,128,128]{1,2,0:T(8,128)S(1)} custom-call(f32[1,128,128]{2,1,0:T(8,128)S(1)} %fusion.20), custom_call_target="InvertDiagBlocksLowerTriangular" | custom-call | tf_op jit(solution)/shard_map/jit(_solve_triangular)/triangular_solve | solution.py:94
  151.2 0.6 fusion.10
  151.9 8.5 %fusion.32 = f32[1024,128]{1,0:T(8,128)S(1)} fusion(f32[1024,1024]{1,0:T(8,128)} %copy-done.1, f32[128,1024]{1,0:T(8,128)S(1)} %fusion.10), kind=kOutput, calls=%fused_computation.66 | convolution fusion | flops 1610612736 | bytes 5242880 | tf_op jit(solution)/shard_map/dot_general | solution.py:146
  160.5 6.6 %collective-permute-done.13 = f32[512,128]{1,0:T(8,128)S(1)} collective-permute-done((f32[512,128]{1,0:T(8,128)S(1)}, f32[512,128]{1,0:T(8,128)S(1)}, u32[]{:S(2)}, u32[]{:S(2)}) %collective-permute-start.13) | collective-permute-done | bytes 262176 | tf_op jit(solution)/shard_map/ppermute | solution.py:80
  167.2 3.8 %collective-permute-start.14 = (f32[256,128]{1,0:T(8,128)S(1)}, f32[256,128]{1,0:T(8,128)S(1)}, u32[]{:S(2)}, u32[]{:S(2)}) collective-permute-start(f32[256,128]{1,0:T(8,128)S(1)} %slice_select_fusion.1), channel_id=1, source_target_pairs={{0,2},{1,3},{2,0},{3,1},{4,6},{5,7},{6,4},{7,5},{8,10},{9,11},{10,... | collective-permute-start | bytes 393224 | tf_op jit(solution)/shard_map/ppermute | solution.py:80
  170.9 6.4 %collective-permute-done.14 = f32[256,128]{1,0:T(8,128)S(1)} collective-permute-done((f32[256,128]{1,0:T(8,128)S(1)}, f32[256,128]{1,0:T(8,128)S(1)}, u32[]{:S(2)}, u32[]{:S(2)}) %collective-permute-start.14) | collective-permute-done | bytes 131104 | tf_op jit(solution)/shard_map/ppermute | solution.py:80
  177.4 7.1 %collective-permute-done.15 = f32[256,128]{1,0:T(8,128)S(1)} collective-permute-done((f32[256,128]{1,0:T(8,128)S(1)}, f32[256,128]{1,0:T(8,128)S(1)}, u32[]{:S(2)}, u32[]{:S(2)}) %collective-permute-start.15) | collective-permute-done | bytes 131104 | tf_op jit(solution)/shard_map/ppermute | solution.py:83
  185.0 6.0 %collective-permute-done.16 = f32[512,128]{1,0:T(8,128)S(1)} collective-permute-done((f32[512,128]{1,0:T(8,128)S(1)}, f32[512,128]{1,0:T(8,128)S(1)}, u32[]{:S(2)}, u32[]{:S(2)}) %collective-permute-start.16) | collective-permute-done | bytes 262176 | tf_op jit(solution)/shard_map/ppermute | solution.py:83
  191.0 1.0 fusion.14
  192.1 1.2 collective-permute-done.17
  193.7 4.0 %collective-permute-done.18 = f32[128,128]{0,1:T(8,128)S(1)} collective-permute-done((f32[128,128]{0,1:T(8,128)S(1)}, f32[128,128]{0,1:T(8,128)S(1)}, u32[]{:S(2)}, u32[]{:S(2)}) %collective-permute-start.18) | collective-permute-done | bytes 65568 | tf_op jit(solution)/shard_map/ppermute | solution.py:26
  197.8 11.7 %cholesky.55 = f32[128,128]{1,0:T(8,128)S(1)} custom-call(f32[128,128]{1,0:T(8,128)S(1)} %fusion.23), custom_call_target="Cholesky" | custom-call | tf_op jit(solution)/shard_map/jit(cholesky)/cholesky | solution.py:93
  209.5 0.6 compare_reduce_fusion
  210.2 0.7 fusion.21
  210.8 9.8 %custom-call.7 = f32[1,128,128]{1,2,0:T(8,128)S(1)} custom-call(f32[1,128,128]{2,1,0:T(8,128)S(1)} %fusion.21), custom_call_target="InvertDiagBlocksLowerTriangular" | custom-call | tf_op jit(solution)/shard_map/jit(_solve_triangular)/triangular_solve | solution.py:94
  220.7 0.6 fusion.8
  221.3 0.8 copy.17
  (50 shorter events, 3.7 us)
Async XLA Ops:
  0.6 9.0 %copy-start = (bf16[8,1024,128]{2,1,0:T(8,128)(2,1)S(1)}, bf16[8,1024,128]{2,1,0:T(8,128)(2,1)}, u32[]{:S(2)}) copy-start(bf16[8,1024,128]{2,1,0:T(8,128)(2,1)} %param.9) | copy-start | bytes 6291460
  0.6 9.0 %copy-start.3 = (bf16[1024,8,16]{0,2,1:T(8,128)(2,1)S(1)}, bf16[1024,8,16]{0,2,1:T(8,128)(2,1)}, u32[]{:S(2)}) copy-start(bf16[1024,8,16]{0,2,1:T(8,128)(2,1)} %param.7) | copy-start | bytes 786436
  2.9 1.5 collective-permute-start
  4.3 5.3 %collective-permute-start.1 = (f32[8,128,16]{1,2,0:T(8,128)S(1)}, f32[8,128,16]{1,2,0:T(8,128)S(1)}, u32[]{:S(2)}, u32[]{:S(2)}) collective-permute-start(f32[8,128,16]{1,2,0:T(8,128)S(1)} %add.48), channel_id=1, source_target_pairs={{0,8},{4,12},{8,0},{12,4},{1,9},{5,13},{9,1},{13,5},{2,10},{6,14},... | collective-permute-start | bytes 196616 | tf_op jit(solution)/shard_map/ppermute | solution.py:26
  10.5 0.7 collective-permute-start.2
  11.2 6.4 %collective-permute-start.3 = (bf16[1,1024,128]{2,1,0:T(8,128)(2,1)S(1)}, bf16[1,1024,128]{2,1,0:T(8,128)(2,1)S(1)}, u32[]{:S(2)}, u32[]{:S(2)}) collective-permute-start(bf16[1,1024,128]{2,1,0:T(8,128)(2,1)S(1)} %select_bitcast_fusion), channel_id=1, source_target_pairs={{0,16},{16,0},{1,17},{17,1},{2,18},{18,2},{3,19},{19,3},{4,20},{20... | collective-permute-start | bytes 786440 | tf_op jit(solution)/shard_map/ppermute | solution.py:52
  17.8 19.9 %copy-start.2 = (bf16[2,1024,128]{2,1,0:T(8,128)(2,1)}, bf16[2,1024,128]{2,1,0:T(8,128)(2,1)S(1)}, u32[]{:S(2)}) copy-start(bf16[2,1024,128]{2,1,0:T(8,128)(2,1)S(1)} %maximum_select_fusion.5) | copy-start | bytes 1572868
  17.8 26.0 %collective-permute-start.4 = (bf16[2,1024,128]{2,1,0:T(8,128)(2,1)S(1)}, bf16[2,1024,128]{2,1,0:T(8,128)(2,1)}, u32[]{:S(2)}, u32[]{:S(2)}) collective-permute-start(bf16[2,1024,128]{2,1,0:T(8,128)(2,1)S(1)} %maximum_select_fusion.5), channel_id=1, source_target_pairs={{0,8},{4,12},{8,0},{12,4},{1,9},{5,13},{9,1},{13,5},{2,10},{6,14},... | collective-permute-start | bytes 1572872 | tf_op jit(solution)/shard_map/ppermute | solution.py:52
  36.7 12.3 %collective-permute-start.6 = (bf16[1,1024,128]{2,1,0:T(8,128)(2,1)S(1)}, bf16[1,1024,128]{2,1,0:T(8,128)(2,1)}, u32[]{:S(2)}, u32[]{:S(2)}) collective-permute-start(bf16[1,1024,128]{2,1,0:T(8,128)(2,1)S(1)} %copy.9), channel_id=1, source_target_pairs={{0,2},{1,3},{2,0},{3,1},{4,6},{5,7},{6,4},{7,5},{8,10},{9,11},{10,... | collective-permute-start | bytes 786440 | tf_op jit(solution)/shard_map/ppermute | solution.py:52
  45.6 22.2 %collective-permute-start.5 = (bf16[4,1024,128]{2,1,0:T(8,128)(2,1)S(1)}, bf16[4,1024,128]{2,1,0:T(8,128)(2,1)}, u32[]{:S(2)}, u32[]{:S(2)}) collective-permute-start(bf16[4,1024,128]{2,1,0:T(8,128)(2,1)S(1)} %maximum_select_fusion.3), channel_id=1, source_target_pairs={{0,4},{4,0},{8,12},{12,8},{1,5},{5,1},{9,13},{13,9},{2,6},{6,2},{1... | collective-permute-start | bytes 3145736 | tf_op jit(solution)/shard_map/ppermute | solution.py:52
  50.9 13.5 %collective-permute-start.7 = (bf16[2,1024,128]{2,1,0:T(8,128)(2,1)}, bf16[2,1024,128]{2,1,0:T(8,128)(2,1)}, u32[]{:S(2)}, u32[]{:S(2)}) collective-permute-start(bf16[2,1024,128]{2,1,0:T(8,128)(2,1)} %maximum_select_fusion.6), channel_id=1, source_target_pairs={{0,1},{1,0},{2,3},{3,2},{4,5},{5,4},{6,7},{7,6},{8,9},{9,8},{10,11... | collective-permute-start | bytes 1572872 | tf_op jit(solution)/shard_map/ppermute | solution.py:52
  66.2 23.7 %collective-permute-start.8 = (bf16[4,1024,128]{2,1,0:T(8,128)(2,1)S(1)}, bf16[4,1024,128]{2,1,0:T(8,128)(2,1)S(1)}, u32[]{:S(2)}, u32[]{:S(2)}) collective-permute-start(bf16[4,1024,128]{2,1,0:T(8,128)(2,1)S(1)} %maximum_select_fusion.4), channel_id=1, source_target_pairs={{0,16},{16,0},{1,17},{17,1},{2,18},{18,2},{3,19},{19,3},{4,20},{20... | collective-permute-start | bytes 3145736 | tf_op jit(solution)/shard_map/ppermute | solution.py:52
  92.3 4.9 %copy-start.1 = (f32[1024,1024]{1,0:T(8,128)}, f32[1024,1024]{1,0:T(8,128)S(1)}, u32[]{:S(2)}) copy-start(f32[1024,1024]{1,0:T(8,128)S(1)} %bitcast_multiply_fusion) | copy-start | bytes 12582916
  97.2 2.0 collective-permute-start.9
  99.2 15.3 %collective-permute-start.10 = (f32[1024,128]{1,0:T(8,128)S(1)}, f32[1024,128]{1,0:T(8,128)S(1)}, u32[]{:S(2)}, u32[]{:S(2)}) collective-permute-start(f32[1024,128]{1,0:T(8,128)S(1)} %add.52), channel_id=1, source_target_pairs={{0,8},{4,12},{8,0},{12,4},{1,9},{5,13},{9,1},{13,5},{2,10},{6,14},... | collective-permute-start | bytes 1572872 | tf_op jit(solution)/shard_map/ppermute | solution.py:26
  115.5 4.3 %collective-permute-start.11 = (f32[128,128]{0,1:T(8,128)S(1)}, f32[128,128]{0,1:T(8,128)S(1)}, u32[]{:S(2)}, u32[]{:S(2)}) collective-permute-start(f32[128,128]{0,1:T(8,128)S(1)} %fusion.18), channel_id=1, source_target_pairs={{0,1},{1,0},{2,3},{3,2},{4,5},{5,4},{6,7},{7,6},{8,9},{9,8},{10,11... | collective-permute-start | bytes 196616 | tf_op jit(solution)/shard_map/ppermute | solution.py:26
  119.8 8.2 %collective-permute-start.12 = (f32[128,128]{0,1:T(8,128)S(1)}, f32[128,128]{0,1:T(8,128)S(1)}, u32[]{:S(2)}, u32[]{:S(2)}) collective-permute-start(f32[128,128]{0,1:T(8,128)S(1)} %add.54), channel_id=1, source_target_pairs={{0,2},{1,3},{2,0},{3,1},{4,6},{5,7},{6,4},{7,5},{8,10},{9,11},{10,... | collective-permute-start | bytes 196616 | tf_op jit(solution)/shard_map/ppermute | solution.py:26
  160.4 6.7 %collective-permute-start.13 = (f32[512,128]{1,0:T(8,128)S(1)}, f32[512,128]{1,0:T(8,128)S(1)}, u32[]{:S(2)}, u32[]{:S(2)}) collective-permute-start(f32[512,128]{1,0:T(8,128)S(1)} %slice_select_fusion), channel_id=1, source_target_pairs={{0,1},{1,0},{2,3},{3,2},{4,5},{5,4},{6,7},{7,6},{8,9},{9,8},{10,11... | collective-permute-start | bytes 786440 | tf_op jit(solution)/shard_map/ppermute | solution.py:80
  167.2 10.2 %collective-permute-start.14 = (f32[256,128]{1,0:T(8,128)S(1)}, f32[256,128]{1,0:T(8,128)S(1)}, u32[]{:S(2)}, u32[]{:S(2)}) collective-permute-start(f32[256,128]{1,0:T(8,128)S(1)} %slice_select_fusion.1), channel_id=1, source_target_pairs={{0,2},{1,3},{2,0},{3,1},{4,6},{5,7},{6,4},{7,5},{8,10},{9,11},{10,... | collective-permute-start | bytes 393224 | tf_op jit(solution)/shard_map/ppermute | solution.py:80
  177.3 7.2 %collective-permute-start.15 = (f32[256,128]{1,0:T(8,128)S(1)}, f32[256,128]{1,0:T(8,128)S(1)}, u32[]{:S(2)}, u32[]{:S(2)}) collective-permute-start(f32[256,128]{1,0:T(8,128)S(1)} %select_add_fusion.1), channel_id=1, source_target_pairs={{0,2},{1,3},{2,0},{3,1},{4,6},{5,7},{6,4},{7,5},{8,10},{9,11},{10,... | collective-permute-start | bytes 393224 | tf_op jit(solution)/shard_map/ppermute | solution.py:83
  184.5 6.4 %collective-permute-start.16 = (f32[512,128]{1,0:T(8,128)S(1)}, f32[512,128]{1,0:T(8,128)S(1)}, u32[]{:S(2)}, u32[]{:S(2)}) collective-permute-start(f32[512,128]{1,0:T(8,128)S(1)} %maximum_select_fusion.10), channel_id=1, source_target_pairs={{0,1},{1,0},{2,3},{3,2},{4,5},{5,4},{6,7},{7,6},{8,9},{9,8},{10,11... | collective-permute-start | bytes 786440 | tf_op jit(solution)/shard_map/ppermute | solution.py:83
  192.0 1.3 collective-permute-start.17
  193.3 4.3 %collective-permute-start.18 = (f32[128,128]{0,1:T(8,128)S(1)}, f32[128,128]{0,1:T(8,128)S(1)}, u32[]{:S(2)}, u32[]{:S(2)}) collective-permute-start(f32[128,128]{0,1:T(8,128)S(1)} %add.58), channel_id=1, source_target_pairs={{0,8},{4,12},{8,0},{12,4},{1,9},{5,13},{9,1},{13,5},{2,10},{6,14},... | collective-permute-start | bytes 196616 | tf_op jit(solution)/shard_map/ppermute | solution.py:26

commit v5 on v4

--- a/solution.py
+++ b/solution.py
@@ -115,14 +115,17 @@
 
     power_of_two = all(n & (n - 1) == 0 for n in (bin_count, row_count, col_count))
     if row_count == col_count and power_of_two:
-        right_plan = _plan(("col", "bin"))
         left_plan = _plan(("bin", "row"))
-        right_rows = _butterfly_gather(local_rows, right_plan)
+        right_rows = lax.all_gather(local_rows, ("bin", "col"), axis=0, tiled=False)
+        right_rows = right_rows.reshape((-1,) + local_rows.shape)
         swapped = lax.ppermute(local_rows, ("row", "col"), _transpose_pairs(row_count, col_count))
         swapped = jnp.where(row_here == col_here, local_rows, swapped)
         left_rows = _butterfly_gather(swapped, left_plan)
         left_keys = _keys(left_plan, {"row": "col"})
-        order = [left_keys.index(key) for key in _keys(right_plan, {})]
+        right_keys = [
+            (("bin", i // col_count), ("col", i % col_count)) for i in range(bin_count * col_count)
+        ]
+        order = [left_keys.index(key) for key in right_keys]
         left_rows = jnp.stack([left_rows[j] for j in order])
     else:
         right_rows = lax.all_gather(local_rows, ("bin", "col"), axis=0, tiled=False)

time: 222 us -> 229 us (1.032)
  between operations: 1.02 us -> 14.4 us
  starting transfers between devices: 41.6 us -> 34.8 us
  local copies, waits for them, and re-layouts: 1.58 us -> 7.75 us
  waiting for transfers between devices: 102 us -> 97.9 us
  other arithmetic: 53.6 us -> 49.9 us
    ppermute x6 -> x3, waiting for transfers between devices: 47.4 us -> 13.6 us  [_butterfly_gather(): other = lax.ppermute(x, axis, [(i, i ^ step) for i in range(count)])]
    all_gather x0 -> x1, waiting for transfers between devices: none -> 29.6 us  [shards(): right_rows = lax.all_gather(local_rows, ('bin', 'col'), axis=0, tiled=False)]
    unnamed x16, local copies, waits for them, and re-layouts: 1.02 us -> 5.82 us
    select_n x5 -> x3, other arithmetic: 7.39 us -> 3.72 us  [_butterfly_gather(): jnp.where(low, jnp.concatenate([x, other], 0), jnp.concatenate([other, x]...]
    ppermute x8, starting transfers between devices: 13.2 us -> 10.2 us  [_butterfly_sum(): x = x + lax.ppermute(x, axis, [(i, i ^ step) for i in range(count)])]
    ppermute x6 -> x3, starting transfers between devices: 23.3 us -> 20.8 us  [_butterfly_gather(): other = lax.ppermute(x, axis, [(i, i ^ step) for i in range(count)])]
  transfers between devices with their start and end apart: 19 -> 17, of which waited for: 17 -> 16; matrix products, arithmetic and copies ran while one was open for 3% -> 4% of each run, Pallas kernels for 0% -> 0%
where the time goes in v5:
time: 229 us
  waiting for transfers between devices  97.9 us (43%)
  other arithmetic  49.9 us (22%)
  starting transfers between devices  34.8 us (15%)
  matrix products  24.1 us (11%)
  between operations  14.4 us (6%)
  local copies, waits for them, and re-layouts  7.75 us (3%)
    all_gather x1, waiting for transfers between devices, shards(): right_rows = lax.all_gather(local_rows, ('bin', 'col'), axis=0, tiled=False)  29.6 us
    ppermute x8, waiting for transfers between devices, _butterfly_sum(): x = x + lax.ppermute(x, axis, [(i, i ^ step) for i in range(count)])  27.8 us
    another operation x6, other arithmetic, _qr_step(): lower_factor = jnp.linalg.cholesky(gram_matrix)  24.8 us
    another operation x4, other arithmetic, _qr_step(): jax.scipy.linalg.solve_triangular(lower_factor, image.T, lower=True)  21.1 us
    ppermute x3, starting transfers between devices, _butterfly_gather(): other = lax.ppermute(x, axis, [(i, i ^ step) for i in range(count)])  20.8 us
    ppermute x2, waiting for transfers between devices, _halving_sum(): x = keep + lax.ppermute(give, axis, [(i, i ^ step) for i in range(count)])  13.7 us
    ppermute x3, waiting for transfers between devices, _butterfly_gather(): other = lax.ppermute(x, axis, [(i, i ^ step) for i in range(count)])  13.6 us
    ppermute x2, waiting for transfers between devices, _halving_sum(): other = lax.ppermute(x, axis, [(i, i ^ step) for i in range(count)])  13.1 us
  transfers between devices with their start and end apart: 17, of which 16 were waited for; matrix products, arithmetic and copies ran while one was open for 4% of the time, Pallas kernels for 0%

profile of v5, /device:TPU:0, one launch (start us, length us, event | category | flops | bytes accessed | tf_op | source)
XLA Modules:
  0.0 228.7 jit_solution(10340013814188939774)
XLA Ops:
  7.2 2.2 fusion.26
  10.0 0.9 collective-permute-done
  10.9 2.9 %collective-permute-start.1 = (f32[8,128,16]{1,2,0:T(8,128)S(1)}, f32[8,128,16]{1,2,0:T(8,128)S(1)}, u32[]{:S(2)}, u32[]{:S(2)}) collective-permute-start(f32[8,128,16]{1,2,0:T(8,128)S(1)} %add.48), channel_id=1, source_target_pairs={{0,8},{4,12},{8,0},{12,4},{1,9},{5,13},{9,1},{13,5},{2,10},{6,14},... | collective-permute-start | bytes 196616 | tf_op jit(solution)/shard_map/ppermute | solution.py:26
  13.8 2.4 %collective-permute-done.1 = f32[8,128,16]{1,2,0:T(8,128)S(1)} collective-permute-done((f32[8,128,16]{1,2,0:T(8,128)S(1)}, f32[8,128,16]{1,2,0:T(8,128)S(1)}, u32[]{:S(2)}, u32[]{:S(2)}) %collective-permute-start.1) | collective-permute-done | bytes 65568 | tf_op jit(solution)/shard_map/ppermute | solution.py:26
  17.1 0.7 collective-permute-start.2
  17.8 1.9 collective-permute-start.3
  19.8 4.5 %collective-permute-done.3 = bf16[1,1024,128]{2,1,0:T(8,128)(2,1)S(1)} collective-permute-done((bf16[1,1024,128]{2,1,0:T(8,128)(2,1)S(1)}, bf16[1,1024,128]{2,1,0:T(8,128)(2,1)S(1)}, u32[]{:S(2)}, u32[]{:S(2)}) %collective-permute-start.3) | collective-permute-done | bytes 262176 | tf_op jit(solution)/shard_map/ppermute | solution.py:52
  24.3 18.7 %collective-permute-start.4 = (bf16[2,1024,128]{2,1,0:T(8,128)(2,1)S(1)}, bf16[2,1024,128]{2,1,0:T(8,128)(2,1)}, u32[]{:S(2)}, u32[]{:S(2)}) collective-permute-start(bf16[2,1024,128]{2,1,0:T(8,128)(2,1)S(1)} %maximum_select_fusion.2), channel_id=1, source_target_pairs={{0,8},{4,12},{8,0},{12,4},{1,9},{5,13},{9,1},{13,5},{2,10},{6,14},... | collective-permute-start | bytes 1572872 | tf_op jit(solution)/shard_map/ppermute | solution.py:52
  43.1 0.8 copy.18
  44.0 6.4 %collective-permute-done.4 = bf16[2,1024,128]{2,1,0:T(8,128)(2,1)} collective-permute-done((bf16[2,1024,128]{2,1,0:T(8,128)(2,1)S(1)}, bf16[2,1024,128]{2,1,0:T(8,128)(2,1)}, u32[]{:S(2)}, u32[]{:S(2)}) %collective-permute-start.4) | collective-permute-done | bytes 524320 | tf_op jit(solution)/shard_map/ppermute | solution.py:52
  50.4 1.7 maximum_select_fusion.1
  52.2 2.8 %collective-permute-done.5 = bf16[4,1024,128]{2,1,0:T(8,128)(2,1)} collective-permute-done((bf16[4,1024,128]{2,1,0:T(8,128)(2,1)S(1)}, bf16[4,1024,128]{2,1,0:T(8,128)(2,1)}, u32[]{:S(2)}, u32[]{:S(2)}) %collective-permute-start.5) | collective-permute-done | bytes 1048608 | tf_op jit(solution)/shard_map/ppermute | solution.py:52
  55.0 1.9 maximum_select_fusion
  56.9 0.7 slice_dynamic-update-slice_fusion.7
  57.6 0.7 slice_dynamic-update-slice_fusion.6
  58.3 0.7 slice_dynamic-update-slice_fusion.5
  59.0 0.7 slice_dynamic-update-slice_fusion.4
  59.7 0.7 slice_dynamic-update-slice_fusion.3
  60.5 0.7 slice_dynamic-update-slice_fusion.2
  61.2 0.7 slice_dynamic-update-slice_fusion.1
  61.9 0.7 slice_dynamic-update-slice_fusion
  62.6 29.6 %all-gather.2.cloned.1.call-done = bf16[8,1024,128]{2,1,0:T(8,128)(2,1)} async-done(((bf16[1,1024,128]{2,1,0:T(8,128)(2,1)}), bf16[8,1024,128]{2,1,0:T(8,128)(2,1)}) %all-gather.2.cloned.1.call-update) | async-done | bytes 2097168 | tf_op jit(solution)/shard_map/all_gather | solution.py:119
  92.2 4.6 %bitcast_multiply_fusion = f32[1024,1024]{1,0:T(8,128)S(1)} fusion(bf16[8,1024,128]{2,1,0:T(8,128)(2,1)} %slice_dynamic-update-slice_fusion, bf16[8,1024,128]{2,1,0:T(8,128)(2,1)} %all-gather.2.cloned.1.call-done), kind=kOutput, calls=%fused_computation | convolution fusion | flops 2148532224 | bytes 8388608 | tf_op jit(solution)/shard_map/dot_general | solution.py:134
  96.8 4.9 %fusion.6 = f32[1024,128]{1,0:T(8,128)S(1)} fusion(f32[1024,1024]{1,0:T(8,128)S(1)} %bitcast_multiply_fusion, f32[4096,128]{1,0:T(8,128)} %param.10, s32[]{:T(128)S(6)} %select_n.91), kind=kOutput, calls=%fused_computation.12 | convolution fusion | flops 1610612736 | bytes 5242884 | tf_op jit(solution)/shard_map/dot_general | solution.py:142
  101.8 1.9 collective-permute-done.6
  103.8 1.5 collective-permute-start.7
  105.3 12.5 %collective-permute-done.7 = f32[1024,128]{1,0:T(8,128)S(1)} collective-permute-done((f32[1024,128]{1,0:T(8,128)S(1)}, f32[1024,128]{1,0:T(8,128)S(1)}, u32[]{:S(2)}, u32[]{:S(2)}) %collective-permute-start.7) | collective-permute-done | bytes 524320 | tf_op jit(solution)/shard_map/ppermute | solution.py:26
  117.8 1.0 fusion.12
  118.8 1.6 collective-permute-start.8
  120.4 2.7 %collective-permute-done.8 = f32[128,128]{0,1:T(8,128)S(1)} collective-permute-done((f32[128,128]{0,1:T(8,128)S(1)}, f32[128,128]{0,1:T(8,128)S(1)}, u32[]{:S(2)}, u32[]{:S(2)}) %collective-permute-start.8) | collective-permute-done | bytes 65568 | tf_op jit(solution)/shard_map/ppermute | solution.py:26
  123.1 1.9 collective-permute-start.9
  125.1 3.3 %collective-permute-done.9 = f32[128,128]{0,1:T(8,128)S(1)} collective-permute-done((f32[128,128]{0,1:T(8,128)S(1)}, f32[128,128]{0,1:T(8,128)S(1)}, u32[]{:S(2)}, u32[]{:S(2)}) %collective-permute-start.9) | collective-permute-done | bytes 65568 | tf_op jit(solution)/shard_map/ppermute | solution.py:26
  128.5 11.7 %cholesky.44 = f32[128,128]{1,0:T(8,128)S(1)} custom-call(f32[128,128]{1,0:T(8,128)S(1)} %fusion.19), custom_call_target="Cholesky" | custom-call | tf_op jit(solution)/shard_map/jit(cholesky)/cholesky | solution.py:93
  141.6 9.9 %custom-call.6 = f32[1,128,128]{1,2,0:T(8,128)S(1)} custom-call(f32[1,128,128]{2,1,0:T(8,128)S(1)} %fusion.14), custom_call_target="InvertDiagBlocksLowerTriangular" | custom-call | tf_op jit(solution)/shard_map/jit(_solve_triangular)/triangular_solve | solution.py:94
  152.1 8.5 %fusion.25 = f32[1024,128]{1,0:T(8,128)S(1)} fusion(f32[1024,1024]{1,0:T(8,128)} %copy-done.1, f32[128,1024]{1,0:T(8,128)S(1)} %fusion.4), kind=kOutput, calls=%fused_computation.56 | convolution fusion | flops 1610612736 | bytes 5242880 | tf_op jit(solution)/shard_map/dot_general | solution.py:149
  160.7 1.6 collective-permute-start.10
  162.3 6.2 %collective-permute-done.10 = f32[512,128]{1,0:T(8,128)S(1)} collective-permute-done((f32[512,128]{1,0:T(8,128)S(1)}, f32[512,128]{1,0:T(8,128)S(1)}, u32[]{:S(2)}, u32[]{:S(2)}) %collective-permute-start.10) | collective-permute-done | bytes 262176 | tf_op jit(solution)/shard_map/ppermute | solution.py:80
  168.6 1.4 collective-permute-start.11
  170.0 7.5 %collective-permute-done.11 = f32[256,128]{1,0:T(8,128)S(1)} collective-permute-done((f32[256,128]{1,0:T(8,128)S(1)}, f32[256,128]{1,0:T(8,128)S(1)}, u32[]{:S(2)}, u32[]{:S(2)}) %collective-permute-start.11) | collective-permute-done | bytes 131104 | tf_op jit(solution)/shard_map/ppermute | solution.py:80
  177.6 6.7 %collective-permute-done.12 = f32[256,128]{1,0:T(8,128)S(1)} collective-permute-done((f32[256,128]{1,0:T(8,128)S(1)}, f32[256,128]{1,0:T(8,128)S(1)}, u32[]{:S(2)}, u32[]{:S(2)}) %collective-permute-start.12) | collective-permute-done | bytes 131104 | tf_op jit(solution)/shard_map/ppermute | solution.py:83
  184.4 6.4 %collective-permute-done.13 = f32[512,128]{1,0:T(8,128)S(1)} collective-permute-done((f32[512,128]{1,0:T(8,128)S(1)}, f32[512,128]{1,0:T(8,128)S(1)}, u32[]{:S(2)}, u32[]{:S(2)}) %collective-permute-start.13) | collective-permute-done | bytes 262176 | tf_op jit(solution)/shard_map/ppermute | solution.py:83
  190.8 1.0 fusion.8
  191.9 1.2 collective-permute-done.14
  193.1 1.5 collective-permute-start.15
  194.7 2.8 %collective-permute-done.15 = f32[128,128]{0,1:T(8,128)S(1)} collective-permute-done((f32[128,128]{0,1:T(8,128)S(1)}, f32[128,128]{0,1:T(8,128)S(1)}, u32[]{:S(2)}, u32[]{:S(2)}) %collective-permute-start.15) | collective-permute-done | bytes 65568 | tf_op jit(solution)/shard_map/ppermute | solution.py:26
  197.6 11.7 %cholesky.55 = f32[128,128]{1,0:T(8,128)S(1)} custom-call(f32[128,128]{1,0:T(8,128)S(1)} %fusion.17), custom_call_target="Cholesky" | custom-call | tf_op jit(solution)/shard_map/jit(cholesky)/cholesky | solution.py:93
  210.6 9.8 %custom-call.7 = f32[1,128,128]{1,2,0:T(8,128)S(1)} custom-call(f32[1,128,128]{2,1,0:T(8,128)S(1)} %fusion.15), custom_call_target="InvertDiagBlocksLowerTriangular" | custom-call | tf_op jit(solution)/shard_map/jit(_solve_triangular)/triangular_solve | solution.py:94
  221.1 0.8 copy.25
  (45 shorter events, 6.3 us)
Async XLA Ops:
  7.2 9.1 %copy-start = (bf16[8,1024,128]{2,1,0:T(8,128)(2,1)S(1)}, bf16[8,1024,128]{2,1,0:T(8,128)(2,1)}, u32[]{:S(2)}) copy-start(bf16[8,1024,128]{2,1,0:T(8,128)(2,1)} %param.9) | copy-start | bytes 6291460
  7.2 9.0 %copy-start.3 = (bf16[1024,8,16]{0,2,1:T(8,128)(2,1)S(1)}, bf16[1024,8,16]{0,2,1:T(8,128)(2,1)}, u32[]{:S(2)}) copy-start(bf16[1024,8,16]{0,2,1:T(8,128)(2,1)} %param.7) | copy-start | bytes 786436
  7.2 85.0 %all-gather.2.cloned.1.call-start = ((), (), s32[]{:S(2)}) async-start(), calls=%async_computation | async-start | bytes 2359296 | tf_op jit(solution)/shard_map/all_gather | solution.py:119
  9.4 1.5 collective-permute-start
  10.9 5.3 %collective-permute-start.1 = (f32[8,128,16]{1,2,0:T(8,128)S(1)}, f32[8,128,16]{1,2,0:T(8,128)S(1)}, u32[]{:S(2)}, u32[]{:S(2)}) collective-permute-start(f32[8,128,16]{1,2,0:T(8,128)S(1)} %add.48), channel_id=1, source_target_pairs={{0,8},{4,12},{8,0},{12,4},{1,9},{5,13},{9,1},{13,5},{2,10},{6,14},... | collective-permute-start | bytes 196616 | tf_op jit(solution)/shard_map/ppermute | solution.py:26
  17.1 0.7 collective-permute-start.2
  17.8 6.4 %collective-permute-start.3 = (bf16[1,1024,128]{2,1,0:T(8,128)(2,1)S(1)}, bf16[1,1024,128]{2,1,0:T(8,128)(2,1)S(1)}, u32[]{:S(2)}, u32[]{:S(2)}) collective-permute-start(bf16[1,1024,128]{2,1,0:T(8,128)(2,1)S(1)} %select_bitcast_fusion), channel_id=1, source_target_pairs={{0,16},{16,0},{1,17},{17,1},{2,18},{18,2},{3,19},{19,3},{4,20},{20... | collective-permute-start | bytes 786440 | tf_op jit(solution)/shard_map/ppermute | solution.py:52
  24.3 19.6 %copy-start.2 = (bf16[2,1024,128]{2,1,0:T(8,128)(2,1)}, bf16[2,1024,128]{2,1,0:T(8,128)(2,1)S(1)}, u32[]{:S(2)}) copy-start(bf16[2,1024,128]{2,1,0:T(8,128)(2,1)S(1)} %maximum_select_fusion.2) | copy-start | bytes 1572868
  24.3 26.0 %collective-permute-start.4 = (bf16[2,1024,128]{2,1,0:T(8,128)(2,1)S(1)}, bf16[2,1024,128]{2,1,0:T(8,128)(2,1)}, u32[]{:S(2)}, u32[]{:S(2)}) collective-permute-start(bf16[2,1024,128]{2,1,0:T(8,128)(2,1)S(1)} %maximum_select_fusion.2), channel_id=1, source_target_pairs={{0,8},{4,12},{8,0},{12,4},{1,9},{5,13},{9,1},{13,5},{2,10},{6,14},... | collective-permute-start | bytes 1572872 | tf_op jit(solution)/shard_map/ppermute | solution.py:52
  52.1 2.9 %collective-permute-start.5 = (bf16[4,1024,128]{2,1,0:T(8,128)(2,1)S(1)}, bf16[4,1024,128]{2,1,0:T(8,128)(2,1)}, u32[]{:S(2)}, u32[]{:S(2)}) collective-permute-start(bf16[4,1024,128]{2,1,0:T(8,128)(2,1)S(1)} %maximum_select_fusion.1), channel_id=1, source_target_pairs={{0,4},{4,0},{8,12},{12,8},{1,5},{5,1},{9,13},{13,9},{2,6},{6,2},{1... | collective-permute-start | bytes 3145736 | tf_op jit(solution)/shard_map/ppermute | solution.py:52
  96.8 4.9 %copy-start.1 = (f32[1024,1024]{1,0:T(8,128)}, f32[1024,1024]{1,0:T(8,128)S(1)}, u32[]{:S(2)}) copy-start(f32[1024,1024]{1,0:T(8,128)S(1)} %bitcast_multiply_fusion) | copy-start | bytes 12582916
  101.7 2.0 collective-permute-start.6
  103.8 14.0 %collective-permute-start.7 = (f32[1024,128]{1,0:T(8,128)S(1)}, f32[1024,128]{1,0:T(8,128)S(1)}, u32[]{:S(2)}, u32[]{:S(2)}) collective-permute-start(f32[1024,128]{1,0:T(8,128)S(1)} %add.52), channel_id=1, source_target_pairs={{0,8},{4,12},{8,0},{12,4},{1,9},{5,13},{9,1},{13,5},{2,10},{6,14},... | collective-permute-start | bytes 1572872 | tf_op jit(solution)/shard_map/ppermute | solution.py:26
  118.8 4.3 %collective-permute-start.8 = (f32[128,128]{0,1:T(8,128)S(1)}, f32[128,128]{0,1:T(8,128)S(1)}, u32[]{:S(2)}, u32[]{:S(2)}) collective-permute-start(f32[128,128]{0,1:T(8,128)S(1)} %fusion.12), channel_id=1, source_target_pairs={{0,1},{1,0},{2,3},{3,2},{4,5},{5,4},{6,7},{7,6},{8,9},{9,8},{10,11... | collective-permute-start | bytes 196616 | tf_op jit(solution)/shard_map/ppermute | solution.py:26
  123.1 5.2 %collective-permute-start.9 = (f32[128,128]{0,1:T(8,128)S(1)}, f32[128,128]{0,1:T(8,128)S(1)}, u32[]{:S(2)}, u32[]{:S(2)}) collective-permute-start(f32[128,128]{0,1:T(8,128)S(1)} %add.54), channel_id=1, source_target_pairs={{0,2},{1,3},{2,0},{3,1},{4,6},{5,7},{6,4},{7,5},{8,10},{9,11},{10,... | collective-permute-start | bytes 196616 | tf_op jit(solution)/shard_map/ppermute | solution.py:26
  160.7 7.8 %collective-permute-start.10 = (f32[512,128]{1,0:T(8,128)S(1)}, f32[512,128]{1,0:T(8,128)S(1)}, u32[]{:S(2)}, u32[]{:S(2)}) collective-permute-start(f32[512,128]{1,0:T(8,128)S(1)} %slice_select_fusion), channel_id=1, source_target_pairs={{0,1},{1,0},{2,3},{3,2},{4,5},{5,4},{6,7},{7,6},{8,9},{9,8},{10,11... | collective-permute-start | bytes 786440 | tf_op jit(solution)/shard_map/ppermute | solution.py:80
  168.6 8.9 %collective-permute-start.11 = (f32[256,128]{1,0:T(8,128)S(1)}, f32[256,128]{1,0:T(8,128)S(1)}, u32[]{:S(2)}, u32[]{:S(2)}) collective-permute-start(f32[256,128]{1,0:T(8,128)S(1)} %slice_select_fusion.1), channel_id=1, source_target_pairs={{0,2},{1,3},{2,0},{3,1},{4,6},{5,7},{6,4},{7,5},{8,10},{9,11},{10,... | collective-permute-start | bytes 393224 | tf_op jit(solution)/shard_map/ppermute | solution.py:80
  177.5 6.8 %collective-permute-start.12 = (f32[256,128]{1,0:T(8,128)S(1)}, f32[256,128]{1,0:T(8,128)S(1)}, u32[]{:S(2)}, u32[]{:S(2)}) collective-permute-start(f32[256,128]{1,0:T(8,128)S(1)} %select_add_fusion.1), channel_id=1, source_target_pairs={{0,2},{1,3},{2,0},{3,1},{4,6},{5,7},{6,4},{7,5},{8,10},{9,11},{10,... | collective-permute-start | bytes 393224 | tf_op jit(solution)/shard_map/ppermute | solution.py:83
  184.3 6.4 %collective-permute-start.13 = (f32[512,128]{1,0:T(8,128)S(1)}, f32[512,128]{1,0:T(8,128)S(1)}, u32[]{:S(2)}, u32[]{:S(2)}) collective-permute-start(f32[512,128]{1,0:T(8,128)S(1)} %maximum_select_fusion.6), channel_id=1, source_target_pairs={{0,1},{1,0},{2,3},{3,2},{4,5},{5,4},{6,7},{7,6},{8,9},{9,8},{10,11... | collective-permute-start | bytes 786440 | tf_op jit(solution)/shard_map/ppermute | solution.py:83
  191.8 1.3 collective-permute-start.14
  193.1 4.3 %collective-permute-start.15 = (f32[128,128]{0,1:T(8,128)S(1)}, f32[128,128]{0,1:T(8,128)S(1)}, u32[]{:S(2)}, u32[]{:S(2)}) collective-permute-start(f32[128,128]{0,1:T(8,128)S(1)} %add.58), channel_id=1, source_target_pairs={{0,8},{4,12},{8,0},{12,4},{1,9},{5,13},{9,1},{13,5},{2,10},{6,14},... | collective-permute-start | bytes 196616 | tf_op jit(solution)/shard_map/ppermute | solution.py:26
Sparse Core Ops, SparseCore 0:
  44.1 48.0 all-gather.1

commit v6 on v3

--- a/solution.py
+++ b/solution.py
@@ -37,20 +37,28 @@
     return steps[::-1] if far_first else steps
 
 
-def _butterfly_gather(x, axes):
-    x = x[None]
-    for axis in axes:
+def _direct_sum(x, axis):
+    count = lax.axis_size(axis)
+    if count != 4:
+        return _butterfly_sum(x, axis)
+    got = [lax.ppermute(x, axis, [(i, i ^ k) for i in range(count)]) for k in (1, 2, 3)]
+    return (x + got[0]) + (got[1] + got[2])
+
+
+def _butterfly_gather(xs, axes_of):
+    xs = [x[None] for x in xs]
+    plans = [[(axis, step) for axis in axes for step in _bits(lax.axis_size(axis), True)] for axes in axes_of]
+    while any(plans):
+        head = next(plan[0] for plan in plans if plan)
+        which = [k for k, plan in enumerate(plans) if plan and plan[0] == head]
+        axis, step = head
         count = lax.axis_size(axis)
-        if count & (count - 1):
-            x = lax.all_gather(x, axis, axis=0, tiled=False)
-            x = x.reshape((-1,) + x.shape[2:])
-            continue
-        here = lax.axis_index(axis)
-        for step in _bits(count, True):
-            other = lax.ppermute(x, axis, [(i, i ^ step) for i in range(count)])
-            low = (here & step) == 0
-            x = jnp.where(low, jnp.concatenate([x, other], 0), jnp.concatenate([other, x], 0))
-    return x
+        low = (lax.axis_index(axis) & step) == 0
+        others = lax.ppermute([xs[k] for k in which], axis, [(i, i ^ step) for i in range(count)])
+        for k, other in zip(which, others):
+            xs[k] = jnp.where(low, jnp.concatenate([xs[k], other], 0), jnp.concatenate([other, xs[k]], 0))
+            plans[k] = plans[k][1:]
+    return xs
 
 
 def _halving_sum(x, axis):
@@ -76,7 +84,7 @@
     gram_part = jnp.dot(
         image.T, image, precision=lax.Precision.HIGHEST, preferred_element_type=jnp.float32
     )
-    gram_matrix = _butterfly_sum(gram_part, gram_axis)
+    gram_matrix = _direct_sum(gram_part, gram_axis)
     lower_factor = jnp.linalg.cholesky(gram_matrix)
     return jax.scipy.linalg.solve_triangular(lower_factor, image.T, lower=True).T
 
@@ -91,7 +99,7 @@
     partial_proj = jnp.einsum(
         "mbs,bmr->brs", snapshots, focus_in, preferred_element_type=jnp.float32
     )
-    projected = _butterfly_sum(partial_proj, "row").astype(jnp.bfloat16)
+    projected = _direct_sum(partial_proj, "row").astype(jnp.bfloat16)
     lifted = jnp.einsum("bmr,brs->mbs", focus_out, projected, preferred_element_type=jnp.float32)
     focused = (snapshots.astype(jnp.float32) + lifted).astype(jnp.bfloat16)
     columns = bins_here * snaps_here
@@ -100,12 +108,15 @@
     col_block = array_size // col_count
     scaling = 1.0 / (columns * col_count * bin_count)
 
-    right_rows = _butterfly_gather(local_rows, ("bin", "col"))
-    if row_count == col_count:
+    power_of_two = all(n & (n - 1) == 0 for n in (bin_count, row_count, col_count))
+    if row_count == col_count and power_of_two:
         swapped = lax.ppermute(local_rows, ("row", "col"), _transpose_pairs(row_count, col_count))
         swapped = jnp.where(row_here == col_here, local_rows, swapped)
-        left_rows = _butterfly_gather(swapped, ("bin", "row"))
+        right_rows, left_rows = _butterfly_gather(
+            [local_rows, swapped], [("bin", "col"), ("bin", "row")]
+        )
     else:
+        right_rows = lax.all_gather(local_rows, ("bin", "col"), axis=0, tiled=False)
         every_row = lax.all_gather(right_rows, "row", axis=1, tiled=True)
         left_rows = lax.dynamic_slice_in_dim(every_row, col_here * col_block, col_block, 1)
     covariance = lax.dot_general(

time: 213 us -> 210 us (0.986)
  waiting for transfers between devices: 107 us -> 96.5 us
  starting transfers between devices: 26.8 us -> 34.3 us
    ppermute x8 -> x2, waiting for transfers between devices: 33.7 us -> 15.8 us  [_butterfly_sum(): x = x + lax.ppermute(x, axis, [(i, i ^ step) for i in range(count)])]
    ppermute x6 -> x15, starting transfers between devices: 20.1 us -> 30.1 us  [the longest x6 20.3 us: _butterfly_gather(): lax.ppermute([xs[k] for k in which], axis, [(i, i ^ step) for i in range(...]
    ppermute x6 -> x15, waiting for transfers between devices: 44 us -> 53.5 us  [the longest x6 43.6 us: _butterfly_gather(): lax.ppermute([xs[k] for k in which], axis, [(i, i ^ step) for i in range(...]
    ppermute x8 -> x2, starting transfers between devices: 4.7 us -> 0.14 us  [_butterfly_sum(): x = x + lax.ppermute(x, axis, [(i, i ^ step) for i in range(count)])]
    ppermute x2, waiting for transfers between devices: 16.1 us -> 14 us  [_halving_sum(): x = keep + lax.ppermute(give, axis, [(i, i ^ step) for i in range(count)])]
  transfers between devices with their start and end apart: 19 -> 22, of which waited for: 15 -> 14; matrix products, arithmetic and copies ran while one was open for 3% -> 3% of each run, Pallas kernels for 0% -> 0%
where the time goes in v6:
time: 210 us
  waiting for transfers between devices  96.5 us (46%)
  other arithmetic  51.9 us (25%)
  starting transfers between devices  34.3 us (16%)
  matrix products  24.8 us (12%)
    ppermute x6, waiting for transfers between devices, _butterfly_gather(): lax.ppermute([xs[k] for k in which], axis, [(i, i ^ step) for i in range(...  43.6 us
    another operation x6, other arithmetic, _qr_step(): lower_factor = jnp.linalg.cholesky(gram_matrix)  24.8 us
    another operation x4, other arithmetic, _qr_step(): jax.scipy.linalg.solve_triangular(lower_factor, image.T, lower=True)  20.9 us
    ppermute x6, starting transfers between devices, _butterfly_gather(): lax.ppermute([xs[k] for k in which], axis, [(i, i ^ step) for i in range(...  20.3 us
    ppermute x2, waiting for transfers between devices, _butterfly_sum(): x = x + lax.ppermute(x, axis, [(i, i ^ step) for i in range(count)])  15.8 us
    ppermute x2, waiting for transfers between devices, _halving_sum(): x = keep + lax.ppermute(give, axis, [(i, i ^ step) for i in range(count)])  14 us
    ppermute x2, waiting for transfers between devices, _halving_sum(): other = lax.ppermute(x, axis, [(i, i ^ step) for i in range(count)])  13.3 us
    ppermute x9, waiting for transfers between devices, _direct_sum(): lax.ppermute(x, axis, [(i, i ^ k) for i in range(count)])  9.83 us
  transfers between devices with their start and end apart: 22, of which 14 were waited for; matrix products, arithmetic and copies ran while one was open for 3% of the time, Pallas kernels for 0%

profile of v6, /device:TPU:0, one launch (start us, length us, event | category | flops | bytes accessed | tf_op | source)
XLA Modules:
  0.0 209.8 jit_solution(13577591641116098104)
XLA Ops:
  0.7 2.2 %fusion.39 = f32[8,128,16]{1,2,0:T(8,128)S(1)} fusion(bf16[1024,8,16]{0,2,1:T(8,128)(2,1)} %param.7, bf16[8,1024,128]{2,1,0:T(8,128)(2,1)} %param.8), kind=kOutput, calls=%fused_computation.67 | convolution fusion | flops 33554432 | bytes 2424832 | tf_op jit(solution)/shard_map/mbs,bmr->brs/dot_general | solution.py:99
  2.9 2.5 %collective-permute-start.2 = (f32[8,128,16]{1,2,0:T(8,128)S(1)}, f32[8,128,16]{1,2,0:T(8,128)S(1)}, u32[]{:S(2)}, u32[]{:S(2)}) collective-permute-start(f32[8,128,16]{1,2,0:T(8,128)S(1)} %fusion.39), channel_id=1, source_target_pairs={{0,12},{4,8},{8,4},{12,0},{1,13},{5,9},{9,5},{13,1},{2,14},{6,10},... | collective-permute-start | bytes 196616 | tf_op jit(solution)/shard_map/ppermute | solution.py:44
  5.3 0.6 collective-permute-start.1
  6.0 1.8 collective-permute-done.2
  7.8 2.2 %collective-permute-done.1 = f32[8,128,16]{1,2,0:T(8,128)S(1)} collective-permute-done((f32[8,128,16]{1,2,0:T(8,128)S(1)}, f32[8,128,16]{1,2,0:T(8,128)S(1)}, u32[]{:S(2)}, u32[]{:S(2)}) %collective-permute-start.1) | collective-permute-done | bytes 65568 | tf_op jit(solution)/shard_map/ppermute | solution.py:44
  10.0 0.7 fusion.13
  10.9 1.4 collective-permute-start.3
  12.4 1.8 collective-permute-start.7
  14.2 0.4 collective-permute-start.4
  14.6 5.6 %collective-permute-done.7 = bf16[1,1024,128]{2,1,0:T(8,128)(2,1)S(1)} collective-permute-done((bf16[1,1024,128]{2,1,0:T(8,128)(2,1)S(1)}, bf16[1,1024,128]{2,1,0:T(8,128)(2,1)S(1)}, u32[]{:S(2)}, u32[]{:S(2)}) %collective-permute-start.7) | collective-permute-done | bytes 262176 | tf_op jit(solution)/shard_map/ppermute | solution.py:57
  20.2 11.1 %collective-permute-start.8 = (bf16[2,1024,128]{2,1,0:T(8,128)(2,1)S(1)}, bf16[2,1024,128]{2,1,0:T(8,128)(2,1)}, u32[]{:S(2)}, u32[]{:S(2)}) collective-permute-start(bf16[2,1024,128]{2,1,0:T(8,128)(2,1)S(1)} %maximum_select_fusion.7), channel_id=1, source_target_pairs={{0,2},{1,3},{2,0},{3,1},{4,6},{5,7},{6,4},{7,5},{8,10},{9,11},{10,... | collective-permute-start | bytes 1572872 | tf_op jit(solution)/shard_map/ppermute | solution.py:57
  31.4 1.1 maximum_select_fusion.6
  32.5 6.9 %collective-permute-start.5 = (bf16[2,1024,128]{2,1,0:T(8,128)(2,1)S(1)}, bf16[2,1024,128]{2,1,0:T(8,128)(2,1)}, u32[]{:S(2)}, u32[]{:S(2)}) collective-permute-start(bf16[2,1024,128]{2,1,0:T(8,128)(2,1)S(1)} %maximum_select_fusion.6), channel_id=1, source_target_pairs={{0,8},{4,12},{8,0},{12,4},{1,9},{5,13},{9,1},{13,5},{2,10},{6,14},... | collective-permute-start | bytes 1572872 | tf_op jit(solution)/shard_map/ppermute | solution.py:57
  39.4 15.0 %collective-permute-done.8 = bf16[2,1024,128]{2,1,0:T(8,128)(2,1)} collective-permute-done((bf16[2,1024,128]{2,1,0:T(8,128)(2,1)S(1)}, bf16[2,1024,128]{2,1,0:T(8,128)(2,1)}, u32[]{:S(2)}, u32[]{:S(2)}) %collective-permute-start.8) | collective-permute-done | bytes 524320 | tf_op jit(solution)/shard_map/ppermute | solution.py:57
  54.4 2.4 %maximum_select_fusion.5 = bf16[4,1024,128]{2,1,0:T(8,128)(2,1)} fusion(bf16[2,1024,128]{2,1,0:T(8,128)(2,1)} %collective-permute-done.8, bf16[2,1024,128]{2,1,0:T(8,128)(2,1)S(1)} %maximum_select_fusion.7, pred[]{:T(512)S(6)} %eq.27), kind=kLoop, calls=%fused_computation.19 | loop fusion | flops 1572864 | bytes 2097153 | tf_op jit(solution)/shard_map/jit(_where)/select_n | solution.py:59
  56.8 2.3 %maximum_select_fusion.4 = bf16[4,1024,128]{2,1,0:T(8,128)(2,1)} fusion(bf16[2,1024,128]{2,1,0:T(8,128)(2,1)} %collective-permute-done.5, bf16[2,1024,128]{2,1,0:T(8,128)(2,1)S(1)} %maximum_select_fusion.6, pred[]{:T(512)S(6)} %eq.23), kind=kLoop, calls=%fused_computation.18 | loop fusion | flops 1572864 | bytes 2097153 | tf_op jit(solution)/shard_map/jit(_where)/select_n | solution.py:59
  59.2 23.0 %collective-permute-done.9 = bf16[4,1024,128]{2,1,0:T(8,128)(2,1)} collective-permute-done((bf16[4,1024,128]{2,1,0:T(8,128)(2,1)}, bf16[4,1024,128]{2,1,0:T(8,128)(2,1)}, u32[]{:S(2)}, u32[]{:S(2)}) %collective-permute-start.9) | collective-permute-done | bytes 1048608 | tf_op jit(solution)/shard_map/ppermute | solution.py:57
  82.3 5.3 %bitcast_multiply_fusion = f32[1024,1024]{1,0:T(8,128)S(1)} fusion(bf16[4,1024,128]{2,1,0:T(8,128)(2,1)S(1)} %collective-permute-done.6, bf16[4,1024,128]{2,1,0:T(8,128)(2,1)} %maximum_select_fusion.4, bf16[4,1024,128]{2,1,0:T(8,128)(2,1)} %collective-permute-done.9, bf16[4,1024,128]{2,1,0:T(8,128)(2,1)} %maximum_select_fusion.5, pred[]{:T(512)S(6)} %eq.26, ...), kind=kOutput, calls=%fused_computation | convolution fusion | flops 2154823680 | bytes 8388610 | tf_op jit(solution)/shard_map/dot_general | solution.py:122
  87.6 4.9 %fusion.18 = f32[1024,128]{1,0:T(8,128)S(1)} fusion(f32[1024,1024]{1,0:T(8,128)S(1)} %bitcast_multiply_fusion, f32[4096,128]{1,0:T(8,128)} %param.10, s32[]{:T(128)S(6)} %select_n.112), kind=kOutput, calls=%fused_computation.27 | convolution fusion | flops 1610612736 | bytes 5242884 | tf_op jit(solution)/shard_map/dot_general | solution.py:130
  92.6 1.9 collective-permute-done.10
  94.6 14.0 %collective-permute-done.11 = f32[1024,128]{1,0:T(8,128)S(1)} collective-permute-done((f32[1024,128]{1,0:T(8,128)S(1)}, f32[1024,128]{1,0:T(8,128)S(1)}, u32[]{:S(2)}, u32[]{:S(2)}) %collective-permute-start.11) | collective-permute-done | bytes 524320 | tf_op jit(solution)/shard_map/ppermute | solution.py:26
  108.6 1.0 fusion.24
  109.7 1.0 collective-permute-start.12
  110.7 3.4 %collective-permute-start.14 = (f32[128,128]{0,1:T(8,128)S(1)}, f32[128,128]{0,1:T(8,128)S(1)}, u32[]{:S(2)}, u32[]{:S(2)}) collective-permute-start(f32[128,128]{0,1:T(8,128)S(1)} %fusion.24), channel_id=1, source_target_pairs={{0,3},{1,2},{2,1},{3,0},{4,7},{5,6},{6,5},{7,4},{8,11},{9,10},{10,... | collective-permute-start | bytes 196616 | tf_op jit(solution)/shard_map/ppermute | solution.py:44
  114.1 2.3 %collective-permute-done.13 = f32[128,128]{0,1:T(8,128)S(1)} collective-permute-done((f32[128,128]{0,1:T(8,128)S(1)}, f32[128,128]{0,1:T(8,128)S(1)}, u32[]{:S(2)}, u32[]{:S(2)}) %collective-permute-start.13) | collective-permute-done | bytes 65568 | tf_op jit(solution)/shard_map/ppermute | solution.py:44
  116.4 0.9 collective-permute-done.14
  117.4 11.7 %cholesky.44 = f32[128,128]{1,0:T(8,128)S(1)} custom-call(f32[128,128]{1,0:T(8,128)S(1)} %fusion.31), custom_call_target="Cholesky" | custom-call | tf_op jit(solution)/shard_map/jit(cholesky)/cholesky | solution.py:88
  129.1 0.6 compare_reduce_fusion.1
  129.8 0.7 fusion.26
  130.4 9.8 %custom-call.6 = f32[1,128,128]{1,2,0:T(8,128)S(1)} custom-call(f32[1,128,128]{2,1,0:T(8,128)S(1)} %fusion.26), custom_call_target="InvertDiagBlocksLowerTriangular" | custom-call | tf_op jit(solution)/shard_map/jit(_solve_triangular)/triangular_solve | solution.py:89
  140.2 0.6 fusion.16
  140.9 8.5 %fusion.38 = f32[1024,128]{1,0:T(8,128)S(1)} fusion(f32[1024,1024]{1,0:T(8,128)} %copy-done.1, f32[128,1024]{1,0:T(8,128)S(1)} %fusion.16), kind=kOutput, calls=%fused_computation.66 | convolution fusion | flops 1610612736 | bytes 5242880 | tf_op jit(solution)/shard_map/dot_general | solution.py:137
  149.4 1.2 collective-permute-start.15
  150.6 5.6 %collective-permute-done.15 = f32[512,128]{1,0:T(8,128)S(1)} collective-permute-done((f32[512,128]{1,0:T(8,128)S(1)}, f32[512,128]{1,0:T(8,128)S(1)}, u32[]{:S(2)}, u32[]{:S(2)}) %collective-permute-start.15) | collective-permute-done | bytes 262176 | tf_op jit(solution)/shard_map/ppermute | solution.py:75
  156.2 1.2 collective-permute-start.16
  157.4 8.4 %collective-permute-done.16 = f32[256,128]{1,0:T(8,128)S(1)} collective-permute-done((f32[256,128]{1,0:T(8,128)S(1)}, f32[256,128]{1,0:T(8,128)S(1)}, u32[]{:S(2)}, u32[]{:S(2)}) %collective-permute-start.16) | collective-permute-done | bytes 131104 | tf_op jit(solution)/shard_map/ppermute | solution.py:75
  165.9 7.1 %collective-permute-done.17 = f32[256,128]{1,0:T(8,128)S(1)} collective-permute-done((f32[256,128]{1,0:T(8,128)S(1)}, f32[256,128]{1,0:T(8,128)S(1)}, u32[]{:S(2)}, u32[]{:S(2)}) %collective-permute-start.17) | collective-permute-done | bytes 131104 | tf_op jit(solution)/shard_map/ppermute | solution.py:78
  173.1 0.3 collective-permute-start.18
  173.4 6.1 %collective-permute-done.18 = f32[512,128]{1,0:T(8,128)S(1)} collective-permute-done((f32[512,128]{1,0:T(8,128)S(1)}, f32[512,128]{1,0:T(8,128)S(1)}, u32[]{:S(2)}, u32[]{:S(2)}) %collective-permute-start.18) | collective-permute-done | bytes 262176 | tf_op jit(solution)/shard_map/ppermute | solution.py:78
  179.5 1.0 fusion.20
  180.7 2.0 collective-permute-start.21
  182.7 2.6 %collective-permute-done.20 = f32[128,128]{0,1:T(8,128)S(1)} collective-permute-done((f32[128,128]{0,1:T(8,128)S(1)}, f32[128,128]{0,1:T(8,128)S(1)}, u32[]{:S(2)}, u32[]{:S(2)}) %collective-permute-start.20) | collective-permute-done | bytes 65568 | tf_op jit(solution)/shard_map/ppermute | solution.py:44
  185.5 11.7 %cholesky.55 = f32[128,128]{1,0:T(8,128)S(1)} custom-call(f32[128,128]{1,0:T(8,128)S(1)} %fusion.29), custom_call_target="Cholesky" | custom-call | tf_op jit(solution)/shard_map/jit(cholesky)/cholesky | solution.py:88
  197.3 0.6 compare_reduce_fusion
  197.9 0.7 fusion.27
  198.6 9.8 %custom-call.7 = f32[1,128,128]{1,2,0:T(8,128)S(1)} custom-call(f32[1,128,128]{2,1,0:T(8,128)S(1)} %fusion.27), custom_call_target="InvertDiagBlocksLowerTriangular" | custom-call | tf_op jit(solution)/shard_map/jit(_solve_triangular)/triangular_solve | solution.py:89
  208.4 0.6 fusion.14
  209.1 0.8 copy.21
  (42 shorter events, 1.6 us)
Async XLA Ops:
  0.6 9.4 %copy-start = (bf16[8,1024,128]{2,1,0:T(8,128)(2,1)S(1)}, bf16[8,1024,128]{2,1,0:T(8,128)(2,1)}, u32[]{:S(2)}) copy-start(bf16[8,1024,128]{2,1,0:T(8,128)(2,1)} %param.9) | copy-start | bytes 6291460
  0.6 9.4 %copy-start.2 = (bf16[1024,8,16]{0,2,1:T(8,128)(2,1)S(1)}, bf16[1024,8,16]{0,2,1:T(8,128)(2,1)}, u32[]{:S(2)}) copy-start(bf16[1024,8,16]{0,2,1:T(8,128)(2,1)} %param.7) | copy-start | bytes 786436
  2.9 5.0 %collective-permute-start.2 = (f32[8,128,16]{1,2,0:T(8,128)S(1)}, f32[8,128,16]{1,2,0:T(8,128)S(1)}, u32[]{:S(2)}, u32[]{:S(2)}) collective-permute-start(f32[8,128,16]{1,2,0:T(8,128)S(1)} %fusion.39), channel_id=1, source_target_pairs={{0,12},{4,8},{8,4},{12,0},{1,13},{5,9},{9,5},{13,1},{2,14},{6,10},... | collective-permute-start | bytes 196616 | tf_op jit(solution)/shard_map/ppermute | solution.py:44
  5.3 4.7 %collective-permute-start.1 = (f32[8,128,16]{1,2,0:T(8,128)S(1)}, f32[8,128,16]{1,2,0:T(8,128)S(1)}, u32[]{:S(2)}, u32[]{:S(2)}) collective-permute-start(f32[8,128,16]{1,2,0:T(8,128)S(1)} %fusion.39), channel_id=1, source_target_pairs={{0,8},{4,12},{8,0},{12,4},{1,9},{5,13},{9,1},{13,5},{2,10},{6,14},... | collective-permute-start | bytes 196616 | tf_op jit(solution)/shard_map/ppermute | solution.py:44
  6.0 4.0 %collective-permute-start = (f32[8,128,16]{1,2,0:T(8,128)S(1)}, f32[8,128,16]{1,2,0:T(8,128)S(1)}, u32[]{:S(2)}, u32[]{:S(2)}) collective-permute-start(f32[8,128,16]{1,2,0:T(8,128)S(1)} %fusion.39), channel_id=1, source_target_pairs={{0,4},{4,0},{8,12},{12,8},{1,5},{5,1},{9,13},{13,9},{2,6},{6,2},{1... | collective-permute-start | bytes 196616 | tf_op jit(solution)/shard_map/ppermute | solution.py:44
  10.9 3.3 %collective-permute-start.3 = (bf16[1024,128]{1,0:T(8,128)(2,1)S(1)}, bf16[1024,128]{1,0:T(8,128)(2,1)}, u32[]{:S(2)}, u32[]{:S(2)}) collective-permute-start(bf16[1024,128]{1,0:T(8,128)(2,1)S(1)} %copy.7), channel_id=1, source_target_pairs={{1,4},{2,8},{3,12},{4,1},{6,9},{7,13},{8,2},{9,6},{11,14},{12,3},{... | collective-permute-start | bytes 786440 | tf_op jit(solution)/shard_map/ppermute | solution.py:113
  12.4 7.8 %collective-permute-start.7 = (bf16[1,1024,128]{2,1,0:T(8,128)(2,1)S(1)}, bf16[1,1024,128]{2,1,0:T(8,128)(2,1)S(1)}, u32[]{:S(2)}, u32[]{:S(2)}) collective-permute-start(bf16[1,1024,128]{2,1,0:T(8,128)(2,1)S(1)} %copy.9), channel_id=1, source_target_pairs={{0,16},{16,0},{1,17},{17,1},{2,18},{18,2},{3,19},{19,3},{4,20},{20... | collective-permute-start | bytes 786440 | tf_op jit(solution)/shard_map/ppermute | solution.py:57
  14.2 17.2 %collective-permute-start.4 = (bf16[1,1024,128]{2,1,0:T(8,128)(2,1)S(1)}, bf16[1,1024,128]{2,1,0:T(8,128)(2,1)}, u32[]{:S(2)}, u32[]{:S(2)}) collective-permute-start(bf16[1,1024,128]{2,1,0:T(8,128)(2,1)S(1)} %select_bitcast_fusion), channel_id=1, source_target_pairs={{0,16},{16,0},{1,17},{17,1},{2,18},{18,2},{3,19},{19,3},{4,20},{20... | collective-permute-start | bytes 786440 | tf_op jit(solution)/shard_map/ppermute | solution.py:57
  20.2 34.1 %collective-permute-start.8 = (bf16[2,1024,128]{2,1,0:T(8,128)(2,1)S(1)}, bf16[2,1024,128]{2,1,0:T(8,128)(2,1)}, u32[]{:S(2)}, u32[]{:S(2)}) collective-permute-start(bf16[2,1024,128]{2,1,0:T(8,128)(2,1)S(1)} %maximum_select_fusion.7), channel_id=1, source_target_pairs={{0,2},{1,3},{2,0},{3,1},{4,6},{5,7},{6,4},{7,5},{8,10},{9,11},{10,... | collective-permute-start | bytes 1572872 | tf_op jit(solution)/shard_map/ppermute | solution.py:57
  32.5 24.3 %collective-permute-start.5 = (bf16[2,1024,128]{2,1,0:T(8,128)(2,1)S(1)}, bf16[2,1024,128]{2,1,0:T(8,128)(2,1)}, u32[]{:S(2)}, u32[]{:S(2)}) collective-permute-start(bf16[2,1024,128]{2,1,0:T(8,128)(2,1)S(1)} %maximum_select_fusion.6), channel_id=1, source_target_pairs={{0,8},{4,12},{8,0},{12,4},{1,9},{5,13},{9,1},{13,5},{2,10},{6,14},... | collective-permute-start | bytes 1572872 | tf_op jit(solution)/shard_map/ppermute | solution.py:57
  56.8 25.5 %collective-permute-start.9 = (bf16[4,1024,128]{2,1,0:T(8,128)(2,1)}, bf16[4,1024,128]{2,1,0:T(8,128)(2,1)}, u32[]{:S(2)}, u32[]{:S(2)}) collective-permute-start(bf16[4,1024,128]{2,1,0:T(8,128)(2,1)} %maximum_select_fusion.5), channel_id=1, source_target_pairs={{0,1},{1,0},{2,3},{3,2},{4,5},{5,4},{6,7},{7,6},{8,9},{9,8},{10,11... | collective-permute-start | bytes 3145736 | tf_op jit(solution)/shard_map/ppermute | solution.py:57
  59.1 23.2 %collective-permute-start.6 = (bf16[4,1024,128]{2,1,0:T(8,128)(2,1)}, bf16[4,1024,128]{2,1,0:T(8,128)(2,1)S(1)}, u32[]{:S(2)}, u32[]{:S(2)}) collective-permute-start(bf16[4,1024,128]{2,1,0:T(8,128)(2,1)} %maximum_select_fusion.4), channel_id=1, source_target_pairs={{0,4},{4,0},{8,12},{12,8},{1,5},{5,1},{9,13},{13,9},{2,6},{6,2},{1... | collective-permute-start | bytes 3145736 | tf_op jit(solution)/shard_map/ppermute | solution.py:57
  87.6 4.9 %copy-start.1 = (f32[1024,1024]{1,0:T(8,128)}, f32[1024,1024]{1,0:T(8,128)S(1)}, u32[]{:S(2)}) copy-start(f32[1024,1024]{1,0:T(8,128)S(1)} %bitcast_multiply_fusion) | copy-start | bytes 12582916
  92.5 2.0 collective-permute-start.10
  94.6 14.0 %collective-permute-start.11 = (f32[1024,128]{1,0:T(8,128)S(1)}, f32[1024,128]{1,0:T(8,128)S(1)}, u32[]{:S(2)}, u32[]{:S(2)}) collective-permute-start(f32[1024,128]{1,0:T(8,128)S(1)} %add.62), channel_id=1, source_target_pairs={{0,8},{4,12},{8,0},{12,4},{1,9},{5,13},{9,1},{13,5},{2,10},{6,14},... | collective-permute-start | bytes 1572872 | tf_op jit(solution)/shard_map/ppermute | solution.py:26
  109.6 6.8 %collective-permute-start.13 = (f32[128,128]{0,1:T(8,128)S(1)}, f32[128,128]{0,1:T(8,128)S(1)}, u32[]{:S(2)}, u32[]{:S(2)}) collective-permute-start(f32[128,128]{0,1:T(8,128)S(1)} %fusion.24), channel_id=1, source_target_pairs={{0,2},{1,3},{2,0},{3,1},{4,6},{5,7},{6,4},{7,5},{8,10},{9,11},{10,... | collective-permute-start | bytes 196616 | tf_op jit(solution)/shard_map/ppermute | solution.py:44
  109.7 6.7 %collective-permute-start.12 = (f32[128,128]{0,1:T(8,128)S(1)}, f32[128,128]{0,1:T(8,128)S(1)}, u32[]{:S(2)}, u32[]{:S(2)}) collective-permute-start(f32[128,128]{0,1:T(8,128)S(1)} %fusion.24), channel_id=1, source_target_pairs={{0,1},{1,0},{2,3},{3,2},{4,5},{5,4},{6,7},{7,6},{8,9},{9,8},{10,11... | collective-permute-start | bytes 196616 | tf_op jit(solution)/shard_map/ppermute | solution.py:44
  110.7 6.6 %collective-permute-start.14 = (f32[128,128]{0,1:T(8,128)S(1)}, f32[128,128]{0,1:T(8,128)S(1)}, u32[]{:S(2)}, u32[]{:S(2)}) collective-permute-start(f32[128,128]{0,1:T(8,128)S(1)} %fusion.24), channel_id=1, source_target_pairs={{0,3},{1,2},{2,1},{3,0},{4,7},{5,6},{6,5},{7,4},{8,11},{9,10},{10,... | collective-permute-start | bytes 196616 | tf_op jit(solution)/shard_map/ppermute | solution.py:44
  149.4 6.7 %collective-permute-start.15 = (f32[512,128]{1,0:T(8,128)S(1)}, f32[512,128]{1,0:T(8,128)S(1)}, u32[]{:S(2)}, u32[]{:S(2)}) collective-permute-start(f32[512,128]{1,0:T(8,128)S(1)} %slice_select_fusion), channel_id=1, source_target_pairs={{0,1},{1,0},{2,3},{3,2},{4,5},{5,4},{6,7},{7,6},{8,9},{9,8},{10,11... | collective-permute-start | bytes 786440 | tf_op jit(solution)/shard_map/ppermute | solution.py:75
  156.2 9.6 %collective-permute-start.16 = (f32[256,128]{1,0:T(8,128)S(1)}, f32[256,128]{1,0:T(8,128)S(1)}, u32[]{:S(2)}, u32[]{:S(2)}) collective-permute-start(f32[256,128]{1,0:T(8,128)S(1)} %slice_select_fusion.1), channel_id=1, source_target_pairs={{0,2},{1,3},{2,0},{3,1},{4,6},{5,7},{6,4},{7,5},{8,10},{9,11},{10,... | collective-permute-start | bytes 393224 | tf_op jit(solution)/shard_map/ppermute | solution.py:75
  165.8 7.2 %collective-permute-start.17 = (f32[256,128]{1,0:T(8,128)S(1)}, f32[256,128]{1,0:T(8,128)S(1)}, u32[]{:S(2)}, u32[]{:S(2)}) collective-permute-start(f32[256,128]{1,0:T(8,128)S(1)} %select_add_fusion.1), channel_id=1, source_target_pairs={{0,2},{1,3},{2,0},{3,1},{4,6},{5,7},{6,4},{7,5},{8,10},{9,11},{10,... | collective-permute-start | bytes 393224 | tf_op jit(solution)/shard_map/ppermute | solution.py:78
  173.1 6.4 %collective-permute-start.18 = (f32[512,128]{1,0:T(8,128)S(1)}, f32[512,128]{1,0:T(8,128)S(1)}, u32[]{:S(2)}, u32[]{:S(2)}) collective-permute-start(f32[512,128]{1,0:T(8,128)S(1)} %maximum_select_fusion.11), channel_id=1, source_target_pairs={{0,1},{1,0},{2,3},{3,2},{4,5},{5,4},{6,7},{7,6},{8,9},{9,8},{10,11... | collective-permute-start | bytes 786440 | tf_op jit(solution)/shard_map/ppermute | solution.py:78
  180.5 4.9 %collective-permute-start.20 = (f32[128,128]{0,1:T(8,128)S(1)}, f32[128,128]{0,1:T(8,128)S(1)}, u32[]{:S(2)}, u32[]{:S(2)}) collective-permute-start(f32[128,128]{0,1:T(8,128)S(1)} %fusion.20), channel_id=1, source_target_pairs={{0,8},{4,12},{8,0},{12,4},{1,9},{5,13},{9,1},{13,5},{2,10},{6,14},... | collective-permute-start | bytes 196616 | tf_op jit(solution)/shard_map/ppermute | solution.py:44
  180.6 4.8 %collective-permute-start.19 = (f32[128,128]{0,1:T(8,128)S(1)}, f32[128,128]{0,1:T(8,128)S(1)}, u32[]{:S(2)}, u32[]{:S(2)}) collective-permute-start(f32[128,128]{0,1:T(8,128)S(1)} %fusion.20), channel_id=1, source_target_pairs={{0,4},{4,0},{8,12},{12,8},{1,5},{5,1},{9,13},{13,9},{2,6},{6,2},{1... | collective-permute-start | bytes 196616 | tf_op jit(solution)/shard_map/ppermute | solution.py:44
  180.7 4.7 %collective-permute-start.21 = (f32[128,128]{0,1:T(8,128)S(1)}, f32[128,128]{0,1:T(8,128)S(1)}, u32[]{:S(2)}, u32[]{:S(2)}) collective-permute-start(f32[128,128]{0,1:T(8,128)S(1)} %fusion.20), channel_id=1, source_target_pairs={{0,12},{4,8},{8,4},{12,0},{1,13},{5,9},{9,5},{13,1},{2,14},{6,10},... | collective-permute-start | bytes 196616 | tf_op jit(solution)/shard_map/ppermute | solution.py:44

commit v7 on v6

--- a/solution.py
+++ b/solution.py
@@ -86,7 +86,13 @@
     )
     gram_matrix = _direct_sum(gram_part, gram_axis)
     lower_factor = jnp.linalg.cholesky(gram_matrix)
-    return jax.scipy.linalg.solve_triangular(lower_factor, image.T, lower=True).T
+    inverse = jax.scipy.linalg.solve_triangular(
+        lower_factor, jnp.eye(lower_factor.shape[0], dtype=lower_factor.dtype), lower=True
+    )
+    return lax.dot_general(
+        image, inverse, (((1,), (1,)), ((), ())),
+        precision=lax.Precision.HIGHEST, preferred_element_type=jnp.float32,
+    )
 
 
 def shards(snapshots, focus_in, focus_out, start_basis):

time: 210 us -> 211 us (level)
  no operation moved by 1% of the time
where the time goes in v7:
time: 211 us; the launch traced here: 210 us
  waiting for transfers between devices  96.6 us (46%)
  other arithmetic  52.8 us (25%)
  starting transfers between devices  34.3 us (16%)
  matrix products  25.3 us (12%)
    ppermute x6, waiting for transfers between devices, _butterfly_gather(): lax.ppermute([xs[k] for k in which], axis, [(i, i ^ step) for i in range(...  43.6 us
    another operation x6, other arithmetic, _qr_step(): lower_factor = jnp.linalg.cholesky(gram_matrix)  24.9 us
    another operation x4, other arithmetic, _qr_step(): jax.scipy.linalg.solve_triangular(lower_factor, jnp.eye(lower_factor.shap...  20.9 us
    ppermute x6, starting transfers between devices, _butterfly_gather(): lax.ppermute([xs[k] for k in which], axis, [(i, i ^ step) for i in range(...  20.3 us
    ppermute x2, waiting for transfers between devices, _butterfly_sum(): x = x + lax.ppermute(x, axis, [(i, i ^ step) for i in range(count)])  15.8 us
    ppermute x2, waiting for transfers between devices, _halving_sum(): x = keep + lax.ppermute(give, axis, [(i, i ^ step) for i in range(count)])  14 us
    ppermute x2, waiting for transfers between devices, _halving_sum(): other = lax.ppermute(x, axis, [(i, i ^ step) for i in range(count)])  13.3 us
    ppermute x9, waiting for transfers between devices, _direct_sum(): lax.ppermute(x, axis, [(i, i ^ k) for i in range(count)])  9.83 us
  transfers between devices with their start and end apart: 22, of which 14 were waited for; matrix products, arithmetic and copies ran while one was open for 3% of the time, Pallas kernels for 0%

profile of v7, /device:TPU:0, one launch (start us, length us, event | category | flops | bytes accessed | tf_op | source)
XLA Modules:
  0.0 210.4 jit_solution(15051057478902374555)
XLA Ops:
  0.7 2.2 %fusion.37 = f32[8,128,16]{1,2,0:T(8,128)S(1)} fusion(bf16[1024,8,16]{0,2,1:T(8,128)(2,1)} %param.7, bf16[8,1024,128]{2,1,0:T(8,128)(2,1)} %param.8), kind=kOutput, calls=%fused_computation.66 | convolution fusion | flops 33554432 | bytes 2424832 | tf_op jit(solution)/shard_map/mbs,bmr->brs/dot_general | solution.py:105
  2.9 2.5 %collective-permute-start.2 = (f32[8,128,16]{1,2,0:T(8,128)S(1)}, f32[8,128,16]{1,2,0:T(8,128)S(1)}, u32[]{:S(2)}, u32[]{:S(2)}) collective-permute-start(f32[8,128,16]{1,2,0:T(8,128)S(1)} %fusion.37), channel_id=1, source_target_pairs={{0,12},{4,8},{8,4},{12,0},{1,13},{5,9},{9,5},{13,1},{2,14},{6,10},... | collective-permute-start | bytes 196616 | tf_op jit(solution)/shard_map/ppermute | solution.py:44
  5.3 0.6 collective-permute-start.1
  6.0 1.8 collective-permute-done.2
  7.8 2.2 %collective-permute-done.1 = f32[8,128,16]{1,2,0:T(8,128)S(1)} collective-permute-done((f32[8,128,16]{1,2,0:T(8,128)S(1)}, f32[8,128,16]{1,2,0:T(8,128)S(1)}, u32[]{:S(2)}, u32[]{:S(2)}) %collective-permute-start.1) | collective-permute-done | bytes 65568 | tf_op jit(solution)/shard_map/ppermute | solution.py:44
  10.0 0.7 fusion.13
  10.9 1.4 collective-permute-start.3
  12.4 1.8 collective-permute-start.7
  14.2 0.4 collective-permute-start.4
  14.6 5.6 %collective-permute-done.7 = bf16[1,1024,128]{2,1,0:T(8,128)(2,1)S(1)} collective-permute-done((bf16[1,1024,128]{2,1,0:T(8,128)(2,1)S(1)}, bf16[1,1024,128]{2,1,0:T(8,128)(2,1)S(1)}, u32[]{:S(2)}, u32[]{:S(2)}) %collective-permute-start.7) | collective-permute-done | bytes 262176 | tf_op jit(solution)/shard_map/ppermute | solution.py:57
  20.2 11.1 %collective-permute-start.8 = (bf16[2,1024,128]{2,1,0:T(8,128)(2,1)S(1)}, bf16[2,1024,128]{2,1,0:T(8,128)(2,1)}, u32[]{:S(2)}, u32[]{:S(2)}) collective-permute-start(bf16[2,1024,128]{2,1,0:T(8,128)(2,1)S(1)} %maximum_select_fusion.7), channel_id=1, source_target_pairs={{0,2},{1,3},{2,0},{3,1},{4,6},{5,7},{6,4},{7,5},{8,10},{9,11},{10,... | collective-permute-start | bytes 1572872 | tf_op jit(solution)/shard_map/ppermute | solution.py:57
  31.4 1.1 maximum_select_fusion.6
  32.5 6.9 %collective-permute-start.5 = (bf16[2,1024,128]{2,1,0:T(8,128)(2,1)S(1)}, bf16[2,1024,128]{2,1,0:T(8,128)(2,1)}, u32[]{:S(2)}, u32[]{:S(2)}) collective-permute-start(bf16[2,1024,128]{2,1,0:T(8,128)(2,1)S(1)} %maximum_select_fusion.6), channel_id=1, source_target_pairs={{0,8},{4,12},{8,0},{12,4},{1,9},{5,13},{9,1},{13,5},{2,10},{6,14},... | collective-permute-start | bytes 1572872 | tf_op jit(solution)/shard_map/ppermute | solution.py:57
  39.4 15.0 %collective-permute-done.8 = bf16[2,1024,128]{2,1,0:T(8,128)(2,1)} collective-permute-done((bf16[2,1024,128]{2,1,0:T(8,128)(2,1)S(1)}, bf16[2,1024,128]{2,1,0:T(8,128)(2,1)}, u32[]{:S(2)}, u32[]{:S(2)}) %collective-permute-start.8) | collective-permute-done | bytes 524320 | tf_op jit(solution)/shard_map/ppermute | solution.py:57
  54.4 2.4 %maximum_select_fusion.5 = bf16[4,1024,128]{2,1,0:T(8,128)(2,1)} fusion(bf16[2,1024,128]{2,1,0:T(8,128)(2,1)} %collective-permute-done.8, bf16[2,1024,128]{2,1,0:T(8,128)(2,1)S(1)} %maximum_select_fusion.7, pred[]{:T(512)S(6)} %eq.33), kind=kLoop, calls=%fused_computation.19 | loop fusion | flops 1572864 | bytes 2097153 | tf_op jit(solution)/shard_map/jit(_where)/select_n | solution.py:59
  56.8 2.3 %maximum_select_fusion.4 = bf16[4,1024,128]{2,1,0:T(8,128)(2,1)} fusion(bf16[2,1024,128]{2,1,0:T(8,128)(2,1)} %collective-permute-done.5, bf16[2,1024,128]{2,1,0:T(8,128)(2,1)S(1)} %maximum_select_fusion.6, pred[]{:T(512)S(6)} %eq.29), kind=kLoop, calls=%fused_computation.18 | loop fusion | flops 1572864 | bytes 2097153 | tf_op jit(solution)/shard_map/jit(_where)/select_n | solution.py:59
  59.2 23.0 %collective-permute-done.9 = bf16[4,1024,128]{2,1,0:T(8,128)(2,1)} collective-permute-done((bf16[4,1024,128]{2,1,0:T(8,128)(2,1)}, bf16[4,1024,128]{2,1,0:T(8,128)(2,1)}, u32[]{:S(2)}, u32[]{:S(2)}) %collective-permute-start.9) | collective-permute-done | bytes 1048608 | tf_op jit(solution)/shard_map/ppermute | solution.py:57
  82.3 5.3 %bitcast_multiply_fusion = f32[1024,1024]{1,0:T(8,128)S(1)} fusion(bf16[4,1024,128]{2,1,0:T(8,128)(2,1)S(1)} %collective-permute-done.6, bf16[4,1024,128]{2,1,0:T(8,128)(2,1)} %maximum_select_fusion.4, bf16[4,1024,128]{2,1,0:T(8,128)(2,1)} %collective-permute-done.9, bf16[4,1024,128]{2,1,0:T(8,128)(2,1)} %maximum_select_fusion.5, pred[]{:T(512)S(6)} %eq.32, ...), kind=kOutput, calls=%fused_computation | convolution fusion | flops 2154823680 | bytes 8388610 | tf_op jit(solution)/shard_map/dot_general | solution.py:128
  87.6 4.9 %fusion.14 = f32[1024,128]{1,0:T(8,128)S(1)} fusion(f32[1024,1024]{1,0:T(8,128)S(1)} %bitcast_multiply_fusion, f32[4096,128]{1,0:T(8,128)} %param.10, s32[]{:T(128)S(6)} %select_n.112), kind=kOutput, calls=%fused_computation.23 | convolution fusion | flops 1610612736 | bytes 5242884 | tf_op jit(solution)/shard_map/dot_general | solution.py:136
  92.6 1.9 collective-permute-done.10
  94.6 14.0 %collective-permute-done.11 = f32[1024,128]{1,0:T(8,128)S(1)} collective-permute-done((f32[1024,128]{1,0:T(8,128)S(1)}, f32[1024,128]{1,0:T(8,128)S(1)}, u32[]{:S(2)}, u32[]{:S(2)}) %collective-permute-start.11) | collective-permute-done | bytes 524320 | tf_op jit(solution)/shard_map/ppermute | solution.py:26
  108.6 1.0 fusion.34
  109.7 1.0 collective-permute-start.12
  110.7 3.4 %collective-permute-start.14 = (f32[128,128]{0,1:T(8,128)S(1)}, f32[128,128]{0,1:T(8,128)S(1)}, u32[]{:S(2)}, u32[]{:S(2)}) collective-permute-start(f32[128,128]{0,1:T(8,128)S(1)} %fusion.34), channel_id=1, source_target_pairs={{0,3},{1,2},{2,1},{3,0},{4,7},{5,6},{6,5},{7,4},{8,11},{9,10},{10,... | collective-permute-start | bytes 196616 | tf_op jit(solution)/shard_map/ppermute | solution.py:44
  114.1 2.3 %collective-permute-done.13 = f32[128,128]{0,1:T(8,128)S(1)} collective-permute-done((f32[128,128]{0,1:T(8,128)S(1)}, f32[128,128]{0,1:T(8,128)S(1)}, u32[]{:S(2)}, u32[]{:S(2)}) %collective-permute-start.13) | collective-permute-done | bytes 65568 | tf_op jit(solution)/shard_map/ppermute | solution.py:44
  116.4 0.9 collective-permute-done.14
  117.4 11.7 %cholesky.44 = f32[128,128]{1,0:T(8,128)S(1)} custom-call(f32[128,128]{1,0:T(8,128)S(1)} %fusion.29), custom_call_target="Cholesky" | custom-call | tf_op jit(solution)/shard_map/jit(cholesky)/cholesky | solution.py:88
  129.2 0.8 compare_reduce_fusion.1
  130.0 0.7 fusion.24
  130.6 9.8 %custom-call.6 = f32[1,128,128]{1,2,0:T(8,128)S(1)} custom-call(f32[1,128,128]{2,1,0:T(8,128)S(1)} %fusion.24), custom_call_target="InvertDiagBlocksLowerTriangular" | custom-call | tf_op jit(solution)/shard_map/jit(_solve_triangular)/triangular_solve | solution.py:89
  140.7 0.6 fusion.35
  141.3 8.5 %fusion.36 = f32[1024,128]{1,0:T(8,128)S(1)} fusion(f32[1024,1024]{1,0:T(8,128)} %copy-done.1, f32[1024,128]{1,0:T(8,128)S(1)} %fusion.35), kind=kOutput, calls=%fused_computation.65 | convolution fusion | flops 1610612736 | bytes 5242880 | tf_op jit(solution)/shard_map/dot_general | solution.py:143
  149.9 1.2 collective-permute-start.15
  151.0 5.6 %collective-permute-done.15 = f32[512,128]{1,0:T(8,128)S(1)} collective-permute-done((f32[512,128]{1,0:T(8,128)S(1)}, f32[512,128]{1,0:T(8,128)S(1)}, u32[]{:S(2)}, u32[]{:S(2)}) %collective-permute-start.15) | collective-permute-done | bytes 262176 | tf_op jit(solution)/shard_map/ppermute | solution.py:75
  156.7 1.2 collective-permute-start.16
  157.9 8.4 %collective-permute-done.16 = f32[256,128]{1,0:T(8,128)S(1)} collective-permute-done((f32[256,128]{1,0:T(8,128)S(1)}, f32[256,128]{1,0:T(8,128)S(1)}, u32[]{:S(2)}, u32[]{:S(2)}) %collective-permute-start.16) | collective-permute-done | bytes 131104 | tf_op jit(solution)/shard_map/ppermute | solution.py:75
  166.4 7.1 %collective-permute-done.17 = f32[256,128]{1,0:T(8,128)S(1)} collective-permute-done((f32[256,128]{1,0:T(8,128)S(1)}, f32[256,128]{1,0:T(8,128)S(1)}, u32[]{:S(2)}, u32[]{:S(2)}) %collective-permute-start.17) | collective-permute-done | bytes 131104 | tf_op jit(solution)/shard_map/ppermute | solution.py:78
  173.5 0.3 collective-permute-start.18
  173.8 6.1 %collective-permute-done.18 = f32[512,128]{1,0:T(8,128)S(1)} collective-permute-done((f32[512,128]{1,0:T(8,128)S(1)}, f32[512,128]{1,0:T(8,128)S(1)}, u32[]{:S(2)}, u32[]{:S(2)}) %collective-permute-start.18) | collective-permute-done | bytes 262176 | tf_op jit(solution)/shard_map/ppermute | solution.py:78
  180.0 1.0 fusion.17
  181.2 2.0 collective-permute-start.21
  183.2 2.6 %collective-permute-done.20 = f32[128,128]{0,1:T(8,128)S(1)} collective-permute-done((f32[128,128]{0,1:T(8,128)S(1)}, f32[128,128]{0,1:T(8,128)S(1)}, u32[]{:S(2)}, u32[]{:S(2)}) %collective-permute-start.20) | collective-permute-done | bytes 65568 | tf_op jit(solution)/shard_map/ppermute | solution.py:44
  186.0 11.7 %cholesky.55 = f32[128,128]{1,0:T(8,128)S(1)} custom-call(f32[128,128]{1,0:T(8,128)S(1)} %fusion.27), custom_call_target="Cholesky" | custom-call | tf_op jit(solution)/shard_map/jit(cholesky)/cholesky | solution.py:88
  197.7 0.6 compare_reduce_fusion
  198.4 0.7 fusion.25
  199.1 9.8 %custom-call.7 = f32[1,128,128]{1,2,0:T(8,128)S(1)} custom-call(f32[1,128,128]{2,1,0:T(8,128)S(1)} %fusion.25), custom_call_target="InvertDiagBlocksLowerTriangular" | custom-call | tf_op jit(solution)/shard_map/jit(_solve_triangular)/triangular_solve | solution.py:89
  209.2 0.6 fusion.16
  209.8 0.7 dynamic-slice_multiply_fusion
  (44 shorter events, 2.2 us)
Async XLA Ops:
  0.6 9.4 %copy-start = (bf16[8,1024,128]{2,1,0:T(8,128)(2,1)S(1)}, bf16[8,1024,128]{2,1,0:T(8,128)(2,1)}, u32[]{:S(2)}) copy-start(bf16[8,1024,128]{2,1,0:T(8,128)(2,1)} %param.9) | copy-start | bytes 6291460
  0.6 9.4 %copy-start.2 = (bf16[1024,8,16]{0,2,1:T(8,128)(2,1)S(1)}, bf16[1024,8,16]{0,2,1:T(8,128)(2,1)}, u32[]{:S(2)}) copy-start(bf16[1024,8,16]{0,2,1:T(8,128)(2,1)} %param.7) | copy-start | bytes 786436
  2.9 5.0 %collective-permute-start.2 = (f32[8,128,16]{1,2,0:T(8,128)S(1)}, f32[8,128,16]{1,2,0:T(8,128)S(1)}, u32[]{:S(2)}, u32[]{:S(2)}) collective-permute-start(f32[8,128,16]{1,2,0:T(8,128)S(1)} %fusion.37), channel_id=1, source_target_pairs={{0,12},{4,8},{8,4},{12,0},{1,13},{5,9},{9,5},{13,1},{2,14},{6,10},... | collective-permute-start | bytes 196616 | tf_op jit(solution)/shard_map/ppermute | solution.py:44
  5.3 4.7 %collective-permute-start.1 = (f32[8,128,16]{1,2,0:T(8,128)S(1)}, f32[8,128,16]{1,2,0:T(8,128)S(1)}, u32[]{:S(2)}, u32[]{:S(2)}) collective-permute-start(f32[8,128,16]{1,2,0:T(8,128)S(1)} %fusion.37), channel_id=1, source_target_pairs={{0,8},{4,12},{8,0},{12,4},{1,9},{5,13},{9,1},{13,5},{2,10},{6,14},... | collective-permute-start | bytes 196616 | tf_op jit(solution)/shard_map/ppermute | solution.py:44
  6.0 4.0 %collective-permute-start = (f32[8,128,16]{1,2,0:T(8,128)S(1)}, f32[8,128,16]{1,2,0:T(8,128)S(1)}, u32[]{:S(2)}, u32[]{:S(2)}) collective-permute-start(f32[8,128,16]{1,2,0:T(8,128)S(1)} %fusion.37), channel_id=1, source_target_pairs={{0,4},{4,0},{8,12},{12,8},{1,5},{5,1},{9,13},{13,9},{2,6},{6,2},{1... | collective-permute-start | bytes 196616 | tf_op jit(solution)/shard_map/ppermute | solution.py:44
  10.9 3.3 %collective-permute-start.3 = (bf16[1024,128]{1,0:T(8,128)(2,1)S(1)}, bf16[1024,128]{1,0:T(8,128)(2,1)}, u32[]{:S(2)}, u32[]{:S(2)}) collective-permute-start(bf16[1024,128]{1,0:T(8,128)(2,1)S(1)} %copy.7), channel_id=1, source_target_pairs={{1,4},{2,8},{3,12},{4,1},{6,9},{7,13},{8,2},{9,6},{11,14},{12,3},{... | collective-permute-start | bytes 786440 | tf_op jit(solution)/shard_map/ppermute | solution.py:119
  12.4 7.8 %collective-permute-start.7 = (bf16[1,1024,128]{2,1,0:T(8,128)(2,1)S(1)}, bf16[1,1024,128]{2,1,0:T(8,128)(2,1)S(1)}, u32[]{:S(2)}, u32[]{:S(2)}) collective-permute-start(bf16[1,1024,128]{2,1,0:T(8,128)(2,1)S(1)} %copy.9), channel_id=1, source_target_pairs={{0,16},{16,0},{1,17},{17,1},{2,18},{18,2},{3,19},{19,3},{4,20},{20... | collective-permute-start | bytes 786440 | tf_op jit(solution)/shard_map/ppermute | solution.py:57
  14.2 17.2 %collective-permute-start.4 = (bf16[1,1024,128]{2,1,0:T(8,128)(2,1)S(1)}, bf16[1,1024,128]{2,1,0:T(8,128)(2,1)}, u32[]{:S(2)}, u32[]{:S(2)}) collective-permute-start(bf16[1,1024,128]{2,1,0:T(8,128)(2,1)S(1)} %select_bitcast_fusion), channel_id=1, source_target_pairs={{0,16},{16,0},{1,17},{17,1},{2,18},{18,2},{3,19},{19,3},{4,20},{20... | collective-permute-start | bytes 786440 | tf_op jit(solution)/shard_map/ppermute | solution.py:57
  20.2 34.1 %collective-permute-start.8 = (bf16[2,1024,128]{2,1,0:T(8,128)(2,1)S(1)}, bf16[2,1024,128]{2,1,0:T(8,128)(2,1)}, u32[]{:S(2)}, u32[]{:S(2)}) collective-permute-start(bf16[2,1024,128]{2,1,0:T(8,128)(2,1)S(1)} %maximum_select_fusion.7), channel_id=1, source_target_pairs={{0,2},{1,3},{2,0},{3,1},{4,6},{5,7},{6,4},{7,5},{8,10},{9,11},{10,... | collective-permute-start | bytes 1572872 | tf_op jit(solution)/shard_map/ppermute | solution.py:57
  32.5 24.3 %collective-permute-start.5 = (bf16[2,1024,128]{2,1,0:T(8,128)(2,1)S(1)}, bf16[2,1024,128]{2,1,0:T(8,128)(2,1)}, u32[]{:S(2)}, u32[]{:S(2)}) collective-permute-start(bf16[2,1024,128]{2,1,0:T(8,128)(2,1)S(1)} %maximum_select_fusion.6), channel_id=1, source_target_pairs={{0,8},{4,12},{8,0},{12,4},{1,9},{5,13},{9,1},{13,5},{2,10},{6,14},... | collective-permute-start | bytes 1572872 | tf_op jit(solution)/shard_map/ppermute | solution.py:57
  56.8 25.5 %collective-permute-start.9 = (bf16[4,1024,128]{2,1,0:T(8,128)(2,1)}, bf16[4,1024,128]{2,1,0:T(8,128)(2,1)}, u32[]{:S(2)}, u32[]{:S(2)}) collective-permute-start(bf16[4,1024,128]{2,1,0:T(8,128)(2,1)} %maximum_select_fusion.5), channel_id=1, source_target_pairs={{0,1},{1,0},{2,3},{3,2},{4,5},{5,4},{6,7},{7,6},{8,9},{9,8},{10,11... | collective-permute-start | bytes 3145736 | tf_op jit(solution)/shard_map/ppermute | solution.py:57
  59.1 23.2 %collective-permute-start.6 = (bf16[4,1024,128]{2,1,0:T(8,128)(2,1)}, bf16[4,1024,128]{2,1,0:T(8,128)(2,1)S(1)}, u32[]{:S(2)}, u32[]{:S(2)}) collective-permute-start(bf16[4,1024,128]{2,1,0:T(8,128)(2,1)} %maximum_select_fusion.4), channel_id=1, source_target_pairs={{0,4},{4,0},{8,12},{12,8},{1,5},{5,1},{9,13},{13,9},{2,6},{6,2},{1... | collective-permute-start | bytes 3145736 | tf_op jit(solution)/shard_map/ppermute | solution.py:57
  87.6 4.9 %copy-start.1 = (f32[1024,1024]{1,0:T(8,128)}, f32[1024,1024]{1,0:T(8,128)S(1)}, u32[]{:S(2)}) copy-start(f32[1024,1024]{1,0:T(8,128)S(1)} %bitcast_multiply_fusion) | copy-start | bytes 12582916
  92.5 2.0 collective-permute-start.10
  94.6 14.0 %collective-permute-start.11 = (f32[1024,128]{1,0:T(8,128)S(1)}, f32[1024,128]{1,0:T(8,128)S(1)}, u32[]{:S(2)}, u32[]{:S(2)}) collective-permute-start(f32[1024,128]{1,0:T(8,128)S(1)} %add.62), channel_id=1, source_target_pairs={{0,8},{4,12},{8,0},{12,4},{1,9},{5,13},{9,1},{13,5},{2,10},{6,14},... | collective-permute-start | bytes 1572872 | tf_op jit(solution)/shard_map/ppermute | solution.py:26
  109.6 6.8 %collective-permute-start.13 = (f32[128,128]{0,1:T(8,128)S(1)}, f32[128,128]{0,1:T(8,128)S(1)}, u32[]{:S(2)}, u32[]{:S(2)}) collective-permute-start(f32[128,128]{0,1:T(8,128)S(1)} %fusion.34), channel_id=1, source_target_pairs={{0,2},{1,3},{2,0},{3,1},{4,6},{5,7},{6,4},{7,5},{8,10},{9,11},{10,... | collective-permute-start | bytes 196616 | tf_op jit(solution)/shard_map/ppermute | solution.py:44
  109.7 6.7 %collective-permute-start.12 = (f32[128,128]{0,1:T(8,128)S(1)}, f32[128,128]{0,1:T(8,128)S(1)}, u32[]{:S(2)}, u32[]{:S(2)}) collective-permute-start(f32[128,128]{0,1:T(8,128)S(1)} %fusion.34), channel_id=1, source_target_pairs={{0,1},{1,0},{2,3},{3,2},{4,5},{5,4},{6,7},{7,6},{8,9},{9,8},{10,11... | collective-permute-start | bytes 196616 | tf_op jit(solution)/shard_map/ppermute | solution.py:44
  110.7 6.6 %collective-permute-start.14 = (f32[128,128]{0,1:T(8,128)S(1)}, f32[128,128]{0,1:T(8,128)S(1)}, u32[]{:S(2)}, u32[]{:S(2)}) collective-permute-start(f32[128,128]{0,1:T(8,128)S(1)} %fusion.34), channel_id=1, source_target_pairs={{0,3},{1,2},{2,1},{3,0},{4,7},{5,6},{6,5},{7,4},{8,11},{9,10},{10,... | collective-permute-start | bytes 196616 | tf_op jit(solution)/shard_map/ppermute | solution.py:44
  149.9 6.7 %collective-permute-start.15 = (f32[512,128]{1,0:T(8,128)S(1)}, f32[512,128]{1,0:T(8,128)S(1)}, u32[]{:S(2)}, u32[]{:S(2)}) collective-permute-start(f32[512,128]{1,0:T(8,128)S(1)} %slice_select_fusion), channel_id=1, source_target_pairs={{0,1},{1,0},{2,3},{3,2},{4,5},{5,4},{6,7},{7,6},{8,9},{9,8},{10,11... | collective-permute-start | bytes 786440 | tf_op jit(solution)/shard_map/ppermute | solution.py:75
  156.7 9.6 %collective-permute-start.16 = (f32[256,128]{1,0:T(8,128)S(1)}, f32[256,128]{1,0:T(8,128)S(1)}, u32[]{:S(2)}, u32[]{:S(2)}) collective-permute-start(f32[256,128]{1,0:T(8,128)S(1)} %slice_select_fusion.1), channel_id=1, source_target_pairs={{0,2},{1,3},{2,0},{3,1},{4,6},{5,7},{6,4},{7,5},{8,10},{9,11},{10,... | collective-permute-start | bytes 393224 | tf_op jit(solution)/shard_map/ppermute | solution.py:75
  166.3 7.2 %collective-permute-start.17 = (f32[256,128]{1,0:T(8,128)S(1)}, f32[256,128]{1,0:T(8,128)S(1)}, u32[]{:S(2)}, u32[]{:S(2)}) collective-permute-start(f32[256,128]{1,0:T(8,128)S(1)} %select_add_fusion.1), channel_id=1, source_target_pairs={{0,2},{1,3},{2,0},{3,1},{4,6},{5,7},{6,4},{7,5},{8,10},{9,11},{10,... | collective-permute-start | bytes 393224 | tf_op jit(solution)/shard_map/ppermute | solution.py:78
  173.5 6.4 %collective-permute-start.18 = (f32[512,128]{1,0:T(8,128)S(1)}, f32[512,128]{1,0:T(8,128)S(1)}, u32[]{:S(2)}, u32[]{:S(2)}) collective-permute-start(f32[512,128]{1,0:T(8,128)S(1)} %maximum_select_fusion.11), channel_id=1, source_target_pairs={{0,1},{1,0},{2,3},{3,2},{4,5},{5,4},{6,7},{7,6},{8,9},{9,8},{10,11... | collective-permute-start | bytes 786440 | tf_op jit(solution)/shard_map/ppermute | solution.py:78
  181.0 4.9 %collective-permute-start.20 = (f32[128,128]{0,1:T(8,128)S(1)}, f32[128,128]{0,1:T(8,128)S(1)}, u32[]{:S(2)}, u32[]{:S(2)}) collective-permute-start(f32[128,128]{0,1:T(8,128)S(1)} %fusion.17), channel_id=1, source_target_pairs={{0,8},{4,12},{8,0},{12,4},{1,9},{5,13},{9,1},{13,5},{2,10},{6,14},... | collective-permute-start | bytes 196616 | tf_op jit(solution)/shard_map/ppermute | solution.py:44
  181.1 4.8 %collective-permute-start.19 = (f32[128,128]{0,1:T(8,128)S(1)}, f32[128,128]{0,1:T(8,128)S(1)}, u32[]{:S(2)}, u32[]{:S(2)}) collective-permute-start(f32[128,128]{0,1:T(8,128)S(1)} %fusion.17), channel_id=1, source_target_pairs={{0,4},{4,0},{8,12},{12,8},{1,5},{5,1},{9,13},{13,9},{2,6},{6,2},{1... | collective-permute-start | bytes 196616 | tf_op jit(solution)/shard_map/ppermute | solution.py:44
  181.2 4.7 %collective-permute-start.21 = (f32[128,128]{0,1:T(8,128)S(1)}, f32[128,128]{0,1:T(8,128)S(1)}, u32[]{:S(2)}, u32[]{:S(2)}) collective-permute-start(f32[128,128]{0,1:T(8,128)S(1)} %fusion.17), channel_id=1, source_target_pairs={{0,12},{4,8},{8,4},{12,0},{1,13},{5,9},{9,5},{13,1},{2,14},{6,10},... | collective-permute-start | bytes 196616 | tf_op jit(solution)/shard_map/ppermute | solution.py:44

commit v8 on v6

--- a/solution.py
+++ b/solution.py
@@ -80,12 +80,14 @@
     return x
 
 
-def _qr_step(image, gram_axis):
+def _lower_factor(image, gram_axis):
     gram_part = jnp.dot(
         image.T, image, precision=lax.Precision.HIGHEST, preferred_element_type=jnp.float32
     )
-    gram_matrix = _direct_sum(gram_part, gram_axis)
-    lower_factor = jnp.linalg.cholesky(gram_matrix)
+    return jnp.linalg.cholesky(_direct_sum(gram_part, gram_axis))
+
+
+def _right_solve(lower_factor, image):
     return jax.scipy.linalg.solve_triangular(lower_factor, image.T, lower=True).T
 
 
@@ -123,23 +125,28 @@
         left_rows, right_rows, (((0, 2), (0, 2)), ((), ())), preferred_element_type=jnp.float32
     ) * scaling
 
-    basis_rows = lax.dynamic_slice_in_dim(start_basis, row_here * rows_here, rows_here, 0)
-    on_rows = True
-    for sweep_index in range(ITERS):
+    def cov_times(block, on_rows):
         if on_rows:
             partial_image = jnp.dot(
-                covariance, basis_rows, precision=lax.Precision.HIGHEST,
+                covariance, block, precision=lax.Precision.HIGHEST,
                 preferred_element_type=jnp.float32,
             )
-            image = _butterfly_sum(partial_image, "row")
-            basis_rows = _qr_step(image, "col")
-        else:
-            partial_image = lax.dot_general(
-                covariance, basis_rows, (((0,), (0,)), ((), ())),
-                precision=lax.Precision.HIGHEST, preferred_element_type=jnp.float32,
-            )
-            image = _halving_sum(partial_image, "col")
-            basis_rows = _qr_step(image, "row")
+            return _butterfly_sum(partial_image, "row")
+        partial_image = lax.dot_general(
+            covariance, block, (((0,), (0,)), ((), ())),
+            precision=lax.Precision.HIGHEST, preferred_element_type=jnp.float32,
+        )
+        return _halving_sum(partial_image, "col")
+
+    basis_rows = lax.dynamic_slice_in_dim(start_basis, row_here * rows_here, rows_here, 0)
+    image = cov_times(basis_rows, True)
+    on_rows = False
+    for sweep_index in range(ITERS):
+        lower_factor = _lower_factor(image, "row" if on_rows else "col")
+        if sweep_index == ITERS - 1:
+            basis_rows = _right_solve(lower_factor, image)
+            break
+        image = _right_solve(lower_factor, cov_times(image, on_rows))
         on_rows = not on_rows
     if not on_rows:
         swapped = lax.ppermute(basis_rows, ("row", "col"), _transpose_pairs(row_count, col_count))

time: 210 us -> 191 us (0.910)
  waiting for transfers between devices: 96.5 us -> 76.8 us
    ppermute x2, waiting for transfers between devices: 13.3 us -> 0.01 us  [_halving_sum(): other = lax.ppermute(x, axis, [(i, i ^ step) for i in range(count)])]
    ppermute x2, waiting for transfers between devices: 14 us -> 8.29 us  [_halving_sum(): x = keep + lax.ppermute(give, axis, [(i, i ^ step) for i in range(count)])]
    ppermute x2, starting transfers between devices: 0.37 us -> 4.28 us  [_halving_sum(): other = lax.ppermute(x, axis, [(i, i ^ step) for i in range(count)])]
  transfers between devices with their start and end apart: 22 -> 22, of which waited for: 14 -> 12; matrix products, arithmetic and copies ran while one was open for 3% -> 16% of each run, Pallas kernels for 0% -> 0%
where the time goes in v8:
time: 191 us; the launch traced here: 190 us
  waiting for transfers between devices  76.8 us (40%)
  other arithmetic  52.1 us (27%)
  starting transfers between devices  36.3 us (19%)
  matrix products  22.9 us (12%)
    ppermute x6, waiting for transfers between devices, _butterfly_gather(): lax.ppermute([xs[k] for k in which], axis, [(i, i ^ step) for i in range(...  43.6 us
    another operation x6, other arithmetic, _lower_factor(): return jnp.linalg.cholesky(_direct_sum(gram_part, gram_axis))  25 us
    another operation x4, other arithmetic, _right_solve(): jax.scipy.linalg.solve_triangular(lower_factor, image.T, lower=True)  20.9 us
    ppermute x6, starting transfers between devices, _butterfly_gather(): lax.ppermute([xs[k] for k in which], axis, [(i, i ^ step) for i in range(...  20.3 us
    ppermute x2, waiting for transfers between devices, _butterfly_sum(): x = x + lax.ppermute(x, axis, [(i, i ^ step) for i in range(count)])  15.8 us
    ppermute x9, starting transfers between devices, _direct_sum(): lax.ppermute(x, axis, [(i, i ^ k) for i in range(count)])  9.79 us
    ppermute x9, waiting for transfers between devices, _direct_sum(): lax.ppermute(x, axis, [(i, i ^ k) for i in range(count)])  9.05 us
    ppermute x2, waiting for transfers between devices, _halving_sum(): x = keep + lax.ppermute(give, axis, [(i, i ^ step) for i in range(count)])  8.29 us
  transfers between devices with their start and end apart: 22, of which 12 were waited for; matrix products, arithmetic and copies ran while one was open for 16% of the time, Pallas kernels for 0%

profile of v8, /device:TPU:0, one launch (start us, length us, event | category | flops | bytes accessed | tf_op | source)
XLA Modules:
  0.0 190.4 jit_solution(6082422715298892427)
XLA Ops:
  0.7 2.2 %fusion.42 = f32[8,128,16]{1,2,0:T(8,128)S(1)} fusion(bf16[1024,8,16]{0,2,1:T(8,128)(2,1)} %param.7, bf16[8,1024,128]{2,1,0:T(8,128)(2,1)} %param.8), kind=kOutput, calls=%fused_computation.69 | convolution fusion | flops 33554432 | bytes 2424832 | tf_op jit(solution)/shard_map/mbs,bmr->brs/dot_general | solution.py:101
  2.9 2.5 %collective-permute-start.2 = (f32[8,128,16]{1,2,0:T(8,128)S(1)}, f32[8,128,16]{1,2,0:T(8,128)S(1)}, u32[]{:S(2)}, u32[]{:S(2)}) collective-permute-start(f32[8,128,16]{1,2,0:T(8,128)S(1)} %fusion.42), channel_id=1, source_target_pairs={{0,12},{4,8},{8,4},{12,0},{1,13},{5,9},{9,5},{13,1},{2,14},{6,10},... | collective-permute-start | bytes 196616 | tf_op jit(solution)/shard_map/ppermute | solution.py:44
  5.3 0.6 collective-permute-start.1
  6.0 1.8 collective-permute-done.2
  7.8 2.2 %collective-permute-done.1 = f32[8,128,16]{1,2,0:T(8,128)S(1)} collective-permute-done((f32[8,128,16]{1,2,0:T(8,128)S(1)}, f32[8,128,16]{1,2,0:T(8,128)S(1)}, u32[]{:S(2)}, u32[]{:S(2)}) %collective-permute-start.1) | collective-permute-done | bytes 65568 | tf_op jit(solution)/shard_map/ppermute | solution.py:44
  10.0 0.7 fusion.13
  10.7 0.2 copy.7
  10.9 1.4 collective-permute-start.3
  12.2 0.2 copy.9
  12.4 1.8 collective-permute-start.7
  14.2 0.4 collective-permute-start.4
  14.6 5.6 %collective-permute-done.7 = bf16[1,1024,128]{2,1,0:T(8,128)(2,1)S(1)} collective-permute-done((bf16[1,1024,128]{2,1,0:T(8,128)(2,1)S(1)}, bf16[1,1024,128]{2,1,0:T(8,128)(2,1)S(1)}, u32[]{:S(2)}, u32[]{:S(2)}) %collective-permute-start.7) | collective-permute-done | bytes 262176 | tf_op jit(solution)/shard_map/ppermute | solution.py:57
  20.2 11.1 %collective-permute-start.8 = (bf16[2,1024,128]{2,1,0:T(8,128)(2,1)S(1)}, bf16[2,1024,128]{2,1,0:T(8,128)(2,1)}, u32[]{:S(2)}, u32[]{:S(2)}) collective-permute-start(bf16[2,1024,128]{2,1,0:T(8,128)(2,1)S(1)} %maximum_select_fusion.7), channel_id=1, source_target_pairs={{0,2},{1,3},{2,0},{3,1},{4,6},{5,7},{6,4},{7,5},{8,10},{9,11},{10,... | collective-permute-start | bytes 1572872 | tf_op jit(solution)/shard_map/ppermute | solution.py:57
  31.4 1.1 maximum_select_fusion.6
  32.5 6.9 %collective-permute-start.5 = (bf16[2,1024,128]{2,1,0:T(8,128)(2,1)S(1)}, bf16[2,1024,128]{2,1,0:T(8,128)(2,1)}, u32[]{:S(2)}, u32[]{:S(2)}) collective-permute-start(bf16[2,1024,128]{2,1,0:T(8,128)(2,1)S(1)} %maximum_select_fusion.6), channel_id=1, source_target_pairs={{0,8},{4,12},{8,0},{12,4},{1,9},{5,13},{9,1},{13,5},{2,10},{6,14},... | collective-permute-start | bytes 1572872 | tf_op jit(solution)/shard_map/ppermute | solution.py:57
  39.4 15.0 %collective-permute-done.8 = bf16[2,1024,128]{2,1,0:T(8,128)(2,1)} collective-permute-done((bf16[2,1024,128]{2,1,0:T(8,128)(2,1)S(1)}, bf16[2,1024,128]{2,1,0:T(8,128)(2,1)}, u32[]{:S(2)}, u32[]{:S(2)}) %collective-permute-start.8) | collective-permute-done | bytes 524320 | tf_op jit(solution)/shard_map/ppermute | solution.py:57
  54.4 2.4 %maximum_select_fusion.5 = bf16[4,1024,128]{2,1,0:T(8,128)(2,1)} fusion(bf16[2,1024,128]{2,1,0:T(8,128)(2,1)} %collective-permute-done.8, bf16[2,1024,128]{2,1,0:T(8,128)(2,1)S(1)} %maximum_select_fusion.7, pred[]{:T(512)S(6)} %eq.27), kind=kLoop, calls=%fused_computation.19 | loop fusion | flops 1572864 | bytes 2097153 | tf_op jit(solution)/shard_map/jit(_where)/select_n | solution.py:59
  56.8 2.3 %maximum_select_fusion.4 = bf16[4,1024,128]{2,1,0:T(8,128)(2,1)} fusion(bf16[2,1024,128]{2,1,0:T(8,128)(2,1)} %collective-permute-done.5, bf16[2,1024,128]{2,1,0:T(8,128)(2,1)S(1)} %maximum_select_fusion.6, pred[]{:T(512)S(6)} %eq.23), kind=kLoop, calls=%fused_computation.18 | loop fusion | flops 1572864 | bytes 2097153 | tf_op jit(solution)/shard_map/jit(_where)/select_n | solution.py:59
  59.2 23.0 %collective-permute-done.9 = bf16[4,1024,128]{2,1,0:T(8,128)(2,1)} collective-permute-done((bf16[4,1024,128]{2,1,0:T(8,128)(2,1)}, bf16[4,1024,128]{2,1,0:T(8,128)(2,1)}, u32[]{:S(2)}, u32[]{:S(2)}) %collective-permute-start.9) | collective-permute-done | bytes 1048608 | tf_op jit(solution)/shard_map/ppermute | solution.py:57
  82.3 5.3 %bitcast_multiply_fusion = f32[1024,1024]{1,0:T(8,128)S(1)} fusion(bf16[4,1024,128]{2,1,0:T(8,128)(2,1)S(1)} %collective-permute-done.6, bf16[4,1024,128]{2,1,0:T(8,128)(2,1)} %maximum_select_fusion.4, bf16[4,1024,128]{2,1,0:T(8,128)(2,1)} %collective-permute-done.9, bf16[4,1024,128]{2,1,0:T(8,128)(2,1)} %maximum_select_fusion.5, pred[]{:T(512)S(6)} %eq.26, ...), kind=kOutput, calls=%fused_computation | convolution fusion | flops 2154823680 | bytes 8388610 | tf_op jit(solution)/shard_map/dot_general | solution.py:124
  87.6 4.9 %fusion.22 = f32[1024,128]{1,0:T(8,128)S(1)} fusion(f32[1024,1024]{1,0:T(8,128)S(1)} %bitcast_multiply_fusion, f32[4096,128]{1,0:T(8,128)} %param.10, s32[]{:T(128)S(6)} %select_n.108), kind=kOutput, calls=%fused_computation.30 | convolution fusion | flops 1610612736 | bytes 5242884 | tf_op jit(solution)/shard_map/dot_general | solution.py:130
  92.6 1.9 collective-permute-done.10
  94.6 14.0 %collective-permute-done.11 = f32[1024,128]{1,0:T(8,128)S(1)} collective-permute-done((f32[1024,128]{1,0:T(8,128)S(1)}, f32[1024,128]{1,0:T(8,128)S(1)}, u32[]{:S(2)}, u32[]{:S(2)}) %collective-permute-start.11) | collective-permute-done | bytes 524320 | tf_op jit(solution)/shard_map/ppermute | solution.py:26
  108.6 7.0 %fusion.25 = f32[1024,128]{1,0:T(8,128)S(1)} fusion(f32[1024,1024]{1,0:T(8,128)S(1)} %bitcast_multiply_fusion, f32[1024,128]{1,0:T(8,128)S(1)} %add.62, f32[1024,128]{1,0:T(8,128)S(1)} %collective-permute-done.11), kind=kOutput, calls=%fused_computation.37 | convolution fusion | flops 1610743808 | bytes 5767168 | tf_op jit(solution)/shard_map/dot_general | solution.py:135
  115.6 0.3 collective-permute-start.15
  116.0 1.0 fusion.27
  117.0 0.8 collective-permute-start.13
  117.8 1.1 collective-permute-start.12
  118.9 2.6 %collective-permute-start.14 = (f32[128,128]{0,1:T(8,128)S(1)}, f32[128,128]{0,1:T(8,128)S(1)}, u32[]{:S(2)}, u32[]{:S(2)}) collective-permute-start(f32[128,128]{0,1:T(8,128)S(1)} %fusion.27), channel_id=1, source_target_pairs={{0,3},{1,2},{2,1},{3,0},{4,7},{5,6},{6,5},{7,4},{8,11},{9,10},{10,... | collective-permute-start | bytes 196616 | tf_op jit(solution)/shard_map/ppermute | solution.py:44
  121.4 4.5 %collective-permute-done.15 = f32[512,128]{1,0:T(8,128)S(1)} collective-permute-done((f32[512,128]{1,0:T(8,128)S(1)}, f32[512,128]{1,0:T(8,128)S(1)}, u32[]{:S(2)}, u32[]{:S(2)}) %collective-permute-start.15) | collective-permute-done | bytes 262176 | tf_op jit(solution)/shard_map/ppermute | solution.py:75
  126.1 1.0 collective-permute-done.12
  127.2 1.4 collective-permute-done.14
  128.7 3.7 %collective-permute-done.16 = f32[256,128]{1,0:T(8,128)S(1)} collective-permute-done((f32[256,128]{1,0:T(8,128)S(1)}, f32[256,128]{1,0:T(8,128)S(1)}, u32[]{:S(2)}, u32[]{:S(2)}) %collective-permute-start.16) | collective-permute-done | bytes 131104 | tf_op jit(solution)/shard_map/ppermute | solution.py:75
  132.5 11.7 %cholesky.44 = f32[128,128]{1,0:T(8,128)S(1)} custom-call(f32[128,128]{1,0:T(8,128)S(1)} %fusion.35), custom_call_target="Cholesky" | custom-call | tf_op jit(solution)/shard_map/jit(cholesky)/cholesky | solution.py:87
  144.3 4.2 %collective-permute-start.18 = (f32[512,128]{1,0:T(8,128)S(1)}, f32[512,128]{1,0:T(8,128)S(1)}, u32[]{:S(2)}, u32[]{:S(2)}) collective-permute-start(f32[512,128]{1,0:T(8,128)S(1)} %maximum_select_fusion.9), channel_id=1, source_target_pairs={{0,1},{1,0},{2,3},{3,2},{4,5},{5,4},{6,7},{7,6},{8,9},{9,8},{10,11... | collective-permute-start | bytes 786440 | tf_op jit(solution)/shard_map/ppermute | solution.py:78
  148.5 0.6 compare_reduce_fusion.1
  149.2 0.7 fusion.29
  149.8 9.8 %custom-call.6 = f32[1,128,128]{1,2,0:T(8,128)S(1)} custom-call(f32[1,128,128]{2,1,0:T(8,128)S(1)} %fusion.29), custom_call_target="InvertDiagBlocksLowerTriangular" | custom-call | tf_op jit(solution)/shard_map/jit(_solve_triangular)/triangular_solve | solution.py:91
  159.6 0.6 fusion.15
  160.3 0.6 fusion.41
  161.0 2.0 %collective-permute-start.21 = (f32[128,128]{0,1:T(8,128)S(1)}, f32[128,128]{0,1:T(8,128)S(1)}, u32[]{:S(2)}, u32[]{:S(2)}) collective-permute-start(f32[128,128]{0,1:T(8,128)S(1)} %fusion.41), channel_id=1, source_target_pairs={{0,12},{4,8},{8,4},{12,0},{1,13},{5,9},{9,5},{13,1},{2,14},{6,10},... | collective-permute-start | bytes 196616 | tf_op jit(solution)/shard_map/ppermute | solution.py:44
  163.1 2.6 %collective-permute-done.20 = f32[128,128]{0,1:T(8,128)S(1)} collective-permute-done((f32[128,128]{0,1:T(8,128)S(1)}, f32[128,128]{0,1:T(8,128)S(1)}, u32[]{:S(2)}, u32[]{:S(2)}) %collective-permute-start.20) | collective-permute-done | bytes 65568 | tf_op jit(solution)/shard_map/ppermute | solution.py:44
  165.9 11.9 %cholesky.55 = f32[128,128]{1,0:T(8,128)S(1)} custom-call(f32[128,128]{1,0:T(8,128)S(1)} %fusion.33), custom_call_target="Cholesky" | custom-call | tf_op jit(solution)/shard_map/jit(cholesky)/cholesky | solution.py:87
  177.8 0.6 compare_reduce_fusion
  178.5 0.7 fusion.30
  179.1 9.8 %custom-call.7 = f32[1,128,128]{1,2,0:T(8,128)S(1)} custom-call(f32[1,128,128]{2,1,0:T(8,128)S(1)} %fusion.30), custom_call_target="InvertDiagBlocksLowerTriangular" | custom-call | tf_op jit(solution)/shard_map/jit(_solve_triangular)/triangular_solve | solution.py:91
  188.9 0.6 fusion.31
  189.6 0.8 copy.21
  (42 shorter events, 1.3 us)
Async XLA Ops:
  0.6 9.4 %copy-start = (bf16[8,1024,128]{2,1,0:T(8,128)(2,1)S(1)}, bf16[8,1024,128]{2,1,0:T(8,128)(2,1)}, u32[]{:S(2)}) copy-start(bf16[8,1024,128]{2,1,0:T(8,128)(2,1)} %param.9) | copy-start | bytes 6291460
  0.6 9.4 %copy-start.2 = (bf16[1024,8,16]{0,2,1:T(8,128)(2,1)S(1)}, bf16[1024,8,16]{0,2,1:T(8,128)(2,1)}, u32[]{:S(2)}) copy-start(bf16[1024,8,16]{0,2,1:T(8,128)(2,1)} %param.7) | copy-start | bytes 786436
  2.9 5.0 %collective-permute-start.2 = (f32[8,128,16]{1,2,0:T(8,128)S(1)}, f32[8,128,16]{1,2,0:T(8,128)S(1)}, u32[]{:S(2)}, u32[]{:S(2)}) collective-permute-start(f32[8,128,16]{1,2,0:T(8,128)S(1)} %fusion.42), channel_id=1, source_target_pairs={{0,12},{4,8},{8,4},{12,0},{1,13},{5,9},{9,5},{13,1},{2,14},{6,10},... | collective-permute-start | bytes 196616 | tf_op jit(solution)/shard_map/ppermute | solution.py:44
  5.3 4.7 %collective-permute-start.1 = (f32[8,128,16]{1,2,0:T(8,128)S(1)}, f32[8,128,16]{1,2,0:T(8,128)S(1)}, u32[]{:S(2)}, u32[]{:S(2)}) collective-permute-start(f32[8,128,16]{1,2,0:T(8,128)S(1)} %fusion.42), channel_id=1, source_target_pairs={{0,8},{4,12},{8,0},{12,4},{1,9},{5,13},{9,1},{13,5},{2,10},{6,14},... | collective-permute-start | bytes 196616 | tf_op jit(solution)/shard_map/ppermute | solution.py:44
  6.0 4.0 %collective-permute-start = (f32[8,128,16]{1,2,0:T(8,128)S(1)}, f32[8,128,16]{1,2,0:T(8,128)S(1)}, u32[]{:S(2)}, u32[]{:S(2)}) collective-permute-start(f32[8,128,16]{1,2,0:T(8,128)S(1)} %fusion.42), channel_id=1, source_target_pairs={{0,4},{4,0},{8,12},{12,8},{1,5},{5,1},{9,13},{13,9},{2,6},{6,2},{1... | collective-permute-start | bytes 196616 | tf_op jit(solution)/shard_map/ppermute | solution.py:44
  10.9 3.3 %collective-permute-start.3 = (bf16[1024,128]{1,0:T(8,128)(2,1)S(1)}, bf16[1024,128]{1,0:T(8,128)(2,1)}, u32[]{:S(2)}, u32[]{:S(2)}) collective-permute-start(bf16[1024,128]{1,0:T(8,128)(2,1)S(1)} %copy.7), channel_id=1, source_target_pairs={{1,4},{2,8},{3,12},{4,1},{6,9},{7,13},{8,2},{9,6},{11,14},{12,3},{... | collective-permute-start | bytes 786440 | tf_op jit(solution)/shard_map/ppermute | solution.py:115
  12.4 7.8 %collective-permute-start.7 = (bf16[1,1024,128]{2,1,0:T(8,128)(2,1)S(1)}, bf16[1,1024,128]{2,1,0:T(8,128)(2,1)S(1)}, u32[]{:S(2)}, u32[]{:S(2)}) collective-permute-start(bf16[1,1024,128]{2,1,0:T(8,128)(2,1)S(1)} %copy.9), channel_id=1, source_target_pairs={{0,16},{16,0},{1,17},{17,1},{2,18},{18,2},{3,19},{19,3},{4,20},{20... | collective-permute-start | bytes 786440 | tf_op jit(solution)/shard_map/ppermute | solution.py:57
  14.2 17.2 %collective-permute-start.4 = (bf16[1,1024,128]{2,1,0:T(8,128)(2,1)S(1)}, bf16[1,1024,128]{2,1,0:T(8,128)(2,1)}, u32[]{:S(2)}, u32[]{:S(2)}) collective-permute-start(bf16[1,1024,128]{2,1,0:T(8,128)(2,1)S(1)} %select_bitcast_fusion), channel_id=1, source_target_pairs={{0,16},{16,0},{1,17},{17,1},{2,18},{18,2},{3,19},{19,3},{4,20},{20... | collective-permute-start | bytes 786440 | tf_op jit(solution)/shard_map/ppermute | solution.py:57
  20.2 34.1 %collective-permute-start.8 = (bf16[2,1024,128]{2,1,0:T(8,128)(2,1)S(1)}, bf16[2,1024,128]{2,1,0:T(8,128)(2,1)}, u32[]{:S(2)}, u32[]{:S(2)}) collective-permute-start(bf16[2,1024,128]{2,1,0:T(8,128)(2,1)S(1)} %maximum_select_fusion.7), channel_id=1, source_target_pairs={{0,2},{1,3},{2,0},{3,1},{4,6},{5,7},{6,4},{7,5},{8,10},{9,11},{10,... | collective-permute-start | bytes 1572872 | tf_op jit(solution)/shard_map/ppermute | solution.py:57
  32.5 24.3 %collective-permute-start.5 = (bf16[2,1024,128]{2,1,0:T(8,128)(2,1)S(1)}, bf16[2,1024,128]{2,1,0:T(8,128)(2,1)}, u32[]{:S(2)}, u32[]{:S(2)}) collective-permute-start(bf16[2,1024,128]{2,1,0:T(8,128)(2,1)S(1)} %maximum_select_fusion.6), channel_id=1, source_target_pairs={{0,8},{4,12},{8,0},{12,4},{1,9},{5,13},{9,1},{13,5},{2,10},{6,14},... | collective-permute-start | bytes 1572872 | tf_op jit(solution)/shard_map/ppermute | solution.py:57
  56.8 25.5 %collective-permute-start.9 = (bf16[4,1024,128]{2,1,0:T(8,128)(2,1)}, bf16[4,1024,128]{2,1,0:T(8,128)(2,1)}, u32[]{:S(2)}, u32[]{:S(2)}) collective-permute-start(bf16[4,1024,128]{2,1,0:T(8,128)(2,1)} %maximum_select_fusion.5), channel_id=1, source_target_pairs={{0,1},{1,0},{2,3},{3,2},{4,5},{5,4},{6,7},{7,6},{8,9},{9,8},{10,11... | collective-permute-start | bytes 3145736 | tf_op jit(solution)/shard_map/ppermute | solution.py:57
  59.1 23.2 %collective-permute-start.6 = (bf16[4,1024,128]{2,1,0:T(8,128)(2,1)}, bf16[4,1024,128]{2,1,0:T(8,128)(2,1)S(1)}, u32[]{:S(2)}, u32[]{:S(2)}) collective-permute-start(bf16[4,1024,128]{2,1,0:T(8,128)(2,1)} %maximum_select_fusion.4), channel_id=1, source_target_pairs={{0,4},{4,0},{8,12},{12,8},{1,5},{5,1},{9,13},{13,9},{2,6},{6,2},{1... | collective-permute-start | bytes 3145736 | tf_op jit(solution)/shard_map/ppermute | solution.py:57
  87.6 21.0 %copy-start.1 = (f32[1024,1024]{1,0:T(8,128)}, f32[1024,1024]{1,0:T(8,128)S(1)}, u32[]{:S(2)}) copy-start(f32[1024,1024]{1,0:T(8,128)S(1)} %bitcast_multiply_fusion) | copy-start | bytes 12582916
  92.5 2.0 %collective-permute-start.10 = (f32[1024,128]{1,0:T(8,128)S(1)}, f32[1024,128]{1,0:T(8,128)S(1)}, u32[]{:S(2)}, u32[]{:S(2)}) collective-permute-start(f32[1024,128]{1,0:T(8,128)S(1)} %fusion.22), channel_id=1, source_target_pairs={{0,4},{4,0},{8,12},{12,8},{1,5},{5,1},{9,13},{13,9},{2,6},{6,2},{1... | collective-permute-start | bytes 1572872 | tf_op jit(solution)/shard_map/ppermute | solution.py:26
  94.5 14.0 %collective-permute-start.11 = (f32[1024,128]{1,0:T(8,128)S(1)}, f32[1024,128]{1,0:T(8,128)S(1)}, u32[]{:S(2)}, u32[]{:S(2)}) collective-permute-start(f32[1024,128]{1,0:T(8,128)S(1)} %add.62), channel_id=1, source_target_pairs={{0,8},{4,12},{8,0},{12,4},{1,9},{5,13},{9,1},{13,5},{2,10},{6,14},... | collective-permute-start | bytes 1572872 | tf_op jit(solution)/shard_map/ppermute | solution.py:26
  115.6 10.4 %collective-permute-start.15 = (f32[512,128]{1,0:T(8,128)S(1)}, f32[512,128]{1,0:T(8,128)S(1)}, u32[]{:S(2)}, u32[]{:S(2)}) collective-permute-start(f32[512,128]{1,0:T(8,128)S(1)} %slice_select_fusion), channel_id=1, source_target_pairs={{0,1},{1,0},{2,3},{3,2},{4,5},{5,4},{6,7},{7,6},{8,9},{9,8},{10,11... | collective-permute-start | bytes 786440 | tf_op jit(solution)/shard_map/ppermute | solution.py:75
  117.0 9.2 %collective-permute-start.13 = (f32[128,128]{0,1:T(8,128)S(1)}, f32[128,128]{0,1:T(8,128)S(1)}, u32[]{:S(2)}, u32[]{:S(2)}) collective-permute-start(f32[128,128]{0,1:T(8,128)S(1)} %fusion.27), channel_id=1, source_target_pairs={{0,2},{1,3},{2,0},{3,1},{4,6},{5,7},{6,4},{7,5},{8,10},{9,11},{10,... | collective-permute-start | bytes 196616 | tf_op jit(solution)/shard_map/ppermute | solution.py:44
  117.8 9.4 %collective-permute-start.12 = (f32[128,128]{0,1:T(8,128)S(1)}, f32[128,128]{0,1:T(8,128)S(1)}, u32[]{:S(2)}, u32[]{:S(2)}) collective-permute-start(f32[128,128]{0,1:T(8,128)S(1)} %fusion.27), channel_id=1, source_target_pairs={{0,1},{1,0},{2,3},{3,2},{4,5},{5,4},{6,7},{7,6},{8,9},{9,8},{10,11... | collective-permute-start | bytes 196616 | tf_op jit(solution)/shard_map/ppermute | solution.py:44
  118.9 9.7 %collective-permute-start.14 = (f32[128,128]{0,1:T(8,128)S(1)}, f32[128,128]{0,1:T(8,128)S(1)}, u32[]{:S(2)}, u32[]{:S(2)}) collective-permute-start(f32[128,128]{0,1:T(8,128)S(1)} %fusion.27), channel_id=1, source_target_pairs={{0,3},{1,2},{2,1},{3,0},{4,7},{5,6},{6,5},{7,4},{8,11},{9,10},{10,... | collective-permute-start | bytes 196616 | tf_op jit(solution)/shard_map/ppermute | solution.py:44
  126.1 6.3 %collective-permute-start.16 = (f32[256,128]{1,0:T(8,128)S(1)}, f32[256,128]{1,0:T(8,128)S(1)}, u32[]{:S(2)}, u32[]{:S(2)}) collective-permute-start(f32[256,128]{1,0:T(8,128)S(1)} %slice_select_fusion.1), channel_id=1, source_target_pairs={{0,2},{1,3},{2,0},{3,1},{4,6},{5,7},{6,4},{7,5},{8,10},{9,11},{10,... | collective-permute-start | bytes 393224 | tf_op jit(solution)/shard_map/ppermute | solution.py:75
  132.4 11.8 %collective-permute-start.17 = (f32[256,128]{1,0:T(8,128)S(1)}, f32[256,128]{1,0:T(8,128)S(1)}, u32[]{:S(2)}, u32[]{:S(2)}) collective-permute-start(f32[256,128]{1,0:T(8,128)S(1)} %select_add_fusion.1), channel_id=1, source_target_pairs={{0,2},{1,3},{2,0},{3,1},{4,6},{5,7},{6,4},{7,5},{8,10},{9,11},{10,... | collective-permute-start | bytes 393224 | tf_op jit(solution)/shard_map/ppermute | solution.py:78
  144.3 15.3 %collective-permute-start.18 = (f32[512,128]{1,0:T(8,128)S(1)}, f32[512,128]{1,0:T(8,128)S(1)}, u32[]{:S(2)}, u32[]{:S(2)}) collective-permute-start(f32[512,128]{1,0:T(8,128)S(1)} %maximum_select_fusion.9), channel_id=1, source_target_pairs={{0,1},{1,0},{2,3},{3,2},{4,5},{5,4},{6,7},{7,6},{8,9},{9,8},{10,11... | collective-permute-start | bytes 786440 | tf_op jit(solution)/shard_map/ppermute | solution.py:78
  160.9 4.9 %collective-permute-start.20 = (f32[128,128]{0,1:T(8,128)S(1)}, f32[128,128]{0,1:T(8,128)S(1)}, u32[]{:S(2)}, u32[]{:S(2)}) collective-permute-start(f32[128,128]{0,1:T(8,128)S(1)} %fusion.41), channel_id=1, source_target_pairs={{0,8},{4,12},{8,0},{12,4},{1,9},{5,13},{9,1},{13,5},{2,10},{6,14},... | collective-permute-start | bytes 196616 | tf_op jit(solution)/shard_map/ppermute | solution.py:44
  160.9 4.8 %collective-permute-start.19 = (f32[128,128]{0,1:T(8,128)S(1)}, f32[128,128]{0,1:T(8,128)S(1)}, u32[]{:S(2)}, u32[]{:S(2)}) collective-permute-start(f32[128,128]{0,1:T(8,128)S(1)} %fusion.41), channel_id=1, source_target_pairs={{0,4},{4,0},{8,12},{12,8},{1,5},{5,1},{9,13},{13,9},{2,6},{6,2},{1... | collective-permute-start | bytes 196616 | tf_op jit(solution)/shard_map/ppermute | solution.py:44
  161.0 4.7 %collective-permute-start.21 = (f32[128,128]{0,1:T(8,128)S(1)}, f32[128,128]{0,1:T(8,128)S(1)}, u32[]{:S(2)}, u32[]{:S(2)}) collective-permute-start(f32[128,128]{0,1:T(8,128)S(1)} %fusion.41), channel_id=1, source_target_pairs={{0,12},{4,8},{8,4},{12,0},{1,13},{5,9},{9,5},{13,1},{2,14},{6,10},... | collective-permute-start | bytes 196616 | tf_op jit(solution)/shard_map/ppermute | solution.py:44

commit v9 on v8

--- a/solution.py
+++ b/solution.py
@@ -45,20 +45,18 @@
     return (x + got[0]) + (got[1] + got[2])
 
 
-def _butterfly_gather(xs, axes_of):
-    xs = [x[None] for x in xs]
-    plans = [[(axis, step) for axis in axes for step in _bits(lax.axis_size(axis), True)] for axes in axes_of]
-    while any(plans):
-        head = next(plan[0] for plan in plans if plan)
-        which = [k for k, plan in enumerate(plans) if plan and plan[0] == head]
-        axis, step = head
+def _butterfly_gather(x, plan):
+    x = x[None]
+    for axis, step, slot in plan:
         count = lax.axis_size(axis)
         low = (lax.axis_index(axis) & step) == 0
-        others = lax.ppermute([xs[k] for k in which], axis, [(i, i ^ step) for i in range(count)])
-        for k, other in zip(which, others):
-            xs[k] = jnp.where(low, jnp.concatenate([xs[k], other], 0), jnp.concatenate([other, xs[k]], 0))
-            plans[k] = plans[k][1:]
-    return xs
+        other = lax.ppermute(x, axis, [(i, i ^ step) for i in range(count)])
+        below = 2 ** sum(1 for _, _, done in plan[: plan.index((axis, step, slot))] if done < slot)
+        mine = x.reshape((-1, 1, below) + x.shape[1:])
+        theirs = other.reshape(mine.shape)
+        x = jnp.where(low, jnp.concatenate([mine, theirs], 1), jnp.concatenate([theirs, mine], 1))
+        x = x.reshape((-1,) + x.shape[3:])
+    return x
 
 
 def _halving_sum(x, axis):
@@ -114,9 +112,14 @@
     if row_count == col_count and power_of_two:
         swapped = lax.ppermute(local_rows, ("row", "col"), _transpose_pairs(row_count, col_count))
         swapped = jnp.where(row_here == col_here, local_rows, swapped)
-        right_rows, left_rows = _butterfly_gather(
-            [local_rows, swapped], [("bin", "col"), ("bin", "row")]
-        )
+        group = _bits(col_count, True)
+        bins = _bits(bin_count, True)
+        right_plan = [("col", step, k) for k, step in enumerate(group)]
+        right_plan += [("bin", step, len(group) + k) for k, step in enumerate(bins)]
+        left_plan = [("bin", step, len(group) + k) for k, step in enumerate(bins)]
+        left_plan += [("row", step, k) for k, step in enumerate(group)]
+        right_rows = _butterfly_gather(local_rows, right_plan)
+        left_rows = _butterfly_gather(swapped, left_plan)
     else:
         right_rows = lax.all_gather(local_rows, ("bin", "col"), axis=0, tiled=False)
         every_row = lax.all_gather(right_rows, "row", axis=1, tiled=True)

time: 191 us -> 190 us (level)
  starting transfers between devices: 36.3 us -> 24.2 us
  other arithmetic: 52.1 us -> 60.5 us
  waiting for transfers between devices: 76.8 us -> 81 us
  matrix products: 22.9 us -> 20 us
  local copies, waits for them, and re-layouts: 1.3 us -> 3.59 us
    ppermute x6, starting transfers between devices: 20.3 us -> 10.4 us  [_butterfly_gather(): other = lax.ppermute(x, axis, [(i, i ^ step) for i in range(count)])]
    select_n x4 -> x10, other arithmetic: 5.89 us -> 12.3 us  [the longest x9 12.3 us: _butterfly_gather(): jnp.where(low, jnp.concatenate([mine, theirs], 1), jnp.concatenate([their...]
    ppermute x2, starting transfers between devices: 4.28 us -> 0.84 us  [_halving_sum(): other = lax.ppermute(x, axis, [(i, i ^ step) for i in range(count)])]
    ppermute x6, waiting for transfers between devices: 43.6 us -> 46.9 us  [_butterfly_gather(): other = lax.ppermute(x, axis, [(i, i ^ step) for i in range(count)])]
    dot_general x1, matrix products: 5.34 us -> 2.39 us  [shards(): lax.dot_general(left_rows, right_rows, (((0, 2), (0, 2)), ((), ())), pref...]
  transfers between devices with their start and end apart: 22 -> 22, of which waited for: 12 -> 12; matrix products, arithmetic and copies ran while one was open for 16% -> 21% of each run, Pallas kernels for 0% -> 0%
where the time goes in v9:
time: 190 us
  waiting for transfers between devices  81 us (43%)
  other arithmetic  60.5 us (32%)
  starting transfers between devices  24.2 us (13%)
  matrix products  20 us (11%)
  local copies, waits for them, and re-layouts  3.59 us (2%)
    ppermute x6, waiting for transfers between devices, _butterfly_gather(): other = lax.ppermute(x, axis, [(i, i ^ step) for i in range(count)])  46.9 us
    another operation x6, other arithmetic, _lower_factor(): return jnp.linalg.cholesky(_direct_sum(gram_part, gram_axis))  25 us
    another operation x4, other arithmetic, _right_solve(): jax.scipy.linalg.solve_triangular(lower_factor, image.T, lower=True)  20.9 us
    ppermute x2, waiting for transfers between devices, _butterfly_sum(): x = x + lax.ppermute(x, axis, [(i, i ^ step) for i in range(count)])  15.6 us
    select_n x9, other arithmetic, _butterfly_gather(): jnp.where(low, jnp.concatenate([mine, theirs], 1), jnp.concatenate([their...  12.3 us
    ppermute x6, starting transfers between devices, _butterfly_gather(): other = lax.ppermute(x, axis, [(i, i ^ step) for i in range(count)])  10.4 us
    ppermute x9, waiting for transfers between devices, _direct_sum(): lax.ppermute(x, axis, [(i, i ^ k) for i in range(count)])  10.1 us
    ppermute x9, starting transfers between devices, _direct_sum(): lax.ppermute(x, axis, [(i, i ^ k) for i in range(count)])  9.81 us
  transfers between devices with their start and end apart: 22, of which 12 were waited for; matrix products, arithmetic and copies ran while one was open for 21% of the time, Pallas kernels for 0%

profile of v9, /device:TPU:0, one launch (start us, length us, event | category | flops | bytes accessed | tf_op | source)
XLA Modules:
  0.0 190.1 jit_solution(3170831983804870974)
XLA Ops:
  0.7 2.2 %fusion.30 = f32[8,128,16]{1,2,0:T(8,128)S(1)} fusion(bf16[1024,8,16]{0,2,1:T(8,128)(2,1)} %param.7, bf16[8,1024,128]{2,1,0:T(8,128)(2,1)} %param.8), kind=kOutput, calls=%fused_computation.61 | convolution fusion | flops 33554432 | bytes 2424832 | tf_op jit(solution)/shard_map/mbs,bmr->brs/dot_general | solution.py:99
  2.9 2.5 %collective-permute-start.2 = (f32[8,128,16]{1,2,0:T(8,128)S(1)}, f32[8,128,16]{1,2,0:T(8,128)S(1)}, u32[]{:S(2)}, u32[]{:S(2)}) collective-permute-start(f32[8,128,16]{1,2,0:T(8,128)S(1)} %fusion.30), channel_id=1, source_target_pairs={{0,12},{4,8},{8,4},{12,0},{1,13},{5,9},{9,5},{13,1},{2,14},{6,10},... | collective-permute-start | bytes 196616 | tf_op jit(solution)/shard_map/ppermute | solution.py:44
  6.0 1.8 collective-permute-done.2
  7.8 2.2 %collective-permute-done.1 = f32[8,128,16]{1,2,0:T(8,128)S(1)} collective-permute-done((f32[8,128,16]{1,2,0:T(8,128)S(1)}, f32[8,128,16]{1,2,0:T(8,128)S(1)}, u32[]{:S(2)}, u32[]{:S(2)}) %collective-permute-start.1) | collective-permute-done | bytes 65568 | tf_op jit(solution)/shard_map/ppermute | solution.py:44
  10.0 0.7 fusion.1
  10.7 0.7 collective-permute-start.3
  11.4 5.3 %collective-permute-start.7 = (bf16[1,1024,128]{1,2,0:T(8,128)(2,1)S(1)}, bf16[1,1024,128]{1,2,0:T(8,128)(2,1)S(1)}, u32[]{:S(2)}, u32[]{:S(2)}) collective-permute-start(bf16[1,1024,128]{1,2,0:T(8,128)(2,1)S(1)} %bitcast.70), channel_id=1, source_target_pairs={{0,2},{1,3},{2,0},{3,1},{4,6},{5,7},{6,4},{7,5},{8,10},{9,11},{10,... | collective-permute-start | bytes 786440 | tf_op jit(solution)/shard_map/ppermute | solution.py:53
  16.8 1.6 collective-permute-start.4
  18.3 21.8 %collective-permute-done.7 = bf16[1,1024,128]{1,2,0:T(8,128)(2,1)S(1)} collective-permute-done((bf16[1,1024,128]{1,2,0:T(8,128)(2,1)S(1)}, bf16[1,1024,128]{1,2,0:T(8,128)(2,1)S(1)}, u32[]{:S(2)}, u32[]{:S(2)}) %collective-permute-start.7) | collective-permute-done | bytes 262176 | tf_op jit(solution)/shard_map/ppermute | solution.py:53
  40.2 0.9 maximum_select_fusion.9
  41.0 0.9 maximum_select_fusion.6
  41.9 1.9 %collective-permute-start.5 = (bf16[2,1024,128]{1,2,0:T(8,128)(2,1)}, bf16[2,1024,128]{1,2,0:T(8,128)(2,1)}, u32[]{:S(2)}, u32[]{:S(2)}) collective-permute-start(bf16[2,1024,128]{1,2,0:T(8,128)(2,1)} %maximum_select_fusion.6), channel_id=1, source_target_pairs={{0,8},{4,12},{8,0},{12,4},{1,9},{5,13},{9,1},{13,5},{2,10},{6,14},... | collective-permute-start | bytes 1572872 | tf_op jit(solution)/shard_map/ppermute | solution.py:53
  43.9 10.9 %collective-permute-done.8 = bf16[2,1024,128]{1,2,0:T(8,128)(2,1)} collective-permute-done((bf16[2,1024,128]{1,2,0:T(8,128)(2,1)}, bf16[2,1024,128]{1,2,0:T(8,128)(2,1)}, u32[]{:S(2)}, u32[]{:S(2)}) %collective-permute-start.8) | collective-permute-done | bytes 524320 | tf_op jit(solution)/shard_map/ppermute | solution.py:53
  54.8 1.4 maximum_select_fusion.4
  56.2 1.3 copy.7
  57.5 1.5 collective-permute-start.9
  59.1 1.1 maximum_select_fusion.7
  60.2 2.3 %maximum_select_fusion.3 = bf16[2,2,1,1024,128]{3,4,2,1,0:T(8,128)(2,1)} fusion(bf16[2,1,1,1024,128]{3,4,2,1,0:T(8,128)(2,1)} %bitcast.6, bf16[2,1,1,1024,128]{3,4,2,1,0:T(8,128)(2,1)S(1)} %maximum_select_fusion.7, pred[]{:T(512)S(6)} %eq.24), kind=kLoop, calls=%fused_computation.7 | loop fusion | flops 1572864 | bytes 2097153 | tf_op jit(solution)/shard_map/jit(_where)/select_n | solution.py:57
  62.5 1.9 %fusion.2 = bf16[2,1,1,1024,128]{3,4,2,1,0:T(8,128)(2,1)} fusion(bf16[1,1,1024,128]{2,3,0,1:T(8,128)(2,1)} %bitcast.74, bf16[1,1,1024,128]{2,3,0,1:T(8,128)(2,1)S(1)} %bitcast.68, pred[]{:T(512)S(6)} %eq.25), kind=kLoop, calls=%fused_computation.10 | loop fusion | flops 786432 | bytes 1048577 | tf_op jit(solution)/shard_map/concatenate | solution.py:57
  64.4 1.3 copy.8
  65.7 1.8 maximum_select_fusion.2
  67.5 14.2 %collective-permute-done.9 = bf16[4,1024,128]{2,1,0:T(8,128)(2,1)} collective-permute-done((bf16[4,1024,128]{2,1,0:T(8,128)(2,1)}, bf16[4,1024,128]{2,1,0:T(8,128)(2,1)}, u32[]{:S(2)}, u32[]{:S(2)}) %collective-permute-start.9) | collective-permute-done | bytes 1048608 | tf_op jit(solution)/shard_map/ppermute | solution.py:53
  81.7 1.9 %maximum_select_fusion.1 = bf16[1,2,4,1024,128]{4,3,2,1,0:T(8,128)(2,1)S(1)} fusion(bf16[1,1,4,1024,128]{4,3,2,1,0:T(8,128)(2,1)} %bitcast.18, bf16[1,1,4,1024,128]{4,3,2,1,0:T(8,128)(2,1)S(1)} %copy-done.2, pred[]{:T(512)S(6)} %eq.25), kind=kLoop, calls=%fused_computation.2 | loop fusion | flops 3145728 | bytes 4194305 | tf_op jit(solution)/shard_map/jit(_where)/select_n | solution.py:57
  83.7 1.9 %maximum_select_fusion = bf16[2,2,2,1024,128]{3,4,2,1,0:T(8,128)(2,1)S(1)} fusion(bf16[2,1,2,1024,128]{3,4,2,1,0:T(8,128)(2,1)} %bitcast.10, bf16[2,1,2,1024,128]{3,4,2,1,0:T(8,128)(2,1)S(1)} %maximum_select_fusion.2, pred[]{:T(512)S(6)} %eq.23), kind=kLoop, calls=%fused_computation.1 | loop fusion | flops 3145728 | bytes 4194305 | tf_op jit(solution)/shard_map/jit(_where)/select_n | solution.py:57
  85.6 2.4 %bitcast_multiply_fusion = f32[1024,1024]{1,0:T(8,128)S(1)} fusion(bf16[8,1024,128]{1,2,0:T(8,128)(2,1)S(1)} %bitcast.76, bf16[8,1024,128]{2,1,0:T(8,128)(2,1)S(1)} %bitcast.75), kind=kOutput, calls=%fused_computation | convolution fusion | flops 2148532224 | bytes 8388608 | tf_op jit(solution)/shard_map/dot_general | solution.py:127
  88.0 4.9 %fusion.11 = f32[1024,128]{1,0:T(8,128)S(1)} fusion(f32[1024,1024]{1,0:T(8,128)S(1)} %bitcast_multiply_fusion, f32[4096,128]{1,0:T(8,128)} %param.10, s32[]{:T(128)S(6)} %select_n.247), kind=kOutput, calls=%fused_computation.23 | convolution fusion | flops 1610612736 | bytes 5242884 | tf_op jit(solution)/shard_map/dot_general | solution.py:133
  93.0 1.9 collective-permute-done.10
  95.3 13.7 %collective-permute-done.11 = f32[1024,128]{1,0:T(8,128)S(1)} collective-permute-done((f32[1024,128]{1,0:T(8,128)S(1)}, f32[1024,128]{1,0:T(8,128)S(1)}, u32[]{:S(2)}, u32[]{:S(2)}) %collective-permute-start.11) | collective-permute-done | bytes 524320 | tf_op jit(solution)/shard_map/ppermute | solution.py:26
  109.0 7.1 %fusion.14 = f32[1024,128]{1,0:T(8,128)S(1)} fusion(f32[1024,1024]{1,0:T(8,128)S(1)} %bitcast_multiply_fusion, f32[1024,128]{1,0:T(8,128)S(1)} %add.62, f32[1024,128]{1,0:T(8,128)S(1)} %collective-permute-done.11), kind=kOutput, calls=%fused_computation.30 | convolution fusion | flops 1610743808 | bytes 5767168 | tf_op jit(solution)/shard_map/dot_general | solution.py:138
  116.7 1.0 fusion.16
  117.7 2.3 %collective-permute-start.13 = (f32[128,128]{0,1:T(8,128)S(1)}, f32[128,128]{0,1:T(8,128)S(1)}, u32[]{:S(2)}, u32[]{:S(2)}) collective-permute-start(f32[128,128]{0,1:T(8,128)S(1)} %fusion.16), channel_id=1, source_target_pairs={{0,2},{1,3},{2,0},{3,1},{4,6},{5,7},{6,4},{7,5},{8,10},{9,11},{10,... | collective-permute-start | bytes 196616 | tf_op jit(solution)/shard_map/ppermute | solution.py:44
  120.6 1.6 collective-permute-start.14
  122.2 3.6 %collective-permute-done.15 = f32[512,128]{1,0:T(8,128)S(1)} collective-permute-done((f32[512,128]{1,0:T(8,128)S(1)}, f32[512,128]{1,0:T(8,128)S(1)}, u32[]{:S(2)}, u32[]{:S(2)}) %collective-permute-start.15) | collective-permute-done | bytes 262176 | tf_op jit(solution)/shard_map/ppermute | solution.py:73
  125.8 1.4 collective-permute-start.16
  127.2 3.1 %collective-permute-done.14 = f32[128,128]{0,1:T(8,128)S(1)} collective-permute-done((f32[128,128]{0,1:T(8,128)S(1)}, f32[128,128]{0,1:T(8,128)S(1)}, u32[]{:S(2)}, u32[]{:S(2)}) %collective-permute-start.14) | collective-permute-done | bytes 65568 | tf_op jit(solution)/shard_map/ppermute | solution.py:44
  130.4 4.8 %collective-permute-done.16 = f32[256,128]{1,0:T(8,128)S(1)} collective-permute-done((f32[256,128]{1,0:T(8,128)S(1)}, f32[256,128]{1,0:T(8,128)S(1)}, u32[]{:S(2)}, u32[]{:S(2)}) %collective-permute-start.16) | collective-permute-done | bytes 131104 | tf_op jit(solution)/shard_map/ppermute | solution.py:73
  135.3 11.7 %cholesky.44 = f32[128,128]{1,0:T(8,128)S(1)} custom-call(f32[128,128]{1,0:T(8,128)S(1)} %fusion.24), custom_call_target="Cholesky" | custom-call | tf_op jit(solution)/shard_map/jit(cholesky)/cholesky | solution.py:85
  147.1 0.8 collective-permute-start.18
  148.5 0.7 fusion.18
  149.2 9.8 %custom-call.6 = f32[1,128,128]{1,2,0:T(8,128)S(1)} custom-call(f32[1,128,128]{2,1,0:T(8,128)S(1)} %fusion.18), custom_call_target="InvertDiagBlocksLowerTriangular" | custom-call | tf_op jit(solution)/shard_map/jit(_solve_triangular)/triangular_solve | solution.py:89
  160.2 1.5 collective-permute-start.20
  161.7 0.7 collective-permute-start.21
  162.4 2.1 %collective-permute-done.20 = f32[128,128]{0,1:T(8,128)S(1)} collective-permute-done((f32[128,128]{0,1:T(8,128)S(1)}, f32[128,128]{0,1:T(8,128)S(1)}, u32[]{:S(2)}, u32[]{:S(2)}) %collective-permute-start.20) | collective-permute-done | bytes 65568 | tf_op jit(solution)/shard_map/ppermute | solution.py:44
  164.6 0.9 collective-permute-done.21
  165.6 12.0 %cholesky.55 = f32[128,128]{1,0:T(8,128)S(1)} custom-call(f32[128,128]{1,0:T(8,128)S(1)} %fusion.22), custom_call_target="Cholesky" | custom-call | tf_op jit(solution)/shard_map/jit(cholesky)/cholesky | solution.py:85
  178.2 0.7 fusion.19
  178.9 9.8 %custom-call.7 = f32[1,128,128]{1,2,0:T(8,128)S(1)} custom-call(f32[1,128,128]{2,1,0:T(8,128)S(1)} %fusion.19), custom_call_target="InvertDiagBlocksLowerTriangular" | custom-call | tf_op jit(solution)/shard_map/jit(_solve_triangular)/triangular_solve | solution.py:89
  189.4 0.8 copy.20
  (52 shorter events, 6.2 us)
Async XLA Ops:
  0.6 9.4 %copy-start = (bf16[8,1024,128]{2,1,0:T(8,128)(2,1)S(1)}, bf16[8,1024,128]{2,1,0:T(8,128)(2,1)}, u32[]{:S(2)}) copy-start(bf16[8,1024,128]{2,1,0:T(8,128)(2,1)} %param.9) | copy-start | bytes 6291460
  0.6 9.4 %copy-start.4 = (bf16[1024,8,16]{0,2,1:T(8,128)(2,1)S(1)}, bf16[1024,8,16]{0,2,1:T(8,128)(2,1)}, u32[]{:S(2)}) copy-start(bf16[1024,8,16]{0,2,1:T(8,128)(2,1)} %param.7) | copy-start | bytes 786436
  2.9 5.0 %collective-permute-start.2 = (f32[8,128,16]{1,2,0:T(8,128)S(1)}, f32[8,128,16]{1,2,0:T(8,128)S(1)}, u32[]{:S(2)}, u32[]{:S(2)}) collective-permute-start(f32[8,128,16]{1,2,0:T(8,128)S(1)} %fusion.30), channel_id=1, source_target_pairs={{0,12},{4,8},{8,4},{12,0},{1,13},{5,9},{9,5},{13,1},{2,14},{6,10},... | collective-permute-start | bytes 196616 | tf_op jit(solution)/shard_map/ppermute | solution.py:44
  5.3 4.7 %collective-permute-start.1 = (f32[8,128,16]{1,2,0:T(8,128)S(1)}, f32[8,128,16]{1,2,0:T(8,128)S(1)}, u32[]{:S(2)}, u32[]{:S(2)}) collective-permute-start(f32[8,128,16]{1,2,0:T(8,128)S(1)} %fusion.30), channel_id=1, source_target_pairs={{0,8},{4,12},{8,0},{12,4},{1,9},{5,13},{9,1},{13,5},{2,10},{6,14},... | collective-permute-start | bytes 196616 | tf_op jit(solution)/shard_map/ppermute | solution.py:44
  6.0 4.0 %collective-permute-start = (f32[8,128,16]{1,2,0:T(8,128)S(1)}, f32[8,128,16]{1,2,0:T(8,128)S(1)}, u32[]{:S(2)}, u32[]{:S(2)}) collective-permute-start(f32[8,128,16]{1,2,0:T(8,128)S(1)} %fusion.30), channel_id=1, source_target_pairs={{0,4},{4,0},{8,12},{12,8},{1,5},{5,1},{9,13},{13,9},{2,6},{6,2},{1... | collective-permute-start | bytes 196616 | tf_op jit(solution)/shard_map/ppermute | solution.py:44
  10.7 6.0 %collective-permute-start.3 = (bf16[1024,128]{0,1:T(8,128)(2,1)S(1)}, bf16[1024,128]{0,1:T(8,128)(2,1)S(1)}, u32[]{:S(2)}, u32[]{:S(2)}) collective-permute-start(bf16[1024,128]{0,1:T(8,128)(2,1)S(1)} %bitcast.69), channel_id=1, source_target_pairs={{1,4},{2,8},{3,12},{4,1},{6,9},{7,13},{8,2},{9,6},{11,14},{12,3},{... | collective-permute-start | bytes 786440 | tf_op jit(solution)/shard_map/ppermute | solution.py:113
  11.4 28.8 %collective-permute-start.7 = (bf16[1,1024,128]{1,2,0:T(8,128)(2,1)S(1)}, bf16[1,1024,128]{1,2,0:T(8,128)(2,1)S(1)}, u32[]{:S(2)}, u32[]{:S(2)}) collective-permute-start(bf16[1,1024,128]{1,2,0:T(8,128)(2,1)S(1)} %bitcast.70), channel_id=1, source_target_pairs={{0,2},{1,3},{2,0},{3,1},{4,6},{5,7},{6,4},{7,5},{8,10},{9,11},{10,... | collective-permute-start | bytes 786440 | tf_op jit(solution)/shard_map/ppermute | solution.py:53
  16.8 24.3 %collective-permute-start.4 = (bf16[1,1024,128]{1,2,0:T(8,128)(2,1)S(1)}, bf16[1,1024,128]{1,2,0:T(8,128)(2,1)S(1)}, u32[]{:S(2)}, u32[]{:S(2)}) collective-permute-start(bf16[1,1024,128]{1,2,0:T(8,128)(2,1)S(1)} %bitcast.65), channel_id=1, source_target_pairs={{0,16},{16,0},{1,17},{17,1},{2,18},{18,2},{3,19},{19,3},{4,20},{20... | collective-permute-start | bytes 786440 | tf_op jit(solution)/shard_map/ppermute | solution.py:53
  41.0 13.8 %collective-permute-start.8 = (bf16[2,1024,128]{1,2,0:T(8,128)(2,1)}, bf16[2,1024,128]{1,2,0:T(8,128)(2,1)}, u32[]{:S(2)}, u32[]{:S(2)}) collective-permute-start(bf16[2,1024,128]{1,2,0:T(8,128)(2,1)} %maximum_select_fusion.9), channel_id=1, source_target_pairs={{0,1},{1,0},{2,3},{3,2},{4,5},{5,4},{6,7},{7,6},{8,9},{9,8},{10,11... | collective-permute-start | bytes 1572872 | tf_op jit(solution)/shard_map/ppermute | solution.py:53
  41.0 13.8 %copy-start.3 = (bf16[1,1024,128]{1,2,0:T(8,128)(2,1)}, bf16[1,1024,128]{1,2,0:T(8,128)(2,1)S(1)}, u32[]{:S(2)}) copy-start(bf16[1,1024,128]{1,2,0:T(8,128)(2,1)S(1)} %collective-permute-done.4) | copy-start | bytes 786436
  41.9 18.3 %collective-permute-start.5 = (bf16[2,1024,128]{1,2,0:T(8,128)(2,1)}, bf16[2,1024,128]{1,2,0:T(8,128)(2,1)}, u32[]{:S(2)}, u32[]{:S(2)}) collective-permute-start(bf16[2,1024,128]{1,2,0:T(8,128)(2,1)} %maximum_select_fusion.6), channel_id=1, source_target_pairs={{0,8},{4,12},{8,0},{12,4},{1,9},{5,13},{9,1},{13,5},{2,10},{6,14},... | collective-permute-start | bytes 1572872 | tf_op jit(solution)/shard_map/ppermute | solution.py:53
  57.5 24.2 %collective-permute-start.9 = (bf16[4,1024,128]{2,1,0:T(8,128)(2,1)}, bf16[4,1024,128]{2,1,0:T(8,128)(2,1)}, u32[]{:S(2)}, u32[]{:S(2)}) collective-permute-start(bf16[4,1024,128]{2,1,0:T(8,128)(2,1)} %copy.7), channel_id=1, source_target_pairs={{0,16},{16,0},{1,17},{17,1},{2,18},{18,2},{3,19},{19,3},{4,20},{20... | collective-permute-start | bytes 3145736 | tf_op jit(solution)/shard_map/ppermute | solution.py:53
  62.5 21.2 %collective-permute-start.6 = (bf16[4,1024,128]{1,2,0:T(8,128)(2,1)}, bf16[4,1024,128]{1,2,0:T(8,128)(2,1)}, u32[]{:S(2)}, u32[]{:S(2)}) collective-permute-start(bf16[4,1024,128]{1,2,0:T(8,128)(2,1)} %bitcast.9), channel_id=1, source_target_pairs={{0,4},{4,0},{8,12},{12,8},{1,5},{5,1},{9,13},{13,9},{2,6},{6,2},{1... | collective-permute-start | bytes 3145736 | tf_op jit(solution)/shard_map/ppermute | solution.py:53
  65.7 16.0 %copy-start.2 = (bf16[1,1,4,1024,128]{4,3,2,1,0:T(8,128)(2,1)S(1)}, bf16[1,1,4,1024,128]{4,3,2,1,0:T(8,128)(2,1)}, u32[]{:S(2)}) copy-start(bf16[1,1,4,1024,128]{4,3,2,1,0:T(8,128)(2,1)} %copy.8) | copy-start | bytes 3145732
  88.0 21.0 %copy-start.1 = (f32[1024,1024]{1,0:T(8,128)}, f32[1024,1024]{1,0:T(8,128)S(1)}, u32[]{:S(2)}) copy-start(f32[1024,1024]{1,0:T(8,128)S(1)} %bitcast_multiply_fusion) | copy-start | bytes 12582916
  92.9 2.0 %collective-permute-start.10 = (f32[1024,128]{1,0:T(8,128)S(1)}, f32[1024,128]{1,0:T(8,128)S(1)}, u32[]{:S(2)}, u32[]{:S(2)}) collective-permute-start(f32[1024,128]{1,0:T(8,128)S(1)} %fusion.11), channel_id=1, source_target_pairs={{0,4},{4,0},{8,12},{12,8},{1,5},{5,1},{9,13},{13,9},{2,6},{6,2},{1... | collective-permute-start | bytes 1572872 | tf_op jit(solution)/shard_map/ppermute | solution.py:26
  94.9 14.0 %collective-permute-start.11 = (f32[1024,128]{1,0:T(8,128)S(1)}, f32[1024,128]{1,0:T(8,128)S(1)}, u32[]{:S(2)}, u32[]{:S(2)}) collective-permute-start(f32[1024,128]{1,0:T(8,128)S(1)} %add.62), channel_id=1, source_target_pairs={{0,8},{4,12},{8,0},{12,4},{1,9},{5,13},{9,1},{13,5},{2,10},{6,14},... | collective-permute-start | bytes 1572872 | tf_op jit(solution)/shard_map/ppermute | solution.py:26
  116.1 9.7 %collective-permute-start.15 = (f32[512,128]{1,0:T(8,128)S(1)}, f32[512,128]{1,0:T(8,128)S(1)}, u32[]{:S(2)}, u32[]{:S(2)}) collective-permute-start(f32[512,128]{1,0:T(8,128)S(1)} %slice_select_fusion), channel_id=1, source_target_pairs={{0,1},{1,0},{2,3},{3,2},{4,5},{5,4},{6,7},{7,6},{8,9},{9,8},{10,11... | collective-permute-start | bytes 786440 | tf_op jit(solution)/shard_map/ppermute | solution.py:73
  117.7 9.5 %collective-permute-start.13 = (f32[128,128]{0,1:T(8,128)S(1)}, f32[128,128]{0,1:T(8,128)S(1)}, u32[]{:S(2)}, u32[]{:S(2)}) collective-permute-start(f32[128,128]{0,1:T(8,128)S(1)} %fusion.16), channel_id=1, source_target_pairs={{0,2},{1,3},{2,0},{3,1},{4,6},{5,7},{6,4},{7,5},{8,10},{9,11},{10,... | collective-permute-start | bytes 196616 | tf_op jit(solution)/shard_map/ppermute | solution.py:44
  120.0 7.2 %collective-permute-start.12 = (f32[128,128]{0,1:T(8,128)S(1)}, f32[128,128]{0,1:T(8,128)S(1)}, u32[]{:S(2)}, u32[]{:S(2)}) collective-permute-start(f32[128,128]{0,1:T(8,128)S(1)} %fusion.16), channel_id=1, source_target_pairs={{0,1},{1,0},{2,3},{3,2},{4,5},{5,4},{6,7},{7,6},{8,9},{9,8},{10,11... | collective-permute-start | bytes 196616 | tf_op jit(solution)/shard_map/ppermute | solution.py:44
  120.6 9.7 %collective-permute-start.14 = (f32[128,128]{0,1:T(8,128)S(1)}, f32[128,128]{0,1:T(8,128)S(1)}, u32[]{:S(2)}, u32[]{:S(2)}) collective-permute-start(f32[128,128]{0,1:T(8,128)S(1)} %fusion.16), channel_id=1, source_target_pairs={{0,3},{1,2},{2,1},{3,0},{4,7},{5,6},{6,5},{7,4},{8,11},{9,10},{10,... | collective-permute-start | bytes 196616 | tf_op jit(solution)/shard_map/ppermute | solution.py:44
  125.8 9.4 %collective-permute-start.16 = (f32[256,128]{1,0:T(8,128)S(1)}, f32[256,128]{1,0:T(8,128)S(1)}, u32[]{:S(2)}, u32[]{:S(2)}) collective-permute-start(f32[256,128]{1,0:T(8,128)S(1)} %slice_select_fusion.1), channel_id=1, source_target_pairs={{0,2},{1,3},{2,0},{3,1},{4,6},{5,7},{6,4},{7,5},{8,10},{9,11},{10,... | collective-permute-start | bytes 393224 | tf_op jit(solution)/shard_map/ppermute | solution.py:73
  135.2 11.8 %collective-permute-start.17 = (f32[256,128]{1,0:T(8,128)S(1)}, f32[256,128]{1,0:T(8,128)S(1)}, u32[]{:S(2)}, u32[]{:S(2)}) collective-permute-start(f32[256,128]{1,0:T(8,128)S(1)} %select_add_fusion.1), channel_id=1, source_target_pairs={{0,2},{1,3},{2,0},{3,1},{4,6},{5,7},{6,4},{7,5},{8,10},{9,11},{10,... | collective-permute-start | bytes 393224 | tf_op jit(solution)/shard_map/ppermute | solution.py:76
  147.1 11.9 %collective-permute-start.18 = (f32[512,128]{1,0:T(8,128)S(1)}, f32[512,128]{1,0:T(8,128)S(1)}, u32[]{:S(2)}, u32[]{:S(2)}) collective-permute-start(f32[512,128]{1,0:T(8,128)S(1)} %maximum_select_fusion.11), channel_id=1, source_target_pairs={{0,1},{1,0},{2,3},{3,2},{4,5},{5,4},{6,7},{7,6},{8,9},{9,8},{10,11... | collective-permute-start | bytes 786440 | tf_op jit(solution)/shard_map/ppermute | solution.py:76
  160.2 4.3 %collective-permute-start.20 = (f32[128,128]{0,1:T(8,128)S(1)}, f32[128,128]{0,1:T(8,128)S(1)}, u32[]{:S(2)}, u32[]{:S(2)}) collective-permute-start(f32[128,128]{0,1:T(8,128)S(1)} %fusion.29), channel_id=1, source_target_pairs={{0,8},{4,12},{8,0},{12,4},{1,9},{5,13},{9,1},{13,5},{2,10},{6,14},... | collective-permute-start | bytes 196616 | tf_op jit(solution)/shard_map/ppermute | solution.py:44
  161.7 2.8 %collective-permute-start.19 = (f32[128,128]{0,1:T(8,128)S(1)}, f32[128,128]{0,1:T(8,128)S(1)}, u32[]{:S(2)}, u32[]{:S(2)}) collective-permute-start(f32[128,128]{0,1:T(8,128)S(1)} %fusion.29), channel_id=1, source_target_pairs={{0,4},{4,0},{8,12},{12,8},{1,5},{5,1},{9,13},{13,9},{2,6},{6,2},{1... | collective-permute-start | bytes 196616 | tf_op jit(solution)/shard_map/ppermute | solution.py:44
  161.7 3.7 %collective-permute-start.21 = (f32[128,128]{0,1:T(8,128)S(1)}, f32[128,128]{0,1:T(8,128)S(1)}, u32[]{:S(2)}, u32[]{:S(2)}) collective-permute-start(f32[128,128]{0,1:T(8,128)S(1)} %fusion.29), channel_id=1, source_target_pairs={{0,12},{4,8},{8,4},{12,0},{1,13},{5,9},{9,5},{13,1},{2,14},{6,10},... | collective-permute-start | bytes 196616 | tf_op jit(solution)/shard_map/ppermute | solution.py:44

commit v10 on v9

--- a/solution.py
+++ b/solution.py
@@ -54,8 +54,11 @@
         below = 2 ** sum(1 for _, _, done in plan[: plan.index((axis, step, slot))] if done < slot)
         mine = x.reshape((-1, 1, below) + x.shape[1:])
         theirs = other.reshape(mine.shape)
-        x = jnp.where(low, jnp.concatenate([mine, theirs], 1), jnp.concatenate([theirs, mine], 1))
-        x = x.reshape((-1,) + x.shape[3:])
+        first = jnp.where(low, 0, 1)
+        both = jnp.zeros((mine.shape[0], 2) + mine.shape[2:], x.dtype)
+        both = lax.dynamic_update_slice_in_dim(both, mine, first, 1)
+        both = lax.dynamic_update_slice_in_dim(both, theirs, 1 - first, 1)
+        x = both.reshape((-1,) + x.shape[1:])
     return x
 
 
@@ -74,7 +77,10 @@
     for step in steps[::-1]:
         low = (here & step) == 0
         other = lax.ppermute(x, axis, [(i, i ^ step) for i in range(count)])
-        x = jnp.where(low, jnp.concatenate([x, other], 0), jnp.concatenate([other, x], 0))
+        first = jnp.where(low, 0, x.shape[0])
+        both = jnp.zeros((2 * x.shape[0],) + x.shape[1:], x.dtype)
+        both = lax.dynamic_update_slice_in_dim(both, x, first, 0)
+        x = lax.dynamic_update_slice_in_dim(both, other, x.shape[0] - first, 0)
     return x
 
 
@@ -134,7 +140,7 @@
                 covariance, block, precision=lax.Precision.HIGHEST,
                 preferred_element_type=jnp.float32,
             )
-            return _butterfly_sum(partial_image, "row")
+            return _halving_sum(partial_image, "row")
         partial_image = lax.dot_general(
             covariance, block, (((0,), (0,)), ((), ())),
             precision=lax.Precision.HIGHEST, preferred_element_type=jnp.float32,

time: 190 us -> 186 us (0.979)
  waiting for transfers between devices: 81 us -> 65.3 us
  other arithmetic: 60.5 us -> 46.1 us
  local copies, waits for them, and re-layouts: 3.59 us -> 17.5 us
  starting transfers between devices: 24.2 us -> 33.6 us
    ppermute x2 -> x0, waiting for transfers between devices: 15.6 us -> none  [_butterfly_sum(): x = x + lax.ppermute(x, axis, [(i, i ^ step) for i in range(count)])]
    select_n x11 -> x0, other arithmetic: 12.4 us -> none  [the longest x9 12.3 us: _butterfly_gather(): jnp.where(low, jnp.concatenate([mine, theirs], 1), jnp.concatenate([their...]
    dynamic_update_slice x0 -> x18, local copies, waits for them, and re-layouts: none -> 12.2 us  [the longest x6 6.11 us: _butterfly_gather(): both = lax.dynamic_update_slice_in_dim(both, theirs, 1 - first, 1)]
    ppermute x6, waiting for transfers between devices: 46.9 us -> 36.4 us  [_butterfly_gather(): other = lax.ppermute(x, axis, [(i, i ^ step) for i in range(count)])]
    ppermute x2 -> x4, waiting for transfers between devices: 0.01 us -> 8.92 us  [_halving_sum(): other = lax.ppermute(x, axis, [(i, i ^ step) for i in range(count)])]
    ppermute x2 -> x4, starting transfers between devices: 2.04 us -> 7.11 us  [_halving_sum(): x = keep + lax.ppermute(give, axis, [(i, i ^ step) for i in range(count)])]
    ppermute x2 -> x4, starting transfers between devices: 0.84 us -> 4.51 us  [_halving_sum(): other = lax.ppermute(x, axis, [(i, i ^ step) for i in range(count)])]
    ppermute x2 -> x4, waiting for transfers between devices: 8.36 us -> 11.9 us  [_halving_sum(): x = keep + lax.ppermute(give, axis, [(i, i ^ step) for i in range(count)])]
  transfers between devices with their start and end apart: 22 -> 24, of which waited for: 12 -> 15; matrix products, arithmetic and copies ran while one was open for 21% -> 25% of each run, Pallas kernels for 0% -> 0%
where the time goes in v10:
time: 186 us; the launch traced here: 185 us
  waiting for transfers between devices  65.3 us (35%)
  other arithmetic  46.1 us (25%)
  starting transfers between devices  33.6 us (18%)
  matrix products  21.4 us (12%)
  local copies, waits for them, and re-layouts  17.5 us (9%)
    ppermute x6, waiting for transfers between devices, _butterfly_gather(): other = lax.ppermute(x, axis, [(i, i ^ step) for i in range(count)])  36.4 us
    another operation x6, other arithmetic, _lower_factor(): return jnp.linalg.cholesky(_direct_sum(gram_part, gram_axis))  24.8 us
    another operation x4, other arithmetic, _right_solve(): jax.scipy.linalg.solve_triangular(lower_factor, image.T, lower=True)  21 us
    ppermute x4, waiting for transfers between devices, _halving_sum(): x = keep + lax.ppermute(give, axis, [(i, i ^ step) for i in range(count)])  11.9 us
    ppermute x6, starting transfers between devices, _butterfly_gather(): other = lax.ppermute(x, axis, [(i, i ^ step) for i in range(count)])  11.2 us
    ppermute x9, starting transfers between devices, _direct_sum(): lax.ppermute(x, axis, [(i, i ^ k) for i in range(count)])  10.2 us
    ppermute x4, waiting for transfers between devices, _halving_sum(): other = lax.ppermute(x, axis, [(i, i ^ step) for i in range(count)])  8.92 us
    dot_general x1, matrix products, cov_times(): lax.dot_general(covariance, block, (((0,), (0,)), ((), ())), precision=la...  8.48 us
  transfers between devices with their start and end apart: 24, of which 15 were waited for; matrix products, arithmetic and copies ran while one was open for 25% of the time, Pallas kernels for 0%

profile of v10, /device:TPU:0, one launch (start us, length us, event | category | flops | bytes accessed | tf_op | source)
XLA Modules:
  0.0 185.1 jit_solution(17017009210971277925)
XLA Ops:
  0.7 2.2 %fusion.21 = f32[8,128,16]{1,2,0:T(8,128)S(1)} fusion(bf16[1024,8,16]{0,2,1:T(8,128)(2,1)} %param.7, bf16[8,1024,128]{2,1,0:T(8,128)(2,1)} %param.8), kind=kOutput, calls=%fused_computation.65 | convolution fusion | flops 33554432 | bytes 2424832 | tf_op jit(solution)/shard_map/mbs,bmr->brs/dot_general | solution.py:105
  3.4 2.6 %collective-permute-start.1 = (f32[8,128,16]{1,2,0:T(8,128)S(1)}, f32[8,128,16]{1,2,0:T(8,128)S(1)}, u32[]{:S(2)}, u32[]{:S(2)}) collective-permute-start(f32[8,128,16]{1,2,0:T(8,128)S(1)} %fusion.21), channel_id=1, source_target_pairs={{0,8},{4,12},{8,0},{12,4},{1,9},{5,13},{9,1},{13,5},{2,10},{6,14},... | collective-permute-start | bytes 196616 | tf_op jit(solution)/shard_map/ppermute | solution.py:44
  6.0 2.6 %collective-permute-done.1 = f32[8,128,16]{1,2,0:T(8,128)S(1)} collective-permute-done((f32[8,128,16]{1,2,0:T(8,128)S(1)}, f32[8,128,16]{1,2,0:T(8,128)S(1)}, u32[]{:S(2)}, u32[]{:S(2)}) %collective-permute-start.1) | collective-permute-done | bytes 65568 | tf_op jit(solution)/shard_map/ppermute | solution.py:44
  8.7 1.4 collective-permute-done.2
  10.7 2.6 %collective-permute-start.7 = (bf16[1,1024,128]{1,2,0:T(8,128)(2,1)S(1)}, bf16[1,1024,128]{1,2,0:T(8,128)(2,1)S(1)}, u32[]{:S(2)}, u32[]{:S(2)}) collective-permute-start(bf16[1,1024,128]{1,2,0:T(8,128)(2,1)S(1)} %bitcast.81), channel_id=1, source_target_pairs={{0,2},{1,3},{2,0},{3,1},{4,6},{5,7},{6,4},{7,5},{8,10},{9,11},{10,... | collective-permute-start | bytes 786440 | tf_op jit(solution)/shard_map/ppermute | solution.py:53
  14.2 0.9 broadcast.47.clone.1
  15.8 16.3 %collective-permute-done.7 = bf16[1,1024,128]{1,2,0:T(8,128)(2,1)S(1)} collective-permute-done((bf16[1,1024,128]{1,2,0:T(8,128)(2,1)S(1)}, bf16[1,1024,128]{1,2,0:T(8,128)(2,1)S(1)}, u32[]{:S(2)}, u32[]{:S(2)}) %collective-permute-start.7) | collective-permute-done | bytes 262176 | tf_op jit(solution)/shard_map/ppermute | solution.py:53
  32.3 1.6 collective-permute-start.4
  34.8 0.9 broadcast.47.clone
  35.7 0.7 constant_dynamic-update-slice_fusion.12
  36.4 2.7 %collective-permute-done.4 = bf16[1,1024,128]{1,2,0:T(8,128)(2,1)S(1)} collective-permute-done((bf16[1,1024,128]{1,2,0:T(8,128)(2,1)S(1)}, bf16[1,1024,128]{1,2,0:T(8,128)(2,1)S(1)}, u32[]{:S(2)}, u32[]{:S(2)}) %collective-permute-start.4) | collective-permute-done | bytes 262176 | tf_op jit(solution)/shard_map/ppermute | solution.py:53
  40.0 5.9 %collective-permute-start.5 = (bf16[2,1024,128]{2,1,0:T(8,128)(2,1)}, bf16[2,1024,128]{2,1,0:T(8,128)(2,1)S(1)}, u32[]{:S(2)}, u32[]{:S(2)}) collective-permute-start(bf16[2,1024,128]{2,1,0:T(8,128)(2,1)} %bitcast.7), channel_id=1, source_target_pairs={{0,8},{4,12},{8,0},{12,4},{1,9},{5,13},{9,1},{13,5},{2,10},{6,14},... | collective-permute-start | bytes 1572872 | tf_op jit(solution)/shard_map/ppermute | solution.py:53
  46.0 1.1 bitcast_dynamic-update-slice_fusion.5
  47.1 0.9 collective-permute-done.8
  48.0 1.1 bitcast_dynamic-update-slice_fusion.4
  49.1 1.1 collective-permute-start.9
  50.2 1.1 broadcast_in_dim.17
  51.3 1.9 %bitcast_dynamic-update-slice_fusion.3 = bf16[2,2,1,1024,128]{4,3,1,0,2:T(8,128)(2,1)} fusion(bf16[2,2,1,1024,128]{4,3,1,0,2:T(8,128)(2,1)} %broadcast_in_dim.17, s32[]{:T(128)S(6)} %select_n.132, bf16[1,2,1,1024,128]{4,3,1,2,0:T(8,128)(2,1)} %constant_dynamic-update-slice_fusion.11), kind=kLoop, calls=%fused_computation.7 | loop fusion | bytes 1048580 | tf_op jit(solution)/shard_map/dynamic_update_slice | solution.py:59
  53.2 2.6 %collective-permute-done.5 = bf16[2,1024,128]{2,1,0:T(8,128)(2,1)S(1)} collective-permute-done((bf16[2,1024,128]{2,1,0:T(8,128)(2,1)}, bf16[2,1024,128]{2,1,0:T(8,128)(2,1)S(1)}, u32[]{:S(2)}, u32[]{:S(2)}) %collective-permute-start.5) | collective-permute-done | bytes 524320 | tf_op jit(solution)/shard_map/ppermute | solution.py:53
  55.8 0.8 bitcast_dynamic-update-slice_fusion.6
  57.4 1.4 bitcast_dynamic-update-slice_fusion.2
  58.7 14.0 %collective-permute-done.9 = bf16[4,1024,128]{2,1,0:T(8,128)(2,1)} collective-permute-done((bf16[4,1024,128]{2,1,0:T(8,128)(2,1)S(1)}, bf16[4,1024,128]{2,1,0:T(8,128)(2,1)}, u32[]{:S(2)}, u32[]{:S(2)}) %collective-permute-start.9) | collective-permute-done | bytes 1048608 | tf_op jit(solution)/shard_map/ppermute | solution.py:53
  72.7 1.4 bitcast_dynamic-update-slice_fusion
  74.1 1.4 constant_dynamic-update-slice_fusion.10
  75.5 2.4 %bitcast_multiply_fusion = f32[1024,1024]{1,0:T(8,128)S(1)} fusion(bf16[8,1024,128]{2,1,0:T(8,128)(2,1)S(1)} %bitcast.84, bf16[8,1024,128]{2,1,0:T(8,128)(2,1)S(1)} %bitcast.85), kind=kOutput, calls=%fused_computation | convolution fusion | flops 2148532224 | bytes 8388608 | tf_op jit(solution)/shard_map/dot_general | solution.py:133
  77.8 4.9 %fusion.4 = f32[1024,128]{1,0:T(8,128)S(1)} fusion(f32[1024,1024]{1,0:T(8,128)S(1)} %bitcast_multiply_fusion, f32[4096,128]{1,0:T(8,128)} %param.10, s32[]{:T(128)S(6)} %select_n.142), kind=kOutput, calls=%fused_computation.13 | convolution fusion | flops 1610612736 | bytes 5242884 | tf_op jit(solution)/shard_map/dot_general | solution.py:139
  82.9 1.5 collective-permute-done.10
  84.5 5.4 %collective-permute-start.11 = (f32[256,128]{1,0:T(8,128)S(1)}, f32[256,128]{1,0:T(8,128)S(1)}, u32[]{:S(2)}, u32[]{:S(2)}) collective-permute-start(f32[256,128]{1,0:T(8,128)S(1)} %slice_select_fusion.3), channel_id=1, source_target_pairs={{0,8},{4,12},{8,0},{12,4},{1,9},{5,13},{9,1},{13,5},{2,10},{6,14},... | collective-permute-start | bytes 393224 | tf_op jit(solution)/shard_map/ppermute | solution.py:76
  89.8 3.8 %collective-permute-done.11 = f32[256,128]{1,0:T(8,128)S(1)} collective-permute-done((f32[256,128]{1,0:T(8,128)S(1)}, f32[256,128]{1,0:T(8,128)S(1)}, u32[]{:S(2)}, u32[]{:S(2)}) %collective-permute-start.11) | collective-permute-done | bytes 131104 | tf_op jit(solution)/shard_map/ppermute | solution.py:76
  93.7 1.8 collective-permute-start.12
  95.5 3.2 %collective-permute-done.12 = f32[256,128]{1,0:T(8,128)S(1)} collective-permute-done((f32[256,128]{1,0:T(8,128)S(1)}, f32[256,128]{1,0:T(8,128)S(1)}, u32[]{:S(2)}, u32[]{:S(2)}) %collective-permute-start.12) | collective-permute-done | bytes 131104 | tf_op jit(solution)/shard_map/ppermute | solution.py:79
  98.9 1.4 collective-permute-done.13
  100.4 1.0 fusion.18
  101.4 2.5 %collective-permute-start.14 = (f32[128,128]{0,1:T(8,128)S(1)}, f32[128,128]{0,1:T(8,128)S(1)}, u32[]{:S(2)}, u32[]{:S(2)}) collective-permute-start(f32[128,128]{0,1:T(8,128)S(1)} %fusion.18), channel_id=1, source_target_pairs={{0,1},{1,0},{2,3},{3,2},{4,5},{5,4},{6,7},{7,6},{8,9},{9,8},{10,11... | collective-permute-start | bytes 196616 | tf_op jit(solution)/shard_map/ppermute | solution.py:44
  103.9 2.4 %collective-permute-start.16 = (f32[128,128]{0,1:T(8,128)S(1)}, f32[128,128]{0,1:T(8,128)S(1)}, u32[]{:S(2)}, u32[]{:S(2)}) collective-permute-start(f32[128,128]{0,1:T(8,128)S(1)} %fusion.18), channel_id=1, source_target_pairs={{0,3},{1,2},{2,1},{3,0},{4,7},{5,6},{6,5},{7,4},{8,11},{9,10},{10,... | collective-permute-start | bytes 196616 | tf_op jit(solution)/shard_map/ppermute | solution.py:44
  106.4 8.5 %fusion.19 = f32[1024,128]{1,0:T(8,128)S(1)} fusion(f32[1024,1024]{1,0:T(8,128)} %copy-done.1, f32[1024,128]{1,0:T(8,128)S(1)} %constant_dynamic-update-slice_fusion.4), kind=kOutput, calls=%fused_computation.63 | convolution fusion | flops 1610612736 | bytes 5242880 | tf_op jit(solution)/shard_map/dot_general | solution.py:144
  114.9 1.1 collective-permute-start.17
  116.1 6.6 %collective-permute-done.17 = f32[512,128]{1,0:T(8,128)S(1)} collective-permute-done((f32[512,128]{1,0:T(8,128)S(1)}, f32[512,128]{1,0:T(8,128)S(1)}, u32[]{:S(2)}, u32[]{:S(2)}) %collective-permute-start.17) | collective-permute-done | bytes 262176 | tf_op jit(solution)/shard_map/ppermute | solution.py:76
  123.4 11.7 %cholesky.44 = f32[128,128]{1,0:T(8,128)S(1)} custom-call(f32[128,128]{1,0:T(8,128)S(1)} %fusion.14), custom_call_target="Cholesky" | custom-call | tf_op jit(solution)/shard_map/jit(cholesky)/cholesky | solution.py:91
  135.2 2.5 %collective-permute-start.19 = (f32[256,128]{1,0:T(8,128)S(1)}, f32[256,128]{1,0:T(8,128)S(1)}, u32[]{:S(2)}, u32[]{:S(2)}) collective-permute-start(f32[256,128]{1,0:T(8,128)S(1)} %get-tuple-element.7), channel_id=1, source_target_pairs={{0,2},{1,3},{2,0},{3,1},{4,6},{5,7},{6,4},{7,5},{8,10},{9,11},{10,... | collective-permute-start | bytes 393224 | tf_op jit(solution)/shard_map/ppermute | solution.py:79
  138.3 4.2 %collective-permute-done.19 = f32[256,128]{1,0:T(8,128)S(1)} collective-permute-done((f32[256,128]{1,0:T(8,128)S(1)}, f32[256,128]{1,0:T(8,128)S(1)}, u32[]{:S(2)}, u32[]{:S(2)}) %collective-permute-start.19) | collective-permute-done | bytes 131104 | tf_op jit(solution)/shard_map/ppermute | solution.py:79
  143.4 9.8 %custom-call.6 = f32[1,128,128]{1,2,0:T(8,128)S(1)} custom-call(f32[1,128,128]{2,1,0:T(8,128)S(1)} %fusion.8), custom_call_target="InvertDiagBlocksLowerTriangular" | custom-call | tf_op jit(solution)/shard_map/jit(_solve_triangular)/triangular_solve | solution.py:95
  154.6 1.9 %collective-permute-start.22 = (f32[128,128]{0,1:T(8,128)S(1)}, f32[128,128]{0,1:T(8,128)S(1)}, u32[]{:S(2)}, u32[]{:S(2)}) collective-permute-start(f32[128,128]{0,1:T(8,128)S(1)} %fusion.20), channel_id=1, source_target_pairs={{0,8},{4,12},{8,0},{12,4},{1,9},{5,13},{9,1},{13,5},{2,10},{6,14},... | collective-permute-start | bytes 196616 | tf_op jit(solution)/shard_map/ppermute | solution.py:44
  156.6 2.6 %collective-permute-done.22 = f32[128,128]{0,1:T(8,128)S(1)} collective-permute-done((f32[128,128]{0,1:T(8,128)S(1)}, f32[128,128]{0,1:T(8,128)S(1)}, u32[]{:S(2)}, u32[]{:S(2)}) %collective-permute-start.22) | collective-permute-done | bytes 65568 | tf_op jit(solution)/shard_map/ppermute | solution.py:44
  159.3 1.4 collective-permute-done.23
  160.8 11.7 %cholesky.55 = f32[128,128]{1,0:T(8,128)S(1)} custom-call(f32[128,128]{1,0:T(8,128)S(1)} %fusion.12), custom_call_target="Cholesky" | custom-call | tf_op jit(solution)/shard_map/jit(cholesky)/cholesky | solution.py:91
  173.8 9.9 %custom-call.7 = f32[1,128,128]{1,2,0:T(8,128)S(1)} custom-call(f32[1,128,128]{2,1,0:T(8,128)S(1)} %fusion.9), custom_call_target="InvertDiagBlocksLowerTriangular" | custom-call | tf_op jit(solution)/shard_map/jit(_solve_triangular)/triangular_solve | solution.py:95
  184.4 0.8 copy.21
  (74 shorter events, 11.8 us)
Async XLA Ops:
  0.6 9.4 %copy-start = (bf16[8,1024,128]{2,1,0:T(8,128)(2,1)S(1)}, bf16[8,1024,128]{2,1,0:T(8,128)(2,1)}, u32[]{:S(2)}) copy-start(bf16[8,1024,128]{2,1,0:T(8,128)(2,1)} %param.9) | copy-start | bytes 6291460
  0.6 9.4 %copy-start.2 = (bf16[1024,8,16]{0,2,1:T(8,128)(2,1)S(1)}, bf16[1024,8,16]{0,2,1:T(8,128)(2,1)}, u32[]{:S(2)}) copy-start(bf16[1024,8,16]{0,2,1:T(8,128)(2,1)} %param.7) | copy-start | bytes 786436
  2.9 3.2 %collective-permute-start = (f32[8,128,16]{1,2,0:T(8,128)S(1)}, f32[8,128,16]{1,2,0:T(8,128)S(1)}, u32[]{:S(2)}, u32[]{:S(2)}) collective-permute-start(f32[8,128,16]{1,2,0:T(8,128)S(1)} %fusion.21), channel_id=1, source_target_pairs={{0,4},{4,0},{8,12},{12,8},{1,5},{5,1},{9,13},{13,9},{2,6},{6,2},{1... | collective-permute-start | bytes 196616 | tf_op jit(solution)/shard_map/ppermute | solution.py:44
  3.4 5.2 %collective-permute-start.1 = (f32[8,128,16]{1,2,0:T(8,128)S(1)}, f32[8,128,16]{1,2,0:T(8,128)S(1)}, u32[]{:S(2)}, u32[]{:S(2)}) collective-permute-start(f32[8,128,16]{1,2,0:T(8,128)S(1)} %fusion.21), channel_id=1, source_target_pairs={{0,8},{4,12},{8,0},{12,4},{1,9},{5,13},{9,1},{13,5},{2,10},{6,14},... | collective-permute-start | bytes 196616 | tf_op jit(solution)/shard_map/ppermute | solution.py:44
  6.0 4.1 %collective-permute-start.2 = (f32[8,128,16]{1,2,0:T(8,128)S(1)}, f32[8,128,16]{1,2,0:T(8,128)S(1)}, u32[]{:S(2)}, u32[]{:S(2)}) collective-permute-start(f32[8,128,16]{1,2,0:T(8,128)S(1)} %fusion.21), channel_id=1, source_target_pairs={{0,12},{4,8},{8,4},{12,0},{1,13},{5,9},{9,5},{13,1},{2,14},{6,10},... | collective-permute-start | bytes 196616 | tf_op jit(solution)/shard_map/ppermute | solution.py:44
  10.7 21.4 %collective-permute-start.7 = (bf16[1,1024,128]{1,2,0:T(8,128)(2,1)S(1)}, bf16[1,1024,128]{1,2,0:T(8,128)(2,1)S(1)}, u32[]{:S(2)}, u32[]{:S(2)}) collective-permute-start(bf16[1,1024,128]{1,2,0:T(8,128)(2,1)S(1)} %bitcast.81), channel_id=1, source_target_pairs={{0,2},{1,3},{2,0},{3,1},{4,6},{5,7},{6,4},{7,5},{8,10},{9,11},{10,... | collective-permute-start | bytes 786440 | tf_op jit(solution)/shard_map/ppermute | solution.py:53
  13.3 18.9 %collective-permute-start.3 = (bf16[1024,128]{0,1:T(8,128)(2,1)S(1)}, bf16[1024,128]{0,1:T(8,128)(2,1)S(1)}, u32[]{:S(2)}, u32[]{:S(2)}) collective-permute-start(bf16[1024,128]{0,1:T(8,128)(2,1)S(1)} %bitcast.82), channel_id=1, source_target_pairs={{1,4},{2,8},{3,12},{4,1},{6,9},{7,13},{8,2},{9,6},{11,14},{12,3},{... | collective-permute-start | bytes 786440 | tf_op jit(solution)/shard_map/ppermute | solution.py:119
  32.3 6.8 %collective-permute-start.4 = (bf16[1,1024,128]{1,2,0:T(8,128)(2,1)S(1)}, bf16[1,1024,128]{1,2,0:T(8,128)(2,1)S(1)}, u32[]{:S(2)}, u32[]{:S(2)}) collective-permute-start(bf16[1,1024,128]{1,2,0:T(8,128)(2,1)S(1)} %get-tuple-element.10), channel_id=1, source_target_pairs={{0,16},{16,0},{1,17},{17,1},{2,18},{18,2},{3,19},{19,3},{4,20},{20... | collective-permute-start | bytes 786440 | tf_op jit(solution)/shard_map/ppermute | solution.py:53
  34.6 13.4 %collective-permute-start.8 = (bf16[2,1024,128]{2,1,0:T(8,128)(2,1)}, bf16[2,1024,128]{2,1,0:T(8,128)(2,1)}, u32[]{:S(2)}, u32[]{:S(2)}) collective-permute-start(bf16[2,1024,128]{2,1,0:T(8,128)(2,1)} %bitcast.17), channel_id=1, source_target_pairs={{0,1},{1,0},{2,3},{3,2},{4,5},{5,4},{6,7},{7,6},{8,9},{9,8},{10,11... | collective-permute-start | bytes 1572872 | tf_op jit(solution)/shard_map/ppermute | solution.py:53
  40.0 15.9 %collective-permute-start.5 = (bf16[2,1024,128]{2,1,0:T(8,128)(2,1)}, bf16[2,1024,128]{2,1,0:T(8,128)(2,1)S(1)}, u32[]{:S(2)}, u32[]{:S(2)}) collective-permute-start(bf16[2,1024,128]{2,1,0:T(8,128)(2,1)} %bitcast.7), channel_id=1, source_target_pairs={{0,8},{4,12},{8,0},{12,4},{1,9},{5,13},{9,1},{13,5},{2,10},{6,14},... | collective-permute-start | bytes 1572872 | tf_op jit(solution)/shard_map/ppermute | solution.py:53
  49.1 23.6 %collective-permute-start.9 = (bf16[4,1024,128]{2,1,0:T(8,128)(2,1)S(1)}, bf16[4,1024,128]{2,1,0:T(8,128)(2,1)}, u32[]{:S(2)}, u32[]{:S(2)}) collective-permute-start(bf16[4,1024,128]{2,1,0:T(8,128)(2,1)S(1)} %bitcast.79), channel_id=1, source_target_pairs={{0,16},{16,0},{1,17},{17,1},{2,18},{18,2},{3,19},{19,3},{4,20},{20... | collective-permute-start | bytes 3145736 | tf_op jit(solution)/shard_map/ppermute | solution.py:53
  56.7 17.4 %collective-permute-start.6 = (bf16[4,1024,128]{2,1,0:T(8,128)(2,1)}, bf16[4,1024,128]{2,1,0:T(8,128)(2,1)}, u32[]{:S(2)}, u32[]{:S(2)}) collective-permute-start(bf16[4,1024,128]{2,1,0:T(8,128)(2,1)} %bitcast.10), channel_id=1, source_target_pairs={{0,4},{4,0},{8,12},{12,8},{1,5},{5,1},{9,13},{13,9},{2,6},{6,2},{1... | collective-permute-start | bytes 3145736 | tf_op jit(solution)/shard_map/ppermute | solution.py:53
  77.8 4.9 %copy-start.1 = (f32[1024,1024]{1,0:T(8,128)}, f32[1024,1024]{1,0:T(8,128)S(1)}, u32[]{:S(2)}) copy-start(f32[1024,1024]{1,0:T(8,128)S(1)} %bitcast_multiply_fusion) | copy-start | bytes 12582916
  82.8 1.6 collective-permute-start.10
  84.5 9.2 %collective-permute-start.11 = (f32[256,128]{1,0:T(8,128)S(1)}, f32[256,128]{1,0:T(8,128)S(1)}, u32[]{:S(2)}, u32[]{:S(2)}) collective-permute-start(f32[256,128]{1,0:T(8,128)S(1)} %slice_select_fusion.3), channel_id=1, source_target_pairs={{0,8},{4,12},{8,0},{12,4},{1,9},{5,13},{9,1},{13,5},{2,10},{6,14},... | collective-permute-start | bytes 393224 | tf_op jit(solution)/shard_map/ppermute | solution.py:76
  93.7 5.0 %collective-permute-start.12 = (f32[256,128]{1,0:T(8,128)S(1)}, f32[256,128]{1,0:T(8,128)S(1)}, u32[]{:S(2)}, u32[]{:S(2)}) collective-permute-start(f32[256,128]{1,0:T(8,128)S(1)} %get-tuple-element.9), channel_id=1, source_target_pairs={{0,8},{4,12},{8,0},{12,4},{1,9},{5,13},{9,1},{13,5},{2,10},{6,14},... | collective-permute-start | bytes 393224 | tf_op jit(solution)/shard_map/ppermute | solution.py:79
  98.7 1.6 collective-permute-start.13
  101.4 14.6 %collective-permute-start.14 = (f32[128,128]{0,1:T(8,128)S(1)}, f32[128,128]{0,1:T(8,128)S(1)}, u32[]{:S(2)}, u32[]{:S(2)}) collective-permute-start(f32[128,128]{0,1:T(8,128)S(1)} %fusion.18), channel_id=1, source_target_pairs={{0,1},{1,0},{2,3},{3,2},{4,5},{5,4},{6,7},{7,6},{8,9},{9,8},{10,11... | collective-permute-start | bytes 196616 | tf_op jit(solution)/shard_map/ppermute | solution.py:44
  103.9 12.1 %collective-permute-start.15 = (f32[128,128]{0,1:T(8,128)S(1)}, f32[128,128]{0,1:T(8,128)S(1)}, u32[]{:S(2)}, u32[]{:S(2)}) collective-permute-start(f32[128,128]{0,1:T(8,128)S(1)} %fusion.18), channel_id=1, source_target_pairs={{0,2},{1,3},{2,0},{3,1},{4,6},{5,7},{6,4},{7,5},{8,10},{9,11},{10,... | collective-permute-start | bytes 196616 | tf_op jit(solution)/shard_map/ppermute | solution.py:44
  103.9 12.1 %collective-permute-start.16 = (f32[128,128]{0,1:T(8,128)S(1)}, f32[128,128]{0,1:T(8,128)S(1)}, u32[]{:S(2)}, u32[]{:S(2)}) collective-permute-start(f32[128,128]{0,1:T(8,128)S(1)} %fusion.18), channel_id=1, source_target_pairs={{0,3},{1,2},{2,1},{3,0},{4,7},{5,6},{6,5},{7,4},{8,11},{9,10},{10,... | collective-permute-start | bytes 196616 | tf_op jit(solution)/shard_map/ppermute | solution.py:44
  114.9 7.9 %collective-permute-start.17 = (f32[512,128]{1,0:T(8,128)S(1)}, f32[512,128]{1,0:T(8,128)S(1)}, u32[]{:S(2)}, u32[]{:S(2)}) collective-permute-start(f32[512,128]{1,0:T(8,128)S(1)} %slice_select_fusion), channel_id=1, source_target_pairs={{0,1},{1,0},{2,3},{3,2},{4,5},{5,4},{6,7},{7,6},{8,9},{9,8},{10,11... | collective-permute-start | bytes 786440 | tf_op jit(solution)/shard_map/ppermute | solution.py:76
  122.8 12.3 %collective-permute-start.18 = (f32[256,128]{1,0:T(8,128)S(1)}, f32[256,128]{1,0:T(8,128)S(1)}, u32[]{:S(2)}, u32[]{:S(2)}) collective-permute-start(f32[256,128]{1,0:T(8,128)S(1)} %slice_select_fusion.2), channel_id=1, source_target_pairs={{0,2},{1,3},{2,0},{3,1},{4,6},{5,7},{6,4},{7,5},{8,10},{9,11},{10,... | collective-permute-start | bytes 393224 | tf_op jit(solution)/shard_map/ppermute | solution.py:76
  135.2 7.4 %collective-permute-start.19 = (f32[256,128]{1,0:T(8,128)S(1)}, f32[256,128]{1,0:T(8,128)S(1)}, u32[]{:S(2)}, u32[]{:S(2)}) collective-permute-start(f32[256,128]{1,0:T(8,128)S(1)} %get-tuple-element.7), channel_id=1, source_target_pairs={{0,2},{1,3},{2,0},{3,1},{4,6},{5,7},{6,4},{7,5},{8,10},{9,11},{10,... | collective-permute-start | bytes 393224 | tf_op jit(solution)/shard_map/ppermute | solution.py:79
  142.6 10.7 %collective-permute-start.20 = (f32[512,128]{1,0:T(8,128)S(1)}, f32[512,128]{1,0:T(8,128)S(1)}, u32[]{:S(2)}, u32[]{:S(2)}) collective-permute-start(f32[512,128]{1,0:T(8,128)S(1)} %constant_dynamic-update-slice_fusion.2), channel_id=1, source_target_pairs={{0,1},{1,0},{2,3},{3,2},{4,5},{5,4},{6,7},{7,6},{8,9},{9,8},{10,11... | collective-permute-start | bytes 786440 | tf_op jit(solution)/shard_map/ppermute | solution.py:79
  154.6 2.1 %collective-permute-start.21 = (f32[128,128]{0,1:T(8,128)S(1)}, f32[128,128]{0,1:T(8,128)S(1)}, u32[]{:S(2)}, u32[]{:S(2)}) collective-permute-start(f32[128,128]{0,1:T(8,128)S(1)} %fusion.20), channel_id=1, source_target_pairs={{0,4},{4,0},{8,12},{12,8},{1,5},{5,1},{9,13},{13,9},{2,6},{6,2},{1... | collective-permute-start | bytes 196616 | tf_op jit(solution)/shard_map/ppermute | solution.py:44
  154.6 4.6 %collective-permute-start.22 = (f32[128,128]{0,1:T(8,128)S(1)}, f32[128,128]{0,1:T(8,128)S(1)}, u32[]{:S(2)}, u32[]{:S(2)}) collective-permute-start(f32[128,128]{0,1:T(8,128)S(1)} %fusion.20), channel_id=1, source_target_pairs={{0,8},{4,12},{8,0},{12,4},{1,9},{5,13},{9,1},{13,5},{2,10},{6,14},... | collective-permute-start | bytes 196616 | tf_op jit(solution)/shard_map/ppermute | solution.py:44
  156.6 4.1 %collective-permute-start.23 = (f32[128,128]{0,1:T(8,128)S(1)}, f32[128,128]{0,1:T(8,128)S(1)}, u32[]{:S(2)}, u32[]{:S(2)}) collective-permute-start(f32[128,128]{0,1:T(8,128)S(1)} %fusion.20), channel_id=1, source_target_pairs={{0,12},{4,8},{8,4},{12,0},{1,13},{5,9},{9,5},{13,1},{2,14},{6,10},... | collective-permute-start | bytes 196616 | tf_op jit(solution)/shard_map/ppermute | solution.py:44

commit v11 on v10

--- a/solution.py
+++ b/solution.py
@@ -124,7 +124,16 @@
         right_plan += [("bin", step, len(group) + k) for k, step in enumerate(bins)]
         left_plan = [("bin", step, len(group) + k) for k, step in enumerate(bins)]
         left_plan += [("row", step, k) for k, step in enumerate(group)]
-        right_rows = _butterfly_gather(local_rows, right_plan)
+        half = rows_here // 2
+        early_bin = [step for step in right_plan if step[0] == "bin"]
+        early_bin += [step for step in right_plan if step[0] != "bin"]
+        right_rows = jnp.concatenate(
+            [
+                _butterfly_gather(local_rows[:half], right_plan),
+                _butterfly_gather(local_rows[half:], early_bin),
+            ],
+            1,
+        )
         left_rows = _butterfly_gather(swapped, left_plan)
     else:
         right_rows = lax.all_gather(local_rows, ("bin", "col"), axis=0, tiled=False)
@@ -140,7 +149,7 @@
                 covariance, block, precision=lax.Precision.HIGHEST,
                 preferred_element_type=jnp.float32,
             )
-            return _halving_sum(partial_image, "row")
+            return _butterfly_sum(partial_image, "row")
         partial_image = lax.dot_general(
             covariance, block, (((0,), (0,)), ((), ())),
             precision=lax.Precision.HIGHEST, preferred_element_type=jnp.float32,

time: 186 us -> 177 us (0.952)
  waiting for transfers between devices: 65.3 us -> 42 us
  starting transfers between devices: 33.6 us -> 47.5 us
    ppermute x6 -> x9, waiting for transfers between devices: 36.4 us -> 7.61 us  [_butterfly_gather(): other = lax.ppermute(x, axis, [(i, i ^ step) for i in range(count)])]
    ppermute x6 -> x9, starting transfers between devices: 11.2 us -> 32.2 us  [_butterfly_gather(): other = lax.ppermute(x, axis, [(i, i ^ step) for i in range(count)])]
    ppermute x0 -> x2, waiting for transfers between devices: none -> 15.6 us  [_butterfly_sum(): x = x + lax.ppermute(x, axis, [(i, i ^ step) for i in range(count)])]
    ppermute x4 -> x2, starting transfers between devices: 7.11 us -> 0.77 us  [_halving_sum(): x = keep + lax.ppermute(give, axis, [(i, i ^ step) for i in range(count)])]
    ppermute x4 -> x2, waiting for transfers between devices: 11.9 us -> 6.48 us  [_halving_sum(): x = keep + lax.ppermute(give, axis, [(i, i ^ step) for i in range(count)])]
    ppermute x4 -> x2, waiting for transfers between devices: 8.92 us -> 4.06 us  [_halving_sum(): other = lax.ppermute(x, axis, [(i, i ^ step) for i in range(count)])]
    ppermute x4 -> x2, starting transfers between devices: 4.51 us -> 3.49 us  [_halving_sum(): other = lax.ppermute(x, axis, [(i, i ^ step) for i in range(count)])]
    dynamic_update_slice x6 -> x9, local copies, waits for them, and re-layouts: 6.11 us -> 6.81 us  [_butterfly_gather(): both = lax.dynamic_update_slice_in_dim(both, theirs, 1 - first, 1)]
  transfers between devices with their start and end apart: 24 -> 25, of which waited for: 15 -> 12; matrix products, arithmetic and copies ran while one was open for 25% -> 27% of each run, Pallas kernels for 0% -> 0%
where the time goes in v11:
time: 177 us; the launch traced here: 176 us
  starting transfers between devices  47.5 us (27%)
  other arithmetic  46.7 us (26%)
  waiting for transfers between devices  42 us (24%)
  matrix products  20 us (11%)
  local copies, waits for them, and re-layouts  18.8 us (11%)
    ppermute x9, starting transfers between devices, _butterfly_gather(): other = lax.ppermute(x, axis, [(i, i ^ step) for i in range(count)])  32.2 us
    another operation x6, other arithmetic, _lower_factor(): return jnp.linalg.cholesky(_direct_sum(gram_part, gram_axis))  24.8 us
    another operation x4, other arithmetic, _right_solve(): jax.scipy.linalg.solve_triangular(lower_factor, image.T, lower=True)  20.9 us
    ppermute x2, waiting for transfers between devices, _butterfly_sum(): x = x + lax.ppermute(x, axis, [(i, i ^ step) for i in range(count)])  15.6 us
    ppermute x9, starting transfers between devices, _direct_sum(): lax.ppermute(x, axis, [(i, i ^ k) for i in range(count)])  9.31 us
    ppermute x9, waiting for transfers between devices, _direct_sum(): lax.ppermute(x, axis, [(i, i ^ k) for i in range(count)])  8.3 us
    ppermute x9, waiting for transfers between devices, _butterfly_gather(): other = lax.ppermute(x, axis, [(i, i ^ step) for i in range(count)])  7.61 us
    dot_general x1, matrix products, cov_times(): lax.dot_general(covariance, block, (((0,), (0,)), ((), ())), precision=la...  7.03 us
  transfers between devices with their start and end apart: 25, of which 12 were waited for; matrix products, arithmetic and copies ran while one was open for 27% of the time, Pallas kernels for 0%

profile of v11, /device:TPU:0, one launch (start us, length us, event | category | flops | bytes accessed | tf_op | source)
XLA Modules:
  0.0 176.4 jit_solution(4737946650930755674)
XLA Ops:
  0.7 2.2 %fusion.28 = f32[8,128,16]{1,2,0:T(8,128)S(1)} fusion(bf16[1024,8,16]{0,2,1:T(8,128)(2,1)} %param.7, bf16[8,1024,128]{2,1,0:T(8,128)(2,1)} %param.8), kind=kOutput, calls=%fused_computation.70 | convolution fusion | flops 33554432 | bytes 2424832 | tf_op jit(solution)/shard_map/mbs,bmr->brs/dot_general | solution.py:105
  3.4 2.6 %collective-permute-start.1 = (f32[8,128,16]{1,2,0:T(8,128)S(1)}, f32[8,128,16]{1,2,0:T(8,128)S(1)}, u32[]{:S(2)}, u32[]{:S(2)}) collective-permute-start(f32[8,128,16]{1,2,0:T(8,128)S(1)} %fusion.28), channel_id=1, source_target_pairs={{0,8},{4,12},{8,0},{12,4},{1,9},{5,13},{9,1},{13,5},{2,10},{6,14},... | collective-permute-start | bytes 196616 | tf_op jit(solution)/shard_map/ppermute | solution.py:44
  6.0 2.6 %collective-permute-done.1 = f32[8,128,16]{1,2,0:T(8,128)S(1)} collective-permute-done((f32[8,128,16]{1,2,0:T(8,128)S(1)}, f32[8,128,16]{1,2,0:T(8,128)S(1)}, u32[]{:S(2)}, u32[]{:S(2)}) %collective-permute-start.1) | collective-permute-done | bytes 65568 | tf_op jit(solution)/shard_map/ppermute | solution.py:44
  8.7 1.4 collective-permute-done.2
  10.9 1.6 collective-permute-start.10
  12.4 2.6 %collective-permute-start.7 = (bf16[1,512,128]{1,2,0:T(8,128)(2,1)S(1)}, bf16[1,512,128]{1,2,0:T(8,128)(2,1)S(1)}, u32[]{:S(2)}, u32[]{:S(2)}) collective-permute-start(bf16[1,512,128]{1,2,0:T(8,128)(2,1)S(1)} %bitcast.97), channel_id=1, source_target_pairs={{0,2},{1,3},{2,0},{3,1},{4,6},{5,7},{6,4},{7,5},{8,10},{9,11},{10,... | collective-permute-start | bytes 393224 | tf_op jit(solution)/shard_map/ppermute | solution.py:53
  15.0 1.3 collective-permute-start.3
  16.8 4.2 %collective-permute-start.11 = (bf16[2,512,128]{2,1,0:T(8,128)(2,1)S(1)}, bf16[2,512,128]{2,1,0:T(8,128)(2,1)S(1)}, u32[]{:S(2)}, u32[]{:S(2)}) collective-permute-start(bf16[2,512,128]{2,1,0:T(8,128)(2,1)S(1)} %bitcast.93), channel_id=1, source_target_pairs={{0,2},{1,3},{2,0},{3,1},{4,6},{5,7},{6,4},{7,5},{8,10},{9,11},{10,... | collective-permute-start | bytes 786440 | tf_op jit(solution)/shard_map/ppermute | solution.py:53
  21.7 0.9 broadcast_in_dim.45
  23.3 0.8 fusion.13
  24.6 0.9 broadcast_in_dim.42
  25.4 0.7 bitcast_dynamic-update-slice_fusion.9
  26.2 3.0 %collective-permute-start.8 = (bf16[2,512,128]{2,1,0:T(8,128)(2,1)S(1)}, bf16[2,512,128]{2,1,0:T(8,128)(2,1)}, u32[]{:S(2)}, u32[]{:S(2)}) collective-permute-start(bf16[2,512,128]{2,1,0:T(8,128)(2,1)S(1)} %bitcast.94), channel_id=1, source_target_pairs={{0,1},{1,0},{2,3},{3,2},{4,5},{5,4},{6,7},{7,6},{8,9},{9,8},{10,11... | collective-permute-start | bytes 786440 | tf_op jit(solution)/shard_map/ppermute | solution.py:53
  29.4 0.9 broadcast_in_dim.39
  31.0 1.1 copy.7
  32.1 0.7 constant_dynamic-update-slice_fusion.10
  32.8 17.9 %collective-permute-start.5 = (bf16[2,1024,128]{2,1,0:T(8,128)(2,1)}, bf16[2,1024,128]{2,1,0:T(8,128)(2,1)S(1)}, u32[]{:S(2)}, u32[]{:S(2)}) collective-permute-start(bf16[2,1024,128]{2,1,0:T(8,128)(2,1)} %bitcast.7), channel_id=1, source_target_pairs={{0,8},{4,12},{8,0},{12,4},{1,9},{5,13},{9,1},{13,5},{2,10},{6,14},... | collective-permute-start | bytes 1572872 | tf_op jit(solution)/shard_map/ppermute | solution.py:53
  51.5 1.7 collective-permute-start.12
  53.2 1.7 bitcast_dynamic-update-slice_fusion.8
  55.5 1.1 bitcast_dynamic-update-slice_fusion.1
  56.7 2.9 %collective-permute-done.5 = bf16[2,1024,128]{2,1,0:T(8,128)(2,1)S(1)} collective-permute-done((bf16[2,1024,128]{2,1,0:T(8,128)(2,1)}, bf16[2,1024,128]{2,1,0:T(8,128)(2,1)S(1)}, u32[]{:S(2)}, u32[]{:S(2)}) %collective-permute-start.5) | collective-permute-done | bytes 524320 | tf_op jit(solution)/shard_map/ppermute | solution.py:53
  59.9 1.1 bitcast_dynamic-update-slice_fusion.4
  61.1 1.1 bitcast_dynamic-update-slice_fusion.2
  62.2 2.2 %collective-permute-done.12 = bf16[4,512,128]{2,1,0:T(8,128)(2,1)} collective-permute-done((bf16[4,512,128]{2,1,0:T(8,128)(2,1)}, bf16[4,512,128]{2,1,0:T(8,128)(2,1)}, u32[]{:S(2)}, u32[]{:S(2)}) %collective-permute-start.12) | collective-permute-done | bytes 524320 | tf_op jit(solution)/shard_map/ppermute | solution.py:53
  64.4 1.1 constant_dynamic-update-slice_fusion.4
  65.6 2.0 %collective-permute-done.9 = bf16[4,512,128]{2,1,0:T(8,128)(2,1)} collective-permute-done((bf16[4,512,128]{2,1,0:T(8,128)(2,1)}, bf16[4,512,128]{2,1,0:T(8,128)(2,1)}, u32[]{:S(2)}, u32[]{:S(2)}) %collective-permute-start.9) | collective-permute-done | bytes 524320 | tf_op jit(solution)/shard_map/ppermute | solution.py:53
  67.6 1.1 bitcast_dynamic-update-slice_fusion.3
  69.1 1.4 constant_dynamic-update-slice_fusion.9
  70.5 2.4 %bitcast_multiply_fusion = f32[1024,1024]{1,0:T(8,128)S(1)} fusion(bf16[8,1024,128]{2,1,0:T(8,128)(2,1)S(1)} %bitcast.92, bf16[8,512,128]{2,1,0:T(8,128)(2,1)S(1)} %bitcast.96, bf16[8,512,128]{2,1,0:T(8,128)(2,1)S(1)} %bitcast.95), kind=kOutput, calls=%fused_computation | convolution fusion | flops 2152726528 | bytes 8388608 | tf_op jit(solution)/shard_map/dot_general | solution.py:142
  72.9 4.9 %fusion.7 = f32[1024,128]{1,0:T(8,128)S(1)} fusion(f32[1024,1024]{1,0:T(8,128)S(1)} %bitcast_multiply_fusion, f32[4096,128]{1,0:T(8,128)} %param.10, s32[]{:T(128)S(6)} %select_n.115), kind=kOutput, calls=%fused_computation.15 | convolution fusion | flops 1610612736 | bytes 5242884 | tf_op jit(solution)/shard_map/dot_general | solution.py:148
  77.8 1.9 %collective-permute-done.13 = f32[1024,128]{1,0:T(8,128)S(1)} collective-permute-done((f32[1024,128]{1,0:T(8,128)S(1)}, f32[1024,128]{1,0:T(8,128)S(1)}, u32[]{:S(2)}, u32[]{:S(2)}) %collective-permute-start.13) | collective-permute-done | bytes 524320 | tf_op jit(solution)/shard_map/ppermute | solution.py:26
  80.1 13.7 %collective-permute-done.14 = f32[1024,128]{1,0:T(8,128)S(1)} collective-permute-done((f32[1024,128]{1,0:T(8,128)S(1)}, f32[1024,128]{1,0:T(8,128)S(1)}, u32[]{:S(2)}, u32[]{:S(2)}) %collective-permute-start.14) | collective-permute-done | bytes 524320 | tf_op jit(solution)/shard_map/ppermute | solution.py:26
  93.8 1.0 fusion.11
  95.4 1.6 collective-permute-start.16
  97.0 2.3 %collective-permute-start.17 = (f32[128,128]{0,1:T(8,128)S(1)}, f32[128,128]{0,1:T(8,128)S(1)}, u32[]{:S(2)}, u32[]{:S(2)}) collective-permute-start(f32[128,128]{0,1:T(8,128)S(1)} %fusion.11), channel_id=1, source_target_pairs={{0,3},{1,2},{2,1},{3,0},{4,7},{5,6},{6,5},{7,4},{8,11},{9,10},{10,... | collective-permute-start | bytes 196616 | tf_op jit(solution)/shard_map/ppermute | solution.py:44
  99.3 7.0 %fusion.9 = f32[1024,128]{1,0:T(8,128)S(1)} fusion(f32[1024,1024]{1,0:T(8,128)S(1)} %bitcast_multiply_fusion, f32[1024,128]{1,0:T(8,128)S(1)} %add.110, f32[1024,128]{1,0:T(8,128)S(1)} %collective-permute-done.14), kind=kOutput, calls=%fused_computation.24 | convolution fusion | flops 1610743808 | bytes 5767168 | tf_op jit(solution)/shard_map/dot_general | solution.py:153
  106.6 6.5 %collective-permute-done.18 = f32[512,128]{1,0:T(8,128)S(1)} collective-permute-done((f32[512,128]{1,0:T(8,128)S(1)}, f32[512,128]{1,0:T(8,128)S(1)}, u32[]{:S(2)}, u32[]{:S(2)}) %collective-permute-start.18) | collective-permute-done | bytes 262176 | tf_op jit(solution)/shard_map/ppermute | solution.py:76
  113.9 11.7 %cholesky.44 = f32[128,128]{1,0:T(8,128)S(1)} custom-call(f32[128,128]{1,0:T(8,128)S(1)} %fusion.21), custom_call_target="Cholesky" | custom-call | tf_op jit(solution)/shard_map/jit(cholesky)/cholesky | solution.py:91
  125.7 2.4 %collective-permute-start.20 = (f32[256,128]{1,0:T(8,128)S(1)}, f32[256,128]{1,0:T(8,128)S(1)}, u32[]{:S(2)}, u32[]{:S(2)}) collective-permute-start(f32[256,128]{1,0:T(8,128)S(1)} %get-tuple-element.7), channel_id=1, source_target_pairs={{0,2},{1,3},{2,0},{3,1},{4,6},{5,7},{6,4},{7,5},{8,10},{9,11},{10,... | collective-permute-start | bytes 393224 | tf_op jit(solution)/shard_map/ppermute | solution.py:79
  128.7 4.1 %collective-permute-done.20 = f32[256,128]{1,0:T(8,128)S(1)} collective-permute-done((f32[256,128]{1,0:T(8,128)S(1)}, f32[256,128]{1,0:T(8,128)S(1)}, u32[]{:S(2)}, u32[]{:S(2)}) %collective-permute-start.20) | collective-permute-done | bytes 131104 | tf_op jit(solution)/shard_map/ppermute | solution.py:79
  132.8 1.1 collective-permute-start.21
  134.6 9.8 %custom-call.6 = f32[1,128,128]{1,2,0:T(8,128)S(1)} custom-call(f32[1,128,128]{2,1,0:T(8,128)S(1)} %fusion.15), custom_call_target="InvertDiagBlocksLowerTriangular" | custom-call | tf_op jit(solution)/shard_map/jit(_solve_triangular)/triangular_solve | solution.py:95
  146.0 1.6 collective-permute-start.23
  147.7 2.7 %collective-permute-done.23 = f32[128,128]{0,1:T(8,128)S(1)} collective-permute-done((f32[128,128]{0,1:T(8,128)S(1)}, f32[128,128]{0,1:T(8,128)S(1)}, u32[]{:S(2)}, u32[]{:S(2)}) %collective-permute-start.23) | collective-permute-done | bytes 65568 | tf_op jit(solution)/shard_map/ppermute | solution.py:44
  150.4 1.6 collective-permute-done.24
  152.1 11.7 %cholesky.55 = f32[128,128]{1,0:T(8,128)S(1)} custom-call(f32[128,128]{1,0:T(8,128)S(1)} %fusion.19), custom_call_target="Cholesky" | custom-call | tf_op jit(solution)/shard_map/jit(cholesky)/cholesky | solution.py:91
  165.1 9.8 %custom-call.7 = f32[1,128,128]{1,2,0:T(8,128)S(1)} custom-call(f32[1,128,128]{2,1,0:T(8,128)S(1)} %fusion.16), custom_call_target="InvertDiagBlocksLowerTriangular" | custom-call | tf_op jit(solution)/shard_map/jit(_solve_triangular)/triangular_solve | solution.py:95
  175.6 0.8 copy.24
  (80 shorter events, 13.7 us)
Async XLA Ops:
  0.6 9.4 %copy-start = (bf16[8,1024,128]{2,1,0:T(8,128)(2,1)S(1)}, bf16[8,1024,128]{2,1,0:T(8,128)(2,1)}, u32[]{:S(2)}) copy-start(bf16[8,1024,128]{2,1,0:T(8,128)(2,1)} %param.9) | copy-start | bytes 6291460
  0.6 9.4 %copy-start.2 = (bf16[1024,8,16]{0,2,1:T(8,128)(2,1)S(1)}, bf16[1024,8,16]{0,2,1:T(8,128)(2,1)}, u32[]{:S(2)}) copy-start(bf16[1024,8,16]{0,2,1:T(8,128)(2,1)} %param.7) | copy-start | bytes 786436
  2.9 3.2 %collective-permute-start = (f32[8,128,16]{1,2,0:T(8,128)S(1)}, f32[8,128,16]{1,2,0:T(8,128)S(1)}, u32[]{:S(2)}, u32[]{:S(2)}) collective-permute-start(f32[8,128,16]{1,2,0:T(8,128)S(1)} %fusion.28), channel_id=1, source_target_pairs={{0,4},{4,0},{8,12},{12,8},{1,5},{5,1},{9,13},{13,9},{2,6},{6,2},{1... | collective-permute-start | bytes 196616 | tf_op jit(solution)/shard_map/ppermute | solution.py:44
  3.4 5.2 %collective-permute-start.1 = (f32[8,128,16]{1,2,0:T(8,128)S(1)}, f32[8,128,16]{1,2,0:T(8,128)S(1)}, u32[]{:S(2)}, u32[]{:S(2)}) collective-permute-start(f32[8,128,16]{1,2,0:T(8,128)S(1)} %fusion.28), channel_id=1, source_target_pairs={{0,8},{4,12},{8,0},{12,4},{1,9},{5,13},{9,1},{13,5},{2,10},{6,14},... | collective-permute-start | bytes 196616 | tf_op jit(solution)/shard_map/ppermute | solution.py:44
  6.0 4.1 %collective-permute-start.2 = (f32[8,128,16]{1,2,0:T(8,128)S(1)}, f32[8,128,16]{1,2,0:T(8,128)S(1)}, u32[]{:S(2)}, u32[]{:S(2)}) collective-permute-start(f32[8,128,16]{1,2,0:T(8,128)S(1)} %fusion.28), channel_id=1, source_target_pairs={{0,12},{4,8},{8,4},{12,0},{1,13},{5,9},{9,5},{13,1},{2,14},{6,10},... | collective-permute-start | bytes 196616 | tf_op jit(solution)/shard_map/ppermute | solution.py:44
  10.9 5.8 %collective-permute-start.10 = (bf16[1,512,128]{1,2,0:T(8,128)(2,1)S(1)}, bf16[1,512,128]{1,2,0:T(8,128)(2,1)S(1)}, u32[]{:S(2)}, u32[]{:S(2)}) collective-permute-start(bf16[1,512,128]{1,2,0:T(8,128)(2,1)S(1)} %bitcast.100), channel_id=1, source_target_pairs={{0,16},{16,0},{1,17},{17,1},{2,18},{18,2},{3,19},{19,3},{4,20},{20... | collective-permute-start | bytes 393224 | tf_op jit(solution)/shard_map/ppermute | solution.py:53
  12.4 9.1 %collective-permute-start.7 = (bf16[1,512,128]{1,2,0:T(8,128)(2,1)S(1)}, bf16[1,512,128]{1,2,0:T(8,128)(2,1)S(1)}, u32[]{:S(2)}, u32[]{:S(2)}) collective-permute-start(bf16[1,512,128]{1,2,0:T(8,128)(2,1)S(1)} %bitcast.97), channel_id=1, source_target_pairs={{0,2},{1,3},{2,0},{3,1},{4,6},{5,7},{6,4},{7,5},{8,10},{9,11},{10,... | collective-permute-start | bytes 393224 | tf_op jit(solution)/shard_map/ppermute | solution.py:53
  15.0 8.2 %collective-permute-start.3 = (bf16[1024,128]{0,1:T(8,128)(2,1)S(1)}, bf16[1024,128]{0,1:T(8,128)(2,1)}, u32[]{:S(2)}, u32[]{:S(2)}) collective-permute-start(bf16[1024,128]{0,1:T(8,128)(2,1)S(1)} %bitcast.91), channel_id=1, source_target_pairs={{1,4},{2,8},{3,12},{4,1},{6,9},{7,13},{8,2},{9,6},{11,14},{12,3},{... | collective-permute-start | bytes 786440 | tf_op jit(solution)/shard_map/ppermute | solution.py:119
  16.8 33.9 %collective-permute-start.11 = (bf16[2,512,128]{2,1,0:T(8,128)(2,1)S(1)}, bf16[2,512,128]{2,1,0:T(8,128)(2,1)S(1)}, u32[]{:S(2)}, u32[]{:S(2)}) collective-permute-start(bf16[2,512,128]{2,1,0:T(8,128)(2,1)S(1)} %bitcast.93), channel_id=1, source_target_pairs={{0,2},{1,3},{2,0},{3,1},{4,6},{5,7},{6,4},{7,5},{8,10},{9,11},{10,... | collective-permute-start | bytes 786440 | tf_op jit(solution)/shard_map/ppermute | solution.py:53
  24.1 6.9 %collective-permute-start.4 = (bf16[1,1024,128]{1,2,0:T(8,128)(2,1)}, bf16[1,1024,128]{1,2,0:T(8,128)(2,1)}, u32[]{:S(2)}, u32[]{:S(2)}) collective-permute-start(bf16[1,1024,128]{1,2,0:T(8,128)(2,1)} %get-tuple-element.8), channel_id=1, source_target_pairs={{0,16},{16,0},{1,17},{17,1},{2,18},{18,2},{3,19},{19,3},{4,20},{20... | collective-permute-start | bytes 786440 | tf_op jit(solution)/shard_map/ppermute | solution.py:53
  26.2 27.1 %collective-permute-start.8 = (bf16[2,512,128]{2,1,0:T(8,128)(2,1)S(1)}, bf16[2,512,128]{2,1,0:T(8,128)(2,1)}, u32[]{:S(2)}, u32[]{:S(2)}) collective-permute-start(bf16[2,512,128]{2,1,0:T(8,128)(2,1)S(1)} %bitcast.94), channel_id=1, source_target_pairs={{0,1},{1,0},{2,3},{3,2},{4,5},{5,4},{6,7},{7,6},{8,9},{9,8},{10,11... | collective-permute-start | bytes 786440 | tf_op jit(solution)/shard_map/ppermute | solution.py:53
  32.8 26.7 %collective-permute-start.5 = (bf16[2,1024,128]{2,1,0:T(8,128)(2,1)}, bf16[2,1024,128]{2,1,0:T(8,128)(2,1)S(1)}, u32[]{:S(2)}, u32[]{:S(2)}) collective-permute-start(bf16[2,1024,128]{2,1,0:T(8,128)(2,1)} %bitcast.7), channel_id=1, source_target_pairs={{0,8},{4,12},{8,0},{12,4},{1,9},{5,13},{9,1},{13,5},{2,10},{6,14},... | collective-permute-start | bytes 1572872 | tf_op jit(solution)/shard_map/ppermute | solution.py:53
  51.5 13.0 %collective-permute-start.12 = (bf16[4,512,128]{2,1,0:T(8,128)(2,1)}, bf16[4,512,128]{2,1,0:T(8,128)(2,1)}, u32[]{:S(2)}, u32[]{:S(2)}) collective-permute-start(bf16[4,512,128]{2,1,0:T(8,128)(2,1)} %bitcast.31), channel_id=1, source_target_pairs={{0,1},{1,0},{2,3},{3,2},{4,5},{5,4},{6,7},{7,6},{8,9},{9,8},{10,11... | collective-permute-start | bytes 1572872 | tf_op jit(solution)/shard_map/ppermute | solution.py:53
  54.9 12.7 %collective-permute-start.9 = (bf16[4,512,128]{2,1,0:T(8,128)(2,1)}, bf16[4,512,128]{2,1,0:T(8,128)(2,1)}, u32[]{:S(2)}, u32[]{:S(2)}) collective-permute-start(bf16[4,512,128]{2,1,0:T(8,128)(2,1)} %bitcast.20), channel_id=1, source_target_pairs={{0,16},{16,0},{1,17},{17,1},{2,18},{18,2},{3,19},{19,3},{4,20},{20... | collective-permute-start | bytes 1572872 | tf_op jit(solution)/shard_map/ppermute | solution.py:53
  59.6 9.5 %collective-permute-start.6 = (bf16[4,1024,128]{2,1,0:T(8,128)(2,1)S(1)}, bf16[4,1024,128]{2,1,0:T(8,128)(2,1)}, u32[]{:S(2)}, u32[]{:S(2)}) collective-permute-start(bf16[4,1024,128]{2,1,0:T(8,128)(2,1)S(1)} %bitcast.90), channel_id=1, source_target_pairs={{0,4},{4,0},{8,12},{12,8},{1,5},{5,1},{9,13},{13,9},{2,6},{6,2},{1... | collective-permute-start | bytes 3145736 | tf_op jit(solution)/shard_map/ppermute | solution.py:53
  72.9 26.4 %copy-start.1 = (f32[1024,1024]{1,0:T(8,128)}, f32[1024,1024]{1,0:T(8,128)S(1)}, u32[]{:S(2)}) copy-start(f32[1024,1024]{1,0:T(8,128)S(1)} %bitcast_multiply_fusion) | copy-start | bytes 12582916
  77.8 2.0 %collective-permute-start.13 = (f32[1024,128]{1,0:T(8,128)S(1)}, f32[1024,128]{1,0:T(8,128)S(1)}, u32[]{:S(2)}, u32[]{:S(2)}) collective-permute-start(f32[1024,128]{1,0:T(8,128)S(1)} %fusion.7), channel_id=1, source_target_pairs={{0,4},{4,0},{8,12},{12,8},{1,5},{5,1},{9,13},{13,9},{2,6},{6,2},{1... | collective-permute-start | bytes 1572872 | tf_op jit(solution)/shard_map/ppermute | solution.py:26
  79.8 14.0 %collective-permute-start.14 = (f32[1024,128]{1,0:T(8,128)S(1)}, f32[1024,128]{1,0:T(8,128)S(1)}, u32[]{:S(2)}, u32[]{:S(2)}) collective-permute-start(f32[1024,128]{1,0:T(8,128)S(1)} %add.110), channel_id=1, source_target_pairs={{0,8},{4,12},{8,0},{12,4},{1,9},{5,13},{9,1},{13,5},{2,10},{6,14},... | collective-permute-start | bytes 1572872 | tf_op jit(solution)/shard_map/ppermute | solution.py:26
  94.8 11.6 %collective-permute-start.15 = (f32[128,128]{0,1:T(8,128)S(1)}, f32[128,128]{0,1:T(8,128)S(1)}, u32[]{:S(2)}, u32[]{:S(2)}) collective-permute-start(f32[128,128]{0,1:T(8,128)S(1)} %fusion.11), channel_id=1, source_target_pairs={{0,1},{1,0},{2,3},{3,2},{4,5},{5,4},{6,7},{7,6},{8,9},{9,8},{10,11... | collective-permute-start | bytes 196616 | tf_op jit(solution)/shard_map/ppermute | solution.py:44
  95.4 11.1 %collective-permute-start.16 = (f32[128,128]{0,1:T(8,128)S(1)}, f32[128,128]{0,1:T(8,128)S(1)}, u32[]{:S(2)}, u32[]{:S(2)}) collective-permute-start(f32[128,128]{0,1:T(8,128)S(1)} %fusion.11), channel_id=1, source_target_pairs={{0,2},{1,3},{2,0},{3,1},{4,6},{5,7},{6,4},{7,5},{8,10},{9,11},{10,... | collective-permute-start | bytes 196616 | tf_op jit(solution)/shard_map/ppermute | solution.py:44
  97.0 9.5 %collective-permute-start.17 = (f32[128,128]{0,1:T(8,128)S(1)}, f32[128,128]{0,1:T(8,128)S(1)}, u32[]{:S(2)}, u32[]{:S(2)}) collective-permute-start(f32[128,128]{0,1:T(8,128)S(1)} %fusion.11), channel_id=1, source_target_pairs={{0,3},{1,2},{2,1},{3,0},{4,7},{5,6},{6,5},{7,4},{8,11},{9,10},{10,... | collective-permute-start | bytes 196616 | tf_op jit(solution)/shard_map/ppermute | solution.py:44
  106.4 6.7 %collective-permute-start.18 = (f32[512,128]{1,0:T(8,128)S(1)}, f32[512,128]{1,0:T(8,128)S(1)}, u32[]{:S(2)}, u32[]{:S(2)}) collective-permute-start(f32[512,128]{1,0:T(8,128)S(1)} %slice_select_fusion), channel_id=1, source_target_pairs={{0,1},{1,0},{2,3},{3,2},{4,5},{5,4},{6,7},{7,6},{8,9},{9,8},{10,11... | collective-permute-start | bytes 786440 | tf_op jit(solution)/shard_map/ppermute | solution.py:76
  113.2 12.4 %collective-permute-start.19 = (f32[256,128]{1,0:T(8,128)S(1)}, f32[256,128]{1,0:T(8,128)S(1)}, u32[]{:S(2)}, u32[]{:S(2)}) collective-permute-start(f32[256,128]{1,0:T(8,128)S(1)} %slice_select_fusion.1), channel_id=1, source_target_pairs={{0,2},{1,3},{2,0},{3,1},{4,6},{5,7},{6,4},{7,5},{8,10},{9,11},{10,... | collective-permute-start | bytes 393224 | tf_op jit(solution)/shard_map/ppermute | solution.py:76
  125.7 7.1 %collective-permute-start.20 = (f32[256,128]{1,0:T(8,128)S(1)}, f32[256,128]{1,0:T(8,128)S(1)}, u32[]{:S(2)}, u32[]{:S(2)}) collective-permute-start(f32[256,128]{1,0:T(8,128)S(1)} %get-tuple-element.7), channel_id=1, source_target_pairs={{0,2},{1,3},{2,0},{3,1},{4,6},{5,7},{6,4},{7,5},{8,10},{9,11},{10,... | collective-permute-start | bytes 393224 | tf_op jit(solution)/shard_map/ppermute | solution.py:79
  132.8 11.7 %collective-permute-start.21 = (f32[512,128]{1,0:T(8,128)S(1)}, f32[512,128]{1,0:T(8,128)S(1)}, u32[]{:S(2)}, u32[]{:S(2)}) collective-permute-start(f32[512,128]{1,0:T(8,128)S(1)} %constant_dynamic-update-slice_fusion.2), channel_id=1, source_target_pairs={{0,1},{1,0},{2,3},{3,2},{4,5},{5,4},{6,7},{7,6},{8,9},{9,8},{10,11... | collective-permute-start | bytes 786440 | tf_op jit(solution)/shard_map/ppermute | solution.py:79
  145.7 1.9 %collective-permute-start.22 = (f32[128,128]{0,1:T(8,128)S(1)}, f32[128,128]{0,1:T(8,128)S(1)}, u32[]{:S(2)}, u32[]{:S(2)}) collective-permute-start(f32[128,128]{0,1:T(8,128)S(1)} %fusion.27), channel_id=1, source_target_pairs={{0,4},{4,0},{8,12},{12,8},{1,5},{5,1},{9,13},{13,9},{2,6},{6,2},{1... | collective-permute-start | bytes 196616 | tf_op jit(solution)/shard_map/ppermute | solution.py:44
  146.0 4.3 %collective-permute-start.23 = (f32[128,128]{0,1:T(8,128)S(1)}, f32[128,128]{0,1:T(8,128)S(1)}, u32[]{:S(2)}, u32[]{:S(2)}) collective-permute-start(f32[128,128]{0,1:T(8,128)S(1)} %fusion.27), channel_id=1, source_target_pairs={{0,8},{4,12},{8,0},{12,4},{1,9},{5,13},{9,1},{13,5},{2,10},{6,14},... | collective-permute-start | bytes 196616 | tf_op jit(solution)/shard_map/ppermute | solution.py:44
  147.7 4.3 %collective-permute-start.24 = (f32[128,128]{0,1:T(8,128)S(1)}, f32[128,128]{0,1:T(8,128)S(1)}, u32[]{:S(2)}, u32[]{:S(2)}) collective-permute-start(f32[128,128]{0,1:T(8,128)S(1)} %fusion.27), channel_id=1, source_target_pairs={{0,12},{4,8},{8,4},{12,0},{1,13},{5,9},{9,5},{13,1},{2,14},{6,10},... | collective-permute-start | bytes 196616 | tf_op jit(solution)/shard_map/ppermute | solution.py:44

commit v12 on v11

--- a/solution.py
+++ b/solution.py
@@ -84,6 +84,23 @@
     return x
 
 
+def _pair_split_sum(x, axis):
+    count = lax.axis_size(axis)
+    if count != 4 or x.shape[0] % 2:
+        return _butterfly_sum(x, axis)
+    pairs = [(i, i ^ 1) for i in range(count)]
+    near_low = (lax.axis_index(axis) & 1) == 0
+    x = x + lax.ppermute(x, axis, pairs)
+    half = x.shape[0] // 2
+    mine = jnp.where(near_low, x[:half], x[half:])
+    mine = mine + lax.ppermute(mine, axis, [(i, i ^ 2) for i in range(count)])
+    other = lax.ppermute(mine, axis, pairs)
+    first = jnp.where(near_low, 0, half)
+    both = jnp.zeros(x.shape, x.dtype)
+    both = lax.dynamic_update_slice_in_dim(both, mine, first, 0)
+    return lax.dynamic_update_slice_in_dim(both, other, half - first, 0)
+
+
 def _lower_factor(image, gram_axis):
     gram_part = jnp.dot(
         image.T, image, precision=lax.Precision.HIGHEST, preferred_element_type=jnp.float32
@@ -149,7 +166,7 @@
                 covariance, block, precision=lax.Precision.HIGHEST,
                 preferred_element_type=jnp.float32,
             )
-            return _butterfly_sum(partial_image, "row")
+            return _pair_split_sum(partial_image, "row")
         partial_image = lax.dot_general(
             covariance, block, (((0,), (0,)), ((), ())),
             precision=lax.Precision.HIGHEST, preferred_element_type=jnp.float32,

time: 177 us -> 176 us (level)
  waiting for transfers between devices: 42 us -> 38 us
  other arithmetic: 46.7 us -> 48.6 us
    ppermute x2 -> x3, waiting for transfers between devices: 15.6 us -> 11.6 us  [the longest x1 8.17 us: _pair_split_sum(): mine = mine + lax.ppermute(mine, axis, [(i, i ^ 2) for i in range(count)])]
  transfers between devices with their start and end apart: 25 -> 26, of which waited for: 12 -> 13; matrix products, arithmetic and copies ran while one was open for 27% -> 28% of each run, Pallas kernels for 0% -> 0%
where the time goes in v12:
time: 176 us; the launch traced here: 175 us
  other arithmetic  48.6 us (28%)
  starting transfers between devices  47.1 us (27%)
  waiting for transfers between devices  38 us (22%)
  matrix products  21.4 us (12%)
  local copies, waits for them, and re-layouts  18.8 us (11%)
    ppermute x9, starting transfers between devices, _butterfly_gather(): other = lax.ppermute(x, axis, [(i, i ^ step) for i in range(count)])  32.2 us
    another operation x6, other arithmetic, _lower_factor(): return jnp.linalg.cholesky(_direct_sum(gram_part, gram_axis))  24.8 us
    another operation x4, other arithmetic, _right_solve(): jax.scipy.linalg.solve_triangular(lower_factor, image.T, lower=True)  20.9 us
    ppermute x9, starting transfers between devices, _direct_sum(): lax.ppermute(x, axis, [(i, i ^ k) for i in range(count)])  9.67 us
    dot_general x1, matrix products, cov_times(): lax.dot_general(covariance, block, (((0,), (0,)), ((), ())), precision=la...  8.46 us
    ppermute x1, waiting for transfers between devices, _pair_split_sum(): mine = mine + lax.ppermute(mine, axis, [(i, i ^ 2) for i in range(count)])  8.17 us
    ppermute x9, waiting for transfers between devices, _direct_sum(): lax.ppermute(x, axis, [(i, i ^ k) for i in range(count)])  8.04 us
    ppermute x9, waiting for transfers between devices, _butterfly_gather(): other = lax.ppermute(x, axis, [(i, i ^ step) for i in range(count)])  7.6 us
  transfers between devices with their start and end apart: 26, of which 13 were waited for; matrix products, arithmetic and copies ran while one was open for 28% of the time, Pallas kernels for 0%

profile of v12, /device:TPU:0, one launch (start us, length us, event | category | flops | bytes accessed | tf_op | source)
XLA Modules:
  0.0 175.0 jit_solution(6354590852336359248)
XLA Ops:
  0.7 2.2 %fusion.26 = f32[8,128,16]{1,2,0:T(8,128)S(1)} fusion(bf16[1024,8,16]{0,2,1:T(8,128)(2,1)} %param.7, bf16[8,1024,128]{2,1,0:T(8,128)(2,1)} %param.8), kind=kOutput, calls=%fused_computation.71 | convolution fusion | flops 33554432 | bytes 2424832 | tf_op jit(solution)/shard_map/mbs,bmr->brs/dot_general | solution.py:122
  3.4 2.6 %collective-permute-start.1 = (f32[8,128,16]{1,2,0:T(8,128)S(1)}, f32[8,128,16]{1,2,0:T(8,128)S(1)}, u32[]{:S(2)}, u32[]{:S(2)}) collective-permute-start(f32[8,128,16]{1,2,0:T(8,128)S(1)} %fusion.26), channel_id=1, source_target_pairs={{0,8},{4,12},{8,0},{12,4},{1,9},{5,13},{9,1},{13,5},{2,10},{6,14},... | collective-permute-start | bytes 196616 | tf_op jit(solution)/shard_map/ppermute | solution.py:44
  6.0 2.6 %collective-permute-done.1 = f32[8,128,16]{1,2,0:T(8,128)S(1)} collective-permute-done((f32[8,128,16]{1,2,0:T(8,128)S(1)}, f32[8,128,16]{1,2,0:T(8,128)S(1)}, u32[]{:S(2)}, u32[]{:S(2)}) %collective-permute-start.1) | collective-permute-done | bytes 65568 | tf_op jit(solution)/shard_map/ppermute | solution.py:44
  8.7 1.4 collective-permute-done.2
  10.9 1.6 collective-permute-start.10
  12.4 2.6 %collective-permute-start.7 = (bf16[1,512,128]{1,2,0:T(8,128)(2,1)S(1)}, bf16[1,512,128]{1,2,0:T(8,128)(2,1)S(1)}, u32[]{:S(2)}, u32[]{:S(2)}) collective-permute-start(bf16[1,512,128]{1,2,0:T(8,128)(2,1)S(1)} %bitcast.100), channel_id=1, source_target_pairs={{0,2},{1,3},{2,0},{3,1},{4,6},{5,7},{6,4},{7,5},{8,10},{9,11},{10,... | collective-permute-start | bytes 393224 | tf_op jit(solution)/shard_map/ppermute | solution.py:53
  15.0 1.4 collective-permute-start.3
  16.8 4.2 %collective-permute-start.11 = (bf16[2,512,128]{2,1,0:T(8,128)(2,1)S(1)}, bf16[2,512,128]{2,1,0:T(8,128)(2,1)S(1)}, u32[]{:S(2)}, u32[]{:S(2)}) collective-permute-start(bf16[2,512,128]{2,1,0:T(8,128)(2,1)S(1)} %bitcast.96), channel_id=1, source_target_pairs={{0,2},{1,3},{2,0},{3,1},{4,6},{5,7},{6,4},{7,5},{8,10},{9,11},{10,... | collective-permute-start | bytes 786440 | tf_op jit(solution)/shard_map/ppermute | solution.py:53
  21.7 0.9 broadcast_in_dim.42
  23.3 0.8 fusion.9
  24.5 0.9 broadcast_in_dim.39
  26.1 3.1 %collective-permute-start.8 = (bf16[2,512,128]{2,1,0:T(8,128)(2,1)S(1)}, bf16[2,512,128]{2,1,0:T(8,128)(2,1)}, u32[]{:S(2)}, u32[]{:S(2)}) collective-permute-start(bf16[2,512,128]{2,1,0:T(8,128)(2,1)S(1)} %bitcast.97), channel_id=1, source_target_pairs={{0,1},{1,0},{2,3},{3,2},{4,5},{5,4},{6,7},{7,6},{8,9},{9,8},{10,11... | collective-permute-start | bytes 786440 | tf_op jit(solution)/shard_map/ppermute | solution.py:53
  29.4 0.9 broadcast_in_dim.36
  31.0 1.1 copy.7
  32.8 17.9 %collective-permute-start.5 = (bf16[2,1024,128]{2,1,0:T(8,128)(2,1)}, bf16[2,1024,128]{2,1,0:T(8,128)(2,1)S(1)}, u32[]{:S(2)}, u32[]{:S(2)}) collective-permute-start(bf16[2,1024,128]{2,1,0:T(8,128)(2,1)} %bitcast.7), channel_id=1, source_target_pairs={{0,8},{4,12},{8,0},{12,4},{1,9},{5,13},{9,1},{13,5},{2,10},{6,14},... | collective-permute-start | bytes 1572872 | tf_op jit(solution)/shard_map/ppermute | solution.py:53
  51.5 1.7 collective-permute-start.12
  53.2 1.7 bitcast_dynamic-update-slice_fusion.8
  55.5 1.1 bitcast_dynamic-update-slice_fusion.1
  56.6 2.9 %collective-permute-done.5 = bf16[2,1024,128]{2,1,0:T(8,128)(2,1)S(1)} collective-permute-done((bf16[2,1024,128]{2,1,0:T(8,128)(2,1)}, bf16[2,1024,128]{2,1,0:T(8,128)(2,1)S(1)}, u32[]{:S(2)}, u32[]{:S(2)}) %collective-permute-start.5) | collective-permute-done | bytes 524320 | tf_op jit(solution)/shard_map/ppermute | solution.py:53
  59.9 1.1 bitcast_dynamic-update-slice_fusion.4
  61.1 1.1 bitcast_dynamic-update-slice_fusion.2
  62.2 2.2 %collective-permute-done.12 = bf16[4,512,128]{2,1,0:T(8,128)(2,1)} collective-permute-done((bf16[4,512,128]{2,1,0:T(8,128)(2,1)}, bf16[4,512,128]{2,1,0:T(8,128)(2,1)}, u32[]{:S(2)}, u32[]{:S(2)}) %collective-permute-start.12) | collective-permute-done | bytes 524320 | tf_op jit(solution)/shard_map/ppermute | solution.py:53
  64.4 1.1 constant_dynamic-update-slice_fusion.6
  65.5 2.0 %collective-permute-done.9 = bf16[4,512,128]{2,1,0:T(8,128)(2,1)} collective-permute-done((bf16[4,512,128]{2,1,0:T(8,128)(2,1)}, bf16[4,512,128]{2,1,0:T(8,128)(2,1)}, u32[]{:S(2)}, u32[]{:S(2)}) %collective-permute-start.9) | collective-permute-done | bytes 524320 | tf_op jit(solution)/shard_map/ppermute | solution.py:53
  67.5 1.1 bitcast_dynamic-update-slice_fusion.3
  69.1 1.4 constant_dynamic-update-slice_fusion.11
  70.5 2.4 %bitcast_multiply_fusion = f32[1024,1024]{1,0:T(8,128)S(1)} fusion(bf16[8,1024,128]{2,1,0:T(8,128)(2,1)S(1)} %bitcast.95, bf16[8,512,128]{2,1,0:T(8,128)(2,1)S(1)} %bitcast.99, bf16[8,512,128]{2,1,0:T(8,128)(2,1)S(1)} %bitcast.98), kind=kOutput, calls=%fused_computation | convolution fusion | flops 2152726528 | bytes 8388608 | tf_op jit(solution)/shard_map/dot_general | solution.py:159
  72.9 4.9 %fusion.7 = f32[1024,128]{1,0:T(8,128)S(1)} fusion(f32[1024,1024]{1,0:T(8,128)S(1)} %bitcast_multiply_fusion, f32[4096,128]{1,0:T(8,128)} %param.10, s32[]{:T(128)S(6)} %select_n.129), kind=kOutput, calls=%fused_computation.15 | convolution fusion | flops 1610612736 | bytes 5242884 | tf_op jit(solution)/shard_map/dot_general | solution.py:165
  77.8 1.9 %collective-permute-done.13 = f32[1024,128]{1,0:T(8,128)S(1)} collective-permute-done((f32[1024,128]{1,0:T(8,128)S(1)}, f32[1024,128]{1,0:T(8,128)S(1)}, u32[]{:S(2)}, u32[]{:S(2)}) %collective-permute-start.13) | collective-permute-done | bytes 524320 | tf_op jit(solution)/shard_map/ppermute | solution.py:93
  80.2 8.2 %collective-permute-done.14 = f32[512,128]{1,0:T(8,128)} collective-permute-done((f32[512,128]{1,0:T(8,128)S(1)}, f32[512,128]{1,0:T(8,128)}, u32[]{:S(2)}, u32[]{:S(2)}) %collective-permute-start.14) | collective-permute-done | bytes 262176 | tf_op jit(solution)/shard_map/ppermute | solution.py:96
  88.4 1.0 constant_dynamic-update-slice_fusion.5
  89.5 1.5 collective-permute-done.15
  91.0 1.0 fusion.23
  92.6 1.5 collective-permute-start.17
  94.1 2.3 %collective-permute-start.18 = (f32[128,128]{0,1:T(8,128)S(1)}, f32[128,128]{0,1:T(8,128)}, u32[]{:S(2)}, u32[]{:S(2)}) collective-permute-start(f32[128,128]{0,1:T(8,128)S(1)} %fusion.23), channel_id=1, source_target_pairs={{0,3},{1,2},{2,1},{3,0},{4,7},{5,6},{6,5},{7,4},{8,11},{9,10},{10,... | collective-permute-start | bytes 196616 | tf_op jit(solution)/shard_map/ppermute | solution.py:44
  96.5 8.5 %fusion.24 = f32[1024,128]{1,0:T(8,128)S(1)} fusion(f32[1024,1024]{1,0:T(8,128)} %copy-done.1, f32[1024,128]{1,0:T(8,128)S(1)} %constant_dynamic-update-slice_fusion.4), kind=kOutput, calls=%fused_computation.69 | convolution fusion | flops 1610612736 | bytes 5242880 | tf_op jit(solution)/shard_map/dot_general | solution.py:170
  105.1 0.9 add_add_fusion.1
  106.1 6.5 %collective-permute-done.19 = f32[512,128]{1,0:T(8,128)S(1)} collective-permute-done((f32[512,128]{1,0:T(8,128)S(1)}, f32[512,128]{1,0:T(8,128)S(1)}, u32[]{:S(2)}, u32[]{:S(2)}) %collective-permute-start.19) | collective-permute-done | bytes 262176 | tf_op jit(solution)/shard_map/ppermute | solution.py:76
  113.0 11.7 %cholesky.44 = f32[128,128]{1,0:T(8,128)S(1)} custom-call(f32[128,128]{1,0:T(8,128)S(1)} %fusion.17), custom_call_target="Cholesky" | custom-call | tf_op jit(solution)/shard_map/jit(cholesky)/cholesky | solution.py:108
  124.8 2.7 %collective-permute-start.21 = (f32[256,128]{1,0:T(8,128)S(1)}, f32[256,128]{1,0:T(8,128)S(1)}, u32[]{:S(2)}, u32[]{:S(2)}) collective-permute-start(f32[256,128]{1,0:T(8,128)S(1)} %get-tuple-element.7), channel_id=1, source_target_pairs={{0,2},{1,3},{2,0},{3,1},{4,6},{5,7},{6,4},{7,5},{8,10},{9,11},{10,... | collective-permute-start | bytes 393224 | tf_op jit(solution)/shard_map/ppermute | solution.py:79
  128.1 4.3 %collective-permute-done.21 = f32[256,128]{1,0:T(8,128)S(1)} collective-permute-done((f32[256,128]{1,0:T(8,128)S(1)}, f32[256,128]{1,0:T(8,128)S(1)}, u32[]{:S(2)}, u32[]{:S(2)}) %collective-permute-start.21) | collective-permute-done | bytes 131104 | tf_op jit(solution)/shard_map/ppermute | solution.py:79
  133.3 9.8 %custom-call.6 = f32[1,128,128]{1,2,0:T(8,128)S(1)} custom-call(f32[1,128,128]{2,1,0:T(8,128)S(1)} %fusion.11), custom_call_target="InvertDiagBlocksLowerTriangular" | custom-call | tf_op jit(solution)/shard_map/jit(_solve_triangular)/triangular_solve | solution.py:112
  144.6 2.0 %collective-permute-start.24 = (f32[128,128]{0,1:T(8,128)S(1)}, f32[128,128]{0,1:T(8,128)S(1)}, u32[]{:S(2)}, u32[]{:S(2)}) collective-permute-start(f32[128,128]{0,1:T(8,128)S(1)} %fusion.25), channel_id=1, source_target_pairs={{0,8},{4,12},{8,0},{12,4},{1,9},{5,13},{9,1},{13,5},{2,10},{6,14},... | collective-permute-start | bytes 196616 | tf_op jit(solution)/shard_map/ppermute | solution.py:44
  146.6 2.6 %collective-permute-done.24 = f32[128,128]{0,1:T(8,128)S(1)} collective-permute-done((f32[128,128]{0,1:T(8,128)S(1)}, f32[128,128]{0,1:T(8,128)S(1)}, u32[]{:S(2)}, u32[]{:S(2)}) %collective-permute-start.24) | collective-permute-done | bytes 65568 | tf_op jit(solution)/shard_map/ppermute | solution.py:44
  149.2 1.4 collective-permute-done.25
  150.7 11.7 %cholesky.55 = f32[128,128]{1,0:T(8,128)S(1)} custom-call(f32[128,128]{1,0:T(8,128)S(1)} %fusion.15), custom_call_target="Cholesky" | custom-call | tf_op jit(solution)/shard_map/jit(cholesky)/cholesky | solution.py:108
  163.8 9.8 %custom-call.7 = f32[1,128,128]{1,2,0:T(8,128)S(1)} custom-call(f32[1,128,128]{2,1,0:T(8,128)S(1)} %fusion.12), custom_call_target="InvertDiagBlocksLowerTriangular" | custom-call | tf_op jit(solution)/shard_map/jit(_solve_triangular)/triangular_solve | solution.py:112
  174.3 0.8 copy.24
  (86 shorter events, 15.2 us)
Async XLA Ops:
  0.6 9.4 %copy-start = (bf16[8,1024,128]{2,1,0:T(8,128)(2,1)S(1)}, bf16[8,1024,128]{2,1,0:T(8,128)(2,1)}, u32[]{:S(2)}) copy-start(bf16[8,1024,128]{2,1,0:T(8,128)(2,1)} %param.9) | copy-start | bytes 6291460
  0.6 9.4 %copy-start.2 = (bf16[1024,8,16]{0,2,1:T(8,128)(2,1)S(1)}, bf16[1024,8,16]{0,2,1:T(8,128)(2,1)}, u32[]{:S(2)}) copy-start(bf16[1024,8,16]{0,2,1:T(8,128)(2,1)} %param.7) | copy-start | bytes 786436
  2.9 3.2 %collective-permute-start = (f32[8,128,16]{1,2,0:T(8,128)S(1)}, f32[8,128,16]{1,2,0:T(8,128)S(1)}, u32[]{:S(2)}, u32[]{:S(2)}) collective-permute-start(f32[8,128,16]{1,2,0:T(8,128)S(1)} %fusion.26), channel_id=1, source_target_pairs={{0,4},{4,0},{8,12},{12,8},{1,5},{5,1},{9,13},{13,9},{2,6},{6,2},{1... | collective-permute-start | bytes 196616 | tf_op jit(solution)/shard_map/ppermute | solution.py:44
  3.4 5.2 %collective-permute-start.1 = (f32[8,128,16]{1,2,0:T(8,128)S(1)}, f32[8,128,16]{1,2,0:T(8,128)S(1)}, u32[]{:S(2)}, u32[]{:S(2)}) collective-permute-start(f32[8,128,16]{1,2,0:T(8,128)S(1)} %fusion.26), channel_id=1, source_target_pairs={{0,8},{4,12},{8,0},{12,4},{1,9},{5,13},{9,1},{13,5},{2,10},{6,14},... | collective-permute-start | bytes 196616 | tf_op jit(solution)/shard_map/ppermute | solution.py:44
  6.0 4.1 %collective-permute-start.2 = (f32[8,128,16]{1,2,0:T(8,128)S(1)}, f32[8,128,16]{1,2,0:T(8,128)S(1)}, u32[]{:S(2)}, u32[]{:S(2)}) collective-permute-start(f32[8,128,16]{1,2,0:T(8,128)S(1)} %fusion.26), channel_id=1, source_target_pairs={{0,12},{4,8},{8,4},{12,0},{1,13},{5,9},{9,5},{13,1},{2,14},{6,10},... | collective-permute-start | bytes 196616 | tf_op jit(solution)/shard_map/ppermute | solution.py:44
  10.9 5.8 %collective-permute-start.10 = (bf16[1,512,128]{1,2,0:T(8,128)(2,1)S(1)}, bf16[1,512,128]{1,2,0:T(8,128)(2,1)S(1)}, u32[]{:S(2)}, u32[]{:S(2)}) collective-permute-start(bf16[1,512,128]{1,2,0:T(8,128)(2,1)S(1)} %bitcast.103), channel_id=1, source_target_pairs={{0,16},{16,0},{1,17},{17,1},{2,18},{18,2},{3,19},{19,3},{4,20},{20... | collective-permute-start | bytes 393224 | tf_op jit(solution)/shard_map/ppermute | solution.py:53
  12.4 9.1 %collective-permute-start.7 = (bf16[1,512,128]{1,2,0:T(8,128)(2,1)S(1)}, bf16[1,512,128]{1,2,0:T(8,128)(2,1)S(1)}, u32[]{:S(2)}, u32[]{:S(2)}) collective-permute-start(bf16[1,512,128]{1,2,0:T(8,128)(2,1)S(1)} %bitcast.100), channel_id=1, source_target_pairs={{0,2},{1,3},{2,0},{3,1},{4,6},{5,7},{6,4},{7,5},{8,10},{9,11},{10,... | collective-permute-start | bytes 393224 | tf_op jit(solution)/shard_map/ppermute | solution.py:53
  15.0 8.2 %collective-permute-start.3 = (bf16[1024,128]{0,1:T(8,128)(2,1)S(1)}, bf16[1024,128]{0,1:T(8,128)(2,1)}, u32[]{:S(2)}, u32[]{:S(2)}) collective-permute-start(bf16[1024,128]{0,1:T(8,128)(2,1)S(1)} %bitcast.94), channel_id=1, source_target_pairs={{1,4},{2,8},{3,12},{4,1},{6,9},{7,13},{8,2},{9,6},{11,14},{12,3},{... | collective-permute-start | bytes 786440 | tf_op jit(solution)/shard_map/ppermute | solution.py:136
  16.8 33.9 %collective-permute-start.11 = (bf16[2,512,128]{2,1,0:T(8,128)(2,1)S(1)}, bf16[2,512,128]{2,1,0:T(8,128)(2,1)S(1)}, u32[]{:S(2)}, u32[]{:S(2)}) collective-permute-start(bf16[2,512,128]{2,1,0:T(8,128)(2,1)S(1)} %bitcast.96), channel_id=1, source_target_pairs={{0,2},{1,3},{2,0},{3,1},{4,6},{5,7},{6,4},{7,5},{8,10},{9,11},{10,... | collective-permute-start | bytes 786440 | tf_op jit(solution)/shard_map/ppermute | solution.py:53
  24.0 6.9 %collective-permute-start.4 = (bf16[1,1024,128]{1,2,0:T(8,128)(2,1)}, bf16[1,1024,128]{1,2,0:T(8,128)(2,1)}, u32[]{:S(2)}, u32[]{:S(2)}) collective-permute-start(bf16[1,1024,128]{1,2,0:T(8,128)(2,1)} %get-tuple-element.10), channel_id=1, source_target_pairs={{0,16},{16,0},{1,17},{17,1},{2,18},{18,2},{3,19},{19,3},{4,20},{20... | collective-permute-start | bytes 786440 | tf_op jit(solution)/shard_map/ppermute | solution.py:53
  26.1 27.1 %collective-permute-start.8 = (bf16[2,512,128]{2,1,0:T(8,128)(2,1)S(1)}, bf16[2,512,128]{2,1,0:T(8,128)(2,1)}, u32[]{:S(2)}, u32[]{:S(2)}) collective-permute-start(bf16[2,512,128]{2,1,0:T(8,128)(2,1)S(1)} %bitcast.97), channel_id=1, source_target_pairs={{0,1},{1,0},{2,3},{3,2},{4,5},{5,4},{6,7},{7,6},{8,9},{9,8},{10,11... | collective-permute-start | bytes 786440 | tf_op jit(solution)/shard_map/ppermute | solution.py:53
  32.8 26.7 %collective-permute-start.5 = (bf16[2,1024,128]{2,1,0:T(8,128)(2,1)}, bf16[2,1024,128]{2,1,0:T(8,128)(2,1)S(1)}, u32[]{:S(2)}, u32[]{:S(2)}) collective-permute-start(bf16[2,1024,128]{2,1,0:T(8,128)(2,1)} %bitcast.7), channel_id=1, source_target_pairs={{0,8},{4,12},{8,0},{12,4},{1,9},{5,13},{9,1},{13,5},{2,10},{6,14},... | collective-permute-start | bytes 1572872 | tf_op jit(solution)/shard_map/ppermute | solution.py:53
  51.5 13.0 %collective-permute-start.12 = (bf16[4,512,128]{2,1,0:T(8,128)(2,1)}, bf16[4,512,128]{2,1,0:T(8,128)(2,1)}, u32[]{:S(2)}, u32[]{:S(2)}) collective-permute-start(bf16[4,512,128]{2,1,0:T(8,128)(2,1)} %bitcast.31), channel_id=1, source_target_pairs={{0,1},{1,0},{2,3},{3,2},{4,5},{5,4},{6,7},{7,6},{8,9},{9,8},{10,11... | collective-permute-start | bytes 1572872 | tf_op jit(solution)/shard_map/ppermute | solution.py:53
  54.9 12.7 %collective-permute-start.9 = (bf16[4,512,128]{2,1,0:T(8,128)(2,1)}, bf16[4,512,128]{2,1,0:T(8,128)(2,1)}, u32[]{:S(2)}, u32[]{:S(2)}) collective-permute-start(bf16[4,512,128]{2,1,0:T(8,128)(2,1)} %bitcast.20), channel_id=1, source_target_pairs={{0,16},{16,0},{1,17},{17,1},{2,18},{18,2},{3,19},{19,3},{4,20},{20... | collective-permute-start | bytes 1572872 | tf_op jit(solution)/shard_map/ppermute | solution.py:53
  59.6 9.5 %collective-permute-start.6 = (bf16[4,1024,128]{2,1,0:T(8,128)(2,1)S(1)}, bf16[4,1024,128]{2,1,0:T(8,128)(2,1)}, u32[]{:S(2)}, u32[]{:S(2)}) collective-permute-start(bf16[4,1024,128]{2,1,0:T(8,128)(2,1)S(1)} %bitcast.93), channel_id=1, source_target_pairs={{0,4},{4,0},{8,12},{12,8},{1,5},{5,1},{9,13},{13,9},{2,6},{6,2},{1... | collective-permute-start | bytes 3145736 | tf_op jit(solution)/shard_map/ppermute | solution.py:53
  72.8 4.9 %copy-start.1 = (f32[1024,1024]{1,0:T(8,128)}, f32[1024,1024]{1,0:T(8,128)S(1)}, u32[]{:S(2)}) copy-start(f32[1024,1024]{1,0:T(8,128)S(1)} %bitcast_multiply_fusion) | copy-start | bytes 12582916
  77.7 2.0 %collective-permute-start.13 = (f32[1024,128]{1,0:T(8,128)S(1)}, f32[1024,128]{1,0:T(8,128)S(1)}, u32[]{:S(2)}, u32[]{:S(2)}) collective-permute-start(f32[1024,128]{1,0:T(8,128)S(1)} %fusion.7), channel_id=1, source_target_pairs={{0,4},{4,0},{8,12},{12,8},{1,5},{5,1},{9,13},{13,9},{2,6},{6,2},{1... | collective-permute-start | bytes 1572872 | tf_op jit(solution)/shard_map/ppermute | solution.py:93
  79.8 8.5 %collective-permute-start.14 = (f32[512,128]{1,0:T(8,128)S(1)}, f32[512,128]{1,0:T(8,128)}, u32[]{:S(2)}, u32[]{:S(2)}) collective-permute-start(f32[512,128]{1,0:T(8,128)S(1)} %slice_select_fusion), channel_id=1, source_target_pairs={{0,8},{4,12},{8,0},{12,4},{1,9},{5,13},{9,1},{13,5},{2,10},{6,14},... | collective-permute-start | bytes 786440 | tf_op jit(solution)/shard_map/ppermute | solution.py:96
  89.4 1.6 collective-permute-start.15
  92.0 13.1 %collective-permute-start.16 = (f32[128,128]{0,1:T(8,128)S(1)}, f32[128,128]{0,1:T(8,128)S(1)}, u32[]{:S(2)}, u32[]{:S(2)}) collective-permute-start(f32[128,128]{0,1:T(8,128)S(1)} %fusion.23), channel_id=1, source_target_pairs={{0,1},{1,0},{2,3},{3,2},{4,5},{5,4},{6,7},{7,6},{8,9},{9,8},{10,11... | collective-permute-start | bytes 196616 | tf_op jit(solution)/shard_map/ppermute | solution.py:44
  92.6 12.5 %collective-permute-start.17 = (f32[128,128]{0,1:T(8,128)S(1)}, f32[128,128]{0,1:T(8,128)}, u32[]{:S(2)}, u32[]{:S(2)}) collective-permute-start(f32[128,128]{0,1:T(8,128)S(1)} %fusion.23), channel_id=1, source_target_pairs={{0,2},{1,3},{2,0},{3,1},{4,6},{5,7},{6,4},{7,5},{8,10},{9,11},{10,... | collective-permute-start | bytes 196616 | tf_op jit(solution)/shard_map/ppermute | solution.py:44
  94.1 10.9 %collective-permute-start.18 = (f32[128,128]{0,1:T(8,128)S(1)}, f32[128,128]{0,1:T(8,128)}, u32[]{:S(2)}, u32[]{:S(2)}) collective-permute-start(f32[128,128]{0,1:T(8,128)S(1)} %fusion.23), channel_id=1, source_target_pairs={{0,3},{1,2},{2,1},{3,0},{4,7},{5,6},{6,5},{7,4},{8,11},{9,10},{10,... | collective-permute-start | bytes 196616 | tf_op jit(solution)/shard_map/ppermute | solution.py:44
  105.0 7.6 %collective-permute-start.19 = (f32[512,128]{1,0:T(8,128)S(1)}, f32[512,128]{1,0:T(8,128)S(1)}, u32[]{:S(2)}, u32[]{:S(2)}) collective-permute-start(f32[512,128]{1,0:T(8,128)S(1)} %slice_select_fusion.1), channel_id=1, source_target_pairs={{0,1},{1,0},{2,3},{3,2},{4,5},{5,4},{6,7},{7,6},{8,9},{9,8},{10,11... | collective-permute-start | bytes 786440 | tf_op jit(solution)/shard_map/ppermute | solution.py:76
  112.6 12.1 %collective-permute-start.20 = (f32[256,128]{1,0:T(8,128)S(1)}, f32[256,128]{1,0:T(8,128)S(1)}, u32[]{:S(2)}, u32[]{:S(2)}) collective-permute-start(f32[256,128]{1,0:T(8,128)S(1)} %slice_select_fusion.2), channel_id=1, source_target_pairs={{0,2},{1,3},{2,0},{3,1},{4,6},{5,7},{6,4},{7,5},{8,10},{9,11},{10,... | collective-permute-start | bytes 393224 | tf_op jit(solution)/shard_map/ppermute | solution.py:76
  124.8 7.6 %collective-permute-start.21 = (f32[256,128]{1,0:T(8,128)S(1)}, f32[256,128]{1,0:T(8,128)S(1)}, u32[]{:S(2)}, u32[]{:S(2)}) collective-permute-start(f32[256,128]{1,0:T(8,128)S(1)} %get-tuple-element.7), channel_id=1, source_target_pairs={{0,2},{1,3},{2,0},{3,1},{4,6},{5,7},{6,4},{7,5},{8,10},{9,11},{10,... | collective-permute-start | bytes 393224 | tf_op jit(solution)/shard_map/ppermute | solution.py:79
  132.4 10.8 %collective-permute-start.22 = (f32[512,128]{1,0:T(8,128)S(1)}, f32[512,128]{1,0:T(8,128)S(1)}, u32[]{:S(2)}, u32[]{:S(2)}) collective-permute-start(f32[512,128]{1,0:T(8,128)S(1)} %constant_dynamic-update-slice_fusion.2), channel_id=1, source_target_pairs={{0,1},{1,0},{2,3},{3,2},{4,5},{5,4},{6,7},{7,6},{8,9},{9,8},{10,11... | collective-permute-start | bytes 786440 | tf_op jit(solution)/shard_map/ppermute | solution.py:79
  144.5 2.1 %collective-permute-start.23 = (f32[128,128]{0,1:T(8,128)S(1)}, f32[128,128]{0,1:T(8,128)S(1)}, u32[]{:S(2)}, u32[]{:S(2)}) collective-permute-start(f32[128,128]{0,1:T(8,128)S(1)} %fusion.25), channel_id=1, source_target_pairs={{0,4},{4,0},{8,12},{12,8},{1,5},{5,1},{9,13},{13,9},{2,6},{6,2},{1... | collective-permute-start | bytes 196616 | tf_op jit(solution)/shard_map/ppermute | solution.py:44
  144.6 4.6 %collective-permute-start.24 = (f32[128,128]{0,1:T(8,128)S(1)}, f32[128,128]{0,1:T(8,128)S(1)}, u32[]{:S(2)}, u32[]{:S(2)}) collective-permute-start(f32[128,128]{0,1:T(8,128)S(1)} %fusion.25), channel_id=1, source_target_pairs={{0,8},{4,12},{8,0},{12,4},{1,9},{5,13},{9,1},{13,5},{2,10},{6,14},... | collective-permute-start | bytes 196616 | tf_op jit(solution)/shard_map/ppermute | solution.py:44
  146.5 4.1 %collective-permute-start.25 = (f32[128,128]{0,1:T(8,128)S(1)}, f32[128,128]{0,1:T(8,128)S(1)}, u32[]{:S(2)}, u32[]{:S(2)}) collective-permute-start(f32[128,128]{0,1:T(8,128)S(1)} %fusion.25), channel_id=1, source_target_pairs={{0,12},{4,8},{8,4},{12,0},{1,13},{5,9},{9,5},{13,1},{2,14},{6,10},... | collective-permute-start | bytes 196616 | tf_op jit(solution)/shard_map/ppermute | solution.py:44

commit v13 on v12

--- a/solution.py
+++ b/solution.py
@@ -159,6 +159,9 @@
     covariance = lax.dot_general(
         left_rows, right_rows, (((0, 2), (0, 2)), ((), ())), preferred_element_type=jnp.float32
     ) * scaling
+    covariance_t = lax.dot_general(
+        right_rows, left_rows, (((0, 2), (0, 2)), ((), ())), preferred_element_type=jnp.float32
+    ) * scaling
 
     def cov_times(block, on_rows):
         if on_rows:
@@ -167,9 +170,9 @@
                 preferred_element_type=jnp.float32,
             )
             return _pair_split_sum(partial_image, "row")
-        partial_image = lax.dot_general(
-            covariance, block, (((0,), (0,)), ((), ())),
-            precision=lax.Precision.HIGHEST, preferred_element_type=jnp.float32,
+        partial_image = jnp.dot(
+            covariance_t, block, precision=lax.Precision.HIGHEST,
+            preferred_element_type=jnp.float32,
         )
         return _halving_sum(partial_image, "col")
 

time: 176 us -> 173 us (0.983)
    dot_general x1 -> x2, matrix products: 8.46 us -> 8.21 us  [the longest x1 4.6 us: shards(): lax.dot_general(right_rows, left_rows, (((0, 2), (0, 2)), ((), ())), pref...]
where the time goes in v13:
time: 173 us
  other arithmetic  47 us (27%)
  starting transfers between devices  46.8 us (27%)
  waiting for transfers between devices  37.9 us (22%)
  matrix products  21.2 us (12%)
  local copies, waits for them, and re-layouts  18.8 us (11%)
    ppermute x9, starting transfers between devices, _butterfly_gather(): other = lax.ppermute(x, axis, [(i, i ^ step) for i in range(count)])  32.2 us
    another operation x6, other arithmetic, _lower_factor(): return jnp.linalg.cholesky(_direct_sum(gram_part, gram_axis))  25 us
    another operation x4, other arithmetic, _right_solve(): jax.scipy.linalg.solve_triangular(lower_factor, image.T, lower=True)  20.9 us
    ppermute x9, starting transfers between devices, _direct_sum(): lax.ppermute(x, axis, [(i, i ^ k) for i in range(count)])  9.52 us
    ppermute x9, waiting for transfers between devices, _direct_sum(): lax.ppermute(x, axis, [(i, i ^ k) for i in range(count)])  9.35 us
    ppermute x1, waiting for transfers between devices, _pair_split_sum(): mine = mine + lax.ppermute(mine, axis, [(i, i ^ 2) for i in range(count)])  8.06 us
    ppermute x9, waiting for transfers between devices, _butterfly_gather(): other = lax.ppermute(x, axis, [(i, i ^ step) for i in range(count)])  7.59 us
    dynamic_update_slice x9, local copies, waits for them, and re-layouts, _butterfly_gather(): both = lax.dynamic_update_slice_in_dim(both, theirs, 1 - first, 1)  6.81 us
  transfers between devices with their start and end apart: 26, of which 13 were waited for; matrix products, arithmetic and copies ran while one was open for 28% of the time, Pallas kernels for 0%

profile of v13, /device:TPU:0, one launch (start us, length us, event | category | flops | bytes accessed | tf_op | source)
XLA Modules:
  0.0 172.9 jit_solution(17214307685031747965)
XLA Ops:
  0.7 2.2 %fusion.27 = f32[8,128,16]{1,2,0:T(8,128)S(1)} fusion(bf16[1024,8,16]{0,2,1:T(8,128)(2,1)} %param.7, bf16[8,1024,128]{2,1,0:T(8,128)(2,1)} %param.8), kind=kOutput, calls=%fused_computation.74 | convolution fusion | flops 33554432 | bytes 2424832 | tf_op jit(solution)/shard_map/mbs,bmr->brs/dot_general | solution.py:122
  3.4 2.6 %collective-permute-start.1 = (f32[8,128,16]{1,2,0:T(8,128)S(1)}, f32[8,128,16]{1,2,0:T(8,128)S(1)}, u32[]{:S(2)}, u32[]{:S(2)}) collective-permute-start(f32[8,128,16]{1,2,0:T(8,128)S(1)} %fusion.27), channel_id=1, source_target_pairs={{0,8},{4,12},{8,0},{12,4},{1,9},{5,13},{9,1},{13,5},{2,10},{6,14},... | collective-permute-start | bytes 196616 | tf_op jit(solution)/shard_map/ppermute | solution.py:44
  6.0 2.6 %collective-permute-done.1 = f32[8,128,16]{1,2,0:T(8,128)S(1)} collective-permute-done((f32[8,128,16]{1,2,0:T(8,128)S(1)}, f32[8,128,16]{1,2,0:T(8,128)S(1)}, u32[]{:S(2)}, u32[]{:S(2)}) %collective-permute-start.1) | collective-permute-done | bytes 65568 | tf_op jit(solution)/shard_map/ppermute | solution.py:44
  8.7 1.4 collective-permute-done.2
  10.9 1.6 collective-permute-start.10
  12.4 2.6 %collective-permute-start.7 = (bf16[1,512,128]{1,2,0:T(8,128)(2,1)S(1)}, bf16[1,512,128]{1,2,0:T(8,128)(2,1)S(1)}, u32[]{:S(2)}, u32[]{:S(2)}) collective-permute-start(bf16[1,512,128]{1,2,0:T(8,128)(2,1)S(1)} %bitcast.106), channel_id=1, source_target_pairs={{0,2},{1,3},{2,0},{3,1},{4,6},{5,7},{6,4},{7,5},{8,10},{9,11},{10,... | collective-permute-start | bytes 393224 | tf_op jit(solution)/shard_map/ppermute | solution.py:53
  15.0 1.4 collective-permute-start.3
  16.8 4.2 %collective-permute-start.11 = (bf16[2,512,128]{2,1,0:T(8,128)(2,1)S(1)}, bf16[2,512,128]{2,1,0:T(8,128)(2,1)S(1)}, u32[]{:S(2)}, u32[]{:S(2)}) collective-permute-start(bf16[2,512,128]{2,1,0:T(8,128)(2,1)S(1)} %bitcast.100), channel_id=1, source_target_pairs={{0,2},{1,3},{2,0},{3,1},{4,6},{5,7},{6,4},{7,5},{8,10},{9,11},{10,... | collective-permute-start | bytes 786440 | tf_op jit(solution)/shard_map/ppermute | solution.py:53
  21.7 0.9 broadcast_in_dim.42
  23.3 0.8 fusion.9
  24.5 0.9 broadcast_in_dim.39
  26.1 3.1 %collective-permute-start.8 = (bf16[2,512,128]{2,1,0:T(8,128)(2,1)S(1)}, bf16[2,512,128]{2,1,0:T(8,128)(2,1)}, u32[]{:S(2)}, u32[]{:S(2)}) collective-permute-start(bf16[2,512,128]{2,1,0:T(8,128)(2,1)S(1)} %bitcast.101), channel_id=1, source_target_pairs={{0,1},{1,0},{2,3},{3,2},{4,5},{5,4},{6,7},{7,6},{8,9},{9,8},{10,11... | collective-permute-start | bytes 786440 | tf_op jit(solution)/shard_map/ppermute | solution.py:53
  29.4 0.9 broadcast_in_dim.36
  31.0 1.1 copy.7
  32.8 17.9 %collective-permute-start.5 = (bf16[2,1024,128]{2,1,0:T(8,128)(2,1)}, bf16[2,1024,128]{2,1,0:T(8,128)(2,1)S(1)}, u32[]{:S(2)}, u32[]{:S(2)}) collective-permute-start(bf16[2,1024,128]{2,1,0:T(8,128)(2,1)} %bitcast.7), channel_id=1, source_target_pairs={{0,8},{4,12},{8,0},{12,4},{1,9},{5,13},{9,1},{13,5},{2,10},{6,14},... | collective-permute-start | bytes 1572872 | tf_op jit(solution)/shard_map/ppermute | solution.py:53
  51.5 1.7 %collective-permute-start.12 = (bf16[4,512,128]{2,1,0:T(8,128)(2,1)}, bf16[4,512,128]{2,1,0:T(8,128)(2,1)}, u32[]{:S(2)}, u32[]{:S(2)}) collective-permute-start(bf16[4,512,128]{2,1,0:T(8,128)(2,1)} %bitcast.31), channel_id=1, source_target_pairs={{0,1},{1,0},{2,3},{3,2},{4,5},{5,4},{6,7},{7,6},{8,9},{9,8},{10,11... | collective-permute-start | bytes 1572872 | tf_op jit(solution)/shard_map/ppermute | solution.py:53
  53.2 1.7 bitcast_dynamic-update-slice_fusion.8
  55.5 1.1 bitcast_dynamic-update-slice_fusion.1
  56.6 2.9 %collective-permute-done.5 = bf16[2,1024,128]{2,1,0:T(8,128)(2,1)S(1)} collective-permute-done((bf16[2,1024,128]{2,1,0:T(8,128)(2,1)}, bf16[2,1024,128]{2,1,0:T(8,128)(2,1)S(1)}, u32[]{:S(2)}, u32[]{:S(2)}) %collective-permute-start.5) | collective-permute-done | bytes 524320 | tf_op jit(solution)/shard_map/ppermute | solution.py:53
  59.9 1.1 bitcast_dynamic-update-slice_fusion.4
  61.1 1.1 bitcast_dynamic-update-slice_fusion.2
  62.2 2.2 %collective-permute-done.12 = bf16[4,512,128]{2,1,0:T(8,128)(2,1)} collective-permute-done((bf16[4,512,128]{2,1,0:T(8,128)(2,1)}, bf16[4,512,128]{2,1,0:T(8,128)(2,1)}, u32[]{:S(2)}, u32[]{:S(2)}) %collective-permute-start.12) | collective-permute-done | bytes 524320 | tf_op jit(solution)/shard_map/ppermute | solution.py:53
  64.4 1.1 constant_dynamic-update-slice_fusion.6
  65.5 2.0 %collective-permute-done.9 = bf16[4,512,128]{2,1,0:T(8,128)(2,1)} collective-permute-done((bf16[4,512,128]{2,1,0:T(8,128)(2,1)}, bf16[4,512,128]{2,1,0:T(8,128)(2,1)}, u32[]{:S(2)}, u32[]{:S(2)}) %collective-permute-start.9) | collective-permute-done | bytes 524320 | tf_op jit(solution)/shard_map/ppermute | solution.py:53
  67.6 1.1 bitcast_dynamic-update-slice_fusion.3
  69.1 1.4 constant_dynamic-update-slice_fusion.11
  70.5 2.4 %bitcast_multiply_fusion.2 = f32[1024,1024]{1,0:T(8,128)S(1)} fusion(bf16[8,1024,128]{2,1,0:T(8,128)(2,1)S(1)} %bitcast.98, bf16[8,512,128]{2,1,0:T(8,128)(2,1)S(1)} %bitcast.104, bf16[8,512,128]{2,1,0:T(8,128)(2,1)S(1)} %bitcast.102), kind=kOutput, calls=%fused_computation.2 | convolution fusion | flops 2152726528 | bytes 8388608 | tf_op jit(solution)/shard_map/dot_general | solution.py:159
  72.9 4.9 %fusion.7 = f32[1024,128]{1,0:T(8,128)S(1)} fusion(f32[1024,1024]{1,0:T(8,128)S(1)} %bitcast_multiply_fusion.2, f32[4096,128]{1,0:T(8,128)} %param.10, s32[]{:T(128)S(6)} %select_n.129), kind=kOutput, calls=%fused_computation.17 | convolution fusion | flops 1610612736 | bytes 5242884 | tf_op jit(solution)/shard_map/dot_general | solution.py:168
  77.9 1.9 %collective-permute-done.13 = f32[1024,128]{1,0:T(8,128)S(1)} collective-permute-done((f32[1024,128]{1,0:T(8,128)S(1)}, f32[1024,128]{1,0:T(8,128)S(1)}, u32[]{:S(2)}, u32[]{:S(2)}) %collective-permute-start.13) | collective-permute-done | bytes 524320 | tf_op jit(solution)/shard_map/ppermute | solution.py:93
  80.2 8.1 %collective-permute-done.14 = f32[512,128]{1,0:T(8,128)S(1)} collective-permute-done((f32[512,128]{1,0:T(8,128)S(1)}, f32[512,128]{1,0:T(8,128)S(1)}, u32[]{:S(2)}, u32[]{:S(2)}) %collective-permute-start.14) | collective-permute-done | bytes 262176 | tf_op jit(solution)/shard_map/ppermute | solution.py:96
  88.5 4.6 %fusion.2 = f32[1024,1024,1]{1,0,2:T(8,128)S(1)} fusion(bf16[8,1024,128]{2,1,0:T(8,128)(2,1)} %bitcast.99, bf16[8,512,128]{2,1,0:T(8,128)(2,1)} %bitcast.105, bf16[8,512,128]{2,1,0:T(8,128)(2,1)} %bitcast.103), kind=kOutput, calls=%fused_computation.5 | convolution fusion | flops 2151677952 | bytes 8388608 | tf_op jit(solution)/shard_map/dot_general | solution.py:162
  93.1 1.0 fusion.25
  94.1 1.0 collective-permute-start.16
  95.1 1.2 collective-permute-start.17
  96.3 2.3 %collective-permute-start.18 = (f32[128,128]{0,1:T(8,128)S(1)}, f32[128,128]{0,1:T(8,128)S(1)}, u32[]{:S(2)}, u32[]{:S(2)}) collective-permute-start(f32[128,128]{0,1:T(8,128)S(1)} %fusion.25), channel_id=1, source_target_pairs={{0,3},{1,2},{2,1},{3,0},{4,7},{5,6},{6,5},{7,4},{8,11},{9,10},{10,... | collective-permute-start | bytes 196616 | tf_op jit(solution)/shard_map/ppermute | solution.py:44
  98.6 3.6 %fusion = f32[1024,128]{1,0:T(8,128)S(1)} fusion(f32[1024,128]{1,0:T(8,128)S(1)} %constant_dynamic-update-slice_fusion.4, f32[1024,1024,1]{1,0,2:T(8,128)S(1)} %fusion.2), kind=kOutput, calls=%fused_computation.1 | convolution fusion | flops 1611661312 | bytes 5242880 | tf_op jit(solution)/shard_map/dot_general | solution.py:173
  102.3 1.3 collective-permute-done.17
  103.8 6.4 %collective-permute-done.19 = f32[512,128]{1,0:T(8,128)S(1)} collective-permute-done((f32[512,128]{1,0:T(8,128)S(1)}, f32[512,128]{1,0:T(8,128)S(1)}, u32[]{:S(2)}, u32[]{:S(2)}) %collective-permute-start.19) | collective-permute-done | bytes 262176 | tf_op jit(solution)/shard_map/ppermute | solution.py:76
  110.7 11.7 %cholesky.44 = f32[128,128]{1,0:T(8,128)S(1)} custom-call(f32[128,128]{1,0:T(8,128)S(1)} %fusion.17), custom_call_target="Cholesky" | custom-call | tf_op jit(solution)/shard_map/jit(cholesky)/cholesky | solution.py:108
  122.4 2.7 %collective-permute-start.21 = (f32[256,128]{1,0:T(8,128)S(1)}, f32[256,128]{1,0:T(8,128)S(1)}, u32[]{:S(2)}, u32[]{:S(2)}) collective-permute-start(f32[256,128]{1,0:T(8,128)S(1)} %get-tuple-element.7), channel_id=1, source_target_pairs={{0,2},{1,3},{2,0},{3,1},{4,6},{5,7},{6,4},{7,5},{8,10},{9,11},{10,... | collective-permute-start | bytes 393224 | tf_op jit(solution)/shard_map/ppermute | solution.py:79
  125.8 4.6 %collective-permute-done.21 = f32[256,128]{1,0:T(8,128)S(1)} collective-permute-done((f32[256,128]{1,0:T(8,128)S(1)}, f32[256,128]{1,0:T(8,128)S(1)}, u32[]{:S(2)}, u32[]{:S(2)}) %collective-permute-start.21) | collective-permute-done | bytes 131104 | tf_op jit(solution)/shard_map/ppermute | solution.py:79
  131.2 9.8 %custom-call.6 = f32[1,128,128]{1,2,0:T(8,128)S(1)} custom-call(f32[1,128,128]{2,1,0:T(8,128)S(1)} %fusion.11), custom_call_target="InvertDiagBlocksLowerTriangular" | custom-call | tf_op jit(solution)/shard_map/jit(_solve_triangular)/triangular_solve | solution.py:112
  142.4 1.8 %collective-permute-start.24 = (f32[128,128]{0,1:T(8,128)S(1)}, f32[128,128]{0,1:T(8,128)S(1)}, u32[]{:S(2)}, u32[]{:S(2)}) collective-permute-start(f32[128,128]{0,1:T(8,128)S(1)} %fusion.26), channel_id=1, source_target_pairs={{0,8},{4,12},{8,0},{12,4},{1,9},{5,13},{9,1},{13,5},{2,10},{6,14},... | collective-permute-start | bytes 196616 | tf_op jit(solution)/shard_map/ppermute | solution.py:44
  144.3 2.6 %collective-permute-done.24 = f32[128,128]{0,1:T(8,128)S(1)} collective-permute-done((f32[128,128]{0,1:T(8,128)S(1)}, f32[128,128]{0,1:T(8,128)S(1)}, u32[]{:S(2)}, u32[]{:S(2)}) %collective-permute-start.24) | collective-permute-done | bytes 65568 | tf_op jit(solution)/shard_map/ppermute | solution.py:44
  146.9 1.3 collective-permute-done.25
  148.4 11.9 %cholesky.55 = f32[128,128]{1,0:T(8,128)S(1)} custom-call(f32[128,128]{1,0:T(8,128)S(1)} %fusion.15), custom_call_target="Cholesky" | custom-call | tf_op jit(solution)/shard_map/jit(cholesky)/cholesky | solution.py:108
  161.7 9.8 %custom-call.7 = f32[1,128,128]{1,2,0:T(8,128)S(1)} custom-call(f32[1,128,128]{2,1,0:T(8,128)S(1)} %fusion.12), custom_call_target="InvertDiagBlocksLowerTriangular" | custom-call | tf_op jit(solution)/shard_map/jit(_solve_triangular)/triangular_solve | solution.py:112
  172.2 0.8 copy.24
  (93 shorter events, 14.6 us)
Async XLA Ops:
  0.6 9.4 %copy-start = (bf16[8,1024,128]{2,1,0:T(8,128)(2,1)S(1)}, bf16[8,1024,128]{2,1,0:T(8,128)(2,1)}, u32[]{:S(2)}) copy-start(bf16[8,1024,128]{2,1,0:T(8,128)(2,1)} %param.9) | copy-start | bytes 6291460
  0.6 9.4 %copy-start.5 = (bf16[1024,8,16]{0,2,1:T(8,128)(2,1)S(1)}, bf16[1024,8,16]{0,2,1:T(8,128)(2,1)}, u32[]{:S(2)}) copy-start(bf16[1024,8,16]{0,2,1:T(8,128)(2,1)} %param.7) | copy-start | bytes 786436
  2.9 3.2 %collective-permute-start = (f32[8,128,16]{1,2,0:T(8,128)S(1)}, f32[8,128,16]{1,2,0:T(8,128)S(1)}, u32[]{:S(2)}, u32[]{:S(2)}) collective-permute-start(f32[8,128,16]{1,2,0:T(8,128)S(1)} %fusion.27), channel_id=1, source_target_pairs={{0,4},{4,0},{8,12},{12,8},{1,5},{5,1},{9,13},{13,9},{2,6},{6,2},{1... | collective-permute-start | bytes 196616 | tf_op jit(solution)/shard_map/ppermute | solution.py:44
  3.4 5.2 %collective-permute-start.1 = (f32[8,128,16]{1,2,0:T(8,128)S(1)}, f32[8,128,16]{1,2,0:T(8,128)S(1)}, u32[]{:S(2)}, u32[]{:S(2)}) collective-permute-start(f32[8,128,16]{1,2,0:T(8,128)S(1)} %fusion.27), channel_id=1, source_target_pairs={{0,8},{4,12},{8,0},{12,4},{1,9},{5,13},{9,1},{13,5},{2,10},{6,14},... | collective-permute-start | bytes 196616 | tf_op jit(solution)/shard_map/ppermute | solution.py:44
  6.0 4.1 %collective-permute-start.2 = (f32[8,128,16]{1,2,0:T(8,128)S(1)}, f32[8,128,16]{1,2,0:T(8,128)S(1)}, u32[]{:S(2)}, u32[]{:S(2)}) collective-permute-start(f32[8,128,16]{1,2,0:T(8,128)S(1)} %fusion.27), channel_id=1, source_target_pairs={{0,12},{4,8},{8,4},{12,0},{1,13},{5,9},{9,5},{13,1},{2,14},{6,10},... | collective-permute-start | bytes 196616 | tf_op jit(solution)/shard_map/ppermute | solution.py:44
  10.9 5.8 %collective-permute-start.10 = (bf16[1,512,128]{1,2,0:T(8,128)(2,1)S(1)}, bf16[1,512,128]{1,2,0:T(8,128)(2,1)S(1)}, u32[]{:S(2)}, u32[]{:S(2)}) collective-permute-start(bf16[1,512,128]{1,2,0:T(8,128)(2,1)S(1)} %bitcast.109), channel_id=1, source_target_pairs={{0,16},{16,0},{1,17},{17,1},{2,18},{18,2},{3,19},{19,3},{4,20},{20... | collective-permute-start | bytes 393224 | tf_op jit(solution)/shard_map/ppermute | solution.py:53
  12.4 9.1 %collective-permute-start.7 = (bf16[1,512,128]{1,2,0:T(8,128)(2,1)S(1)}, bf16[1,512,128]{1,2,0:T(8,128)(2,1)S(1)}, u32[]{:S(2)}, u32[]{:S(2)}) collective-permute-start(bf16[1,512,128]{1,2,0:T(8,128)(2,1)S(1)} %bitcast.106), channel_id=1, source_target_pairs={{0,2},{1,3},{2,0},{3,1},{4,6},{5,7},{6,4},{7,5},{8,10},{9,11},{10,... | collective-permute-start | bytes 393224 | tf_op jit(solution)/shard_map/ppermute | solution.py:53
  15.0 8.2 %collective-permute-start.3 = (bf16[1024,128]{0,1:T(8,128)(2,1)S(1)}, bf16[1024,128]{0,1:T(8,128)(2,1)}, u32[]{:S(2)}, u32[]{:S(2)}) collective-permute-start(bf16[1024,128]{0,1:T(8,128)(2,1)S(1)} %bitcast.97), channel_id=1, source_target_pairs={{1,4},{2,8},{3,12},{4,1},{6,9},{7,13},{8,2},{9,6},{11,14},{12,3},{... | collective-permute-start | bytes 786440 | tf_op jit(solution)/shard_map/ppermute | solution.py:136
  16.8 33.9 %collective-permute-start.11 = (bf16[2,512,128]{2,1,0:T(8,128)(2,1)S(1)}, bf16[2,512,128]{2,1,0:T(8,128)(2,1)S(1)}, u32[]{:S(2)}, u32[]{:S(2)}) collective-permute-start(bf16[2,512,128]{2,1,0:T(8,128)(2,1)S(1)} %bitcast.100), channel_id=1, source_target_pairs={{0,2},{1,3},{2,0},{3,1},{4,6},{5,7},{6,4},{7,5},{8,10},{9,11},{10,... | collective-permute-start | bytes 786440 | tf_op jit(solution)/shard_map/ppermute | solution.py:53
  24.0 6.9 %collective-permute-start.4 = (bf16[1,1024,128]{1,2,0:T(8,128)(2,1)}, bf16[1,1024,128]{1,2,0:T(8,128)(2,1)}, u32[]{:S(2)}, u32[]{:S(2)}) collective-permute-start(bf16[1,1024,128]{1,2,0:T(8,128)(2,1)} %get-tuple-element.10), channel_id=1, source_target_pairs={{0,16},{16,0},{1,17},{17,1},{2,18},{18,2},{3,19},{19,3},{4,20},{20... | collective-permute-start | bytes 786440 | tf_op jit(solution)/shard_map/ppermute | solution.py:53
  26.1 27.1 %collective-permute-start.8 = (bf16[2,512,128]{2,1,0:T(8,128)(2,1)S(1)}, bf16[2,512,128]{2,1,0:T(8,128)(2,1)}, u32[]{:S(2)}, u32[]{:S(2)}) collective-permute-start(bf16[2,512,128]{2,1,0:T(8,128)(2,1)S(1)} %bitcast.101), channel_id=1, source_target_pairs={{0,1},{1,0},{2,3},{3,2},{4,5},{5,4},{6,7},{7,6},{8,9},{9,8},{10,11... | collective-permute-start | bytes 786440 | tf_op jit(solution)/shard_map/ppermute | solution.py:53
  32.8 26.7 %collective-permute-start.5 = (bf16[2,1024,128]{2,1,0:T(8,128)(2,1)}, bf16[2,1024,128]{2,1,0:T(8,128)(2,1)S(1)}, u32[]{:S(2)}, u32[]{:S(2)}) collective-permute-start(bf16[2,1024,128]{2,1,0:T(8,128)(2,1)} %bitcast.7), channel_id=1, source_target_pairs={{0,8},{4,12},{8,0},{12,4},{1,9},{5,13},{9,1},{13,5},{2,10},{6,14},... | collective-permute-start | bytes 1572872 | tf_op jit(solution)/shard_map/ppermute | solution.py:53
  51.5 13.0 %collective-permute-start.12 = (bf16[4,512,128]{2,1,0:T(8,128)(2,1)}, bf16[4,512,128]{2,1,0:T(8,128)(2,1)}, u32[]{:S(2)}, u32[]{:S(2)}) collective-permute-start(bf16[4,512,128]{2,1,0:T(8,128)(2,1)} %bitcast.31), channel_id=1, source_target_pairs={{0,1},{1,0},{2,3},{3,2},{4,5},{5,4},{6,7},{7,6},{8,9},{9,8},{10,11... | collective-permute-start | bytes 1572872 | tf_op jit(solution)/shard_map/ppermute | solution.py:53
  54.9 12.7 %collective-permute-start.9 = (bf16[4,512,128]{2,1,0:T(8,128)(2,1)}, bf16[4,512,128]{2,1,0:T(8,128)(2,1)}, u32[]{:S(2)}, u32[]{:S(2)}) collective-permute-start(bf16[4,512,128]{2,1,0:T(8,128)(2,1)} %bitcast.20), channel_id=1, source_target_pairs={{0,16},{16,0},{1,17},{17,1},{2,18},{18,2},{3,19},{19,3},{4,20},{20... | collective-permute-start | bytes 1572872 | tf_op jit(solution)/shard_map/ppermute | solution.py:53
  59.6 9.5 %collective-permute-start.6 = (bf16[4,1024,128]{2,1,0:T(8,128)(2,1)S(1)}, bf16[4,1024,128]{2,1,0:T(8,128)(2,1)}, u32[]{:S(2)}, u32[]{:S(2)}) collective-permute-start(bf16[4,1024,128]{2,1,0:T(8,128)(2,1)S(1)} %bitcast.96), channel_id=1, source_target_pairs={{0,4},{4,0},{8,12},{12,8},{1,5},{5,1},{9,13},{13,9},{2,6},{6,2},{1... | collective-permute-start | bytes 3145736 | tf_op jit(solution)/shard_map/ppermute | solution.py:53
  65.5 5.0 %copy-start.4 = (bf16[2,2,2,512,128]{4,3,2,1,0:T(8,128)(2,1)}, bf16[2,2,2,512,128]{4,3,2,1,0:T(8,128)(2,1)S(1)}, u32[]{:S(2)}) copy-start(bf16[2,2,2,512,128]{4,3,2,1,0:T(8,128)(2,1)S(1)} %constant_dynamic-update-slice_fusion.6) | copy-start | bytes 3145732
  68.7 1.8 %copy-start.3 = (bf16[1,2,4,512,128]{4,3,2,1,0:T(8,128)(2,1)}, bf16[1,2,4,512,128]{4,3,2,1,0:T(8,128)(2,1)S(1)}, u32[]{:S(2)}) copy-start(bf16[1,2,4,512,128]{4,3,2,1,0:T(8,128)(2,1)S(1)} %bitcast_dynamic-update-slice_fusion.3) | copy-start | bytes 3145732
  70.5 2.4 %copy-start.2 = (bf16[2,2,2,1024,128]{4,3,2,1,0:T(8,128)(2,1)}, bf16[2,2,2,1024,128]{4,3,2,1,0:T(8,128)(2,1)S(1)}, u32[]{:S(2)}) copy-start(bf16[2,2,2,1024,128]{4,3,2,1,0:T(8,128)(2,1)S(1)} %constant_dynamic-update-slice_fusion.11) | copy-start | bytes 6291460
  72.9 4.9 %copy-start.1 = (f32[1024,1024]{1,0:T(8,128)}, f32[1024,1024]{1,0:T(8,128)S(1)}, u32[]{:S(2)}) copy-start(f32[1024,1024]{1,0:T(8,128)S(1)} %bitcast_multiply_fusion.2) | copy-start | bytes 12582916
  77.8 2.0 %collective-permute-start.13 = (f32[1024,128]{1,0:T(8,128)S(1)}, f32[1024,128]{1,0:T(8,128)S(1)}, u32[]{:S(2)}, u32[]{:S(2)}) collective-permute-start(f32[1024,128]{1,0:T(8,128)S(1)} %fusion.7), channel_id=1, source_target_pairs={{0,4},{4,0},{8,12},{12,8},{1,5},{5,1},{9,13},{13,9},{2,6},{6,2},{1... | collective-permute-start | bytes 1572872 | tf_op jit(solution)/shard_map/ppermute | solution.py:93
  79.9 8.4 %collective-permute-start.14 = (f32[512,128]{1,0:T(8,128)S(1)}, f32[512,128]{1,0:T(8,128)S(1)}, u32[]{:S(2)}, u32[]{:S(2)}) collective-permute-start(f32[512,128]{1,0:T(8,128)S(1)} %slice_select_fusion), channel_id=1, source_target_pairs={{0,8},{4,12},{8,0},{12,4},{1,9},{5,13},{9,1},{13,5},{2,10},{6,14},... | collective-permute-start | bytes 786440 | tf_op jit(solution)/shard_map/ppermute | solution.py:96
  88.4 4.7 %collective-permute-start.15 = (f32[512,128]{1,0:T(8,128)S(1)}, f32[512,128]{1,0:T(8,128)S(1)}, u32[]{:S(2)}, u32[]{:S(2)}) collective-permute-start(f32[512,128]{1,0:T(8,128)S(1)} %get-tuple-element.9), channel_id=1, source_target_pairs={{0,4},{4,0},{8,12},{12,8},{1,5},{5,1},{9,13},{13,9},{2,6},{6,2},{1... | collective-permute-start | bytes 786440 | tf_op jit(solution)/shard_map/ppermute | solution.py:97
  94.1 8.2 %collective-permute-start.16 = (f32[128,128]{0,1:T(8,128)S(1)}, f32[128,128]{0,1:T(8,128)S(1)}, u32[]{:S(2)}, u32[]{:S(2)}) collective-permute-start(f32[128,128]{0,1:T(8,128)S(1)} %fusion.25), channel_id=1, source_target_pairs={{0,1},{1,0},{2,3},{3,2},{4,5},{5,4},{6,7},{7,6},{8,9},{9,8},{10,11... | collective-permute-start | bytes 196616 | tf_op jit(solution)/shard_map/ppermute | solution.py:44
  95.1 8.6 %collective-permute-start.17 = (f32[128,128]{0,1:T(8,128)S(1)}, f32[128,128]{0,1:T(8,128)S(1)}, u32[]{:S(2)}, u32[]{:S(2)}) collective-permute-start(f32[128,128]{0,1:T(8,128)S(1)} %fusion.25), channel_id=1, source_target_pairs={{0,2},{1,3},{2,0},{3,1},{4,6},{5,7},{6,4},{7,5},{8,10},{9,11},{10,... | collective-permute-start | bytes 196616 | tf_op jit(solution)/shard_map/ppermute | solution.py:44
  96.3 7.4 %collective-permute-start.18 = (f32[128,128]{0,1:T(8,128)S(1)}, f32[128,128]{0,1:T(8,128)S(1)}, u32[]{:S(2)}, u32[]{:S(2)}) collective-permute-start(f32[128,128]{0,1:T(8,128)S(1)} %fusion.25), channel_id=1, source_target_pairs={{0,3},{1,2},{2,1},{3,0},{4,7},{5,6},{6,5},{7,4},{8,11},{9,10},{10,... | collective-permute-start | bytes 196616 | tf_op jit(solution)/shard_map/ppermute | solution.py:44
  102.2 7.9 %collective-permute-start.19 = (f32[512,128]{1,0:T(8,128)S(1)}, f32[512,128]{1,0:T(8,128)S(1)}, u32[]{:S(2)}, u32[]{:S(2)}) collective-permute-start(f32[512,128]{1,0:T(8,128)S(1)} %slice_select_fusion.1), channel_id=1, source_target_pairs={{0,1},{1,0},{2,3},{3,2},{4,5},{5,4},{6,7},{7,6},{8,9},{9,8},{10,11... | collective-permute-start | bytes 786440 | tf_op jit(solution)/shard_map/ppermute | solution.py:76
  110.2 12.1 %collective-permute-start.20 = (f32[256,128]{1,0:T(8,128)S(1)}, f32[256,128]{1,0:T(8,128)S(1)}, u32[]{:S(2)}, u32[]{:S(2)}) collective-permute-start(f32[256,128]{1,0:T(8,128)S(1)} %slice_select_fusion.2), channel_id=1, source_target_pairs={{0,2},{1,3},{2,0},{3,1},{4,6},{5,7},{6,4},{7,5},{8,10},{9,11},{10,... | collective-permute-start | bytes 393224 | tf_op jit(solution)/shard_map/ppermute | solution.py:76
  122.4 8.0 %collective-permute-start.21 = (f32[256,128]{1,0:T(8,128)S(1)}, f32[256,128]{1,0:T(8,128)S(1)}, u32[]{:S(2)}, u32[]{:S(2)}) collective-permute-start(f32[256,128]{1,0:T(8,128)S(1)} %get-tuple-element.7), channel_id=1, source_target_pairs={{0,2},{1,3},{2,0},{3,1},{4,6},{5,7},{6,4},{7,5},{8,10},{9,11},{10,... | collective-permute-start | bytes 393224 | tf_op jit(solution)/shard_map/ppermute | solution.py:79
  130.4 10.6 %collective-permute-start.22 = (f32[512,128]{1,0:T(8,128)S(1)}, f32[512,128]{1,0:T(8,128)S(1)}, u32[]{:S(2)}, u32[]{:S(2)}) collective-permute-start(f32[512,128]{1,0:T(8,128)S(1)} %constant_dynamic-update-slice_fusion.2), channel_id=1, source_target_pairs={{0,1},{1,0},{2,3},{3,2},{4,5},{5,4},{6,7},{7,6},{8,9},{9,8},{10,11... | collective-permute-start | bytes 786440 | tf_op jit(solution)/shard_map/ppermute | solution.py:79
  142.4 1.9 %collective-permute-start.23 = (f32[128,128]{0,1:T(8,128)S(1)}, f32[128,128]{0,1:T(8,128)S(1)}, u32[]{:S(2)}, u32[]{:S(2)}) collective-permute-start(f32[128,128]{0,1:T(8,128)S(1)} %fusion.26), channel_id=1, source_target_pairs={{0,4},{4,0},{8,12},{12,8},{1,5},{5,1},{9,13},{13,9},{2,6},{6,2},{1... | collective-permute-start | bytes 196616 | tf_op jit(solution)/shard_map/ppermute | solution.py:44
  142.4 4.5 %collective-permute-start.24 = (f32[128,128]{0,1:T(8,128)S(1)}, f32[128,128]{0,1:T(8,128)S(1)}, u32[]{:S(2)}, u32[]{:S(2)}) collective-permute-start(f32[128,128]{0,1:T(8,128)S(1)} %fusion.26), channel_id=1, source_target_pairs={{0,8},{4,12},{8,0},{12,4},{1,9},{5,13},{9,1},{13,5},{2,10},{6,14},... | collective-permute-start | bytes 196616 | tf_op jit(solution)/shard_map/ppermute | solution.py:44
  144.2 4.1 %collective-permute-start.25 = (f32[128,128]{0,1:T(8,128)S(1)}, f32[128,128]{0,1:T(8,128)S(1)}, u32[]{:S(2)}, u32[]{:S(2)}) collective-permute-start(f32[128,128]{0,1:T(8,128)S(1)} %fusion.26), channel_id=1, source_target_pairs={{0,12},{4,8},{8,4},{12,0},{1,13},{5,9},{9,5},{13,1},{2,14},{6,10},... | collective-permute-start | bytes 196616 | tf_op jit(solution)/shard_map/ppermute | solution.py:44

commit v14 on v13

--- a/solution.py
+++ b/solution.py
@@ -99,6 +99,27 @@
     both = jnp.zeros(x.shape, x.dtype)
     both = lax.dynamic_update_slice_in_dim(both, mine, first, 0)
     return lax.dynamic_update_slice_in_dim(both, other, half - first, 0)
+
+
+def _scatter_gather_sum(x, axis):
+    count = lax.axis_size(axis)
+    if count != 4 or x.shape[0] % count:
+        return _halving_sum(x, axis)
+    here = lax.axis_index(axis)
+    quarter = x.shape[0] // count
+    parts = x.reshape((count, quarter) + x.shape[1:])
+    got = [parts[here]]
+    for k in (1, 2, 3):
+        got.append(lax.ppermute(parts[here ^ k], axis, [(i, i ^ k) for i in range(count)]))
+    got = jnp.stack(got)
+    terms = [got[here ^ j] for j in range(count)]
+    mine = (terms[0] + terms[1]) + (terms[2] + terms[3])
+    whole = jnp.zeros(parts.shape, x.dtype)
+    whole = lax.dynamic_update_slice_in_dim(whole, mine[None], here, 0)
+    for k in (1, 2, 3):
+        other = lax.ppermute(mine, axis, [(i, i ^ k) for i in range(count)])
+        whole = lax.dynamic_update_slice_in_dim(whole, other[None], here ^ k, 0)
+    return whole.reshape(x.shape)
 
 
 def _lower_factor(image, gram_axis):
@@ -169,12 +190,12 @@
                 covariance, block, precision=lax.Precision.HIGHEST,
                 preferred_element_type=jnp.float32,
             )
-            return _pair_split_sum(partial_image, "row")
+            return _scatter_gather_sum(partial_image, "row")
         partial_image = jnp.dot(
             covariance_t, block, precision=lax.Precision.HIGHEST,
             preferred_element_type=jnp.float32,
         )
-        return _halving_sum(partial_image, "col")
+        return _scatter_gather_sum(partial_image, "col")
 
     basis_rows = lax.dynamic_slice_in_dim(start_basis, row_here * rows_here, rows_here, 0)
     image = cov_times(basis_rows, True)

time: 173 us -> 184 us (1.064)
  waiting for transfers between devices: 37.9 us -> 56.9 us
  starting transfers between devices: 46.8 us -> 37.6 us
    ppermute x9, waiting for transfers between devices: 7.59 us -> 29.2 us  [_butterfly_gather(): other = lax.ppermute(x, axis, [(i, i ^ step) for i in range(count)])]
    ppermute x9, starting transfers between devices: 32.2 us -> 14.2 us  [_butterfly_gather(): other = lax.ppermute(x, axis, [(i, i ^ step) for i in range(count)])]
    ppermute x7 -> x12, starting transfers between devices: 3.69 us -> 13 us  [the longest x6 6.56 us: _scatter_gather_sum(): lax.ppermute(parts[here ^ k], axis, [(i, i ^ k) for i in range(count)])]
    ppermute x9, waiting for transfers between devices: 9.35 us -> 7.11 us  [_direct_sum(): lax.ppermute(x, axis, [(i, i ^ k) for i in range(count)])]
    ppermute x7 -> x12, waiting for transfers between devices: 21 us -> 20.6 us  [the longest x6 13.8 us: _scatter_gather_sum(): other = lax.ppermute(mine, axis, [(i, i ^ k) for i in range(count)])]
  transfers between devices with their start and end apart: 26 -> 31, of which waited for: 13 -> 12; matrix products, arithmetic and copies ran while one was open for 28% -> 26% of each run, Pallas kernels for 0% -> 0%
where the time goes in v14:
time: 184 us
  waiting for transfers between devices  56.9 us (31%)
  other arithmetic  47.9 us (26%)
  starting transfers between devices  37.6 us (20%)
  matrix products  20.2 us (11%)
  local copies, waits for them, and re-layouts  20 us (11%)
    ppermute x9, waiting for transfers between devices, _butterfly_gather(): other = lax.ppermute(x, axis, [(i, i ^ step) for i in range(count)])  29.2 us
    another operation x6, other arithmetic, _lower_factor(): return jnp.linalg.cholesky(_direct_sum(gram_part, gram_axis))  25 us
    another operation x4, other arithmetic, _right_solve(): jax.scipy.linalg.solve_triangular(lower_factor, image.T, lower=True)  20.9 us
    ppermute x9, starting transfers between devices, _butterfly_gather(): other = lax.ppermute(x, axis, [(i, i ^ step) for i in range(count)])  14.2 us
    ppermute x6, waiting for transfers between devices, _scatter_gather_sum(): other = lax.ppermute(mine, axis, [(i, i ^ k) for i in range(count)])  13.8 us
    ppermute x9, starting transfers between devices, _direct_sum(): lax.ppermute(x, axis, [(i, i ^ k) for i in range(count)])  8.98 us
    dynamic_update_slice x9, local copies, waits for them, and re-layouts, _butterfly_gather(): both = lax.dynamic_update_slice_in_dim(both, theirs, 1 - first, 1)  7.22 us
    ppermute x9, waiting for transfers between devices, _direct_sum(): lax.ppermute(x, axis, [(i, i ^ k) for i in range(count)])  7.11 us
  transfers between devices with their start and end apart: 31, of which 12 were waited for; matrix products, arithmetic and copies ran while one was open for 26% of the time, Pallas kernels for 0%

profile of v14, /device:TPU:0, one launch (start us, length us, event | category | flops | bytes accessed | tf_op | source)
XLA Modules:
  0.0 183.7 jit_solution(17186197960375396812)
XLA Ops:
  0.7 2.2 %fusion.22 = f32[8,128,16]{1,2,0:T(8,128)S(1)} fusion(bf16[1024,8,16]{0,2,1:T(8,128)(2,1)} %param.7, bf16[8,1024,128]{2,1,0:T(8,128)(2,1)} %param.8), kind=kOutput, calls=%fused_computation.79 | convolution fusion | flops 33554432 | bytes 2424832 | tf_op jit(solution)/shard_map/mbs,bmr->brs/dot_general | solution.py:143
  2.9 3.0 %collective-permute-start.1 = (f32[8,128,16]{1,2,0:T(8,128)S(1)}, f32[8,128,16]{1,2,0:T(8,128)S(1)}, u32[]{:S(2)}, u32[]{:S(2)}) collective-permute-start(f32[8,128,16]{1,2,0:T(8,128)S(1)} %fusion.22), channel_id=1, source_target_pairs={{0,8},{4,12},{8,0},{12,4},{1,9},{5,13},{9,1},{13,5},{2,10},{6,14},... | collective-permute-start | bytes 196616 | tf_op jit(solution)/shard_map/ppermute | solution.py:44
  6.1 2.1 %collective-permute-done.1 = f32[8,128,16]{1,2,0:T(8,128)S(1)} collective-permute-done((f32[8,128,16]{1,2,0:T(8,128)S(1)}, f32[8,128,16]{1,2,0:T(8,128)S(1)}, u32[]{:S(2)}, u32[]{:S(2)}) %collective-permute-start.1) | collective-permute-done | bytes 65568 | tf_op jit(solution)/shard_map/ppermute | solution.py:44
  8.1 1.9 %collective-permute-done.2 = f32[8,128,16]{1,2,0:T(8,128)S(1)} collective-permute-done((f32[8,128,16]{1,2,0:T(8,128)S(1)}, f32[8,128,16]{1,2,0:T(8,128)S(1)}, u32[]{:S(2)}, u32[]{:S(2)}) %collective-permute-start.2) | collective-permute-done | bytes 65568 | tf_op jit(solution)/shard_map/ppermute | solution.py:44
  10.7 1.4 collective-permute-start.3
  12.2 1.6 collective-permute-start.10
  13.8 3.7 %collective-permute-start.7 = (bf16[1,512,128]{1,2,0:T(8,128)(2,1)S(1)}, bf16[1,512,128]{1,2,0:T(8,128)(2,1)S(1)}, u32[]{:S(2)}, u32[]{:S(2)}) collective-permute-start(bf16[1,512,128]{1,2,0:T(8,128)(2,1)S(1)} %bitcast.154), channel_id=1, source_target_pairs={{0,2},{1,3},{2,0},{3,1},{4,6},{5,7},{6,4},{7,5},{8,10},{9,11},{10,... | collective-permute-start | bytes 393224 | tf_op jit(solution)/shard_map/ppermute | solution.py:53
  18.0 3.9 %collective-permute-start.11 = (bf16[2,512,128]{2,1,0:T(8,128)(2,1)S(1)}, bf16[2,512,128]{2,1,0:T(8,128)(2,1)S(1)}, u32[]{:S(2)}, u32[]{:S(2)}) collective-permute-start(bf16[2,512,128]{2,1,0:T(8,128)(2,1)S(1)} %bitcast.148), channel_id=1, source_target_pairs={{0,2},{1,3},{2,0},{3,1},{4,6},{5,7},{6,4},{7,5},{8,10},{9,11},{10,... | collective-permute-start | bytes 786440 | tf_op jit(solution)/shard_map/ppermute | solution.py:53
  21.9 17.6 %collective-permute-done.7 = bf16[1,512,128]{1,2,0:T(8,128)(2,1)S(1)} collective-permute-done((bf16[1,512,128]{1,2,0:T(8,128)(2,1)S(1)}, bf16[1,512,128]{1,2,0:T(8,128)(2,1)S(1)}, u32[]{:S(2)}, u32[]{:S(2)}) %collective-permute-start.7) | collective-permute-done | bytes 131104 | tf_op jit(solution)/shard_map/ppermute | solution.py:53
  41.9 1.9 %collective-permute-start.4 = (bf16[1,1024,128]{1,2,0:T(8,128)(2,1)}, bf16[1,1024,128]{1,2,0:T(8,128)(2,1)}, u32[]{:S(2)}, u32[]{:S(2)}) collective-permute-start(bf16[1,1024,128]{1,2,0:T(8,128)(2,1)} %get-tuple-element.20), channel_id=1, source_target_pairs={{0,16},{16,0},{1,17},{17,1},{2,18},{18,2},{3,19},{19,3},{4,20},{20... | collective-permute-start | bytes 786440 | tf_op jit(solution)/shard_map/ppermute | solution.py:53
  47.2 4.2 %collective-permute-done.4 = bf16[1,1024,128]{1,2,0:T(8,128)(2,1)} collective-permute-done((bf16[1,1024,128]{1,2,0:T(8,128)(2,1)}, bf16[1,1024,128]{1,2,0:T(8,128)(2,1)}, u32[]{:S(2)}, u32[]{:S(2)}) %collective-permute-start.4) | collective-permute-done | bytes 262176 | tf_op jit(solution)/shard_map/ppermute | solution.py:53
  51.4 1.1 copy.36
  54.0 1.5 collective-permute-start.12
  55.4 1.7 bitcast_dynamic-update-slice_fusion.8
  57.1 1.5 collective-permute-start.9
  58.8 1.1 bitcast_dynamic-update-slice_fusion.1
  59.9 7.4 %collective-permute-done.5 = bf16[2,1024,128]{2,1,0:T(8,128)(2,1)S(1)} collective-permute-done((bf16[2,1024,128]{2,1,0:T(8,128)(2,1)}, bf16[2,1024,128]{2,1,0:T(8,128)(2,1)S(1)}, u32[]{:S(2)}, u32[]{:S(2)}) %collective-permute-start.5) | collective-permute-done | bytes 524320 | tf_op jit(solution)/shard_map/ppermute | solution.py:53
  67.6 1.1 bitcast_dynamic-update-slice_fusion.4
  68.9 1.1 bitcast_dynamic-update-slice_fusion.2
  70.0 1.1 constant_dynamic-update-slice_fusion.2
  71.2 1.5 bitcast_dynamic-update-slice_fusion.3
  73.1 1.4 constant_dynamic-update-slice_fusion.7
  74.5 2.4 %bitcast_multiply_fusion.1 = f32[1024,1024]{1,0:T(8,128)S(1)} fusion(bf16[8,1024,128]{2,1,0:T(8,128)(2,1)S(1)} %bitcast.144, bf16[8,512,128]{2,1,0:T(8,128)(2,1)S(1)} %bitcast.152, bf16[8,512,128]{2,1,0:T(8,128)(2,1)S(1)} %bitcast.150), kind=kOutput, calls=%fused_computation.1 | convolution fusion | flops 2152726528 | bytes 8388608 | tf_op jit(solution)/shard_map/dot_general | solution.py:180
  76.9 4.9 %fusion.2 = f32[1024,128]{1,0:T(8,128)S(1)} fusion(f32[1024,1024]{1,0:T(8,128)S(1)} %bitcast_multiply_fusion.1, f32[4096,128]{1,0:T(8,128)} %param.10, s32[]{:T(128)S(6)} %select_n.117), kind=kOutput, calls=%fused_computation.15 | convolution fusion | flops 1610612736 | bytes 5242884 | tf_op jit(solution)/shard_map/dot_general | solution.py:189
  82.9 1.7 collective-permute-start.14
  84.7 3.2 %collective-permute-done.15 = f32[256,128]{1,0:T(8,128)S(1)} collective-permute-done((f32[256,128]{1,0:T(8,128)}, f32[256,128]{1,0:T(8,128)S(1)}, u32[]{:S(2)}, u32[]{:S(2)}) %collective-permute-start.15) | collective-permute-done | bytes 131104 | tf_op jit(solution)/shard_map/ppermute | solution.py:113
  87.9 3.6 %collective-permute-done.14 = f32[256,128]{1,0:T(8,128)} collective-permute-done((f32[256,128]{1,0:T(8,128)}, f32[256,128]{1,0:T(8,128)}, u32[]{:S(2)}, u32[]{:S(2)}) %collective-permute-start.14) | collective-permute-done | bytes 131104 | tf_op jit(solution)/shard_map/ppermute | solution.py:113
  91.5 1.0 pad_maximum_fusion.3
  92.7 3.6 %bitcast_multiply_fusion = f32[1024,1024]{1,0:T(8,128)S(1)} fusion(bf16[8,1024,128]{2,1,0:T(8,128)(2,1)S(1)} %bitcast.145, bf16[8,512,128]{2,1,0:T(8,128)(2,1)} %bitcast.153, bf16[8,512,128]{2,1,0:T(8,128)(2,1)S(1)} %bitcast.151), kind=kOutput, calls=%fused_computation | convolution fusion | flops 2152726528 | bytes 8388608 | tf_op jit(solution)/shard_map/dot_general | solution.py:183
  96.7 1.5 collective-permute-start.18
  98.2 4.5 %collective-permute-done.17 = f32[256,128]{1,0:T(8,128)S(1)} collective-permute-done((f32[256,128]{1,0:T(8,128)S(1)}, f32[256,128]{1,0:T(8,128)S(1)}, u32[]{:S(2)}, u32[]{:S(2)}) %collective-permute-start.17) | collective-permute-done | bytes 131104 | tf_op jit(solution)/shard_map/ppermute | solution.py:120
  102.7 1.8 collective-permute-done.18
  104.6 1.0 convolution_bitcast_fusion.1
  105.7 2.4 %collective-permute-start.21 = (f32[128,128]{0,1:T(8,128)S(1)}, f32[128,128]{0,1:T(8,128)S(1)}, u32[]{:S(2)}, u32[]{:S(2)}) collective-permute-start(f32[128,128]{0,1:T(8,128)S(1)} %convolution_bitcast_fusion.1), channel_id=1, source_target_pairs={{0,3},{1,2},{2,1},{3,0},{4,7},{5,6},{6,5},{7,4},{8,11},{9,10},{10,... | collective-permute-start | bytes 196616 | tf_op jit(solution)/shard_map/ppermute | solution.py:44
  108.0 1.1 collective-permute-start.19
  109.1 3.6 %fusion.20 = f32[4,256,128]{2,1,0:T(8,128)S(1)} fusion(f32[4,256,1024]{2,1,0:T(8,128)S(1)} %bitcast.141, f32[1024,128,1]{1,0,2:T(8,128)S(1)} %bitcast.140), kind=kOutput, calls=%fused_computation.77 | convolution fusion | flops 1610612736 | bytes 5242880 | tf_op jit(solution)/shard_map/dot_general | solution.py:194
  113.8 1.5 collective-permute-start.23
  115.3 2.0 %collective-permute-start.22 = (f32[256,128]{1,0:T(8,128)S(1)}, f32[256,128]{1,0:T(8,128)S(1)}, u32[]{:S(2)}, u32[]{:S(2)}) collective-permute-start(f32[256,128]{1,0:T(8,128)S(1)} %get-tuple-element.15), channel_id=1, source_target_pairs={{0,1},{1,0},{2,3},{3,2},{4,5},{5,4},{6,7},{7,6},{8,9},{9,8},{10,11... | collective-permute-start | bytes 393224 | tf_op jit(solution)/shard_map/ppermute | solution.py:113
  117.4 11.7 %cholesky.44 = f32[128,128]{1,0:T(8,128)S(1)} custom-call(f32[128,128]{1,0:T(8,128)S(1)} %fusion.13), custom_call_target="Cholesky" | custom-call | tf_op jit(solution)/shard_map/jit(cholesky)/cholesky | solution.py:129
  130.7 9.8 %custom-call.6 = f32[1,128,128]{1,2,0:T(8,128)S(1)} custom-call(f32[1,128,128]{2,1,0:T(8,128)S(1)} %fusion.6), custom_call_target="InvertDiagBlocksLowerTriangular" | custom-call | tf_op jit(solution)/shard_map/jit(_solve_triangular)/triangular_solve | solution.py:133
  140.5 1.5 collective-permute-start.26
  142.0 2.9 %collective-permute-start.27 = (f32[256,128]{1,0:T(8,128)S(1)}, f32[256,128]{1,0:T(8,128)S(1)}, u32[]{:S(2)}, u32[]{:S(2)}) collective-permute-start(f32[256,128]{1,0:T(8,128)S(1)} %bitcast.162), channel_id=1, source_target_pairs={{0,3},{1,2},{2,1},{3,0},{4,7},{5,6},{6,5},{7,4},{8,11},{9,10},{10,... | collective-permute-start | bytes 393224 | tf_op jit(solution)/shard_map/ppermute | solution.py:120
  145.0 7.4 %collective-permute-done.26 = f32[256,128]{1,0:T(8,128)S(1)} collective-permute-done((f32[256,128]{1,0:T(8,128)S(1)}, f32[256,128]{1,0:T(8,128)S(1)}, u32[]{:S(2)}, u32[]{:S(2)}) %collective-permute-start.26) | collective-permute-done | bytes 131104 | tf_op jit(solution)/shard_map/ppermute | solution.py:120
  153.7 1.0 collective-permute-start.29
  154.7 1.2 collective-permute-start.28
  155.9 2.5 %collective-permute-done.29 = f32[128,128]{0,1:T(8,128)S(1)} collective-permute-done((f32[128,128]{0,1:T(8,128)S(1)}, f32[128,128]{0,1:T(8,128)S(1)}, u32[]{:S(2)}, u32[]{:S(2)}) %collective-permute-start.29) | collective-permute-done | bytes 65568 | tf_op jit(solution)/shard_map/ppermute | solution.py:44
  159.2 11.9 %cholesky.55 = f32[128,128]{1,0:T(8,128)S(1)} custom-call(f32[128,128]{1,0:T(8,128)S(1)} %fusion.10), custom_call_target="Cholesky" | custom-call | tf_op jit(solution)/shard_map/jit(cholesky)/cholesky | solution.py:129
  172.5 9.8 %custom-call.7 = f32[1,128,128]{1,2,0:T(8,128)S(1)} custom-call(f32[1,128,128]{2,1,0:T(8,128)S(1)} %fusion.7), custom_call_target="InvertDiagBlocksLowerTriangular" | custom-call | tf_op jit(solution)/shard_map/jit(_solve_triangular)/triangular_solve | solution.py:133
  (107 shorter events, 19.0 us)
Async XLA Ops:
  0.6 9.4 %copy-start = (bf16[8,1024,128]{2,1,0:T(8,128)(2,1)S(1)}, bf16[8,1024,128]{2,1,0:T(8,128)(2,1)}, u32[]{:S(2)}) copy-start(bf16[8,1024,128]{2,1,0:T(8,128)(2,1)} %param.9) | copy-start | bytes 6291460
  0.6 9.4 %copy-start.7 = (bf16[1024,8,16]{0,2,1:T(8,128)(2,1)S(1)}, bf16[1024,8,16]{0,2,1:T(8,128)(2,1)}, u32[]{:S(2)}) copy-start(bf16[1024,8,16]{0,2,1:T(8,128)(2,1)} %param.7) | copy-start | bytes 786436
  2.9 5.3 %collective-permute-start.1 = (f32[8,128,16]{1,2,0:T(8,128)S(1)}, f32[8,128,16]{1,2,0:T(8,128)S(1)}, u32[]{:S(2)}, u32[]{:S(2)}) collective-permute-start(f32[8,128,16]{1,2,0:T(8,128)S(1)} %fusion.22), channel_id=1, source_target_pairs={{0,8},{4,12},{8,0},{12,4},{1,9},{5,13},{9,1},{13,5},{2,10},{6,14},... | collective-permute-start | bytes 196616 | tf_op jit(solution)/shard_map/ppermute | solution.py:44
  5.9 4.1 %collective-permute-start.2 = (f32[8,128,16]{1,2,0:T(8,128)S(1)}, f32[8,128,16]{1,2,0:T(8,128)S(1)}, u32[]{:S(2)}, u32[]{:S(2)}) collective-permute-start(f32[8,128,16]{1,2,0:T(8,128)S(1)} %fusion.22), channel_id=1, source_target_pairs={{0,12},{4,8},{8,4},{12,0},{1,13},{5,9},{9,5},{13,1},{2,14},{6,10},... | collective-permute-start | bytes 196616 | tf_op jit(solution)/shard_map/ppermute | solution.py:44
  5.9 4.1 %collective-permute-start = (f32[8,128,16]{1,2,0:T(8,128)S(1)}, f32[8,128,16]{1,2,0:T(8,128)S(1)}, u32[]{:S(2)}, u32[]{:S(2)}) collective-permute-start(f32[8,128,16]{1,2,0:T(8,128)S(1)} %fusion.22), channel_id=1, source_target_pairs={{0,4},{4,0},{8,12},{12,8},{1,5},{5,1},{9,13},{13,9},{2,6},{6,2},{1... | collective-permute-start | bytes 196616 | tf_op jit(solution)/shard_map/ppermute | solution.py:44
  10.7 30.4 %collective-permute-start.3 = (bf16[1024,128]{0,1:T(8,128)(2,1)S(1)}, bf16[1024,128]{0,1:T(8,128)(2,1)}, u32[]{:S(2)}, u32[]{:S(2)}) collective-permute-start(bf16[1024,128]{0,1:T(8,128)(2,1)S(1)} %bitcast.143), channel_id=1, source_target_pairs={{1,4},{2,8},{3,12},{4,1},{6,9},{7,13},{8,2},{9,6},{11,14},{12,3},{... | collective-permute-start | bytes 786440 | tf_op jit(solution)/shard_map/ppermute | solution.py:157
  12.2 5.6 %collective-permute-start.10 = (bf16[1,512,128]{1,2,0:T(8,128)(2,1)S(1)}, bf16[1,512,128]{1,2,0:T(8,128)(2,1)S(1)}, u32[]{:S(2)}, u32[]{:S(2)}) collective-permute-start(bf16[1,512,128]{1,2,0:T(8,128)(2,1)S(1)} %bitcast.157), channel_id=1, source_target_pairs={{0,16},{16,0},{1,17},{17,1},{2,18},{18,2},{3,19},{19,3},{4,20},{20... | collective-permute-start | bytes 393224 | tf_op jit(solution)/shard_map/ppermute | solution.py:53
  13.8 25.6 %collective-permute-start.7 = (bf16[1,512,128]{1,2,0:T(8,128)(2,1)S(1)}, bf16[1,512,128]{1,2,0:T(8,128)(2,1)S(1)}, u32[]{:S(2)}, u32[]{:S(2)}) collective-permute-start(bf16[1,512,128]{1,2,0:T(8,128)(2,1)S(1)} %bitcast.154), channel_id=1, source_target_pairs={{0,2},{1,3},{2,0},{3,1},{4,6},{5,7},{6,4},{7,5},{8,10},{9,11},{10,... | collective-permute-start | bytes 393224 | tf_op jit(solution)/shard_map/ppermute | solution.py:53
  18.0 35.3 %collective-permute-start.11 = (bf16[2,512,128]{2,1,0:T(8,128)(2,1)S(1)}, bf16[2,512,128]{2,1,0:T(8,128)(2,1)S(1)}, u32[]{:S(2)}, u32[]{:S(2)}) collective-permute-start(bf16[2,512,128]{2,1,0:T(8,128)(2,1)S(1)} %bitcast.148), channel_id=1, source_target_pairs={{0,2},{1,3},{2,0},{3,1},{4,6},{5,7},{6,4},{7,5},{8,10},{9,11},{10,... | collective-permute-start | bytes 786440 | tf_op jit(solution)/shard_map/ppermute | solution.py:53
  41.9 9.4 %collective-permute-start.4 = (bf16[1,1024,128]{1,2,0:T(8,128)(2,1)}, bf16[1,1024,128]{1,2,0:T(8,128)(2,1)}, u32[]{:S(2)}, u32[]{:S(2)}) collective-permute-start(bf16[1,1024,128]{1,2,0:T(8,128)(2,1)} %get-tuple-element.20), channel_id=1, source_target_pairs={{0,16},{16,0},{1,17},{17,1},{2,18},{18,2},{3,19},{19,3},{4,20},{20... | collective-permute-start | bytes 786440 | tf_op jit(solution)/shard_map/ppermute | solution.py:53
  45.4 10.0 %collective-permute-start.8 = (bf16[2,512,128]{2,1,0:T(8,128)(2,1)S(1)}, bf16[2,512,128]{2,1,0:T(8,128)(2,1)}, u32[]{:S(2)}, u32[]{:S(2)}) collective-permute-start(bf16[2,512,128]{2,1,0:T(8,128)(2,1)S(1)} %bitcast.149), channel_id=1, source_target_pairs={{0,1},{1,0},{2,3},{3,2},{4,5},{5,4},{6,7},{7,6},{8,9},{9,8},{10,11... | collective-permute-start | bytes 786440 | tf_op jit(solution)/shard_map/ppermute | solution.py:53
  53.2 14.1 %collective-permute-start.5 = (bf16[2,1024,128]{2,1,0:T(8,128)(2,1)}, bf16[2,1024,128]{2,1,0:T(8,128)(2,1)S(1)}, u32[]{:S(2)}, u32[]{:S(2)}) collective-permute-start(bf16[2,1024,128]{2,1,0:T(8,128)(2,1)} %bitcast.7), channel_id=1, source_target_pairs={{0,8},{4,12},{8,0},{12,4},{1,9},{5,13},{9,1},{13,5},{2,10},{6,14},... | collective-permute-start | bytes 1572872 | tf_op jit(solution)/shard_map/ppermute | solution.py:53
  54.0 16.1 %collective-permute-start.12 = (bf16[4,512,128]{2,1,0:T(8,128)(2,1)}, bf16[4,512,128]{2,1,0:T(8,128)(2,1)}, u32[]{:S(2)}, u32[]{:S(2)}) collective-permute-start(bf16[4,512,128]{2,1,0:T(8,128)(2,1)} %bitcast.31), channel_id=1, source_target_pairs={{0,1},{1,0},{2,3},{3,2},{4,5},{5,4},{6,7},{7,6},{8,9},{9,8},{10,11... | collective-permute-start | bytes 1572872 | tf_op jit(solution)/shard_map/ppermute | solution.py:53
  57.1 14.1 %collective-permute-start.9 = (bf16[4,512,128]{2,1,0:T(8,128)(2,1)}, bf16[4,512,128]{2,1,0:T(8,128)(2,1)}, u32[]{:S(2)}, u32[]{:S(2)}) collective-permute-start(bf16[4,512,128]{2,1,0:T(8,128)(2,1)} %bitcast.20), channel_id=1, source_target_pairs={{0,16},{16,0},{1,17},{17,1},{2,18},{18,2},{3,19},{19,3},{4,20},{20... | collective-permute-start | bytes 1572872 | tf_op jit(solution)/shard_map/ppermute | solution.py:53
  67.4 5.7 %collective-permute-start.6 = (bf16[4,1024,128]{2,1,0:T(8,128)(2,1)S(1)}, bf16[4,1024,128]{2,1,0:T(8,128)(2,1)}, u32[]{:S(2)}, u32[]{:S(2)}) collective-permute-start(bf16[4,1024,128]{2,1,0:T(8,128)(2,1)S(1)} %bitcast.142), channel_id=1, source_target_pairs={{0,4},{4,0},{8,12},{12,8},{1,5},{5,1},{9,13},{13,9},{2,6},{6,2},{1... | collective-permute-start | bytes 3145736 | tf_op jit(solution)/shard_map/ppermute | solution.py:53
  71.1 3.3 %copy-start.6 = (bf16[2,2,2,512,128]{4,3,2,1,0:T(8,128)(2,1)}, bf16[2,2,2,512,128]{4,3,2,1,0:T(8,128)(2,1)S(1)}, u32[]{:S(2)}) copy-start(bf16[2,2,2,512,128]{4,3,2,1,0:T(8,128)(2,1)S(1)} %constant_dynamic-update-slice_fusion.2) | copy-start | bytes 3145732
  72.7 1.8 %copy-start.4 = (bf16[1,2,4,512,128]{4,3,2,1,0:T(8,128)(2,1)}, bf16[1,2,4,512,128]{4,3,2,1,0:T(8,128)(2,1)S(1)}, u32[]{:S(2)}) copy-start(bf16[1,2,4,512,128]{4,3,2,1,0:T(8,128)(2,1)S(1)} %bitcast_dynamic-update-slice_fusion.3) | copy-start | bytes 3145732
  74.5 2.4 %copy-start.2 = (bf16[2,2,2,1024,128]{4,3,2,1,0:T(8,128)(2,1)}, bf16[2,2,2,1024,128]{4,3,2,1,0:T(8,128)(2,1)S(1)}, u32[]{:S(2)}) copy-start(bf16[2,2,2,1024,128]{4,3,2,1,0:T(8,128)(2,1)S(1)} %constant_dynamic-update-slice_fusion.7) | copy-start | bytes 6291460
  76.9 4.9 %copy-start.1 = (f32[1024,1024]{1,0:T(8,128)}, f32[1024,1024]{1,0:T(8,128)S(1)}, u32[]{:S(2)}) copy-start(f32[1024,1024]{1,0:T(8,128)S(1)} %bitcast_multiply_fusion.1) | copy-start | bytes 12582916
  81.8 10.9 %copy-start.5 = (bf16[1,2,4,512,128]{4,3,2,1,0:T(8,128)(2,1)S(1)}, bf16[1,2,4,512,128]{4,3,2,1,0:T(8,128)(2,1)}, u32[]{:S(2)}) copy-start(bf16[1,2,4,512,128]{4,3,2,1,0:T(8,128)(2,1)} %copy-done.4) | copy-start | bytes 3145732
  82.6 5.4 %collective-permute-start.15 = (f32[256,128]{1,0:T(8,128)}, f32[256,128]{1,0:T(8,128)S(1)}, u32[]{:S(2)}, u32[]{:S(2)}) collective-permute-start(f32[256,128]{1,0:T(8,128)} %get-tuple-element.17), channel_id=1, source_target_pairs={{0,12},{4,8},{8,4},{12,0},{1,13},{5,9},{9,5},{13,1},{2,14},{6,10},... | collective-permute-start | bytes 393224 | tf_op jit(solution)/shard_map/ppermute | solution.py:113
  82.9 8.6 %collective-permute-start.14 = (f32[256,128]{1,0:T(8,128)}, f32[256,128]{1,0:T(8,128)}, u32[]{:S(2)}, u32[]{:S(2)}) collective-permute-start(f32[256,128]{1,0:T(8,128)} %get-tuple-element.18), channel_id=1, source_target_pairs={{0,8},{4,12},{8,0},{12,4},{1,9},{5,13},{9,1},{13,5},{2,10},{6,14},... | collective-permute-start | bytes 393224 | tf_op jit(solution)/shard_map/ppermute | solution.py:113
  84.7 6.8 %collective-permute-start.13 = (f32[256,128]{1,0:T(8,128)S(1)}, f32[256,128]{1,0:T(8,128)}, u32[]{:S(2)}, u32[]{:S(2)}) collective-permute-start(f32[256,128]{1,0:T(8,128)S(1)} %get-tuple-element.19), channel_id=1, source_target_pairs={{0,4},{4,0},{8,12},{12,8},{1,5},{5,1},{9,13},{13,9},{2,6},{6,2},{1... | collective-permute-start | bytes 393224 | tf_op jit(solution)/shard_map/ppermute | solution.py:113
  84.7 8.0 %copy-start.3 = (bf16[2,2,2,1024,128]{4,3,2,1,0:T(8,128)(2,1)S(1)}, bf16[2,2,2,1024,128]{4,3,2,1,0:T(8,128)(2,1)}, u32[]{:S(2)}) copy-start(bf16[2,2,2,1024,128]{4,3,2,1,0:T(8,128)(2,1)} %copy-done.2) | copy-start | bytes 6291460
  92.6 5.6 %collective-permute-start.16 = (f32[256,128]{1,0:T(8,128)S(1)}, f32[256,128]{1,0:T(8,128)S(1)}, u32[]{:S(2)}, u32[]{:S(2)}) collective-permute-start(f32[256,128]{1,0:T(8,128)S(1)} %bitcast.163), channel_id=1, source_target_pairs={{0,4},{4,0},{8,12},{12,8},{1,5},{5,1},{9,13},{13,9},{2,6},{6,2},{1... | collective-permute-start | bytes 393224 | tf_op jit(solution)/shard_map/ppermute | solution.py:120
  96.3 6.4 %collective-permute-start.17 = (f32[256,128]{1,0:T(8,128)S(1)}, f32[256,128]{1,0:T(8,128)S(1)}, u32[]{:S(2)}, u32[]{:S(2)}) collective-permute-start(f32[256,128]{1,0:T(8,128)S(1)} %bitcast.164), channel_id=1, source_target_pairs={{0,8},{4,12},{8,0},{12,4},{1,9},{5,13},{9,1},{13,5},{2,10},{6,14},... | collective-permute-start | bytes 393224 | tf_op jit(solution)/shard_map/ppermute | solution.py:120
  96.7 7.8 %collective-permute-start.18 = (f32[256,128]{1,0:T(8,128)S(1)}, f32[256,128]{1,0:T(8,128)S(1)}, u32[]{:S(2)}, u32[]{:S(2)}) collective-permute-start(f32[256,128]{1,0:T(8,128)S(1)} %bitcast.165), channel_id=1, source_target_pairs={{0,12},{4,8},{8,4},{12,0},{1,13},{5,9},{9,5},{13,1},{2,14},{6,10},... | collective-permute-start | bytes 393224 | tf_op jit(solution)/shard_map/ppermute | solution.py:120
  105.6 9.7 %collective-permute-start.20 = (f32[128,128]{0,1:T(8,128)S(1)}, f32[128,128]{0,1:T(8,128)S(1)}, u32[]{:S(2)}, u32[]{:S(2)}) collective-permute-start(f32[128,128]{0,1:T(8,128)S(1)} %convolution_bitcast_fusion.1), channel_id=1, source_target_pairs={{0,2},{1,3},{2,0},{3,1},{4,6},{5,7},{6,4},{7,5},{8,10},{9,11},{10,... | collective-permute-start | bytes 196616 | tf_op jit(solution)/shard_map/ppermute | solution.py:44
  105.7 11.6 %collective-permute-start.21 = (f32[128,128]{0,1:T(8,128)S(1)}, f32[128,128]{0,1:T(8,128)S(1)}, u32[]{:S(2)}, u32[]{:S(2)}) collective-permute-start(f32[128,128]{0,1:T(8,128)S(1)} %convolution_bitcast_fusion.1), channel_id=1, source_target_pairs={{0,3},{1,2},{2,1},{3,0},{4,7},{5,6},{6,5},{7,4},{8,11},{9,10},{10,... | collective-permute-start | bytes 196616 | tf_op jit(solution)/shard_map/ppermute | solution.py:44
  108.0 9.3 %collective-permute-start.19 = (f32[128,128]{0,1:T(8,128)S(1)}, f32[128,128]{0,1:T(8,128)S(1)}, u32[]{:S(2)}, u32[]{:S(2)}) collective-permute-start(f32[128,128]{0,1:T(8,128)S(1)} %convolution_bitcast_fusion.1), channel_id=1, source_target_pairs={{0,1},{1,0},{2,3},{3,2},{4,5},{5,4},{6,7},{7,6},{8,9},{9,8},{10,11... | collective-permute-start | bytes 196616 | tf_op jit(solution)/shard_map/ppermute | solution.py:44
  112.8 17.0 %collective-permute-start.24 = (f32[256,128]{1,0:T(8,128)S(1)}, f32[256,128]{1,0:T(8,128)S(1)}, u32[]{:S(2)}, u32[]{:S(2)}) collective-permute-start(f32[256,128]{1,0:T(8,128)S(1)} %get-tuple-element.13), channel_id=1, source_target_pairs={{0,3},{1,2},{2,1},{3,0},{4,7},{5,6},{6,5},{7,4},{8,11},{9,10},{10,... | collective-permute-start | bytes 393224 | tf_op jit(solution)/shard_map/ppermute | solution.py:113
  113.8 16.0 %collective-permute-start.23 = (f32[256,128]{1,0:T(8,128)S(1)}, f32[256,128]{1,0:T(8,128)S(1)}, u32[]{:S(2)}, u32[]{:S(2)}) collective-permute-start(f32[256,128]{1,0:T(8,128)S(1)} %get-tuple-element.14), channel_id=1, source_target_pairs={{0,2},{1,3},{2,0},{3,1},{4,6},{5,7},{6,4},{7,5},{8,10},{9,11},{10,... | collective-permute-start | bytes 393224 | tf_op jit(solution)/shard_map/ppermute | solution.py:113
  115.3 14.5 %collective-permute-start.22 = (f32[256,128]{1,0:T(8,128)S(1)}, f32[256,128]{1,0:T(8,128)S(1)}, u32[]{:S(2)}, u32[]{:S(2)}) collective-permute-start(f32[256,128]{1,0:T(8,128)S(1)} %get-tuple-element.15), channel_id=1, source_target_pairs={{0,1},{1,0},{2,3},{3,2},{4,5},{5,4},{6,7},{7,6},{8,9},{9,8},{10,11... | collective-permute-start | bytes 393224 | tf_op jit(solution)/shard_map/ppermute | solution.py:113
  130.0 15.0 %collective-permute-start.25 = (f32[256,128]{1,0:T(8,128)S(1)}, f32[256,128]{1,0:T(8,128)S(1)}, u32[]{:S(2)}, u32[]{:S(2)}) collective-permute-start(f32[256,128]{1,0:T(8,128)S(1)} %bitcast.160), channel_id=1, source_target_pairs={{0,1},{1,0},{2,3},{3,2},{4,5},{5,4},{6,7},{7,6},{8,9},{9,8},{10,11... | collective-permute-start | bytes 393224 | tf_op jit(solution)/shard_map/ppermute | solution.py:120
  140.5 11.9 %collective-permute-start.26 = (f32[256,128]{1,0:T(8,128)S(1)}, f32[256,128]{1,0:T(8,128)S(1)}, u32[]{:S(2)}, u32[]{:S(2)}) collective-permute-start(f32[256,128]{1,0:T(8,128)S(1)} %bitcast.161), channel_id=1, source_target_pairs={{0,2},{1,3},{2,0},{3,1},{4,6},{5,7},{6,4},{7,5},{8,10},{9,11},{10,... | collective-permute-start | bytes 393224 | tf_op jit(solution)/shard_map/ppermute | solution.py:120
  142.0 10.4 %collective-permute-start.27 = (f32[256,128]{1,0:T(8,128)S(1)}, f32[256,128]{1,0:T(8,128)S(1)}, u32[]{:S(2)}, u32[]{:S(2)}) collective-permute-start(f32[256,128]{1,0:T(8,128)S(1)} %bitcast.162), channel_id=1, source_target_pairs={{0,3},{1,2},{2,1},{3,0},{4,7},{5,6},{6,5},{7,4},{8,11},{9,10},{10,... | collective-permute-start | bytes 393224 | tf_op jit(solution)/shard_map/ppermute | solution.py:120
  153.7 4.7 %collective-permute-start.29 = (f32[128,128]{0,1:T(8,128)S(1)}, f32[128,128]{0,1:T(8,128)S(1)}, u32[]{:S(2)}, u32[]{:S(2)}) collective-permute-start(f32[128,128]{0,1:T(8,128)S(1)} %fusion.21), channel_id=1, source_target_pairs={{0,8},{4,12},{8,0},{12,4},{1,9},{5,13},{9,1},{13,5},{2,10},{6,14},... | collective-permute-start | bytes 196616 | tf_op jit(solution)/shard_map/ppermute | solution.py:44
  154.7 4.4 %collective-permute-start.30 = (f32[128,128]{0,1:T(8,128)S(1)}, f32[128,128]{0,1:T(8,128)S(1)}, u32[]{:S(2)}, u32[]{:S(2)}) collective-permute-start(f32[128,128]{0,1:T(8,128)S(1)} %fusion.21), channel_id=1, source_target_pairs={{0,12},{4,8},{8,4},{12,0},{1,13},{5,9},{9,5},{13,1},{2,14},{6,10},... | collective-permute-start | bytes 196616 | tf_op jit(solution)/shard_map/ppermute | solution.py:44
  154.7 4.4 %collective-permute-start.28 = (f32[128,128]{0,1:T(8,128)S(1)}, f32[128,128]{0,1:T(8,128)S(1)}, u32[]{:S(2)}, u32[]{:S(2)}) collective-permute-start(f32[128,128]{0,1:T(8,128)S(1)} %fusion.21), channel_id=1, source_target_pairs={{0,4},{4,0},{8,12},{12,8},{1,5},{5,1},{9,13},{13,9},{2,6},{6,2},{1... | collective-permute-start | bytes 196616 | tf_op jit(solution)/shard_map/ppermute | solution.py:44

commit v15 on v13

--- a/solution.py
+++ b/solution.py
@@ -151,7 +151,13 @@
             ],
             1,
         )
-        left_rows = _butterfly_gather(swapped, left_plan)
+        left_rows = jnp.concatenate(
+            [
+                _butterfly_gather(swapped[:half], left_plan),
+                _butterfly_gather(swapped[half:], left_plan),
+            ],
+            1,
+        )
     else:
         right_rows = lax.all_gather(local_rows, ("bin", "col"), axis=0, tiled=False)
         every_row = lax.all_gather(right_rows, "row", axis=1, tiled=True)

time: 173 us -> 172 us (level)
  starting transfers between devices: 46.8 us -> 29.6 us
  waiting for transfers between devices: 37.9 us -> 54.1 us
    ppermute x9 -> x12, starting transfers between devices: 32.2 us -> 15 us  [_butterfly_gather(): other = lax.ppermute(x, axis, [(i, i ^ step) for i in range(count)])]
    ppermute x9 -> x12, waiting for transfers between devices: 7.59 us -> 24.3 us  [_butterfly_gather(): other = lax.ppermute(x, axis, [(i, i ^ step) for i in range(count)])]
    broadcast_in_dim x7 -> x2, local copies, waits for them, and re-layouts: 3.29 us -> 0.21 us  [_butterfly_gather(): both = jnp.zeros((mine.shape[0], 2) + mine.shape[2:], x.dtype)]
    another operation x4 -> x12, local copies, waits for them, and re-layouts: 0.14 us -> 2.97 us
    dynamic_update_slice x9 -> x12, local copies, waits for them, and re-layouts: 6.81 us -> 5.33 us  [_butterfly_gather(): both = lax.dynamic_update_slice_in_dim(both, theirs, 1 - first, 1)]
    dynamic_update_slice x9 -> x12, local copies, waits for them, and re-layouts: 5.7 us -> 5.3 us  [_butterfly_gather(): both = lax.dynamic_update_slice_in_dim(both, mine, first, 1)]
  transfers between devices with their start and end apart: 26 -> 29, of which waited for: 13 -> 13; matrix products, arithmetic and copies ran while one was open for 28% -> 29% of each run, Pallas kernels for 0% -> 0%
where the time goes in v15:
time: 172 us
  waiting for transfers between devices  54.1 us (31%)
  other arithmetic  46.3 us (27%)
  starting transfers between devices  29.6 us (17%)
  matrix products  21.1 us (12%)
  local copies, waits for them, and re-layouts  19.3 us (11%)
    another operation x6, other arithmetic, _lower_factor(): return jnp.linalg.cholesky(_direct_sum(gram_part, gram_axis))  25 us
    ppermute x12, waiting for transfers between devices, _butterfly_gather(): other = lax.ppermute(x, axis, [(i, i ^ step) for i in range(count)])  24.3 us
    another operation x4, other arithmetic, _right_solve(): jax.scipy.linalg.solve_triangular(lower_factor, image.T, lower=True)  20.9 us
    ppermute x12, starting transfers between devices, _butterfly_gather(): other = lax.ppermute(x, axis, [(i, i ^ step) for i in range(count)])  15 us
    ppermute x9, starting transfers between devices, _direct_sum(): lax.ppermute(x, axis, [(i, i ^ k) for i in range(count)])  9.52 us
    ppermute x9, waiting for transfers between devices, _direct_sum(): lax.ppermute(x, axis, [(i, i ^ k) for i in range(count)])  8.33 us
    ppermute x1, waiting for transfers between devices, _pair_split_sum(): mine = mine + lax.ppermute(mine, axis, [(i, i ^ 2) for i in range(count)])  8.06 us
    ppermute x2, waiting for transfers between devices, _halving_sum(): x = keep + lax.ppermute(give, axis, [(i, i ^ step) for i in range(count)])  6.9 us
  transfers between devices with their start and end apart: 29, of which 13 were waited for; matrix products, arithmetic and copies ran while one was open for 29% of the time, Pallas kernels for 0%

profile of v15, /device:TPU:0, one launch (start us, length us, event | category | flops | bytes accessed | tf_op | source)
XLA Modules:
  0.0 171.8 jit_solution(8493304472411701142)
XLA Ops:
  0.7 2.2 %fusion.25 = f32[8,128,16]{1,2,0:T(8,128)S(1)} fusion(bf16[1024,8,16]{0,2,1:T(8,128)(2,1)} %param.7, bf16[8,1024,128]{2,1,0:T(8,128)(2,1)} %param.8), kind=kOutput, calls=%fused_computation.83 | convolution fusion | flops 33554432 | bytes 2424832 | tf_op jit(solution)/shard_map/mbs,bmr->brs/dot_general | solution.py:122
  3.4 2.6 %collective-permute-start.1 = (f32[8,128,16]{1,2,0:T(8,128)S(1)}, f32[8,128,16]{1,2,0:T(8,128)S(1)}, u32[]{:S(2)}, u32[]{:S(2)}) collective-permute-start(f32[8,128,16]{1,2,0:T(8,128)S(1)} %fusion.25), channel_id=1, source_target_pairs={{0,8},{4,12},{8,0},{12,4},{1,9},{5,13},{9,1},{13,5},{2,10},{6,14},... | collective-permute-start | bytes 196616 | tf_op jit(solution)/shard_map/ppermute | solution.py:44
  6.0 2.6 %collective-permute-done.1 = f32[8,128,16]{1,2,0:T(8,128)S(1)} collective-permute-done((f32[8,128,16]{1,2,0:T(8,128)S(1)}, f32[8,128,16]{1,2,0:T(8,128)S(1)}, u32[]{:S(2)}, u32[]{:S(2)}) %collective-permute-start.1) | collective-permute-done | bytes 65568 | tf_op jit(solution)/shard_map/ppermute | solution.py:44
  8.7 1.4 collective-permute-done.2
  10.7 1.4 collective-permute-start.3
  12.2 4.2 %collective-permute-start.10 = (bf16[1,512,128]{1,2,0:T(8,128)(2,1)S(1)}, bf16[1,512,128]{1,2,0:T(8,128)(2,1)S(1)}, u32[]{:S(2)}, u32[]{:S(2)}) collective-permute-start(bf16[1,512,128]{1,2,0:T(8,128)(2,1)S(1)} %bitcast.139), channel_id=1, source_target_pairs={{0,2},{1,3},{2,0},{3,1},{4,6},{5,7},{6,4},{7,5},{8,10},{9,11},{10,... | collective-permute-start | bytes 393224 | tf_op jit(solution)/shard_map/ppermute | solution.py:53
  16.4 1.5 collective-permute-start.13
  17.9 0.8 broadcast.55.clone.1
  19.5 0.7 broadcast.55.clone
  20.9 13.3 %collective-permute-done.10 = bf16[1,512,128]{1,2,0:T(8,128)(2,1)S(1)} collective-permute-done((bf16[1,512,128]{1,2,0:T(8,128)(2,1)S(1)}, bf16[1,512,128]{1,2,0:T(8,128)(2,1)S(1)}, u32[]{:S(2)}, u32[]{:S(2)}) %collective-permute-start.10) | collective-permute-done | bytes 131104 | tf_op jit(solution)/shard_map/ppermute | solution.py:53
  35.0 1.0 bitcast_dynamic-update-slice_fusion.12
  36.1 0.7 constant_dynamic-update-slice_fusion.7
  36.9 1.0 bitcast_dynamic-update-slice_fusion.5
  38.0 0.8 slice_bitcast_fusion.2
  38.8 1.6 collective-permute-start.4
  41.0 1.0 copy.11
  42.0 0.7 broadcast.55.clone.2
  43.4 2.2 %collective-permute-done.4 = bf16[1,512,128]{1,2,0:T(8,128)(2,1)} collective-permute-done((bf16[1,512,128]{1,2,0:T(8,128)(2,1)}, bf16[1,512,128]{1,2,0:T(8,128)(2,1)}, u32[]{:S(2)}, u32[]{:S(2)}) %collective-permute-start.4) | collective-permute-done | bytes 131104 | tf_op jit(solution)/shard_map/ppermute | solution.py:53
  45.6 1.0 copy.7
  46.7 4.7 %collective-permute-start.5 = (bf16[2,512,128]{2,1,0:T(8,128)(2,1)S(1)}, bf16[2,512,128]{2,1,0:T(8,128)(2,1)}, u32[]{:S(2)}, u32[]{:S(2)}) collective-permute-start(bf16[2,512,128]{2,1,0:T(8,128)(2,1)S(1)} %bitcast.124), channel_id=1, source_target_pairs={{0,8},{4,12},{8,0},{12,4},{1,9},{5,13},{9,1},{13,5},{2,10},{6,14},... | collective-permute-start | bytes 786440 | tf_op jit(solution)/shard_map/ppermute | solution.py:53
  51.4 1.0 copy.12
  53.5 1.0 bitcast_dynamic-update-slice_fusion.11
  54.5 1.6 collective-permute-start.12
  56.2 1.0 bitcast_dynamic-update-slice_fusion.10
  57.8 1.0 bitcast_dynamic-update-slice_fusion.7
  59.1 1.0 bitcast_dynamic-update-slice_fusion.8
  60.1 1.2 collective-permute-done.8
  61.9 7.7 %collective-permute-done.15 = bf16[4,512,128]{2,1,0:T(8,128)(2,1)S(1)} collective-permute-done((bf16[4,512,128]{2,1,0:T(8,128)(2,1)S(1)}, bf16[4,512,128]{2,1,0:T(8,128)(2,1)S(1)}, u32[]{:S(2)}, u32[]{:S(2)}) %collective-permute-start.15) | collective-permute-done | bytes 524320 | tf_op jit(solution)/shard_map/ppermute | solution.py:53
  70.0 2.4 %bitcast_multiply_fusion.2 = f32[1024,1024]{1,0:T(8,128)S(1)} fusion(bf16[8,512,128]{2,1,0:T(8,128)(2,1)S(1)} %bitcast.127, bf16[8,512,128]{2,1,0:T(8,128)(2,1)S(1)} %bitcast.129, bf16[8,512,128]{2,1,0:T(8,128)(2,1)S(1)} %bitcast.125, bf16[8,512,128]{2,1,0:T(8,128)(2,1)S(1)} %bitcast.131), kind=kOutput, calls=%fused_computation.2 | convolution fusion | flops 2156920832 | bytes 8388608 | tf_op jit(solution)/shard_map/dot_general | solution.py:165
  72.4 4.9 %fusion.7 = f32[1024,128]{1,0:T(8,128)S(1)} fusion(f32[1024,1024]{1,0:T(8,128)S(1)} %bitcast_multiply_fusion.2, f32[4096,128]{1,0:T(8,128)} %param.10, s32[]{:T(128)S(6)} %select_n.138), kind=kOutput, calls=%fused_computation.17 | convolution fusion | flops 1610612736 | bytes 5242884 | tf_op jit(solution)/shard_map/dot_general | solution.py:174
  77.4 1.9 %collective-permute-done.16 = f32[1024,128]{1,0:T(8,128)S(1)} collective-permute-done((f32[1024,128]{1,0:T(8,128)S(1)}, f32[1024,128]{1,0:T(8,128)S(1)}, u32[]{:S(2)}, u32[]{:S(2)}) %collective-permute-start.16) | collective-permute-done | bytes 524320 | tf_op jit(solution)/shard_map/ppermute | solution.py:93
  79.7 8.1 %collective-permute-done.17 = f32[512,128]{1,0:T(8,128)S(1)} collective-permute-done((f32[512,128]{1,0:T(8,128)S(1)}, f32[512,128]{1,0:T(8,128)S(1)}, u32[]{:S(2)}, u32[]{:S(2)}) %collective-permute-start.17) | collective-permute-done | bytes 262176 | tf_op jit(solution)/shard_map/ppermute | solution.py:96
  87.9 4.5 %fusion.2 = f32[1024,1024,1]{1,0,2:T(8,128)S(1)} fusion(bf16[8,512,128]{2,1,0:T(8,128)(2,1)} %bitcast.128, bf16[8,512,128]{2,1,0:T(8,128)(2,1)} %bitcast.130, bf16[8,512,128]{2,1,0:T(8,128)(2,1)} %bitcast.126, bf16[8,512,128]{2,1,0:T(8,128)(2,1)} %bitcast.132), kind=kOutput, calls=%fused_computation.6 | convolution fusion | flops 2155872256 | bytes 8388608 | tf_op jit(solution)/shard_map/dot_general | solution.py:168
  92.5 1.0 fusion.23
  94.2 1.2 collective-permute-start.20
  95.4 2.6 %collective-permute-start.21 = (f32[128,128]{0,1:T(8,128)S(1)}, f32[128,128]{0,1:T(8,128)S(1)}, u32[]{:S(2)}, u32[]{:S(2)}) collective-permute-start(f32[128,128]{0,1:T(8,128)S(1)} %fusion.23), channel_id=1, source_target_pairs={{0,3},{1,2},{2,1},{3,0},{4,7},{5,6},{6,5},{7,4},{8,11},{9,10},{10,... | collective-permute-start | bytes 196616 | tf_op jit(solution)/shard_map/ppermute | solution.py:44
  98.0 3.6 %fusion = f32[1024,128]{1,0:T(8,128)S(1)} fusion(f32[1024,128]{1,0:T(8,128)S(1)} %constant_dynamic-update-slice_fusion.4, f32[1024,1024,1]{1,0,2:T(8,128)S(1)} %fusion.2), kind=kOutput, calls=%fused_computation.1 | convolution fusion | flops 1611661312 | bytes 5242880 | tf_op jit(solution)/shard_map/dot_general | solution.py:179
  101.7 0.8 collective-permute-done.20
  102.7 6.9 %collective-permute-done.22 = f32[512,128]{1,0:T(8,128)S(1)} collective-permute-done((f32[512,128]{1,0:T(8,128)S(1)}, f32[512,128]{1,0:T(8,128)S(1)}, u32[]{:S(2)}, u32[]{:S(2)}) %collective-permute-start.22) | collective-permute-done | bytes 262176 | tf_op jit(solution)/shard_map/ppermute | solution.py:76
  110.3 11.7 %cholesky.44 = f32[128,128]{1,0:T(8,128)S(1)} custom-call(f32[128,128]{1,0:T(8,128)S(1)} %fusion.15), custom_call_target="Cholesky" | custom-call | tf_op jit(solution)/shard_map/jit(cholesky)/cholesky | solution.py:108
  122.1 2.4 %collective-permute-start.24 = (f32[256,128]{1,0:T(8,128)S(1)}, f32[256,128]{1,0:T(8,128)S(1)}, u32[]{:S(2)}, u32[]{:S(2)}) collective-permute-start(f32[256,128]{1,0:T(8,128)S(1)} %get-tuple-element.7), channel_id=1, source_target_pairs={{0,2},{1,3},{2,0},{3,1},{4,6},{5,7},{6,4},{7,5},{8,10},{9,11},{10,... | collective-permute-start | bytes 393224 | tf_op jit(solution)/shard_map/ppermute | solution.py:79
  125.1 4.6 %collective-permute-done.24 = f32[256,128]{1,0:T(8,128)S(1)} collective-permute-done((f32[256,128]{1,0:T(8,128)S(1)}, f32[256,128]{1,0:T(8,128)S(1)}, u32[]{:S(2)}, u32[]{:S(2)}) %collective-permute-start.24) | collective-permute-done | bytes 131104 | tf_op jit(solution)/shard_map/ppermute | solution.py:79
  130.5 9.8 %custom-call.6 = f32[1,128,128]{1,2,0:T(8,128)S(1)} custom-call(f32[1,128,128]{2,1,0:T(8,128)S(1)} %fusion.9), custom_call_target="InvertDiagBlocksLowerTriangular" | custom-call | tf_op jit(solution)/shard_map/jit(_solve_triangular)/triangular_solve | solution.py:112
  142.1 1.5 collective-permute-start.28
  143.6 3.2 %collective-permute-done.27 = f32[128,128]{0,1:T(8,128)S(1)} collective-permute-done((f32[128,128]{0,1:T(8,128)S(1)}, f32[128,128]{0,1:T(8,128)S(1)}, u32[]{:S(2)}, u32[]{:S(2)}) %collective-permute-start.27) | collective-permute-done | bytes 65568 | tf_op jit(solution)/shard_map/ppermute | solution.py:44
  147.3 11.9 %cholesky.55 = f32[128,128]{1,0:T(8,128)S(1)} custom-call(f32[128,128]{1,0:T(8,128)S(1)} %fusion.13), custom_call_target="Cholesky" | custom-call | tf_op jit(solution)/shard_map/jit(cholesky)/cholesky | solution.py:108
  160.5 9.8 %custom-call.7 = f32[1,128,128]{1,2,0:T(8,128)S(1)} custom-call(f32[1,128,128]{2,1,0:T(8,128)S(1)} %fusion.10), custom_call_target="InvertDiagBlocksLowerTriangular" | custom-call | tf_op jit(solution)/shard_map/jit(_solve_triangular)/triangular_solve | solution.py:112
  171.0 0.8 copy.31
  (113 shorter events, 16.2 us)
Async XLA Ops:
  0.6 9.4 %copy-start = (bf16[8,1024,128]{2,1,0:T(8,128)(2,1)S(1)}, bf16[8,1024,128]{2,1,0:T(8,128)(2,1)}, u32[]{:S(2)}) copy-start(bf16[8,1024,128]{2,1,0:T(8,128)(2,1)} %param.9) | copy-start | bytes 6291460
  0.6 9.4 %copy-start.6 = (bf16[1024,8,16]{0,2,1:T(8,128)(2,1)S(1)}, bf16[1024,8,16]{0,2,1:T(8,128)(2,1)}, u32[]{:S(2)}) copy-start(bf16[1024,8,16]{0,2,1:T(8,128)(2,1)} %param.7) | copy-start | bytes 786436
  2.9 3.2 %collective-permute-start = (f32[8,128,16]{1,2,0:T(8,128)S(1)}, f32[8,128,16]{1,2,0:T(8,128)S(1)}, u32[]{:S(2)}, u32[]{:S(2)}) collective-permute-start(f32[8,128,16]{1,2,0:T(8,128)S(1)} %fusion.25), channel_id=1, source_target_pairs={{0,4},{4,0},{8,12},{12,8},{1,5},{5,1},{9,13},{13,9},{2,6},{6,2},{1... | collective-permute-start | bytes 196616 | tf_op jit(solution)/shard_map/ppermute | solution.py:44
  3.4 5.2 %collective-permute-start.1 = (f32[8,128,16]{1,2,0:T(8,128)S(1)}, f32[8,128,16]{1,2,0:T(8,128)S(1)}, u32[]{:S(2)}, u32[]{:S(2)}) collective-permute-start(f32[8,128,16]{1,2,0:T(8,128)S(1)} %fusion.25), channel_id=1, source_target_pairs={{0,8},{4,12},{8,0},{12,4},{1,9},{5,13},{9,1},{13,5},{2,10},{6,14},... | collective-permute-start | bytes 196616 | tf_op jit(solution)/shard_map/ppermute | solution.py:44
  6.0 4.1 %collective-permute-start.2 = (f32[8,128,16]{1,2,0:T(8,128)S(1)}, f32[8,128,16]{1,2,0:T(8,128)S(1)}, u32[]{:S(2)}, u32[]{:S(2)}) collective-permute-start(f32[8,128,16]{1,2,0:T(8,128)S(1)} %fusion.25), channel_id=1, source_target_pairs={{0,12},{4,8},{8,4},{12,0},{1,13},{5,9},{9,5},{13,1},{2,14},{6,10},... | collective-permute-start | bytes 196616 | tf_op jit(solution)/shard_map/ppermute | solution.py:44
  10.7 27.2 %collective-permute-start.3 = (bf16[1024,128]{0,1:T(8,128)(2,1)S(1)}, bf16[1024,128]{0,1:T(8,128)(2,1)}, u32[]{:S(2)}, u32[]{:S(2)}) collective-permute-start(bf16[1024,128]{0,1:T(8,128)(2,1)S(1)} %bitcast.118), channel_id=1, source_target_pairs={{1,4},{2,8},{3,12},{4,1},{6,9},{7,13},{8,2},{9,6},{11,14},{12,3},{... | collective-permute-start | bytes 786440 | tf_op jit(solution)/shard_map/ppermute | solution.py:136
  12.2 21.9 %collective-permute-start.10 = (bf16[1,512,128]{1,2,0:T(8,128)(2,1)S(1)}, bf16[1,512,128]{1,2,0:T(8,128)(2,1)S(1)}, u32[]{:S(2)}, u32[]{:S(2)}) collective-permute-start(bf16[1,512,128]{1,2,0:T(8,128)(2,1)S(1)} %bitcast.139), channel_id=1, source_target_pairs={{0,2},{1,3},{2,0},{3,1},{4,6},{5,7},{6,4},{7,5},{8,10},{9,11},{10,... | collective-permute-start | bytes 393224 | tf_op jit(solution)/shard_map/ppermute | solution.py:53
  16.4 19.6 %collective-permute-start.13 = (bf16[1,512,128]{1,2,0:T(8,128)(2,1)S(1)}, bf16[1,512,128]{1,2,0:T(8,128)(2,1)S(1)}, u32[]{:S(2)}, u32[]{:S(2)}) collective-permute-start(bf16[1,512,128]{1,2,0:T(8,128)(2,1)S(1)} %bitcast.136), channel_id=1, source_target_pairs={{0,16},{16,0},{1,17},{17,1},{2,18},{18,2},{3,19},{19,3},{4,20},{20... | collective-permute-start | bytes 393224 | tf_op jit(solution)/shard_map/ppermute | solution.py:53
  34.9 18.5 %collective-permute-start.11 = (bf16[2,512,128]{2,1,0:T(8,128)(2,1)}, bf16[2,512,128]{2,1,0:T(8,128)(2,1)}, u32[]{:S(2)}, u32[]{:S(2)}) collective-permute-start(bf16[2,512,128]{2,1,0:T(8,128)(2,1)} %bitcast.32), channel_id=1, source_target_pairs={{0,1},{1,0},{2,3},{3,2},{4,5},{5,4},{6,7},{7,6},{8,9},{9,8},{10,11... | collective-permute-start | bytes 786440 | tf_op jit(solution)/shard_map/ppermute | solution.py:53
  36.8 19.4 %collective-permute-start.14 = (bf16[2,512,128]{2,1,0:T(8,128)(2,1)}, bf16[2,512,128]{2,1,0:T(8,128)(2,1)}, u32[]{:S(2)}, u32[]{:S(2)}) collective-permute-start(bf16[2,512,128]{2,1,0:T(8,128)(2,1)} %bitcast.43), channel_id=1, source_target_pairs={{0,2},{1,3},{2,0},{3,1},{4,6},{5,7},{6,4},{7,5},{8,10},{9,11},{10,... | collective-permute-start | bytes 786440 | tf_op jit(solution)/shard_map/ppermute | solution.py:53
  38.8 6.7 %collective-permute-start.4 = (bf16[1,512,128]{1,2,0:T(8,128)(2,1)}, bf16[1,512,128]{1,2,0:T(8,128)(2,1)}, u32[]{:S(2)}, u32[]{:S(2)}) collective-permute-start(bf16[1,512,128]{1,2,0:T(8,128)(2,1)} %get-tuple-element.10), channel_id=1, source_target_pairs={{0,16},{16,0},{1,17},{17,1},{2,18},{18,2},{3,19},{19,3},{4,20},{20... | collective-permute-start | bytes 393224 | tf_op jit(solution)/shard_map/ppermute | solution.py:53
  40.4 10.9 %collective-permute-start.7 = (bf16[1,512,128]{1,2,0:T(8,128)(2,1)}, bf16[1,512,128]{1,2,0:T(8,128)(2,1)}, u32[]{:S(2)}, u32[]{:S(2)}) collective-permute-start(bf16[1,512,128]{1,2,0:T(8,128)(2,1)} %get-tuple-element.11), channel_id=1, source_target_pairs={{0,16},{16,0},{1,17},{17,1},{2,18},{18,2},{3,19},{19,3},{4,20},{20... | collective-permute-start | bytes 393224 | tf_op jit(solution)/shard_map/ppermute | solution.py:53
  46.7 12.4 %collective-permute-start.5 = (bf16[2,512,128]{2,1,0:T(8,128)(2,1)S(1)}, bf16[2,512,128]{2,1,0:T(8,128)(2,1)}, u32[]{:S(2)}, u32[]{:S(2)}) collective-permute-start(bf16[2,512,128]{2,1,0:T(8,128)(2,1)S(1)} %bitcast.124), channel_id=1, source_target_pairs={{0,8},{4,12},{8,0},{12,4},{1,9},{5,13},{9,1},{13,5},{2,10},{6,14},... | collective-permute-start | bytes 786440 | tf_op jit(solution)/shard_map/ppermute | solution.py:53
  53.1 8.3 %collective-permute-start.8 = (bf16[2,512,128]{2,1,0:T(8,128)(2,1)}, bf16[2,512,128]{2,1,0:T(8,128)(2,1)S(1)}, u32[]{:S(2)}, u32[]{:S(2)}) collective-permute-start(bf16[2,512,128]{2,1,0:T(8,128)(2,1)} %bitcast.20), channel_id=1, source_target_pairs={{0,8},{4,12},{8,0},{12,4},{1,9},{5,13},{9,1},{13,5},{2,10},{6,14},... | collective-permute-start | bytes 786440 | tf_op jit(solution)/shard_map/ppermute | solution.py:53
  54.5 15.2 %collective-permute-start.12 = (bf16[4,512,128]{2,1,0:T(8,128)(2,1)S(1)}, bf16[4,512,128]{2,1,0:T(8,128)(2,1)S(1)}, u32[]{:S(2)}, u32[]{:S(2)}) collective-permute-start(bf16[4,512,128]{2,1,0:T(8,128)(2,1)S(1)} %bitcast.121), channel_id=1, source_target_pairs={{0,16},{16,0},{1,17},{17,1},{2,18},{18,2},{3,19},{19,3},{4,20},{20... | collective-permute-start | bytes 1572872 | tf_op jit(solution)/shard_map/ppermute | solution.py:53
  57.4 12.2 %collective-permute-start.15 = (bf16[4,512,128]{2,1,0:T(8,128)(2,1)S(1)}, bf16[4,512,128]{2,1,0:T(8,128)(2,1)S(1)}, u32[]{:S(2)}, u32[]{:S(2)}) collective-permute-start(bf16[4,512,128]{2,1,0:T(8,128)(2,1)S(1)} %bitcast.119), channel_id=1, source_target_pairs={{0,1},{1,0},{2,3},{3,2},{4,5},{5,4},{6,7},{7,6},{8,9},{9,8},{10,11... | collective-permute-start | bytes 1572872 | tf_op jit(solution)/shard_map/ppermute | solution.py:53
  60.1 9.7 %collective-permute-start.6 = (bf16[4,512,128]{2,1,0:T(8,128)(2,1)S(1)}, bf16[4,512,128]{2,1,0:T(8,128)(2,1)S(1)}, u32[]{:S(2)}, u32[]{:S(2)}) collective-permute-start(bf16[4,512,128]{2,1,0:T(8,128)(2,1)S(1)} %bitcast.123), channel_id=1, source_target_pairs={{0,4},{4,0},{8,12},{12,8},{1,5},{5,1},{9,13},{13,9},{2,6},{6,2},{1... | collective-permute-start | bytes 1572872 | tf_op jit(solution)/shard_map/ppermute | solution.py:53
  61.4 8.5 %collective-permute-start.9 = (bf16[4,512,128]{2,1,0:T(8,128)(2,1)S(1)}, bf16[4,512,128]{2,1,0:T(8,128)(2,1)S(1)}, u32[]{:S(2)}, u32[]{:S(2)}) collective-permute-start(bf16[4,512,128]{2,1,0:T(8,128)(2,1)S(1)} %bitcast.120), channel_id=1, source_target_pairs={{0,4},{4,0},{8,12},{12,8},{1,5},{5,1},{9,13},{13,9},{2,6},{6,2},{1... | collective-permute-start | bytes 1572872 | tf_op jit(solution)/shard_map/ppermute | solution.py:53
  69.7 2.7 %copy-start.3 = (bf16[2,2,2,512,128]{4,3,2,1,0:T(8,128)(2,1)}, bf16[2,2,2,512,128]{4,3,2,1,0:T(8,128)(2,1)S(1)}, u32[]{:S(2)}) copy-start(bf16[2,2,2,512,128]{4,3,2,1,0:T(8,128)(2,1)S(1)} %constant_dynamic-update-slice_fusion.6) | copy-start | bytes 3145732
  69.8 2.6 %copy-start.4 = (bf16[1,2,4,512,128]{4,3,2,1,0:T(8,128)(2,1)}, bf16[1,2,4,512,128]{4,3,2,1,0:T(8,128)(2,1)S(1)}, u32[]{:S(2)}) copy-start(bf16[1,2,4,512,128]{4,3,2,1,0:T(8,128)(2,1)S(1)} %bitcast_dynamic-update-slice_fusion.3) | copy-start | bytes 3145732
  69.9 2.5 %copy-start.5 = (bf16[2,2,2,512,128]{4,3,2,1,0:T(8,128)(2,1)}, bf16[2,2,2,512,128]{4,3,2,1,0:T(8,128)(2,1)S(1)}, u32[]{:S(2)}) copy-start(bf16[2,2,2,512,128]{4,3,2,1,0:T(8,128)(2,1)S(1)} %constant_dynamic-update-slice_fusion.14) | copy-start | bytes 3145732
  70.0 2.4 %copy-start.2 = (bf16[2,2,2,512,128]{4,3,2,1,0:T(8,128)(2,1)}, bf16[2,2,2,512,128]{4,3,2,1,0:T(8,128)(2,1)S(1)}, u32[]{:S(2)}) copy-start(bf16[2,2,2,512,128]{4,3,2,1,0:T(8,128)(2,1)S(1)} %constant_dynamic-update-slice_fusion.11) | copy-start | bytes 3145732
  72.4 4.9 %copy-start.1 = (f32[1024,1024]{1,0:T(8,128)}, f32[1024,1024]{1,0:T(8,128)S(1)}, u32[]{:S(2)}) copy-start(f32[1024,1024]{1,0:T(8,128)S(1)} %bitcast_multiply_fusion.2) | copy-start | bytes 12582916
  77.3 2.0 %collective-permute-start.16 = (f32[1024,128]{1,0:T(8,128)S(1)}, f32[1024,128]{1,0:T(8,128)S(1)}, u32[]{:S(2)}, u32[]{:S(2)}) collective-permute-start(f32[1024,128]{1,0:T(8,128)S(1)} %fusion.7), channel_id=1, source_target_pairs={{0,4},{4,0},{8,12},{12,8},{1,5},{5,1},{9,13},{13,9},{2,6},{6,2},{1... | collective-permute-start | bytes 1572872 | tf_op jit(solution)/shard_map/ppermute | solution.py:93
  79.4 8.4 %collective-permute-start.17 = (f32[512,128]{1,0:T(8,128)S(1)}, f32[512,128]{1,0:T(8,128)S(1)}, u32[]{:S(2)}, u32[]{:S(2)}) collective-permute-start(f32[512,128]{1,0:T(8,128)S(1)} %slice_select_fusion), channel_id=1, source_target_pairs={{0,8},{4,12},{8,0},{12,4},{1,9},{5,13},{9,1},{13,5},{2,10},{6,14},... | collective-permute-start | bytes 786440 | tf_op jit(solution)/shard_map/ppermute | solution.py:96
  87.9 4.6 %collective-permute-start.18 = (f32[512,128]{1,0:T(8,128)S(1)}, f32[512,128]{1,0:T(8,128)S(1)}, u32[]{:S(2)}, u32[]{:S(2)}) collective-permute-start(f32[512,128]{1,0:T(8,128)S(1)} %get-tuple-element.9), channel_id=1, source_target_pairs={{0,4},{4,0},{8,12},{12,8},{1,5},{5,1},{9,13},{13,9},{2,6},{6,2},{1... | collective-permute-start | bytes 786440 | tf_op jit(solution)/shard_map/ppermute | solution.py:97
  93.5 8.2 %collective-permute-start.19 = (f32[128,128]{0,1:T(8,128)S(1)}, f32[128,128]{0,1:T(8,128)S(1)}, u32[]{:S(2)}, u32[]{:S(2)}) collective-permute-start(f32[128,128]{0,1:T(8,128)S(1)} %fusion.23), channel_id=1, source_target_pairs={{0,1},{1,0},{2,3},{3,2},{4,5},{5,4},{6,7},{7,6},{8,9},{9,8},{10,11... | collective-permute-start | bytes 196616 | tf_op jit(solution)/shard_map/ppermute | solution.py:44
  94.2 8.4 %collective-permute-start.20 = (f32[128,128]{0,1:T(8,128)S(1)}, f32[128,128]{0,1:T(8,128)S(1)}, u32[]{:S(2)}, u32[]{:S(2)}) collective-permute-start(f32[128,128]{0,1:T(8,128)S(1)} %fusion.23), channel_id=1, source_target_pairs={{0,2},{1,3},{2,0},{3,1},{4,6},{5,7},{6,4},{7,5},{8,10},{9,11},{10,... | collective-permute-start | bytes 196616 | tf_op jit(solution)/shard_map/ppermute | solution.py:44
  95.4 7.2 %collective-permute-start.21 = (f32[128,128]{0,1:T(8,128)S(1)}, f32[128,128]{0,1:T(8,128)S(1)}, u32[]{:S(2)}, u32[]{:S(2)}) collective-permute-start(f32[128,128]{0,1:T(8,128)S(1)} %fusion.23), channel_id=1, source_target_pairs={{0,3},{1,2},{2,1},{3,0},{4,7},{5,6},{6,5},{7,4},{8,11},{9,10},{10,... | collective-permute-start | bytes 196616 | tf_op jit(solution)/shard_map/ppermute | solution.py:44
  101.6 7.9 %collective-permute-start.22 = (f32[512,128]{1,0:T(8,128)S(1)}, f32[512,128]{1,0:T(8,128)S(1)}, u32[]{:S(2)}, u32[]{:S(2)}) collective-permute-start(f32[512,128]{1,0:T(8,128)S(1)} %slice_select_fusion.1), channel_id=1, source_target_pairs={{0,1},{1,0},{2,3},{3,2},{4,5},{5,4},{6,7},{7,6},{8,9},{9,8},{10,11... | collective-permute-start | bytes 786440 | tf_op jit(solution)/shard_map/ppermute | solution.py:76
  109.6 12.4 %collective-permute-start.23 = (f32[256,128]{1,0:T(8,128)S(1)}, f32[256,128]{1,0:T(8,128)S(1)}, u32[]{:S(2)}, u32[]{:S(2)}) collective-permute-start(f32[256,128]{1,0:T(8,128)S(1)} %slice_select_fusion.2), channel_id=1, source_target_pairs={{0,2},{1,3},{2,0},{3,1},{4,6},{5,7},{6,4},{7,5},{8,10},{9,11},{10,... | collective-permute-start | bytes 393224 | tf_op jit(solution)/shard_map/ppermute | solution.py:76
  122.1 7.7 %collective-permute-start.24 = (f32[256,128]{1,0:T(8,128)S(1)}, f32[256,128]{1,0:T(8,128)S(1)}, u32[]{:S(2)}, u32[]{:S(2)}) collective-permute-start(f32[256,128]{1,0:T(8,128)S(1)} %get-tuple-element.7), channel_id=1, source_target_pairs={{0,2},{1,3},{2,0},{3,1},{4,6},{5,7},{6,4},{7,5},{8,10},{9,11},{10,... | collective-permute-start | bytes 393224 | tf_op jit(solution)/shard_map/ppermute | solution.py:79
  129.8 10.6 %collective-permute-start.25 = (f32[512,128]{1,0:T(8,128)S(1)}, f32[512,128]{1,0:T(8,128)S(1)}, u32[]{:S(2)}, u32[]{:S(2)}) collective-permute-start(f32[512,128]{1,0:T(8,128)S(1)} %constant_dynamic-update-slice_fusion.2), channel_id=1, source_target_pairs={{0,1},{1,0},{2,3},{3,2},{4,5},{5,4},{6,7},{7,6},{8,9},{9,8},{10,11... | collective-permute-start | bytes 786440 | tf_op jit(solution)/shard_map/ppermute | solution.py:79
  141.7 1.9 %collective-permute-start.26 = (f32[128,128]{0,1:T(8,128)S(1)}, f32[128,128]{0,1:T(8,128)S(1)}, u32[]{:S(2)}, u32[]{:S(2)}) collective-permute-start(f32[128,128]{0,1:T(8,128)S(1)} %fusion.24), channel_id=1, source_target_pairs={{0,4},{4,0},{8,12},{12,8},{1,5},{5,1},{9,13},{13,9},{2,6},{6,2},{1... | collective-permute-start | bytes 196616 | tf_op jit(solution)/shard_map/ppermute | solution.py:44
  141.8 5.0 %collective-permute-start.27 = (f32[128,128]{0,1:T(8,128)S(1)}, f32[128,128]{0,1:T(8,128)S(1)}, u32[]{:S(2)}, u32[]{:S(2)}) collective-permute-start(f32[128,128]{0,1:T(8,128)S(1)} %fusion.24), channel_id=1, source_target_pairs={{0,8},{4,12},{8,0},{12,4},{1,9},{5,13},{9,1},{13,5},{2,10},{6,14},... | collective-permute-start | bytes 196616 | tf_op jit(solution)/shard_map/ppermute | solution.py:44
  142.1 5.0 %collective-permute-start.28 = (f32[128,128]{0,1:T(8,128)S(1)}, f32[128,128]{0,1:T(8,128)S(1)}, u32[]{:S(2)}, u32[]{:S(2)}) collective-permute-start(f32[128,128]{0,1:T(8,128)S(1)} %fusion.24), channel_id=1, source_target_pairs={{0,12},{4,8},{8,4},{12,0},{1,13},{5,9},{9,5},{13,1},{2,14},{6,10},... | collective-permute-start | bytes 196616 | tf_op jit(solution)/shard_map/ppermute | solution.py:44

commit v16 on v15

--- a/solution.py
+++ b/solution.py
@@ -109,7 +109,9 @@
 
 
 def _right_solve(lower_factor, image):
-    return jax.scipy.linalg.solve_triangular(lower_factor, image.T, lower=True).T
+    return lax.linalg.triangular_solve(
+        lower_factor, image, left_side=False, lower=True, transpose_a=True
+    )
 
 
 def shards(snapshots, focus_in, focus_out, start_basis):

time: 172 us -> 172 us (level)
  no operation moved by 1% of the time
where the time goes in v16:
time: 172 us
  waiting for transfers between devices  54.1 us (31%)
  other arithmetic  46.3 us (27%)
  starting transfers between devices  29.6 us (17%)
  matrix products  21.1 us (12%)
  local copies, waits for them, and re-layouts  19.3 us (11%)
    another operation x6, other arithmetic, _lower_factor(): return jnp.linalg.cholesky(_direct_sum(gram_part, gram_axis))  25 us
    ppermute x12, waiting for transfers between devices, _butterfly_gather(): other = lax.ppermute(x, axis, [(i, i ^ step) for i in range(count)])  24.3 us
    another operation x4, other arithmetic, _right_solve(): lax.linalg.triangular_solve(lower_factor, image, left_side=False, lower=T...  20.9 us
    ppermute x12, starting transfers between devices, _butterfly_gather(): other = lax.ppermute(x, axis, [(i, i ^ step) for i in range(count)])  15 us
    ppermute x9, starting transfers between devices, _direct_sum(): lax.ppermute(x, axis, [(i, i ^ k) for i in range(count)])  9.52 us
    ppermute x9, waiting for transfers between devices, _direct_sum(): lax.ppermute(x, axis, [(i, i ^ k) for i in range(count)])  8.33 us
    ppermute x1, waiting for transfers between devices, _pair_split_sum(): mine = mine + lax.ppermute(mine, axis, [(i, i ^ 2) for i in range(count)])  8.06 us
    ppermute x2, waiting for transfers between devices, _halving_sum(): x = keep + lax.ppermute(give, axis, [(i, i ^ step) for i in range(count)])  6.9 us
  transfers between devices with their start and end apart: 29, of which 13 were waited for; matrix products, arithmetic and copies ran while one was open for 29% of the time, Pallas kernels for 0%

profile of v16, /device:TPU:0, one launch (start us, length us, event | category | flops | bytes accessed | tf_op | source)
XLA Modules:
  0.0 171.8 jit_solution(8493304472411701142)
XLA Ops:
  0.7 2.2 %fusion.22 = f32[8,128,16]{1,2,0:T(8,128)S(1)} fusion(bf16[1024,8,16]{0,2,1:T(8,128)(2,1)} %param.7, bf16[8,1024,128]{2,1,0:T(8,128)(2,1)} %param.8), kind=kOutput, calls=%fused_computation.82 | convolution fusion | flops 33554432 | bytes 2424832 | tf_op jit(solution)/shard_map/mbs,bmr->brs/dot_general | solution.py:124
  3.4 2.6 %collective-permute-start.1 = (f32[8,128,16]{1,2,0:T(8,128)S(1)}, f32[8,128,16]{1,2,0:T(8,128)S(1)}, u32[]{:S(2)}, u32[]{:S(2)}) collective-permute-start(f32[8,128,16]{1,2,0:T(8,128)S(1)} %fusion.22), channel_id=1, source_target_pairs={{0,8},{4,12},{8,0},{12,4},{1,9},{5,13},{9,1},{13,5},{2,10},{6,14},... | collective-permute-start | bytes 196616 | tf_op jit(solution)/shard_map/ppermute | solution.py:44
  6.0 2.6 %collective-permute-done.1 = f32[8,128,16]{1,2,0:T(8,128)S(1)} collective-permute-done((f32[8,128,16]{1,2,0:T(8,128)S(1)}, f32[8,128,16]{1,2,0:T(8,128)S(1)}, u32[]{:S(2)}, u32[]{:S(2)}) %collective-permute-start.1) | collective-permute-done | bytes 65568 | tf_op jit(solution)/shard_map/ppermute | solution.py:44
  8.7 1.4 collective-permute-done.2
  10.7 1.4 collective-permute-start.3
  12.2 4.2 %collective-permute-start.10 = (bf16[1,512,128]{1,2,0:T(8,128)(2,1)S(1)}, bf16[1,512,128]{1,2,0:T(8,128)(2,1)S(1)}, u32[]{:S(2)}, u32[]{:S(2)}) collective-permute-start(bf16[1,512,128]{1,2,0:T(8,128)(2,1)S(1)} %bitcast.139), channel_id=1, source_target_pairs={{0,2},{1,3},{2,0},{3,1},{4,6},{5,7},{6,4},{7,5},{8,10},{9,11},{10,... | collective-permute-start | bytes 393224 | tf_op jit(solution)/shard_map/ppermute | solution.py:53
  16.4 1.5 collective-permute-start.13
  17.9 0.8 broadcast.49.clone.1
  19.5 0.7 broadcast.49.clone
  20.9 13.3 %collective-permute-done.10 = bf16[1,512,128]{1,2,0:T(8,128)(2,1)S(1)} collective-permute-done((bf16[1,512,128]{1,2,0:T(8,128)(2,1)S(1)}, bf16[1,512,128]{1,2,0:T(8,128)(2,1)S(1)}, u32[]{:S(2)}, u32[]{:S(2)}) %collective-permute-start.10) | collective-permute-done | bytes 131104 | tf_op jit(solution)/shard_map/ppermute | solution.py:53
  35.0 1.0 bitcast_dynamic-update-slice_fusion.12
  36.1 0.7 constant_dynamic-update-slice_fusion.7
  36.9 1.0 bitcast_dynamic-update-slice_fusion.5
  38.0 0.8 slice_bitcast_fusion.2
  38.8 1.6 collective-permute-start.4
  41.0 1.0 copy.11
  42.0 0.7 broadcast.49.clone.2
  43.4 2.2 %collective-permute-done.4 = bf16[1,512,128]{1,2,0:T(8,128)(2,1)} collective-permute-done((bf16[1,512,128]{1,2,0:T(8,128)(2,1)}, bf16[1,512,128]{1,2,0:T(8,128)(2,1)}, u32[]{:S(2)}, u32[]{:S(2)}) %collective-permute-start.4) | collective-permute-done | bytes 131104 | tf_op jit(solution)/shard_map/ppermute | solution.py:53
  45.6 1.0 copy.7
  46.7 4.7 %collective-permute-start.5 = (bf16[2,512,128]{2,1,0:T(8,128)(2,1)S(1)}, bf16[2,512,128]{2,1,0:T(8,128)(2,1)}, u32[]{:S(2)}, u32[]{:S(2)}) collective-permute-start(bf16[2,512,128]{2,1,0:T(8,128)(2,1)S(1)} %bitcast.124), channel_id=1, source_target_pairs={{0,8},{4,12},{8,0},{12,4},{1,9},{5,13},{9,1},{13,5},{2,10},{6,14},... | collective-permute-start | bytes 786440 | tf_op jit(solution)/shard_map/ppermute | solution.py:53
  51.4 1.0 copy.12
  53.5 1.0 bitcast_dynamic-update-slice_fusion.11
  54.5 1.6 collective-permute-start.12
  56.2 1.0 bitcast_dynamic-update-slice_fusion.10
  57.8 1.0 bitcast_dynamic-update-slice_fusion.7
  59.1 1.0 bitcast_dynamic-update-slice_fusion.8
  60.1 1.2 collective-permute-done.8
  61.9 7.7 %collective-permute-done.15 = bf16[4,512,128]{2,1,0:T(8,128)(2,1)S(1)} collective-permute-done((bf16[4,512,128]{2,1,0:T(8,128)(2,1)S(1)}, bf16[4,512,128]{2,1,0:T(8,128)(2,1)S(1)}, u32[]{:S(2)}, u32[]{:S(2)}) %collective-permute-start.15) | collective-permute-done | bytes 524320 | tf_op jit(solution)/shard_map/ppermute | solution.py:53
  70.0 2.4 %bitcast_multiply_fusion.2 = f32[1024,1024]{1,0:T(8,128)S(1)} fusion(bf16[8,512,128]{2,1,0:T(8,128)(2,1)S(1)} %bitcast.127, bf16[8,512,128]{2,1,0:T(8,128)(2,1)S(1)} %bitcast.129, bf16[8,512,128]{2,1,0:T(8,128)(2,1)S(1)} %bitcast.125, bf16[8,512,128]{2,1,0:T(8,128)(2,1)S(1)} %bitcast.131), kind=kOutput, calls=%fused_computation.2 | convolution fusion | flops 2156920832 | bytes 8388608 | tf_op jit(solution)/shard_map/dot_general | solution.py:167
  72.4 4.9 %fusion.5 = f32[1024,128]{1,0:T(8,128)S(1)} fusion(f32[1024,1024]{1,0:T(8,128)S(1)} %bitcast_multiply_fusion.2, f32[4096,128]{1,0:T(8,128)} %param.10, s32[]{:T(128)S(6)} %select_n.138), kind=kOutput, calls=%fused_computation.17 | convolution fusion | flops 1610612736 | bytes 5242884 | tf_op jit(solution)/shard_map/dot_general | solution.py:176
  77.4 1.9 %collective-permute-done.16 = f32[1024,128]{1,0:T(8,128)S(1)} collective-permute-done((f32[1024,128]{1,0:T(8,128)S(1)}, f32[1024,128]{1,0:T(8,128)S(1)}, u32[]{:S(2)}, u32[]{:S(2)}) %collective-permute-start.16) | collective-permute-done | bytes 524320 | tf_op jit(solution)/shard_map/ppermute | solution.py:93
  79.7 8.1 %collective-permute-done.17 = f32[512,128]{1,0:T(8,128)S(1)} collective-permute-done((f32[512,128]{1,0:T(8,128)S(1)}, f32[512,128]{1,0:T(8,128)S(1)}, u32[]{:S(2)}, u32[]{:S(2)}) %collective-permute-start.17) | collective-permute-done | bytes 262176 | tf_op jit(solution)/shard_map/ppermute | solution.py:96
  87.9 4.5 %fusion.2 = f32[1024,1024,1]{1,0,2:T(8,128)S(1)} fusion(bf16[8,512,128]{2,1,0:T(8,128)(2,1)} %bitcast.128, bf16[8,512,128]{2,1,0:T(8,128)(2,1)} %bitcast.130, bf16[8,512,128]{2,1,0:T(8,128)(2,1)} %bitcast.126, bf16[8,512,128]{2,1,0:T(8,128)(2,1)} %bitcast.132), kind=kOutput, calls=%fused_computation.6 | convolution fusion | flops 2155872256 | bytes 8388608 | tf_op jit(solution)/shard_map/dot_general | solution.py:170
  92.5 1.0 fusion.20
  94.2 1.2 collective-permute-start.20
  95.4 2.6 %collective-permute-start.21 = (f32[128,128]{0,1:T(8,128)S(1)}, f32[128,128]{0,1:T(8,128)S(1)}, u32[]{:S(2)}, u32[]{:S(2)}) collective-permute-start(f32[128,128]{0,1:T(8,128)S(1)} %fusion.20), channel_id=1, source_target_pairs={{0,3},{1,2},{2,1},{3,0},{4,7},{5,6},{6,5},{7,4},{8,11},{9,10},{10,... | collective-permute-start | bytes 196616 | tf_op jit(solution)/shard_map/ppermute | solution.py:44
  98.0 3.6 %fusion = f32[1024,128]{1,0:T(8,128)S(1)} fusion(f32[1024,128]{1,0:T(8,128)S(1)} %constant_dynamic-update-slice_fusion.4, f32[1024,1024,1]{1,0,2:T(8,128)S(1)} %fusion.2), kind=kOutput, calls=%fused_computation.1 | convolution fusion | flops 1611661312 | bytes 5242880 | tf_op jit(solution)/shard_map/dot_general | solution.py:181
  101.7 0.8 collective-permute-done.20
  102.7 6.9 %collective-permute-done.22 = f32[512,128]{1,0:T(8,128)S(1)} collective-permute-done((f32[512,128]{1,0:T(8,128)S(1)}, f32[512,128]{1,0:T(8,128)S(1)}, u32[]{:S(2)}, u32[]{:S(2)}) %collective-permute-start.22) | collective-permute-done | bytes 262176 | tf_op jit(solution)/shard_map/ppermute | solution.py:76
  110.3 11.7 %cholesky.44 = f32[128,128]{1,0:T(8,128)S(1)} custom-call(f32[128,128]{1,0:T(8,128)S(1)} %fusion.12), custom_call_target="Cholesky" | custom-call | tf_op jit(solution)/shard_map/jit(cholesky)/cholesky | solution.py:108
  122.1 2.4 %collective-permute-start.24 = (f32[256,128]{1,0:T(8,128)S(1)}, f32[256,128]{1,0:T(8,128)S(1)}, u32[]{:S(2)}, u32[]{:S(2)}) collective-permute-start(f32[256,128]{1,0:T(8,128)S(1)} %get-tuple-element.7), channel_id=1, source_target_pairs={{0,2},{1,3},{2,0},{3,1},{4,6},{5,7},{6,4},{7,5},{8,10},{9,11},{10,... | collective-permute-start | bytes 393224 | tf_op jit(solution)/shard_map/ppermute | solution.py:79
  125.1 4.6 %collective-permute-done.24 = f32[256,128]{1,0:T(8,128)S(1)} collective-permute-done((f32[256,128]{1,0:T(8,128)S(1)}, f32[256,128]{1,0:T(8,128)S(1)}, u32[]{:S(2)}, u32[]{:S(2)}) %collective-permute-start.24) | collective-permute-done | bytes 131104 | tf_op jit(solution)/shard_map/ppermute | solution.py:79
  130.5 9.8 %custom-call.6 = f32[1,128,128]{1,2,0:T(8,128)S(1)} custom-call(f32[1,128,128]{2,1,0:T(8,128)S(1)} %fusion.7), custom_call_target="InvertDiagBlocksLowerTriangular" | custom-call | tf_op jit(solution)/shard_map/triangular_solve/custom-call.0 | solution.py:112
  142.1 1.5 collective-permute-start.28
  143.6 3.2 %collective-permute-done.27 = f32[128,128]{0,1:T(8,128)S(1)} collective-permute-done((f32[128,128]{0,1:T(8,128)S(1)}, f32[128,128]{0,1:T(8,128)S(1)}, u32[]{:S(2)}, u32[]{:S(2)}) %collective-permute-start.27) | collective-permute-done | bytes 65568 | tf_op jit(solution)/shard_map/ppermute | solution.py:44
  147.3 11.9 %cholesky.55 = f32[128,128]{1,0:T(8,128)S(1)} custom-call(f32[128,128]{1,0:T(8,128)S(1)} %fusion.10), custom_call_target="Cholesky" | custom-call | tf_op jit(solution)/shard_map/jit(cholesky)/cholesky | solution.py:108
  160.5 9.8 %custom-call.7 = f32[1,128,128]{1,2,0:T(8,128)S(1)} custom-call(f32[1,128,128]{2,1,0:T(8,128)S(1)} %fusion.8), custom_call_target="InvertDiagBlocksLowerTriangular" | custom-call | tf_op jit(solution)/shard_map/triangular_solve/custom-call.0 | solution.py:112
  171.0 0.8 copy.31
  (113 shorter events, 16.2 us)
Async XLA Ops:
  0.6 9.4 %copy-start = (bf16[8,1024,128]{2,1,0:T(8,128)(2,1)S(1)}, bf16[8,1024,128]{2,1,0:T(8,128)(2,1)}, u32[]{:S(2)}) copy-start(bf16[8,1024,128]{2,1,0:T(8,128)(2,1)} %param.9) | copy-start | bytes 6291460
  0.6 9.4 %copy-start.6 = (bf16[1024,8,16]{0,2,1:T(8,128)(2,1)S(1)}, bf16[1024,8,16]{0,2,1:T(8,128)(2,1)}, u32[]{:S(2)}) copy-start(bf16[1024,8,16]{0,2,1:T(8,128)(2,1)} %param.7) | copy-start | bytes 786436
  2.9 3.2 %collective-permute-start = (f32[8,128,16]{1,2,0:T(8,128)S(1)}, f32[8,128,16]{1,2,0:T(8,128)S(1)}, u32[]{:S(2)}, u32[]{:S(2)}) collective-permute-start(f32[8,128,16]{1,2,0:T(8,128)S(1)} %fusion.22), channel_id=1, source_target_pairs={{0,4},{4,0},{8,12},{12,8},{1,5},{5,1},{9,13},{13,9},{2,6},{6,2},{1... | collective-permute-start | bytes 196616 | tf_op jit(solution)/shard_map/ppermute | solution.py:44
  3.4 5.2 %collective-permute-start.1 = (f32[8,128,16]{1,2,0:T(8,128)S(1)}, f32[8,128,16]{1,2,0:T(8,128)S(1)}, u32[]{:S(2)}, u32[]{:S(2)}) collective-permute-start(f32[8,128,16]{1,2,0:T(8,128)S(1)} %fusion.22), channel_id=1, source_target_pairs={{0,8},{4,12},{8,0},{12,4},{1,9},{5,13},{9,1},{13,5},{2,10},{6,14},... | collective-permute-start | bytes 196616 | tf_op jit(solution)/shard_map/ppermute | solution.py:44
  6.0 4.1 %collective-permute-start.2 = (f32[8,128,16]{1,2,0:T(8,128)S(1)}, f32[8,128,16]{1,2,0:T(8,128)S(1)}, u32[]{:S(2)}, u32[]{:S(2)}) collective-permute-start(f32[8,128,16]{1,2,0:T(8,128)S(1)} %fusion.22), channel_id=1, source_target_pairs={{0,12},{4,8},{8,4},{12,0},{1,13},{5,9},{9,5},{13,1},{2,14},{6,10},... | collective-permute-start | bytes 196616 | tf_op jit(solution)/shard_map/ppermute | solution.py:44
  10.7 27.2 %collective-permute-start.3 = (bf16[1024,128]{0,1:T(8,128)(2,1)S(1)}, bf16[1024,128]{0,1:T(8,128)(2,1)}, u32[]{:S(2)}, u32[]{:S(2)}) collective-permute-start(bf16[1024,128]{0,1:T(8,128)(2,1)S(1)} %bitcast.118), channel_id=1, source_target_pairs={{1,4},{2,8},{3,12},{4,1},{6,9},{7,13},{8,2},{9,6},{11,14},{12,3},{... | collective-permute-start | bytes 786440 | tf_op jit(solution)/shard_map/ppermute | solution.py:138
  12.2 21.9 %collective-permute-start.10 = (bf16[1,512,128]{1,2,0:T(8,128)(2,1)S(1)}, bf16[1,512,128]{1,2,0:T(8,128)(2,1)S(1)}, u32[]{:S(2)}, u32[]{:S(2)}) collective-permute-start(bf16[1,512,128]{1,2,0:T(8,128)(2,1)S(1)} %bitcast.139), channel_id=1, source_target_pairs={{0,2},{1,3},{2,0},{3,1},{4,6},{5,7},{6,4},{7,5},{8,10},{9,11},{10,... | collective-permute-start | bytes 393224 | tf_op jit(solution)/shard_map/ppermute | solution.py:53
  16.4 19.6 %collective-permute-start.13 = (bf16[1,512,128]{1,2,0:T(8,128)(2,1)S(1)}, bf16[1,512,128]{1,2,0:T(8,128)(2,1)S(1)}, u32[]{:S(2)}, u32[]{:S(2)}) collective-permute-start(bf16[1,512,128]{1,2,0:T(8,128)(2,1)S(1)} %bitcast.136), channel_id=1, source_target_pairs={{0,16},{16,0},{1,17},{17,1},{2,18},{18,2},{3,19},{19,3},{4,20},{20... | collective-permute-start | bytes 393224 | tf_op jit(solution)/shard_map/ppermute | solution.py:53
  34.9 18.5 %collective-permute-start.11 = (bf16[2,512,128]{2,1,0:T(8,128)(2,1)}, bf16[2,512,128]{2,1,0:T(8,128)(2,1)}, u32[]{:S(2)}, u32[]{:S(2)}) collective-permute-start(bf16[2,512,128]{2,1,0:T(8,128)(2,1)} %bitcast.32), channel_id=1, source_target_pairs={{0,1},{1,0},{2,3},{3,2},{4,5},{5,4},{6,7},{7,6},{8,9},{9,8},{10,11... | collective-permute-start | bytes 786440 | tf_op jit(solution)/shard_map/ppermute | solution.py:53
  36.8 19.4 %collective-permute-start.14 = (bf16[2,512,128]{2,1,0:T(8,128)(2,1)}, bf16[2,512,128]{2,1,0:T(8,128)(2,1)}, u32[]{:S(2)}, u32[]{:S(2)}) collective-permute-start(bf16[2,512,128]{2,1,0:T(8,128)(2,1)} %bitcast.43), channel_id=1, source_target_pairs={{0,2},{1,3},{2,0},{3,1},{4,6},{5,7},{6,4},{7,5},{8,10},{9,11},{10,... | collective-permute-start | bytes 786440 | tf_op jit(solution)/shard_map/ppermute | solution.py:53
  38.8 6.7 %collective-permute-start.4 = (bf16[1,512,128]{1,2,0:T(8,128)(2,1)}, bf16[1,512,128]{1,2,0:T(8,128)(2,1)}, u32[]{:S(2)}, u32[]{:S(2)}) collective-permute-start(bf16[1,512,128]{1,2,0:T(8,128)(2,1)} %get-tuple-element.10), channel_id=1, source_target_pairs={{0,16},{16,0},{1,17},{17,1},{2,18},{18,2},{3,19},{19,3},{4,20},{20... | collective-permute-start | bytes 393224 | tf_op jit(solution)/shard_map/ppermute | solution.py:53
  40.4 10.9 %collective-permute-start.7 = (bf16[1,512,128]{1,2,0:T(8,128)(2,1)}, bf16[1,512,128]{1,2,0:T(8,128)(2,1)}, u32[]{:S(2)}, u32[]{:S(2)}) collective-permute-start(bf16[1,512,128]{1,2,0:T(8,128)(2,1)} %get-tuple-element.11), channel_id=1, source_target_pairs={{0,16},{16,0},{1,17},{17,1},{2,18},{18,2},{3,19},{19,3},{4,20},{20... | collective-permute-start | bytes 393224 | tf_op jit(solution)/shard_map/ppermute | solution.py:53
  46.7 12.4 %collective-permute-start.5 = (bf16[2,512,128]{2,1,0:T(8,128)(2,1)S(1)}, bf16[2,512,128]{2,1,0:T(8,128)(2,1)}, u32[]{:S(2)}, u32[]{:S(2)}) collective-permute-start(bf16[2,512,128]{2,1,0:T(8,128)(2,1)S(1)} %bitcast.124), channel_id=1, source_target_pairs={{0,8},{4,12},{8,0},{12,4},{1,9},{5,13},{9,1},{13,5},{2,10},{6,14},... | collective-permute-start | bytes 786440 | tf_op jit(solution)/shard_map/ppermute | solution.py:53
  53.1 8.3 %collective-permute-start.8 = (bf16[2,512,128]{2,1,0:T(8,128)(2,1)}, bf16[2,512,128]{2,1,0:T(8,128)(2,1)S(1)}, u32[]{:S(2)}, u32[]{:S(2)}) collective-permute-start(bf16[2,512,128]{2,1,0:T(8,128)(2,1)} %bitcast.20), channel_id=1, source_target_pairs={{0,8},{4,12},{8,0},{12,4},{1,9},{5,13},{9,1},{13,5},{2,10},{6,14},... | collective-permute-start | bytes 786440 | tf_op jit(solution)/shard_map/ppermute | solution.py:53
  54.5 15.2 %collective-permute-start.12 = (bf16[4,512,128]{2,1,0:T(8,128)(2,1)S(1)}, bf16[4,512,128]{2,1,0:T(8,128)(2,1)S(1)}, u32[]{:S(2)}, u32[]{:S(2)}) collective-permute-start(bf16[4,512,128]{2,1,0:T(8,128)(2,1)S(1)} %bitcast.121), channel_id=1, source_target_pairs={{0,16},{16,0},{1,17},{17,1},{2,18},{18,2},{3,19},{19,3},{4,20},{20... | collective-permute-start | bytes 1572872 | tf_op jit(solution)/shard_map/ppermute | solution.py:53
  57.4 12.2 %collective-permute-start.15 = (bf16[4,512,128]{2,1,0:T(8,128)(2,1)S(1)}, bf16[4,512,128]{2,1,0:T(8,128)(2,1)S(1)}, u32[]{:S(2)}, u32[]{:S(2)}) collective-permute-start(bf16[4,512,128]{2,1,0:T(8,128)(2,1)S(1)} %bitcast.119), channel_id=1, source_target_pairs={{0,1},{1,0},{2,3},{3,2},{4,5},{5,4},{6,7},{7,6},{8,9},{9,8},{10,11... | collective-permute-start | bytes 1572872 | tf_op jit(solution)/shard_map/ppermute | solution.py:53
  60.1 9.7 %collective-permute-start.6 = (bf16[4,512,128]{2,1,0:T(8,128)(2,1)S(1)}, bf16[4,512,128]{2,1,0:T(8,128)(2,1)S(1)}, u32[]{:S(2)}, u32[]{:S(2)}) collective-permute-start(bf16[4,512,128]{2,1,0:T(8,128)(2,1)S(1)} %bitcast.123), channel_id=1, source_target_pairs={{0,4},{4,0},{8,12},{12,8},{1,5},{5,1},{9,13},{13,9},{2,6},{6,2},{1... | collective-permute-start | bytes 1572872 | tf_op jit(solution)/shard_map/ppermute | solution.py:53
  61.4 8.5 %collective-permute-start.9 = (bf16[4,512,128]{2,1,0:T(8,128)(2,1)S(1)}, bf16[4,512,128]{2,1,0:T(8,128)(2,1)S(1)}, u32[]{:S(2)}, u32[]{:S(2)}) collective-permute-start(bf16[4,512,128]{2,1,0:T(8,128)(2,1)S(1)} %bitcast.120), channel_id=1, source_target_pairs={{0,4},{4,0},{8,12},{12,8},{1,5},{5,1},{9,13},{13,9},{2,6},{6,2},{1... | collective-permute-start | bytes 1572872 | tf_op jit(solution)/shard_map/ppermute | solution.py:53
  69.7 2.7 %copy-start.3 = (bf16[2,2,2,512,128]{4,3,2,1,0:T(8,128)(2,1)}, bf16[2,2,2,512,128]{4,3,2,1,0:T(8,128)(2,1)S(1)}, u32[]{:S(2)}) copy-start(bf16[2,2,2,512,128]{4,3,2,1,0:T(8,128)(2,1)S(1)} %constant_dynamic-update-slice_fusion.6) | copy-start | bytes 3145732
  69.8 2.6 %copy-start.4 = (bf16[1,2,4,512,128]{4,3,2,1,0:T(8,128)(2,1)}, bf16[1,2,4,512,128]{4,3,2,1,0:T(8,128)(2,1)S(1)}, u32[]{:S(2)}) copy-start(bf16[1,2,4,512,128]{4,3,2,1,0:T(8,128)(2,1)S(1)} %bitcast_dynamic-update-slice_fusion.3) | copy-start | bytes 3145732
  69.9 2.5 %copy-start.5 = (bf16[2,2,2,512,128]{4,3,2,1,0:T(8,128)(2,1)}, bf16[2,2,2,512,128]{4,3,2,1,0:T(8,128)(2,1)S(1)}, u32[]{:S(2)}) copy-start(bf16[2,2,2,512,128]{4,3,2,1,0:T(8,128)(2,1)S(1)} %constant_dynamic-update-slice_fusion.14) | copy-start | bytes 3145732
  70.0 2.4 %copy-start.2 = (bf16[2,2,2,512,128]{4,3,2,1,0:T(8,128)(2,1)}, bf16[2,2,2,512,128]{4,3,2,1,0:T(8,128)(2,1)S(1)}, u32[]{:S(2)}) copy-start(bf16[2,2,2,512,128]{4,3,2,1,0:T(8,128)(2,1)S(1)} %constant_dynamic-update-slice_fusion.11) | copy-start | bytes 3145732
  72.4 4.9 %copy-start.1 = (f32[1024,1024]{1,0:T(8,128)}, f32[1024,1024]{1,0:T(8,128)S(1)}, u32[]{:S(2)}) copy-start(f32[1024,1024]{1,0:T(8,128)S(1)} %bitcast_multiply_fusion.2) | copy-start | bytes 12582916
  77.3 2.0 %collective-permute-start.16 = (f32[1024,128]{1,0:T(8,128)S(1)}, f32[1024,128]{1,0:T(8,128)S(1)}, u32[]{:S(2)}, u32[]{:S(2)}) collective-permute-start(f32[1024,128]{1,0:T(8,128)S(1)} %fusion.5), channel_id=1, source_target_pairs={{0,4},{4,0},{8,12},{12,8},{1,5},{5,1},{9,13},{13,9},{2,6},{6,2},{1... | collective-permute-start | bytes 1572872 | tf_op jit(solution)/shard_map/ppermute | solution.py:93
  79.4 8.4 %collective-permute-start.17 = (f32[512,128]{1,0:T(8,128)S(1)}, f32[512,128]{1,0:T(8,128)S(1)}, u32[]{:S(2)}, u32[]{:S(2)}) collective-permute-start(f32[512,128]{1,0:T(8,128)S(1)} %slice_select_fusion), channel_id=1, source_target_pairs={{0,8},{4,12},{8,0},{12,4},{1,9},{5,13},{9,1},{13,5},{2,10},{6,14},... | collective-permute-start | bytes 786440 | tf_op jit(solution)/shard_map/ppermute | solution.py:96
  87.9 4.6 %collective-permute-start.18 = (f32[512,128]{1,0:T(8,128)S(1)}, f32[512,128]{1,0:T(8,128)S(1)}, u32[]{:S(2)}, u32[]{:S(2)}) collective-permute-start(f32[512,128]{1,0:T(8,128)S(1)} %get-tuple-element.9), channel_id=1, source_target_pairs={{0,4},{4,0},{8,12},{12,8},{1,5},{5,1},{9,13},{13,9},{2,6},{6,2},{1... | collective-permute-start | bytes 786440 | tf_op jit(solution)/shard_map/ppermute | solution.py:97
  93.5 8.2 %collective-permute-start.19 = (f32[128,128]{0,1:T(8,128)S(1)}, f32[128,128]{0,1:T(8,128)S(1)}, u32[]{:S(2)}, u32[]{:S(2)}) collective-permute-start(f32[128,128]{0,1:T(8,128)S(1)} %fusion.20), channel_id=1, source_target_pairs={{0,1},{1,0},{2,3},{3,2},{4,5},{5,4},{6,7},{7,6},{8,9},{9,8},{10,11... | collective-permute-start | bytes 196616 | tf_op jit(solution)/shard_map/ppermute | solution.py:44
  94.2 8.4 %collective-permute-start.20 = (f32[128,128]{0,1:T(8,128)S(1)}, f32[128,128]{0,1:T(8,128)S(1)}, u32[]{:S(2)}, u32[]{:S(2)}) collective-permute-start(f32[128,128]{0,1:T(8,128)S(1)} %fusion.20), channel_id=1, source_target_pairs={{0,2},{1,3},{2,0},{3,1},{4,6},{5,7},{6,4},{7,5},{8,10},{9,11},{10,... | collective-permute-start | bytes 196616 | tf_op jit(solution)/shard_map/ppermute | solution.py:44
  95.4 7.2 %collective-permute-start.21 = (f32[128,128]{0,1:T(8,128)S(1)}, f32[128,128]{0,1:T(8,128)S(1)}, u32[]{:S(2)}, u32[]{:S(2)}) collective-permute-start(f32[128,128]{0,1:T(8,128)S(1)} %fusion.20), channel_id=1, source_target_pairs={{0,3},{1,2},{2,1},{3,0},{4,7},{5,6},{6,5},{7,4},{8,11},{9,10},{10,... | collective-permute-start | bytes 196616 | tf_op jit(solution)/shard_map/ppermute | solution.py:44
  101.6 7.9 %collective-permute-start.22 = (f32[512,128]{1,0:T(8,128)S(1)}, f32[512,128]{1,0:T(8,128)S(1)}, u32[]{:S(2)}, u32[]{:S(2)}) collective-permute-start(f32[512,128]{1,0:T(8,128)S(1)} %slice_select_fusion.1), channel_id=1, source_target_pairs={{0,1},{1,0},{2,3},{3,2},{4,5},{5,4},{6,7},{7,6},{8,9},{9,8},{10,11... | collective-permute-start | bytes 786440 | tf_op jit(solution)/shard_map/ppermute | solution.py:76
  109.6 12.4 %collective-permute-start.23 = (f32[256,128]{1,0:T(8,128)S(1)}, f32[256,128]{1,0:T(8,128)S(1)}, u32[]{:S(2)}, u32[]{:S(2)}) collective-permute-start(f32[256,128]{1,0:T(8,128)S(1)} %slice_select_fusion.2), channel_id=1, source_target_pairs={{0,2},{1,3},{2,0},{3,1},{4,6},{5,7},{6,4},{7,5},{8,10},{9,11},{10,... | collective-permute-start | bytes 393224 | tf_op jit(solution)/shard_map/ppermute | solution.py:76
  122.1 7.7 %collective-permute-start.24 = (f32[256,128]{1,0:T(8,128)S(1)}, f32[256,128]{1,0:T(8,128)S(1)}, u32[]{:S(2)}, u32[]{:S(2)}) collective-permute-start(f32[256,128]{1,0:T(8,128)S(1)} %get-tuple-element.7), channel_id=1, source_target_pairs={{0,2},{1,3},{2,0},{3,1},{4,6},{5,7},{6,4},{7,5},{8,10},{9,11},{10,... | collective-permute-start | bytes 393224 | tf_op jit(solution)/shard_map/ppermute | solution.py:79
  129.8 10.6 %collective-permute-start.25 = (f32[512,128]{1,0:T(8,128)S(1)}, f32[512,128]{1,0:T(8,128)S(1)}, u32[]{:S(2)}, u32[]{:S(2)}) collective-permute-start(f32[512,128]{1,0:T(8,128)S(1)} %constant_dynamic-update-slice_fusion.2), channel_id=1, source_target_pairs={{0,1},{1,0},{2,3},{3,2},{4,5},{5,4},{6,7},{7,6},{8,9},{9,8},{10,11... | collective-permute-start | bytes 786440 | tf_op jit(solution)/shard_map/ppermute | solution.py:79
  141.7 1.9 %collective-permute-start.26 = (f32[128,128]{0,1:T(8,128)S(1)}, f32[128,128]{0,1:T(8,128)S(1)}, u32[]{:S(2)}, u32[]{:S(2)}) collective-permute-start(f32[128,128]{0,1:T(8,128)S(1)} %fusion.21), channel_id=1, source_target_pairs={{0,4},{4,0},{8,12},{12,8},{1,5},{5,1},{9,13},{13,9},{2,6},{6,2},{1... | collective-permute-start | bytes 196616 | tf_op jit(solution)/shard_map/ppermute | solution.py:44
  141.8 5.0 %collective-permute-start.27 = (f32[128,128]{0,1:T(8,128)S(1)}, f32[128,128]{0,1:T(8,128)S(1)}, u32[]{:S(2)}, u32[]{:S(2)}) collective-permute-start(f32[128,128]{0,1:T(8,128)S(1)} %fusion.21), channel_id=1, source_target_pairs={{0,8},{4,12},{8,0},{12,4},{1,9},{5,13},{9,1},{13,5},{2,10},{6,14},... | collective-permute-start | bytes 196616 | tf_op jit(solution)/shard_map/ppermute | solution.py:44
  142.1 5.0 %collective-permute-start.28 = (f32[128,128]{0,1:T(8,128)S(1)}, f32[128,128]{0,1:T(8,128)S(1)}, u32[]{:S(2)}, u32[]{:S(2)}) collective-permute-start(f32[128,128]{0,1:T(8,128)S(1)} %fusion.21), channel_id=1, source_target_pairs={{0,12},{4,8},{8,4},{12,0},{1,13},{5,9},{9,5},{13,1},{2,14},{6,10},... | collective-permute-start | bytes 196616 | tf_op jit(solution)/shard_map/ppermute | solution.py:44

commit v17 on v15

--- a/solution.py
+++ b/solution.py
@@ -151,10 +151,11 @@
             ],
             1,
         )
+        x_first = left_plan[len(bins):len(bins) + 1] + left_plan[: len(bins)] + left_plan[len(bins) + 1:]
         left_rows = jnp.concatenate(
             [
                 _butterfly_gather(swapped[:half], left_plan),
-                _butterfly_gather(swapped[half:], left_plan),
+                _butterfly_gather(swapped[half:], x_first),
             ],
             1,
         )

time: 172 us -> 173 us (level)
  no operation moved by 1% of the time
where the time goes in v17:
time: 173 us; the launch traced here: 172 us
  waiting for transfers between devices  52.9 us (31%)
  other arithmetic  46.3 us (27%)
  starting transfers between devices  31.2 us (18%)
  matrix products  21.1 us (12%)
  local copies, waits for them, and re-layouts  19.3 us (11%)
    another operation x6, other arithmetic, _lower_factor(): return jnp.linalg.cholesky(_direct_sum(gram_part, gram_axis))  25 us
    ppermute x12, waiting for transfers between devices, _butterfly_gather(): other = lax.ppermute(x, axis, [(i, i ^ step) for i in range(count)])  23.7 us
    another operation x4, other arithmetic, _right_solve(): jax.scipy.linalg.solve_triangular(lower_factor, image.T, lower=True)  20.9 us
    ppermute x12, starting transfers between devices, _butterfly_gather(): other = lax.ppermute(x, axis, [(i, i ^ step) for i in range(count)])  16 us
    ppermute x9, starting transfers between devices, _direct_sum(): lax.ppermute(x, axis, [(i, i ^ k) for i in range(count)])  9.52 us
    ppermute x9, waiting for transfers between devices, _direct_sum(): lax.ppermute(x, axis, [(i, i ^ k) for i in range(count)])  8.33 us
    ppermute x1, waiting for transfers between devices, _pair_split_sum(): mine = mine + lax.ppermute(mine, axis, [(i, i ^ 2) for i in range(count)])  7.43 us
    ppermute x2, waiting for transfers between devices, _halving_sum(): x = keep + lax.ppermute(give, axis, [(i, i ^ step) for i in range(count)])  6.9 us
  transfers between devices with their start and end apart: 29, of which 13 were waited for; matrix products, arithmetic and copies ran while one was open for 29% of the time, Pallas kernels for 0%

profile of v17, /device:TPU:0, one launch (start us, length us, event | category | flops | bytes accessed | tf_op | source)
XLA Modules:
  0.0 172.1 jit_solution(3956451620836619795)
XLA Ops:
  0.7 2.2 %fusion.25 = f32[8,128,16]{1,2,0:T(8,128)S(1)} fusion(bf16[1024,8,16]{0,2,1:T(8,128)(2,1)} %param.7, bf16[8,1024,128]{2,1,0:T(8,128)(2,1)} %param.8), kind=kOutput, calls=%fused_computation.83 | convolution fusion | flops 33554432 | bytes 2424832 | tf_op jit(solution)/shard_map/mbs,bmr->brs/dot_general | solution.py:122
  3.4 2.6 %collective-permute-start.1 = (f32[8,128,16]{1,2,0:T(8,128)S(1)}, f32[8,128,16]{1,2,0:T(8,128)S(1)}, u32[]{:S(2)}, u32[]{:S(2)}) collective-permute-start(f32[8,128,16]{1,2,0:T(8,128)S(1)} %fusion.25), channel_id=1, source_target_pairs={{0,8},{4,12},{8,0},{12,4},{1,9},{5,13},{9,1},{13,5},{2,10},{6,14},... | collective-permute-start | bytes 196616 | tf_op jit(solution)/shard_map/ppermute | solution.py:44
  6.0 2.6 %collective-permute-done.1 = f32[8,128,16]{1,2,0:T(8,128)S(1)} collective-permute-done((f32[8,128,16]{1,2,0:T(8,128)S(1)}, f32[8,128,16]{1,2,0:T(8,128)S(1)}, u32[]{:S(2)}, u32[]{:S(2)}) %collective-permute-start.1) | collective-permute-done | bytes 65568 | tf_op jit(solution)/shard_map/ppermute | solution.py:44
  8.7 1.4 collective-permute-done.2
  10.7 1.4 collective-permute-start.3
  12.2 4.2 %collective-permute-start.10 = (bf16[1,512,128]{1,2,0:T(8,128)(2,1)S(1)}, bf16[1,512,128]{1,2,0:T(8,128)(2,1)S(1)}, u32[]{:S(2)}, u32[]{:S(2)}) collective-permute-start(bf16[1,512,128]{1,2,0:T(8,128)(2,1)S(1)} %bitcast.133), channel_id=1, source_target_pairs={{0,2},{1,3},{2,0},{3,1},{4,6},{5,7},{6,4},{7,5},{8,10},{9,11},{10,... | collective-permute-start | bytes 393224 | tf_op jit(solution)/shard_map/ppermute | solution.py:53
  16.4 1.5 collective-permute-start.13
  17.9 0.8 broadcast.58.clone.1
  20.9 13.3 %collective-permute-done.10 = bf16[1,512,128]{1,2,0:T(8,128)(2,1)S(1)} collective-permute-done((bf16[1,512,128]{1,2,0:T(8,128)(2,1)S(1)}, bf16[1,512,128]{1,2,0:T(8,128)(2,1)S(1)}, u32[]{:S(2)}, u32[]{:S(2)}) %collective-permute-start.10) | collective-permute-done | bytes 131104 | tf_op jit(solution)/shard_map/ppermute | solution.py:53
  35.0 1.0 bitcast_dynamic-update-slice_fusion.10
  36.9 1.0 bitcast_dynamic-update-slice_fusion.5
  38.0 0.8 slice_bitcast_fusion.2
  38.8 1.6 collective-permute-start.4
  40.4 4.6 %collective-permute-start.7 = (bf16[1,512,128]{1,2,0:T(8,128)(2,1)}, bf16[1,512,128]{1,2,0:T(8,128)(2,1)}, u32[]{:S(2)}, u32[]{:S(2)}) collective-permute-start(bf16[1,512,128]{1,2,0:T(8,128)(2,1)} %get-tuple-element.11), channel_id=1, source_target_pairs={{0,8},{4,12},{8,0},{12,4},{1,9},{5,13},{9,1},{13,5},{2,10},{6,14},... | collective-permute-start | bytes 393224 | tf_op jit(solution)/shard_map/ppermute | solution.py:53
  45.1 1.0 copy.11
  46.2 0.7 broadcast.58.clone.2
  47.6 1.0 copy.7
  48.6 1.5 collective-permute-start.5
  50.1 1.0 copy.12
  51.8 1.5 collective-permute-start.8
  53.3 1.0 bitcast_dynamic-update-slice_fusion.9
  55.0 1.0 bitcast_dynamic-update-slice_fusion.8
  56.7 1.0 bitcast_dynamic-update-slice_fusion.12
  57.9 1.0 bitcast_dynamic-update-slice_fusion.6
  59.0 2.2 %collective-permute-done.8 = bf16[2,512,128]{2,1,0:T(8,128)(2,1)S(1)} collective-permute-done((bf16[2,512,128]{2,1,0:T(8,128)(2,1)}, bf16[2,512,128]{2,1,0:T(8,128)(2,1)S(1)}, u32[]{:S(2)}, u32[]{:S(2)}) %collective-permute-start.8) | collective-permute-done | bytes 262176 | tf_op jit(solution)/shard_map/ppermute | solution.py:53
  61.8 6.4 %collective-permute-done.15 = bf16[4,512,128]{2,1,0:T(8,128)(2,1)S(1)} collective-permute-done((bf16[4,512,128]{2,1,0:T(8,128)(2,1)S(1)}, bf16[4,512,128]{2,1,0:T(8,128)(2,1)S(1)}, u32[]{:S(2)}, u32[]{:S(2)}) %collective-permute-start.15) | collective-permute-done | bytes 524320 | tf_op jit(solution)/shard_map/ppermute | solution.py:53
  68.2 1.8 %collective-permute-done.12 = bf16[4,512,128]{2,1,0:T(8,128)(2,1)S(1)} collective-permute-done((bf16[4,512,128]{2,1,0:T(8,128)(2,1)S(1)}, bf16[4,512,128]{2,1,0:T(8,128)(2,1)S(1)}, u32[]{:S(2)}, u32[]{:S(2)}) %collective-permute-start.12) | collective-permute-done | bytes 524320 | tf_op jit(solution)/shard_map/ppermute | solution.py:53
  70.3 2.4 %bitcast_multiply_fusion.2 = f32[1024,1024]{1,0:T(8,128)S(1)} fusion(bf16[8,512,128]{2,1,0:T(8,128)(2,1)S(1)} %bitcast.121, bf16[8,512,128]{2,1,0:T(8,128)(2,1)S(1)} %bitcast.123, bf16[8,512,128]{2,1,0:T(8,128)(2,1)S(1)} %bitcast.119, bf16[8,512,128]{2,1,0:T(8,128)(2,1)S(1)} %bitcast.125), kind=kOutput, calls=%fused_computation.2 | convolution fusion | flops 2156920832 | bytes 8388608 | tf_op jit(solution)/shard_map/dot_general | solution.py:166
  72.7 4.9 %fusion.7 = f32[1024,128]{1,0:T(8,128)S(1)} fusion(f32[1024,1024]{1,0:T(8,128)S(1)} %bitcast_multiply_fusion.2, f32[4096,128]{1,0:T(8,128)} %param.10, s32[]{:T(128)S(6)} %select_n.138), kind=kOutput, calls=%fused_computation.17 | convolution fusion | flops 1610612736 | bytes 5242884 | tf_op jit(solution)/shard_map/dot_general | solution.py:175
  77.7 1.9 %collective-permute-done.16 = f32[1024,128]{1,0:T(8,128)S(1)} collective-permute-done((f32[1024,128]{1,0:T(8,128)S(1)}, f32[1024,128]{1,0:T(8,128)S(1)}, u32[]{:S(2)}, u32[]{:S(2)}) %collective-permute-start.16) | collective-permute-done | bytes 524320 | tf_op jit(solution)/shard_map/ppermute | solution.py:93
  79.7 1.0 collective-permute-start.17
  80.7 7.4 %collective-permute-done.17 = f32[512,128]{1,0:T(8,128)S(1)} collective-permute-done((f32[512,128]{1,0:T(8,128)S(1)}, f32[512,128]{1,0:T(8,128)S(1)}, u32[]{:S(2)}, u32[]{:S(2)}) %collective-permute-start.17) | collective-permute-done | bytes 262176 | tf_op jit(solution)/shard_map/ppermute | solution.py:96
  88.3 4.5 %fusion.2 = f32[1024,1024,1]{1,0,2:T(8,128)S(1)} fusion(bf16[8,512,128]{2,1,0:T(8,128)(2,1)} %bitcast.122, bf16[8,512,128]{2,1,0:T(8,128)(2,1)} %bitcast.124, bf16[8,512,128]{2,1,0:T(8,128)(2,1)} %bitcast.120, bf16[8,512,128]{2,1,0:T(8,128)(2,1)} %bitcast.126), kind=kOutput, calls=%fused_computation.6 | convolution fusion | flops 2155872256 | bytes 8388608 | tf_op jit(solution)/shard_map/dot_general | solution.py:169
  92.9 1.0 fusion.23
  94.5 1.0 collective-permute-start.20
  95.5 2.8 %collective-permute-start.21 = (f32[128,128]{0,1:T(8,128)S(1)}, f32[128,128]{0,1:T(8,128)S(1)}, u32[]{:S(2)}, u32[]{:S(2)}) collective-permute-start(f32[128,128]{0,1:T(8,128)S(1)} %fusion.23), channel_id=1, source_target_pairs={{0,3},{1,2},{2,1},{3,0},{4,7},{5,6},{6,5},{7,4},{8,11},{9,10},{10,... | collective-permute-start | bytes 196616 | tf_op jit(solution)/shard_map/ppermute | solution.py:44
  98.3 3.6 %fusion = f32[1024,128]{1,0:T(8,128)S(1)} fusion(f32[1024,128]{1,0:T(8,128)S(1)} %constant_dynamic-update-slice_fusion.4, f32[1024,1024,1]{1,0,2:T(8,128)S(1)} %fusion.2), kind=kOutput, calls=%fused_computation.1 | convolution fusion | flops 1611661312 | bytes 5242880 | tf_op jit(solution)/shard_map/dot_general | solution.py:180
  102.1 0.8 collective-permute-done.20
  103.0 6.9 %collective-permute-done.22 = f32[512,128]{1,0:T(8,128)S(1)} collective-permute-done((f32[512,128]{1,0:T(8,128)S(1)}, f32[512,128]{1,0:T(8,128)S(1)}, u32[]{:S(2)}, u32[]{:S(2)}) %collective-permute-start.22) | collective-permute-done | bytes 262176 | tf_op jit(solution)/shard_map/ppermute | solution.py:76
  110.6 11.7 %cholesky.44 = f32[128,128]{1,0:T(8,128)S(1)} custom-call(f32[128,128]{1,0:T(8,128)S(1)} %fusion.15), custom_call_target="Cholesky" | custom-call | tf_op jit(solution)/shard_map/jit(cholesky)/cholesky | solution.py:108
  122.4 2.4 %collective-permute-start.24 = (f32[256,128]{1,0:T(8,128)S(1)}, f32[256,128]{1,0:T(8,128)S(1)}, u32[]{:S(2)}, u32[]{:S(2)}) collective-permute-start(f32[256,128]{1,0:T(8,128)S(1)} %get-tuple-element.7), channel_id=1, source_target_pairs={{0,2},{1,3},{2,0},{3,1},{4,6},{5,7},{6,4},{7,5},{8,10},{9,11},{10,... | collective-permute-start | bytes 393224 | tf_op jit(solution)/shard_map/ppermute | solution.py:79
  125.5 4.6 %collective-permute-done.24 = f32[256,128]{1,0:T(8,128)S(1)} collective-permute-done((f32[256,128]{1,0:T(8,128)S(1)}, f32[256,128]{1,0:T(8,128)S(1)}, u32[]{:S(2)}, u32[]{:S(2)}) %collective-permute-start.24) | collective-permute-done | bytes 131104 | tf_op jit(solution)/shard_map/ppermute | solution.py:79
  130.9 9.8 %custom-call.6 = f32[1,128,128]{1,2,0:T(8,128)S(1)} custom-call(f32[1,128,128]{2,1,0:T(8,128)S(1)} %fusion.9), custom_call_target="InvertDiagBlocksLowerTriangular" | custom-call | tf_op jit(solution)/shard_map/jit(_solve_triangular)/triangular_solve | solution.py:112
  142.8 1.2 collective-permute-start.28
  144.0 3.2 %collective-permute-done.27 = f32[128,128]{0,1:T(8,128)S(1)} collective-permute-done((f32[128,128]{0,1:T(8,128)S(1)}, f32[128,128]{0,1:T(8,128)S(1)}, u32[]{:S(2)}, u32[]{:S(2)}) %collective-permute-start.27) | collective-permute-done | bytes 65568 | tf_op jit(solution)/shard_map/ppermute | solution.py:44
  147.6 11.9 %cholesky.55 = f32[128,128]{1,0:T(8,128)S(1)} custom-call(f32[128,128]{1,0:T(8,128)S(1)} %fusion.13), custom_call_target="Cholesky" | custom-call | tf_op jit(solution)/shard_map/jit(cholesky)/cholesky | solution.py:108
  160.9 9.8 %custom-call.7 = f32[1,128,128]{1,2,0:T(8,128)S(1)} custom-call(f32[1,128,128]{2,1,0:T(8,128)S(1)} %fusion.10), custom_call_target="InvertDiagBlocksLowerTriangular" | custom-call | tf_op jit(solution)/shard_map/jit(_solve_triangular)/triangular_solve | solution.py:112
  171.3 0.8 copy.28
  (113 shorter events, 17.2 us)
Async XLA Ops:
  0.6 9.4 %copy-start = (bf16[8,1024,128]{2,1,0:T(8,128)(2,1)S(1)}, bf16[8,1024,128]{2,1,0:T(8,128)(2,1)}, u32[]{:S(2)}) copy-start(bf16[8,1024,128]{2,1,0:T(8,128)(2,1)} %param.9) | copy-start | bytes 6291460
  0.6 9.4 %copy-start.6 = (bf16[1024,8,16]{0,2,1:T(8,128)(2,1)S(1)}, bf16[1024,8,16]{0,2,1:T(8,128)(2,1)}, u32[]{:S(2)}) copy-start(bf16[1024,8,16]{0,2,1:T(8,128)(2,1)} %param.7) | copy-start | bytes 786436
  2.9 3.2 %collective-permute-start = (f32[8,128,16]{1,2,0:T(8,128)S(1)}, f32[8,128,16]{1,2,0:T(8,128)S(1)}, u32[]{:S(2)}, u32[]{:S(2)}) collective-permute-start(f32[8,128,16]{1,2,0:T(8,128)S(1)} %fusion.25), channel_id=1, source_target_pairs={{0,4},{4,0},{8,12},{12,8},{1,5},{5,1},{9,13},{13,9},{2,6},{6,2},{1... | collective-permute-start | bytes 196616 | tf_op jit(solution)/shard_map/ppermute | solution.py:44
  3.4 5.2 %collective-permute-start.1 = (f32[8,128,16]{1,2,0:T(8,128)S(1)}, f32[8,128,16]{1,2,0:T(8,128)S(1)}, u32[]{:S(2)}, u32[]{:S(2)}) collective-permute-start(f32[8,128,16]{1,2,0:T(8,128)S(1)} %fusion.25), channel_id=1, source_target_pairs={{0,8},{4,12},{8,0},{12,4},{1,9},{5,13},{9,1},{13,5},{2,10},{6,14},... | collective-permute-start | bytes 196616 | tf_op jit(solution)/shard_map/ppermute | solution.py:44
  6.0 4.1 %collective-permute-start.2 = (f32[8,128,16]{1,2,0:T(8,128)S(1)}, f32[8,128,16]{1,2,0:T(8,128)S(1)}, u32[]{:S(2)}, u32[]{:S(2)}) collective-permute-start(f32[8,128,16]{1,2,0:T(8,128)S(1)} %fusion.25), channel_id=1, source_target_pairs={{0,12},{4,8},{8,4},{12,0},{1,13},{5,9},{9,5},{13,1},{2,14},{6,10},... | collective-permute-start | bytes 196616 | tf_op jit(solution)/shard_map/ppermute | solution.py:44
  10.7 27.2 %collective-permute-start.3 = (bf16[1024,128]{0,1:T(8,128)(2,1)S(1)}, bf16[1024,128]{0,1:T(8,128)(2,1)}, u32[]{:S(2)}, u32[]{:S(2)}) collective-permute-start(bf16[1024,128]{0,1:T(8,128)(2,1)S(1)} %bitcast.112), channel_id=1, source_target_pairs={{1,4},{2,8},{3,12},{4,1},{6,9},{7,13},{8,2},{9,6},{11,14},{12,3},{... | collective-permute-start | bytes 786440 | tf_op jit(solution)/shard_map/ppermute | solution.py:136
  12.2 21.9 %collective-permute-start.10 = (bf16[1,512,128]{1,2,0:T(8,128)(2,1)S(1)}, bf16[1,512,128]{1,2,0:T(8,128)(2,1)S(1)}, u32[]{:S(2)}, u32[]{:S(2)}) collective-permute-start(bf16[1,512,128]{1,2,0:T(8,128)(2,1)S(1)} %bitcast.133), channel_id=1, source_target_pairs={{0,2},{1,3},{2,0},{3,1},{4,6},{5,7},{6,4},{7,5},{8,10},{9,11},{10,... | collective-permute-start | bytes 393224 | tf_op jit(solution)/shard_map/ppermute | solution.py:53
  16.4 19.6 %collective-permute-start.13 = (bf16[1,512,128]{1,2,0:T(8,128)(2,1)S(1)}, bf16[1,512,128]{1,2,0:T(8,128)(2,1)S(1)}, u32[]{:S(2)}, u32[]{:S(2)}) collective-permute-start(bf16[1,512,128]{1,2,0:T(8,128)(2,1)S(1)} %bitcast.130), channel_id=1, source_target_pairs={{0,16},{16,0},{1,17},{17,1},{2,18},{18,2},{3,19},{19,3},{4,20},{20... | collective-permute-start | bytes 393224 | tf_op jit(solution)/shard_map/ppermute | solution.py:53
  34.9 18.4 %collective-permute-start.11 = (bf16[2,512,128]{2,1,0:T(8,128)(2,1)}, bf16[2,512,128]{2,1,0:T(8,128)(2,1)}, u32[]{:S(2)}, u32[]{:S(2)}) collective-permute-start(bf16[2,512,128]{2,1,0:T(8,128)(2,1)} %bitcast.29), channel_id=1, source_target_pairs={{0,1},{1,0},{2,3},{3,2},{4,5},{5,4},{6,7},{7,6},{8,9},{9,8},{10,11... | collective-permute-start | bytes 786440 | tf_op jit(solution)/shard_map/ppermute | solution.py:53
  36.8 18.2 %collective-permute-start.14 = (bf16[2,512,128]{2,1,0:T(8,128)(2,1)}, bf16[2,512,128]{2,1,0:T(8,128)(2,1)}, u32[]{:S(2)}, u32[]{:S(2)}) collective-permute-start(bf16[2,512,128]{2,1,0:T(8,128)(2,1)} %bitcast.40), channel_id=1, source_target_pairs={{0,2},{1,3},{2,0},{3,1},{4,6},{5,7},{6,4},{7,5},{8,10},{9,11},{10,... | collective-permute-start | bytes 786440 | tf_op jit(solution)/shard_map/ppermute | solution.py:53
  38.8 8.7 %collective-permute-start.4 = (bf16[1,512,128]{1,2,0:T(8,128)(2,1)}, bf16[1,512,128]{1,2,0:T(8,128)(2,1)}, u32[]{:S(2)}, u32[]{:S(2)}) collective-permute-start(bf16[1,512,128]{1,2,0:T(8,128)(2,1)} %get-tuple-element.10), channel_id=1, source_target_pairs={{0,16},{16,0},{1,17},{17,1},{2,18},{18,2},{3,19},{19,3},{4,20},{20... | collective-permute-start | bytes 393224 | tf_op jit(solution)/shard_map/ppermute | solution.py:53
  40.4 9.7 %collective-permute-start.7 = (bf16[1,512,128]{1,2,0:T(8,128)(2,1)}, bf16[1,512,128]{1,2,0:T(8,128)(2,1)}, u32[]{:S(2)}, u32[]{:S(2)}) collective-permute-start(bf16[1,512,128]{1,2,0:T(8,128)(2,1)} %get-tuple-element.11), channel_id=1, source_target_pairs={{0,8},{4,12},{8,0},{12,4},{1,9},{5,13},{9,1},{13,5},{2,10},{6,14},... | collective-permute-start | bytes 393224 | tf_op jit(solution)/shard_map/ppermute | solution.py:53
  48.6 9.2 %collective-permute-start.5 = (bf16[2,512,128]{2,1,0:T(8,128)(2,1)S(1)}, bf16[2,512,128]{2,1,0:T(8,128)(2,1)}, u32[]{:S(2)}, u32[]{:S(2)}) collective-permute-start(bf16[2,512,128]{2,1,0:T(8,128)(2,1)S(1)} %bitcast.118), channel_id=1, source_target_pairs={{0,8},{4,12},{8,0},{12,4},{1,9},{5,13},{9,1},{13,5},{2,10},{6,14},... | collective-permute-start | bytes 786440 | tf_op jit(solution)/shard_map/ppermute | solution.py:53
  51.8 9.4 %collective-permute-start.8 = (bf16[2,512,128]{2,1,0:T(8,128)(2,1)}, bf16[2,512,128]{2,1,0:T(8,128)(2,1)S(1)}, u32[]{:S(2)}, u32[]{:S(2)}) collective-permute-start(bf16[2,512,128]{2,1,0:T(8,128)(2,1)} %bitcast.19), channel_id=1, source_target_pairs={{0,16},{16,0},{1,17},{17,1},{2,18},{18,2},{3,19},{19,3},{4,20},{20... | collective-permute-start | bytes 786440 | tf_op jit(solution)/shard_map/ppermute | solution.py:53
  54.3 15.7 %collective-permute-start.12 = (bf16[4,512,128]{2,1,0:T(8,128)(2,1)S(1)}, bf16[4,512,128]{2,1,0:T(8,128)(2,1)S(1)}, u32[]{:S(2)}, u32[]{:S(2)}) collective-permute-start(bf16[4,512,128]{2,1,0:T(8,128)(2,1)S(1)} %bitcast.115), channel_id=1, source_target_pairs={{0,16},{16,0},{1,17},{17,1},{2,18},{18,2},{3,19},{19,3},{4,20},{20... | collective-permute-start | bytes 1572872 | tf_op jit(solution)/shard_map/ppermute | solution.py:53
  56.2 11.9 %collective-permute-start.15 = (bf16[4,512,128]{2,1,0:T(8,128)(2,1)S(1)}, bf16[4,512,128]{2,1,0:T(8,128)(2,1)S(1)}, u32[]{:S(2)}, u32[]{:S(2)}) collective-permute-start(bf16[4,512,128]{2,1,0:T(8,128)(2,1)S(1)} %bitcast.113), channel_id=1, source_target_pairs={{0,1},{1,0},{2,3},{3,2},{4,5},{5,4},{6,7},{7,6},{8,9},{9,8},{10,11... | collective-permute-start | bytes 1572872 | tf_op jit(solution)/shard_map/ppermute | solution.py:53
  58.9 11.2 %collective-permute-start.6 = (bf16[4,512,128]{2,1,0:T(8,128)(2,1)S(1)}, bf16[4,512,128]{2,1,0:T(8,128)(2,1)S(1)}, u32[]{:S(2)}, u32[]{:S(2)}) collective-permute-start(bf16[4,512,128]{2,1,0:T(8,128)(2,1)S(1)} %bitcast.114), channel_id=1, source_target_pairs={{0,4},{4,0},{8,12},{12,8},{1,5},{5,1},{9,13},{13,9},{2,6},{6,2},{1... | collective-permute-start | bytes 1572872 | tf_op jit(solution)/shard_map/ppermute | solution.py:53
  61.2 9.0 %collective-permute-start.9 = (bf16[4,512,128]{2,1,0:T(8,128)(2,1)S(1)}, bf16[4,512,128]{2,1,0:T(8,128)(2,1)S(1)}, u32[]{:S(2)}, u32[]{:S(2)}) collective-permute-start(bf16[4,512,128]{2,1,0:T(8,128)(2,1)S(1)} %bitcast.117), channel_id=1, source_target_pairs={{0,4},{4,0},{8,12},{12,8},{1,5},{5,1},{9,13},{13,9},{2,6},{6,2},{1... | collective-permute-start | bytes 1572872 | tf_op jit(solution)/shard_map/ppermute | solution.py:53
  68.2 4.5 %copy-start.3 = (bf16[2,2,2,512,128]{4,3,2,1,0:T(8,128)(2,1)}, bf16[2,2,2,512,128]{4,3,2,1,0:T(8,128)(2,1)S(1)}, u32[]{:S(2)}) copy-start(bf16[2,2,2,512,128]{4,3,2,1,0:T(8,128)(2,1)S(1)} %constant_dynamic-update-slice_fusion.6) | copy-start | bytes 3145732
  70.1 2.6 %copy-start.4 = (bf16[1,2,4,512,128]{4,3,2,1,0:T(8,128)(2,1)}, bf16[1,2,4,512,128]{4,3,2,1,0:T(8,128)(2,1)S(1)}, u32[]{:S(2)}) copy-start(bf16[1,2,4,512,128]{4,3,2,1,0:T(8,128)(2,1)S(1)} %bitcast_dynamic-update-slice_fusion.2) | copy-start | bytes 3145732
  70.2 2.5 %copy-start.5 = (bf16[2,2,2,512,128]{4,3,2,1,0:T(8,128)(2,1)}, bf16[2,2,2,512,128]{4,3,2,1,0:T(8,128)(2,1)S(1)}, u32[]{:S(2)}) copy-start(bf16[2,2,2,512,128]{4,3,2,1,0:T(8,128)(2,1)S(1)} %constant_dynamic-update-slice_fusion.14) | copy-start | bytes 3145732
  70.3 2.4 %copy-start.2 = (bf16[2,2,2,512,128]{4,3,2,1,0:T(8,128)(2,1)}, bf16[2,2,2,512,128]{4,3,2,1,0:T(8,128)(2,1)S(1)}, u32[]{:S(2)}) copy-start(bf16[2,2,2,512,128]{4,3,2,1,0:T(8,128)(2,1)S(1)} %constant_dynamic-update-slice_fusion.11) | copy-start | bytes 3145732
  72.7 4.9 %copy-start.1 = (f32[1024,1024]{1,0:T(8,128)}, f32[1024,1024]{1,0:T(8,128)S(1)}, u32[]{:S(2)}) copy-start(f32[1024,1024]{1,0:T(8,128)S(1)} %bitcast_multiply_fusion.2) | copy-start | bytes 12582916
  77.6 2.0 %collective-permute-start.16 = (f32[1024,128]{1,0:T(8,128)S(1)}, f32[1024,128]{1,0:T(8,128)S(1)}, u32[]{:S(2)}, u32[]{:S(2)}) collective-permute-start(f32[1024,128]{1,0:T(8,128)S(1)} %fusion.7), channel_id=1, source_target_pairs={{0,4},{4,0},{8,12},{12,8},{1,5},{5,1},{9,13},{13,9},{2,6},{6,2},{1... | collective-permute-start | bytes 1572872 | tf_op jit(solution)/shard_map/ppermute | solution.py:93
  79.7 8.4 %collective-permute-start.17 = (f32[512,128]{1,0:T(8,128)S(1)}, f32[512,128]{1,0:T(8,128)S(1)}, u32[]{:S(2)}, u32[]{:S(2)}) collective-permute-start(f32[512,128]{1,0:T(8,128)S(1)} %slice_select_fusion), channel_id=1, source_target_pairs={{0,8},{4,12},{8,0},{12,4},{1,9},{5,13},{9,1},{13,5},{2,10},{6,14},... | collective-permute-start | bytes 786440 | tf_op jit(solution)/shard_map/ppermute | solution.py:96
  88.2 4.6 %collective-permute-start.18 = (f32[512,128]{1,0:T(8,128)S(1)}, f32[512,128]{1,0:T(8,128)S(1)}, u32[]{:S(2)}, u32[]{:S(2)}) collective-permute-start(f32[512,128]{1,0:T(8,128)S(1)} %get-tuple-element.9), channel_id=1, source_target_pairs={{0,4},{4,0},{8,12},{12,8},{1,5},{5,1},{9,13},{13,9},{2,6},{6,2},{1... | collective-permute-start | bytes 786440 | tf_op jit(solution)/shard_map/ppermute | solution.py:97
  93.9 8.2 %collective-permute-start.19 = (f32[128,128]{0,1:T(8,128)S(1)}, f32[128,128]{0,1:T(8,128)S(1)}, u32[]{:S(2)}, u32[]{:S(2)}) collective-permute-start(f32[128,128]{0,1:T(8,128)S(1)} %fusion.23), channel_id=1, source_target_pairs={{0,1},{1,0},{2,3},{3,2},{4,5},{5,4},{6,7},{7,6},{8,9},{9,8},{10,11... | collective-permute-start | bytes 196616 | tf_op jit(solution)/shard_map/ppermute | solution.py:44
  94.5 8.4 %collective-permute-start.20 = (f32[128,128]{0,1:T(8,128)S(1)}, f32[128,128]{0,1:T(8,128)S(1)}, u32[]{:S(2)}, u32[]{:S(2)}) collective-permute-start(f32[128,128]{0,1:T(8,128)S(1)} %fusion.23), channel_id=1, source_target_pairs={{0,2},{1,3},{2,0},{3,1},{4,6},{5,7},{6,4},{7,5},{8,10},{9,11},{10,... | collective-permute-start | bytes 196616 | tf_op jit(solution)/shard_map/ppermute | solution.py:44
  95.5 7.4 %collective-permute-start.21 = (f32[128,128]{0,1:T(8,128)S(1)}, f32[128,128]{0,1:T(8,128)S(1)}, u32[]{:S(2)}, u32[]{:S(2)}) collective-permute-start(f32[128,128]{0,1:T(8,128)S(1)} %fusion.23), channel_id=1, source_target_pairs={{0,3},{1,2},{2,1},{3,0},{4,7},{5,6},{6,5},{7,4},{8,11},{9,10},{10,... | collective-permute-start | bytes 196616 | tf_op jit(solution)/shard_map/ppermute | solution.py:44
  102.0 7.9 %collective-permute-start.22 = (f32[512,128]{1,0:T(8,128)S(1)}, f32[512,128]{1,0:T(8,128)S(1)}, u32[]{:S(2)}, u32[]{:S(2)}) collective-permute-start(f32[512,128]{1,0:T(8,128)S(1)} %slice_select_fusion.1), channel_id=1, source_target_pairs={{0,1},{1,0},{2,3},{3,2},{4,5},{5,4},{6,7},{7,6},{8,9},{9,8},{10,11... | collective-permute-start | bytes 786440 | tf_op jit(solution)/shard_map/ppermute | solution.py:76
  110.0 12.4 %collective-permute-start.23 = (f32[256,128]{1,0:T(8,128)S(1)}, f32[256,128]{1,0:T(8,128)S(1)}, u32[]{:S(2)}, u32[]{:S(2)}) collective-permute-start(f32[256,128]{1,0:T(8,128)S(1)} %slice_select_fusion.2), channel_id=1, source_target_pairs={{0,2},{1,3},{2,0},{3,1},{4,6},{5,7},{6,4},{7,5},{8,10},{9,11},{10,... | collective-permute-start | bytes 393224 | tf_op jit(solution)/shard_map/ppermute | solution.py:76
  122.4 7.7 %collective-permute-start.24 = (f32[256,128]{1,0:T(8,128)S(1)}, f32[256,128]{1,0:T(8,128)S(1)}, u32[]{:S(2)}, u32[]{:S(2)}) collective-permute-start(f32[256,128]{1,0:T(8,128)S(1)} %get-tuple-element.7), channel_id=1, source_target_pairs={{0,2},{1,3},{2,0},{3,1},{4,6},{5,7},{6,4},{7,5},{8,10},{9,11},{10,... | collective-permute-start | bytes 393224 | tf_op jit(solution)/shard_map/ppermute | solution.py:79
  130.1 10.6 %collective-permute-start.25 = (f32[512,128]{1,0:T(8,128)S(1)}, f32[512,128]{1,0:T(8,128)S(1)}, u32[]{:S(2)}, u32[]{:S(2)}) collective-permute-start(f32[512,128]{1,0:T(8,128)S(1)} %constant_dynamic-update-slice_fusion.2), channel_id=1, source_target_pairs={{0,1},{1,0},{2,3},{3,2},{4,5},{5,4},{6,7},{7,6},{8,9},{9,8},{10,11... | collective-permute-start | bytes 786440 | tf_op jit(solution)/shard_map/ppermute | solution.py:79
  142.0 1.9 %collective-permute-start.26 = (f32[128,128]{0,1:T(8,128)S(1)}, f32[128,128]{0,1:T(8,128)S(1)}, u32[]{:S(2)}, u32[]{:S(2)}) collective-permute-start(f32[128,128]{0,1:T(8,128)S(1)} %fusion.24), channel_id=1, source_target_pairs={{0,4},{4,0},{8,12},{12,8},{1,5},{5,1},{9,13},{13,9},{2,6},{6,2},{1... | collective-permute-start | bytes 196616 | tf_op jit(solution)/shard_map/ppermute | solution.py:44
  142.1 5.0 %collective-permute-start.27 = (f32[128,128]{0,1:T(8,128)S(1)}, f32[128,128]{0,1:T(8,128)S(1)}, u32[]{:S(2)}, u32[]{:S(2)}) collective-permute-start(f32[128,128]{0,1:T(8,128)S(1)} %fusion.24), channel_id=1, source_target_pairs={{0,8},{4,12},{8,0},{12,4},{1,9},{5,13},{9,1},{13,5},{2,10},{6,14},... | collective-permute-start | bytes 196616 | tf_op jit(solution)/shard_map/ppermute | solution.py:44
  142.8 4.7 %collective-permute-start.28 = (f32[128,128]{0,1:T(8,128)S(1)}, f32[128,128]{0,1:T(8,128)S(1)}, u32[]{:S(2)}, u32[]{:S(2)}) collective-permute-start(f32[128,128]{0,1:T(8,128)S(1)} %fusion.24), channel_id=1, source_target_pairs={{0,12},{4,8},{8,4},{12,0},{1,13},{5,9},{9,5},{13,1},{2,14},{6,10},... | collective-permute-start | bytes 196616 | tf_op jit(solution)/shard_map/ppermute | solution.py:44

commit v18 on v15

--- a/solution.py
+++ b/solution.py
@@ -144,10 +144,11 @@
         half = rows_here // 2
         early_bin = [step for step in right_plan if step[0] == "bin"]
         early_bin += [step for step in right_plan if step[0] != "bin"]
+        z_share = 3 * rows_here // 4 if rows_here % 64 == 0 else half
         right_rows = jnp.concatenate(
             [
-                _butterfly_gather(local_rows[:half], right_plan),
-                _butterfly_gather(local_rows[half:], early_bin),
+                _butterfly_gather(local_rows[:z_share], right_plan),
+                _butterfly_gather(local_rows[z_share:], early_bin),
             ],
             1,
         )

time: 172 us -> 186 us (1.081)
  waiting for transfers between devices: 54.1 us -> 63.4 us
  local copies, waits for them, and re-layouts: 19.3 us -> 22.9 us
    ppermute x12, waiting for transfers between devices: 24.3 us -> 32.1 us  [_butterfly_gather(): other = lax.ppermute(x, axis, [(i, i ^ step) for i in range(count)])]
    dynamic_update_slice x12, local copies, waits for them, and re-layouts: 5.33 us -> 7.66 us  [_butterfly_gather(): both = lax.dynamic_update_slice_in_dim(both, theirs, 1 - first, 1)]
    ppermute x2, starting transfers between devices: 0.73 us -> 3.01 us  [_halving_sum(): x = keep + lax.ppermute(give, axis, [(i, i ^ step) for i in range(count)])]
    ppermute x2, waiting for transfers between devices: 4.61 us -> 6.62 us  [_halving_sum(): other = lax.ppermute(x, axis, [(i, i ^ step) for i in range(count)])]
  transfers between devices with their start and end apart: 29 -> 29, of which waited for: 13 -> 17; matrix products, arithmetic and copies ran while one was open for 29% -> 28% of each run, Pallas kernels for 0% -> 0%
where the time goes in v18:
time: 186 us; the launch traced here: 185 us
  waiting for transfers between devices  63.4 us (34%)
  other arithmetic  47 us (25%)
  starting transfers between devices  29.7 us (16%)
  local copies, waits for them, and re-layouts  22.9 us (12%)
  matrix products  20.7 us (11%)
    ppermute x12, waiting for transfers between devices, _butterfly_gather(): other = lax.ppermute(x, axis, [(i, i ^ step) for i in range(count)])  32.1 us
    another operation x6, other arithmetic, _lower_factor(): return jnp.linalg.cholesky(_direct_sum(gram_part, gram_axis))  25 us
    another operation x4, other arithmetic, _right_solve(): jax.scipy.linalg.solve_triangular(lower_factor, image.T, lower=True)  20.9 us
    ppermute x12, starting transfers between devices, _butterfly_gather(): other = lax.ppermute(x, axis, [(i, i ^ step) for i in range(count)])  14.8 us
    ppermute x9, starting transfers between devices, _direct_sum(): lax.ppermute(x, axis, [(i, i ^ k) for i in range(count)])  9.55 us
    ppermute x9, waiting for transfers between devices, _direct_sum(): lax.ppermute(x, axis, [(i, i ^ k) for i in range(count)])  9.5 us
    ppermute x1, waiting for transfers between devices, _pair_split_sum(): mine = mine + lax.ppermute(mine, axis, [(i, i ^ 2) for i in range(count)])  7.73 us
    dynamic_update_slice x12, local copies, waits for them, and re-layouts, _butterfly_gather(): both = lax.dynamic_update_slice_in_dim(both, theirs, 1 - first, 1)  7.66 us
  transfers between devices with their start and end apart: 29, of which 17 were waited for; matrix products, arithmetic and copies ran while one was open for 28% of the time, Pallas kernels for 0%

profile of v18, /device:TPU:0, one launch (start us, length us, event | category | flops | bytes accessed | tf_op | source)
XLA Modules:
  0.0 185.1 jit_solution(17584928102264447943)
XLA Ops:
  0.7 2.2 %fusion.24 = f32[8,128,16]{1,2,0:T(8,128)S(1)} fusion(bf16[1024,8,16]{0,2,1:T(8,128)(2,1)} %param.7, bf16[8,1024,128]{2,1,0:T(8,128)(2,1)} %param.8), kind=kOutput, calls=%fused_computation.82 | convolution fusion | flops 33554432 | bytes 2424832 | tf_op jit(solution)/shard_map/mbs,bmr->brs/dot_general | solution.py:122
  3.4 2.6 %collective-permute-start.1 = (f32[8,128,16]{1,2,0:T(8,128)S(1)}, f32[8,128,16]{1,2,0:T(8,128)S(1)}, u32[]{:S(2)}, u32[]{:S(2)}) collective-permute-start(f32[8,128,16]{1,2,0:T(8,128)S(1)} %fusion.24), channel_id=1, source_target_pairs={{0,8},{4,12},{8,0},{12,4},{1,9},{5,13},{9,1},{13,5},{2,10},{6,14},... | collective-permute-start | bytes 196616 | tf_op jit(solution)/shard_map/ppermute | solution.py:44
  6.0 2.6 %collective-permute-done.1 = f32[8,128,16]{1,2,0:T(8,128)S(1)} collective-permute-done((f32[8,128,16]{1,2,0:T(8,128)S(1)}, f32[8,128,16]{1,2,0:T(8,128)S(1)}, u32[]{:S(2)}, u32[]{:S(2)}) %collective-permute-start.1) | collective-permute-done | bytes 65568 | tf_op jit(solution)/shard_map/ppermute | solution.py:44
  8.7 1.4 collective-permute-done.2
  11.8 4.9 %collective-permute-start.10 = (bf16[1,768,128]{2,1,0:T(8,128)(2,1)S(1)}, bf16[1,768,128]{2,1,0:T(8,128)(2,1)}, u32[]{:S(2)}, u32[]{:S(2)}) collective-permute-start(bf16[1,768,128]{2,1,0:T(8,128)(2,1)S(1)} %copy.37), channel_id=1, source_target_pairs={{0,2},{1,3},{2,0},{3,1},{4,6},{5,7},{6,4},{7,5},{8,10},{9,11},{10,... | collective-permute-start | bytes 589832 | tf_op jit(solution)/shard_map/ppermute | solution.py:53
  16.8 1.6 collective-permute-start.13
  18.4 0.8 broadcast_in_dim.38
  19.9 1.2 collective-permute-done.13
  23.2 17.2 %collective-permute-done.10 = bf16[1,768,128]{2,1,0:T(8,128)(2,1)} collective-permute-done((bf16[1,768,128]{2,1,0:T(8,128)(2,1)S(1)}, bf16[1,768,128]{2,1,0:T(8,128)(2,1)}, u32[]{:S(2)}, u32[]{:S(2)}) %collective-permute-start.10) | collective-permute-done | bytes 196640 | tf_op jit(solution)/shard_map/ppermute | solution.py:53
  40.3 1.6 bitcast_dynamic-update-slice_fusion.11
  43.3 1.0 bitcast_dynamic-update-slice_fusion.9
  44.3 1.5 collective-permute-start.15
  45.9 1.1 bitcast_dynamic-update-slice_fusion.5
  47.9 1.6 collective-permute-start.4
  49.9 0.7 broadcast.55.clone.1
  54.3 1.0 bitcast_dynamic-update-slice_fusion.8
  55.9 1.0 copy.34
  57.6 2.0 %collective-permute-start.8 = (bf16[2,512,128]{2,1,0:T(8,128)(2,1)}, bf16[2,512,128]{2,1,0:T(8,128)(2,1)S(1)}, u32[]{:S(2)}, u32[]{:S(2)}) collective-permute-start(bf16[2,512,128]{2,1,0:T(8,128)(2,1)} %bitcast.20), channel_id=1, source_target_pairs={{0,8},{4,12},{8,0},{12,4},{1,9},{5,13},{9,1},{13,5},{2,10},{6,14},... | collective-permute-start | bytes 786440 | tf_op jit(solution)/shard_map/ppermute | solution.py:53
  59.7 1.0 bitcast_dynamic-update-slice_fusion.6
  60.7 1.7 constant_dynamic-update-slice_fusion.6
  62.4 1.0 bitcast_dynamic-update-slice_fusion.4
  63.5 1.6 collective-permute-start.12
  65.4 1.0 bitcast_dynamic-update-slice_fusion.7
  67.5 0.8 collective-permute-done.6
  69.2 11.1 %collective-permute-done.12 = bf16[4,768,128]{2,1,0:T(8,128)(2,1)S(1)} collective-permute-done((bf16[4,768,128]{2,1,0:T(8,128)(2,1)S(1)}, bf16[4,768,128]{2,1,0:T(8,128)(2,1)S(1)}, u32[]{:S(2)}, u32[]{:S(2)}) %collective-permute-start.12) | collective-permute-done | bytes 786464 | tf_op jit(solution)/shard_map/ppermute | solution.py:53
  80.4 2.4 %bitcast_multiply_fusion.2 = f32[1024,1024]{1,0:T(8,128)S(1)} fusion(bf16[8,256,128]{2,1,0:T(8,128)(2,1)S(1)} %bitcast.128, bf16[8,768,128]{2,1,0:T(8,128)(2,1)S(1)} %bitcast.122, bf16[8,512,128]{2,1,0:T(8,128)(2,1)S(1)} %bitcast.124, bf16[8,512,128]{2,1,0:T(8,128)(2,1)S(1)} %bitcast.126), kind=kOutput, calls=%fused_computation.2 | convolution fusion | flops 2156920832 | bytes 8388608 | tf_op jit(solution)/shard_map/dot_general | solution.py:166
  82.8 4.9 %fusion.7 = f32[1024,128]{1,0:T(8,128)S(1)} fusion(f32[1024,1024]{1,0:T(8,128)S(1)} %bitcast_multiply_fusion.2, f32[4096,128]{1,0:T(8,128)} %param.10, s32[]{:T(128)S(6)} %select_n.138), kind=kOutput, calls=%fused_computation.16 | convolution fusion | flops 1610612736 | bytes 5242884 | tf_op jit(solution)/shard_map/dot_general | solution.py:175
  87.8 1.9 %collective-permute-done.16 = f32[1024,128]{1,0:T(8,128)S(1)} collective-permute-done((f32[1024,128]{1,0:T(8,128)S(1)}, f32[1024,128]{1,0:T(8,128)S(1)}, u32[]{:S(2)}, u32[]{:S(2)}) %collective-permute-start.16) | collective-permute-done | bytes 524320 | tf_op jit(solution)/shard_map/ppermute | solution.py:93
  89.8 0.7 slice_select_fusion
  90.5 0.8 collective-permute-start.17
  91.3 7.7 %collective-permute-done.17 = f32[512,128]{1,0:T(8,128)S(1)} collective-permute-done((f32[512,128]{1,0:T(8,128)}, f32[512,128]{1,0:T(8,128)S(1)}, u32[]{:S(2)}, u32[]{:S(2)}) %collective-permute-start.17) | collective-permute-done | bytes 262176 | tf_op jit(solution)/shard_map/ppermute | solution.py:96
  99.2 4.4 %fusion.2 = f32[1024,1024,1]{1,0,2:T(8,128)S(1)} fusion(bf16[8,256,128]{2,1,0:T(8,128)(2,1)S(1)} %bitcast.129, bf16[8,768,128]{2,1,0:T(8,128)(2,1)} %bitcast.123, bf16[8,512,128]{2,1,0:T(8,128)(2,1)} %bitcast.125, bf16[8,512,128]{2,1,0:T(8,128)(2,1)} %bitcast.127), kind=kOutput, calls=%fused_computation.6 | convolution fusion | flops 2155872256 | bytes 8388608 | tf_op jit(solution)/shard_map/dot_general | solution.py:169
  103.7 1.0 fusion.22
  104.7 1.2 collective-permute-start.19
  105.9 3.3 %collective-permute-start.20 = (f32[128,128]{0,1:T(8,128)S(1)}, f32[128,128]{0,1:T(8,128)S(1)}, u32[]{:S(2)}, u32[]{:S(2)}) collective-permute-start(f32[128,128]{0,1:T(8,128)S(1)} %fusion.22), channel_id=1, source_target_pairs={{0,2},{1,3},{2,0},{3,1},{4,6},{5,7},{6,4},{7,5},{8,10},{9,11},{10,... | collective-permute-start | bytes 196616 | tf_op jit(solution)/shard_map/ppermute | solution.py:44
  109.2 3.4 %fusion = f32[1024,128]{1,0:T(8,128)S(1)} fusion(f32[1024,128]{1,0:T(8,128)S(1)} %constant_dynamic-update-slice_fusion.4, f32[1024,1024,1]{1,0,2:T(8,128)S(1)} %fusion.2), kind=kOutput, calls=%fused_computation.1 | convolution fusion | flops 1611661312 | bytes 5242880 | tf_op jit(solution)/shard_map/dot_general | solution.py:180
  113.4 1.8 collective-permute-done.21
  115.3 5.5 %collective-permute-done.22 = f32[512,128]{1,0:T(8,128)S(1)} collective-permute-done((f32[512,128]{1,0:T(8,128)S(1)}, f32[512,128]{1,0:T(8,128)S(1)}, u32[]{:S(2)}, u32[]{:S(2)}) %collective-permute-start.22) | collective-permute-done | bytes 262176 | tf_op jit(solution)/shard_map/ppermute | solution.py:76
  120.9 2.4 %collective-permute-start.23 = (f32[256,128]{1,0:T(8,128)S(1)}, f32[256,128]{1,0:T(8,128)S(1)}, u32[]{:S(2)}, u32[]{:S(2)}) collective-permute-start(f32[256,128]{1,0:T(8,128)S(1)} %slice_select_fusion.2), channel_id=1, source_target_pairs={{0,2},{1,3},{2,0},{3,1},{4,6},{5,7},{6,4},{7,5},{8,10},{9,11},{10,... | collective-permute-start | bytes 393224 | tf_op jit(solution)/shard_map/ppermute | solution.py:76
  123.3 11.7 %cholesky.44 = f32[128,128]{1,0:T(8,128)S(1)} custom-call(f32[128,128]{1,0:T(8,128)S(1)} %fusion.15), custom_call_target="Cholesky" | custom-call | tf_op jit(solution)/shard_map/jit(cholesky)/cholesky | solution.py:108
  136.5 6.6 %collective-permute-done.24 = f32[256,128]{1,0:T(8,128)S(1)} collective-permute-done((f32[256,128]{1,0:T(8,128)S(1)}, f32[256,128]{1,0:T(8,128)S(1)}, u32[]{:S(2)}, u32[]{:S(2)}) %collective-permute-start.24) | collective-permute-done | bytes 131104 | tf_op jit(solution)/shard_map/ppermute | solution.py:79
  143.9 9.8 %custom-call.6 = f32[1,128,128]{1,2,0:T(8,128)S(1)} custom-call(f32[1,128,128]{2,1,0:T(8,128)S(1)} %fusion.9), custom_call_target="InvertDiagBlocksLowerTriangular" | custom-call | tf_op jit(solution)/shard_map/jit(_solve_triangular)/triangular_solve | solution.py:112
  155.1 0.9 collective-permute-start.27
  156.0 1.0 collective-permute-start.28
  156.9 3.2 %collective-permute-done.27 = f32[128,128]{0,1:T(8,128)S(1)} collective-permute-done((f32[128,128]{0,1:T(8,128)S(1)}, f32[128,128]{0,1:T(8,128)S(1)}, u32[]{:S(2)}, u32[]{:S(2)}) %collective-permute-start.27) | collective-permute-done | bytes 65568 | tf_op jit(solution)/shard_map/ppermute | solution.py:44
  160.6 11.9 %cholesky.55 = f32[128,128]{1,0:T(8,128)S(1)} custom-call(f32[128,128]{1,0:T(8,128)S(1)} %fusion.13), custom_call_target="Cholesky" | custom-call | tf_op jit(solution)/shard_map/jit(cholesky)/cholesky | solution.py:108
  173.8 9.8 %custom-call.7 = f32[1,128,128]{1,2,0:T(8,128)S(1)} custom-call(f32[1,128,128]{2,1,0:T(8,128)S(1)} %fusion.10), custom_call_target="InvertDiagBlocksLowerTriangular" | custom-call | tf_op jit(solution)/shard_map/jit(_solve_triangular)/triangular_solve | solution.py:112
  184.3 0.8 copy.51
  (120 shorter events, 22.6 us)
Async XLA Ops:
  0.6 9.4 %copy-start = (bf16[8,1024,128]{2,1,0:T(8,128)(2,1)S(1)}, bf16[8,1024,128]{2,1,0:T(8,128)(2,1)}, u32[]{:S(2)}) copy-start(bf16[8,1024,128]{2,1,0:T(8,128)(2,1)} %param.9) | copy-start | bytes 6291460
  0.6 9.4 %copy-start.5 = (bf16[1024,8,16]{0,2,1:T(8,128)(2,1)S(1)}, bf16[1024,8,16]{0,2,1:T(8,128)(2,1)}, u32[]{:S(2)}) copy-start(bf16[1024,8,16]{0,2,1:T(8,128)(2,1)} %param.7) | copy-start | bytes 786436
  2.9 3.2 %collective-permute-start = (f32[8,128,16]{1,2,0:T(8,128)S(1)}, f32[8,128,16]{1,2,0:T(8,128)S(1)}, u32[]{:S(2)}, u32[]{:S(2)}) collective-permute-start(f32[8,128,16]{1,2,0:T(8,128)S(1)} %fusion.24), channel_id=1, source_target_pairs={{0,4},{4,0},{8,12},{12,8},{1,5},{5,1},{9,13},{13,9},{2,6},{6,2},{1... | collective-permute-start | bytes 196616 | tf_op jit(solution)/shard_map/ppermute | solution.py:44
  3.4 5.2 %collective-permute-start.1 = (f32[8,128,16]{1,2,0:T(8,128)S(1)}, f32[8,128,16]{1,2,0:T(8,128)S(1)}, u32[]{:S(2)}, u32[]{:S(2)}) collective-permute-start(f32[8,128,16]{1,2,0:T(8,128)S(1)} %fusion.24), channel_id=1, source_target_pairs={{0,8},{4,12},{8,0},{12,4},{1,9},{5,13},{9,1},{13,5},{2,10},{6,14},... | collective-permute-start | bytes 196616 | tf_op jit(solution)/shard_map/ppermute | solution.py:44
  6.0 4.1 %collective-permute-start.2 = (f32[8,128,16]{1,2,0:T(8,128)S(1)}, f32[8,128,16]{1,2,0:T(8,128)S(1)}, u32[]{:S(2)}, u32[]{:S(2)}) collective-permute-start(f32[8,128,16]{1,2,0:T(8,128)S(1)} %fusion.24), channel_id=1, source_target_pairs={{0,12},{4,8},{8,4},{12,0},{1,13},{5,9},{9,5},{13,1},{2,14},{6,10},... | collective-permute-start | bytes 196616 | tf_op jit(solution)/shard_map/ppermute | solution.py:44
  10.7 36.2 %collective-permute-start.3 = (bf16[1024,128]{0,1:T(8,128)(2,1)S(1)}, bf16[1024,128]{0,1:T(8,128)(2,1)S(1)}, u32[]{:S(2)}, u32[]{:S(2)}) collective-permute-start(bf16[1024,128]{0,1:T(8,128)(2,1)S(1)} %bitcast.117), channel_id=1, source_target_pairs={{1,4},{2,8},{3,12},{4,1},{6,9},{7,13},{8,2},{9,6},{11,14},{12,3},{... | collective-permute-start | bytes 786440 | tf_op jit(solution)/shard_map/ppermute | solution.py:136
  11.8 28.6 %collective-permute-start.10 = (bf16[1,768,128]{2,1,0:T(8,128)(2,1)S(1)}, bf16[1,768,128]{2,1,0:T(8,128)(2,1)}, u32[]{:S(2)}, u32[]{:S(2)}) collective-permute-start(bf16[1,768,128]{2,1,0:T(8,128)(2,1)S(1)} %copy.37), channel_id=1, source_target_pairs={{0,2},{1,3},{2,0},{3,1},{4,6},{5,7},{6,4},{7,5},{8,10},{9,11},{10,... | collective-permute-start | bytes 589832 | tf_op jit(solution)/shard_map/ppermute | solution.py:53
  16.8 4.3 %collective-permute-start.13 = (bf16[1,256,128]{1,2,0:T(8,128)(2,1)S(1)}, bf16[1,256,128]{1,2,0:T(8,128)(2,1)S(1)}, u32[]{:S(2)}, u32[]{:S(2)}) collective-permute-start(bf16[1,256,128]{1,2,0:T(8,128)(2,1)S(1)} %bitcast.134), channel_id=1, source_target_pairs={{0,16},{16,0},{1,17},{17,1},{2,18},{18,2},{3,19},{19,3},{4,20},{20... | collective-permute-start | bytes 196616 | tf_op jit(solution)/shard_map/ppermute | solution.py:53
  21.2 21.3 %collective-permute-start.14 = (bf16[2,256,128]{2,1,0:T(8,128)(2,1)S(1)}, bf16[2,256,128]{2,1,0:T(8,128)(2,1)S(1)}, u32[]{:S(2)}, u32[]{:S(2)}) collective-permute-start(bf16[2,256,128]{2,1,0:T(8,128)(2,1)S(1)} %bitcast.130), channel_id=1, source_target_pairs={{0,2},{1,3},{2,0},{3,1},{4,6},{5,7},{6,4},{7,5},{8,10},{9,11},{10,... | collective-permute-start | bytes 393224 | tf_op jit(solution)/shard_map/ppermute | solution.py:53
  42.0 20.5 %collective-permute-start.11 = (bf16[2,768,128]{2,1,0:T(8,128)(2,1)}, bf16[2,768,128]{2,1,0:T(8,128)(2,1)}, u32[]{:S(2)}, u32[]{:S(2)}) collective-permute-start(bf16[2,768,128]{2,1,0:T(8,128)(2,1)} %bitcast.30), channel_id=1, source_target_pairs={{0,1},{1,0},{2,3},{3,2},{4,5},{5,4},{6,7},{7,6},{8,9},{9,8},{10,11... | collective-permute-start | bytes 1179656 | tf_op jit(solution)/shard_map/ppermute | solution.py:53
  44.3 2.6 %copy-start.6 = (bf16[2,2,2,256,128]{4,3,2,1,0:T(8,128)(2,1)}, bf16[2,2,2,256,128]{4,3,2,1,0:T(8,128)(2,1)S(1)}, u32[]{:S(2)}) copy-start(bf16[2,2,2,256,128]{4,3,2,1,0:T(8,128)(2,1)S(1)} %bitcast_dynamic-update-slice_fusion.9) | copy-start | bytes 1572868
  44.3 16.4 %collective-permute-start.15 = (bf16[4,256,128]{2,1,0:T(8,128)(2,1)}, bf16[4,256,128]{2,1,0:T(8,128)(2,1)}, u32[]{:S(2)}, u32[]{:S(2)}) collective-permute-start(bf16[4,256,128]{2,1,0:T(8,128)(2,1)} %bitcast.44), channel_id=1, source_target_pairs={{0,1},{1,0},{2,3},{3,2},{4,5},{5,4},{6,7},{7,6},{8,9},{9,8},{10,11... | collective-permute-start | bytes 786440 | tf_op jit(solution)/shard_map/ppermute | solution.py:53
  47.9 5.5 %collective-permute-start.4 = (bf16[1,512,128]{1,2,0:T(8,128)(2,1)S(1)}, bf16[1,512,128]{1,2,0:T(8,128)(2,1)S(1)}, u32[]{:S(2)}, u32[]{:S(2)}) collective-permute-start(bf16[1,512,128]{1,2,0:T(8,128)(2,1)S(1)} %get-tuple-element.12), channel_id=1, source_target_pairs={{0,16},{16,0},{1,17},{17,1},{2,18},{18,2},{3,19},{19,3},{4,20},{20... | collective-permute-start | bytes 393224 | tf_op jit(solution)/shard_map/ppermute | solution.py:53
  49.4 5.8 %collective-permute-start.7 = (bf16[1,512,128]{1,2,0:T(8,128)(2,1)}, bf16[1,512,128]{1,2,0:T(8,128)(2,1)S(1)}, u32[]{:S(2)}, u32[]{:S(2)}) collective-permute-start(bf16[1,512,128]{1,2,0:T(8,128)(2,1)} %get-tuple-element.13), channel_id=1, source_target_pairs={{0,16},{16,0},{1,17},{17,1},{2,18},{18,2},{3,19},{19,3},{4,20},{20... | collective-permute-start | bytes 393224 | tf_op jit(solution)/shard_map/ppermute | solution.py:53
  54.2 11.2 %collective-permute-start.5 = (bf16[2,512,128]{2,1,0:T(8,128)(2,1)}, bf16[2,512,128]{2,1,0:T(8,128)(2,1)}, u32[]{:S(2)}, u32[]{:S(2)}) collective-permute-start(bf16[2,512,128]{2,1,0:T(8,128)(2,1)} %bitcast.7), channel_id=1, source_target_pairs={{0,8},{4,12},{8,0},{12,4},{1,9},{5,13},{9,1},{13,5},{2,10},{6,14},... | collective-permute-start | bytes 786440 | tf_op jit(solution)/shard_map/ppermute | solution.py:53
  55.3 0.7 copy-start.9
  57.6 8.8 %collective-permute-start.8 = (bf16[2,512,128]{2,1,0:T(8,128)(2,1)}, bf16[2,512,128]{2,1,0:T(8,128)(2,1)S(1)}, u32[]{:S(2)}, u32[]{:S(2)}) collective-permute-start(bf16[2,512,128]{2,1,0:T(8,128)(2,1)} %bitcast.20), channel_id=1, source_target_pairs={{0,8},{4,12},{8,0},{12,4},{1,9},{5,13},{9,1},{13,5},{2,10},{6,14},... | collective-permute-start | bytes 786440 | tf_op jit(solution)/shard_map/ppermute | solution.py:53
  63.5 16.8 %collective-permute-start.12 = (bf16[4,768,128]{2,1,0:T(8,128)(2,1)S(1)}, bf16[4,768,128]{2,1,0:T(8,128)(2,1)S(1)}, u32[]{:S(2)}, u32[]{:S(2)}) collective-permute-start(bf16[4,768,128]{2,1,0:T(8,128)(2,1)S(1)} %bitcast.115), channel_id=1, source_target_pairs={{0,16},{16,0},{1,17},{17,1},{2,18},{18,2},{3,19},{19,3},{4,20},{20... | collective-permute-start | bytes 2359304 | tf_op jit(solution)/shard_map/ppermute | solution.py:53
  66.4 2.0 %collective-permute-start.6 = (bf16[4,512,128]{2,1,0:T(8,128)(2,1)S(1)}, bf16[4,512,128]{2,1,0:T(8,128)(2,1)S(1)}, u32[]{:S(2)}, u32[]{:S(2)}) collective-permute-start(bf16[4,512,128]{2,1,0:T(8,128)(2,1)S(1)} %bitcast.119), channel_id=1, source_target_pairs={{0,4},{4,0},{8,12},{12,8},{1,5},{5,1},{9,13},{13,9},{2,6},{6,2},{1... | collective-permute-start | bytes 1572872 | tf_op jit(solution)/shard_map/ppermute | solution.py:53
  66.5 2.6 %collective-permute-start.9 = (bf16[4,512,128]{2,1,0:T(8,128)(2,1)S(1)}, bf16[4,512,128]{2,1,0:T(8,128)(2,1)S(1)}, u32[]{:S(2)}, u32[]{:S(2)}) collective-permute-start(bf16[4,512,128]{2,1,0:T(8,128)(2,1)S(1)} %bitcast.118), channel_id=1, source_target_pairs={{0,4},{4,0},{8,12},{12,8},{1,5},{5,1},{9,13},{13,9},{2,6},{6,2},{1... | collective-permute-start | bytes 1572872 | tf_op jit(solution)/shard_map/ppermute | solution.py:53
  67.5 12.9 %copy-start.7 = (bf16[2,2,2,256,128]{4,3,2,1,0:T(8,128)(2,1)S(1)}, bf16[2,2,2,256,128]{4,3,2,1,0:T(8,128)(2,1)}, u32[]{:S(2)}) copy-start(bf16[2,2,2,256,128]{4,3,2,1,0:T(8,128)(2,1)} %constant_dynamic-update-slice_fusion.6) | copy-start | bytes 1572868
  68.4 14.4 %copy-start.4 = (bf16[2,2,2,512,128]{4,3,2,1,0:T(8,128)(2,1)}, bf16[2,2,2,512,128]{4,3,2,1,0:T(8,128)(2,1)S(1)}, u32[]{:S(2)}) copy-start(bf16[2,2,2,512,128]{4,3,2,1,0:T(8,128)(2,1)S(1)} %constant_dynamic-update-slice_fusion.13) | copy-start | bytes 3145732
  69.2 13.6 %copy-start.3 = (bf16[2,2,2,512,128]{4,3,2,1,0:T(8,128)(2,1)}, bf16[2,2,2,512,128]{4,3,2,1,0:T(8,128)(2,1)S(1)}, u32[]{:S(2)}) copy-start(bf16[2,2,2,512,128]{4,3,2,1,0:T(8,128)(2,1)S(1)} %constant_dynamic-update-slice_fusion.10) | copy-start | bytes 3145732
  80.4 2.4 %copy-start.2 = (bf16[1,2,4,768,128]{4,3,2,1,0:T(8,128)(2,1)}, bf16[1,2,4,768,128]{4,3,2,1,0:T(8,128)(2,1)S(1)}, u32[]{:S(2)}) copy-start(bf16[1,2,4,768,128]{4,3,2,1,0:T(8,128)(2,1)S(1)} %bitcast_dynamic-update-slice_fusion) | copy-start | bytes 4718596
  82.8 4.9 %copy-start.1 = (f32[1024,1024]{1,0:T(8,128)}, f32[1024,1024]{1,0:T(8,128)S(1)}, u32[]{:S(2)}) copy-start(f32[1024,1024]{1,0:T(8,128)S(1)} %bitcast_multiply_fusion.2) | copy-start | bytes 12582916
  87.7 11.5 %copy-start.8 = (bf16[2,2,2,256,128]{4,3,2,1,0:T(8,128)(2,1)S(1)}, bf16[2,2,2,256,128]{4,3,2,1,0:T(8,128)(2,1)}, u32[]{:S(2)}) copy-start(bf16[2,2,2,256,128]{4,3,2,1,0:T(8,128)(2,1)} %constant_dynamic-update-slice_fusion.6) | copy-start | bytes 1572868
  87.7 2.0 %collective-permute-start.16 = (f32[1024,128]{1,0:T(8,128)S(1)}, f32[1024,128]{1,0:T(8,128)S(1)}, u32[]{:S(2)}, u32[]{:S(2)}) collective-permute-start(f32[1024,128]{1,0:T(8,128)S(1)} %fusion.7), channel_id=1, source_target_pairs={{0,4},{4,0},{8,12},{12,8},{1,5},{5,1},{9,13},{13,9},{2,6},{6,2},{1... | collective-permute-start | bytes 1572872 | tf_op jit(solution)/shard_map/ppermute | solution.py:93
  90.5 8.6 %collective-permute-start.17 = (f32[512,128]{1,0:T(8,128)}, f32[512,128]{1,0:T(8,128)S(1)}, u32[]{:S(2)}, u32[]{:S(2)}) collective-permute-start(f32[512,128]{1,0:T(8,128)} %slice_select_fusion), channel_id=1, source_target_pairs={{0,8},{4,12},{8,0},{12,4},{1,9},{5,13},{9,1},{13,5},{2,10},{6,14},... | collective-permute-start | bytes 786440 | tf_op jit(solution)/shard_map/ppermute | solution.py:96
  99.2 4.5 %collective-permute-start.18 = (f32[512,128]{1,0:T(8,128)S(1)}, f32[512,128]{1,0:T(8,128)S(1)}, u32[]{:S(2)}, u32[]{:S(2)}) collective-permute-start(f32[512,128]{1,0:T(8,128)S(1)} %get-tuple-element.11), channel_id=1, source_target_pairs={{0,4},{4,0},{8,12},{12,8},{1,5},{5,1},{9,13},{13,9},{2,6},{6,2},{1... | collective-permute-start | bytes 786440 | tf_op jit(solution)/shard_map/ppermute | solution.py:97
  104.7 8.6 %collective-permute-start.19 = (f32[128,128]{0,1:T(8,128)S(1)}, f32[128,128]{0,1:T(8,128)S(1)}, u32[]{:S(2)}, u32[]{:S(2)}) collective-permute-start(f32[128,128]{0,1:T(8,128)S(1)} %fusion.22), channel_id=1, source_target_pairs={{0,1},{1,0},{2,3},{3,2},{4,5},{5,4},{6,7},{7,6},{8,9},{9,8},{10,11... | collective-permute-start | bytes 196616 | tf_op jit(solution)/shard_map/ppermute | solution.py:44
  105.9 7.5 %collective-permute-start.20 = (f32[128,128]{0,1:T(8,128)S(1)}, f32[128,128]{0,1:T(8,128)S(1)}, u32[]{:S(2)}, u32[]{:S(2)}) collective-permute-start(f32[128,128]{0,1:T(8,128)S(1)} %fusion.22), channel_id=1, source_target_pairs={{0,2},{1,3},{2,0},{3,1},{4,6},{5,7},{6,4},{7,5},{8,10},{9,11},{10,... | collective-permute-start | bytes 196616 | tf_op jit(solution)/shard_map/ppermute | solution.py:44
  109.2 6.1 %collective-permute-start.21 = (f32[128,128]{0,1:T(8,128)S(1)}, f32[128,128]{0,1:T(8,128)S(1)}, u32[]{:S(2)}, u32[]{:S(2)}) collective-permute-start(f32[128,128]{0,1:T(8,128)S(1)} %fusion.22), channel_id=1, source_target_pairs={{0,3},{1,2},{2,1},{3,0},{4,7},{5,6},{6,5},{7,4},{8,11},{9,10},{10,... | collective-permute-start | bytes 196616 | tf_op jit(solution)/shard_map/ppermute | solution.py:44
  112.6 8.3 %collective-permute-start.22 = (f32[512,128]{1,0:T(8,128)S(1)}, f32[512,128]{1,0:T(8,128)S(1)}, u32[]{:S(2)}, u32[]{:S(2)}) collective-permute-start(f32[512,128]{1,0:T(8,128)S(1)} %slice_select_fusion.1), channel_id=1, source_target_pairs={{0,1},{1,0},{2,3},{3,2},{4,5},{5,4},{6,7},{7,6},{8,9},{9,8},{10,11... | collective-permute-start | bytes 786440 | tf_op jit(solution)/shard_map/ppermute | solution.py:76
  120.9 14.1 %collective-permute-start.23 = (f32[256,128]{1,0:T(8,128)S(1)}, f32[256,128]{1,0:T(8,128)S(1)}, u32[]{:S(2)}, u32[]{:S(2)}) collective-permute-start(f32[256,128]{1,0:T(8,128)S(1)} %slice_select_fusion.2), channel_id=1, source_target_pairs={{0,2},{1,3},{2,0},{3,1},{4,6},{5,7},{6,4},{7,5},{8,10},{9,11},{10,... | collective-permute-start | bytes 393224 | tf_op jit(solution)/shard_map/ppermute | solution.py:76
  135.1 8.0 %collective-permute-start.24 = (f32[256,128]{1,0:T(8,128)S(1)}, f32[256,128]{1,0:T(8,128)S(1)}, u32[]{:S(2)}, u32[]{:S(2)}) collective-permute-start(f32[256,128]{1,0:T(8,128)S(1)} %get-tuple-element.9), channel_id=1, source_target_pairs={{0,2},{1,3},{2,0},{3,1},{4,6},{5,7},{6,4},{7,5},{8,10},{9,11},{10,... | collective-permute-start | bytes 393224 | tf_op jit(solution)/shard_map/ppermute | solution.py:79
  143.1 10.6 %collective-permute-start.25 = (f32[512,128]{1,0:T(8,128)S(1)}, f32[512,128]{1,0:T(8,128)S(1)}, u32[]{:S(2)}, u32[]{:S(2)}) collective-permute-start(f32[512,128]{1,0:T(8,128)S(1)} %constant_dynamic-update-slice_fusion.2), channel_id=1, source_target_pairs={{0,1},{1,0},{2,3},{3,2},{4,5},{5,4},{6,7},{7,6},{8,9},{9,8},{10,11... | collective-permute-start | bytes 786440 | tf_op jit(solution)/shard_map/ppermute | solution.py:79
  155.0 1.9 %collective-permute-start.26 = (f32[128,128]{0,1:T(8,128)S(1)}, f32[128,128]{0,1:T(8,128)S(1)}, u32[]{:S(2)}, u32[]{:S(2)}) collective-permute-start(f32[128,128]{0,1:T(8,128)S(1)} %fusion.23), channel_id=1, source_target_pairs={{0,4},{4,0},{8,12},{12,8},{1,5},{5,1},{9,13},{13,9},{2,6},{6,2},{1... | collective-permute-start | bytes 196616 | tf_op jit(solution)/shard_map/ppermute | solution.py:44
  155.1 5.0 %collective-permute-start.27 = (f32[128,128]{0,1:T(8,128)S(1)}, f32[128,128]{0,1:T(8,128)S(1)}, u32[]{:S(2)}, u32[]{:S(2)}) collective-permute-start(f32[128,128]{0,1:T(8,128)S(1)} %fusion.23), channel_id=1, source_target_pairs={{0,8},{4,12},{8,0},{12,4},{1,9},{5,13},{9,1},{13,5},{2,10},{6,14},... | collective-permute-start | bytes 196616 | tf_op jit(solution)/shard_map/ppermute | solution.py:44
  156.0 4.5 %collective-permute-start.28 = (f32[128,128]{0,1:T(8,128)S(1)}, f32[128,128]{0,1:T(8,128)S(1)}, u32[]{:S(2)}, u32[]{:S(2)}) collective-permute-start(f32[128,128]{0,1:T(8,128)S(1)} %fusion.23), channel_id=1, source_target_pairs={{0,12},{4,8},{8,4},{12,0},{1,13},{5,9},{9,5},{13,1},{2,14},{6,10},... | collective-permute-start | bytes 196616 | tf_op jit(solution)/shard_map/ppermute | solution.py:44

commit v19 on v18

--- a/solution.py
+++ b/solution.py
@@ -144,7 +144,7 @@
         half = rows_here // 2
         early_bin = [step for step in right_plan if step[0] == "bin"]
         early_bin += [step for step in right_plan if step[0] != "bin"]
-        z_share = 3 * rows_here // 4 if rows_here % 64 == 0 else half
+        z_share = 3 * rows_here // 8 if rows_here % 128 == 0 else half
         right_rows = jnp.concatenate(
             [
                 _butterfly_gather(local_rows[:z_share], right_plan),

time: 186 us -> 180 us (0.968)
  waiting for transfers between devices: 63.4 us -> 53.3 us
  local copies, waits for them, and re-layouts: 22.9 us -> 25.4 us
  matrix products: 20.7 us -> 22.8 us
    ppermute x12, waiting for transfers between devices: 32.1 us -> 24.4 us  [_butterfly_gather(): other = lax.ppermute(x, axis, [(i, i ^ step) for i in range(count)])]
    reshape x3, local copies, waits for them, and re-layouts: 1.25 us -> 3.76 us  [_butterfly_gather(): theirs = other.reshape(mine.shape)]
    ppermute x2, starting transfers between devices: 3.01 us -> 0.74 us  [_halving_sum(): x = keep + lax.ppermute(give, axis, [(i, i ^ step) for i in range(count)])]
  transfers between devices with their start and end apart: 29 -> 29, of which waited for: 17 -> 13; matrix products, arithmetic and copies ran while one was open for 28% -> 31% of each run, Pallas kernels for 0% -> 0%
where the time goes in v19:
time: 180 us; the launch traced here: 179 us
  waiting for transfers between devices  53.3 us (30%)
  other arithmetic  46.3 us (26%)
  starting transfers between devices  29.8 us (17%)
  local copies, waits for them, and re-layouts  25.4 us (14%)
  matrix products  22.8 us (13%)
    another operation x6, other arithmetic, _lower_factor(): return jnp.linalg.cholesky(_direct_sum(gram_part, gram_axis))  25 us
    ppermute x12, waiting for transfers between devices, _butterfly_gather(): other = lax.ppermute(x, axis, [(i, i ^ step) for i in range(count)])  24.4 us
    another operation x4, other arithmetic, _right_solve(): jax.scipy.linalg.solve_triangular(lower_factor, image.T, lower=True)  20.9 us
    ppermute x12, starting transfers between devices, _butterfly_gather(): other = lax.ppermute(x, axis, [(i, i ^ step) for i in range(count)])  14.4 us
    ppermute x9, starting transfers between devices, _direct_sum(): lax.ppermute(x, axis, [(i, i ^ k) for i in range(count)])  9.52 us
    ppermute x9, waiting for transfers between devices, _direct_sum(): lax.ppermute(x, axis, [(i, i ^ k) for i in range(count)])  8.62 us
    dynamic_update_slice x12, local copies, waits for them, and re-layouts, _butterfly_gather(): both = lax.dynamic_update_slice_in_dim(both, theirs, 1 - first, 1)  8.07 us
    ppermute x2, waiting for transfers between devices, _halving_sum(): x = keep + lax.ppermute(give, axis, [(i, i ^ step) for i in range(count)])  6.87 us
  transfers between devices with their start and end apart: 29, of which 13 were waited for; matrix products, arithmetic and copies ran while one was open for 31% of the time, Pallas kernels for 0%

profile of v19, /device:TPU:0, one launch (start us, length us, event | category | flops | bytes accessed | tf_op | source)
XLA Modules:
  0.0 178.9 jit_solution(395296897804455084)
XLA Ops:
  0.7 2.2 %fusion.24 = f32[8,128,16]{1,2,0:T(8,128)S(1)} fusion(bf16[1024,8,16]{0,2,1:T(8,128)(2,1)} %param.7, bf16[8,1024,128]{2,1,0:T(8,128)(2,1)} %param.8), kind=kOutput, calls=%fused_computation.82 | convolution fusion | flops 33554432 | bytes 2424832 | tf_op jit(solution)/shard_map/mbs,bmr->brs/dot_general | solution.py:122
  3.4 2.6 %collective-permute-start.1 = (f32[8,128,16]{1,2,0:T(8,128)S(1)}, f32[8,128,16]{1,2,0:T(8,128)S(1)}, u32[]{:S(2)}, u32[]{:S(2)}) collective-permute-start(f32[8,128,16]{1,2,0:T(8,128)S(1)} %fusion.24), channel_id=1, source_target_pairs={{0,8},{4,12},{8,0},{12,4},{1,9},{5,13},{9,1},{13,5},{2,10},{6,14},... | collective-permute-start | bytes 196616 | tf_op jit(solution)/shard_map/ppermute | solution.py:44
  6.0 2.6 %collective-permute-done.1 = f32[8,128,16]{1,2,0:T(8,128)S(1)} collective-permute-done((f32[8,128,16]{1,2,0:T(8,128)S(1)}, f32[8,128,16]{1,2,0:T(8,128)S(1)}, u32[]{:S(2)}, u32[]{:S(2)}) %collective-permute-start.1) | collective-permute-done | bytes 65568 | tf_op jit(solution)/shard_map/ppermute | solution.py:44
  8.7 1.4 collective-permute-done.2
  11.7 4.9 %collective-permute-start.10 = (bf16[1,384,128]{2,1,0:T(8,128)(2,1)S(1)}, bf16[1,384,128]{2,1,0:T(8,128)(2,1)S(1)}, u32[]{:S(2)}, u32[]{:S(2)}) collective-permute-start(bf16[1,384,128]{2,1,0:T(8,128)(2,1)S(1)} %copy.37), channel_id=1, source_target_pairs={{0,2},{1,3},{2,0},{3,1},{4,6},{5,7},{6,4},{7,5},{8,10},{9,11},{10,... | collective-permute-start | bytes 294920 | tf_op jit(solution)/shard_map/ppermute | solution.py:53
  16.7 1.6 collective-permute-start.13
  18.3 0.8 broadcast_in_dim.42
  19.8 12.9 %collective-permute-done.10 = bf16[1,384,128]{2,1,0:T(8,128)(2,1)S(1)} collective-permute-done((bf16[1,384,128]{2,1,0:T(8,128)(2,1)S(1)}, bf16[1,384,128]{2,1,0:T(8,128)(2,1)S(1)}, u32[]{:S(2)}, u32[]{:S(2)}) %collective-permute-start.10) | collective-permute-done | bytes 98336 | tf_op jit(solution)/shard_map/ppermute | solution.py:53
  32.9 0.8 broadcast_in_dim.37
  35.0 1.1 copy.39
  36.9 1.0 bitcast_dynamic-update-slice_fusion.5
  38.8 1.6 collective-permute-start.4
  41.8 0.9 constant_dynamic-update-slice_fusion.12
  42.8 1.7 bitcast_dynamic-update-slice_fusion.11
  44.5 1.5 collective-permute-start.12
  46.0 1.0 broadcast_in_dim.36
  46.9 1.8 bitcast_dynamic-update-slice_fusion.4
  48.7 1.0 copy.29
  49.8 3.8 %collective-permute-start.5 = (bf16[2,512,128]{2,1,0:T(8,128)(2,1)S(1)}, bf16[2,512,128]{2,1,0:T(8,128)(2,1)}, u32[]{:S(2)}, u32[]{:S(2)}) collective-permute-start(bf16[2,512,128]{2,1,0:T(8,128)(2,1)S(1)} %bitcast.121), channel_id=1, source_target_pairs={{0,8},{4,12},{8,0},{12,4},{1,9},{5,13},{9,1},{13,5},{2,10},{6,14},... | collective-permute-start | bytes 786440 | tf_op jit(solution)/shard_map/ppermute | solution.py:53
  53.7 1.7 copy.34
  55.3 1.6 constant_dynamic-update-slice_fusion.11
  57.0 1.0 bitcast_dynamic-update-slice_fusion.7
  58.0 1.0 bitcast_dynamic-update-slice_fusion.6
  60.2 1.0 bitcast_dynamic-update-slice_fusion.8
  61.2 3.3 %collective-permute-done.8 = bf16[2,512,128]{2,1,0:T(8,128)(2,1)S(1)} collective-permute-done((bf16[2,512,128]{2,1,0:T(8,128)(2,1)}, bf16[2,512,128]{2,1,0:T(8,128)(2,1)S(1)}, u32[]{:S(2)}, u32[]{:S(2)}) %collective-permute-start.8) | collective-permute-done | bytes 262176 | tf_op jit(solution)/shard_map/ppermute | solution.py:53
  65.1 1.8 bitcast_dynamic-update-slice_fusion.3
  66.9 7.7 %collective-permute-done.15 = bf16[4,640,128]{2,1,0:T(8,128)(2,1)S(1)} collective-permute-done((bf16[4,640,128]{2,1,0:T(8,128)(2,1)S(1)}, bf16[4,640,128]{2,1,0:T(8,128)(2,1)S(1)}, u32[]{:S(2)}, u32[]{:S(2)}) %collective-permute-start.15) | collective-permute-done | bytes 655392 | tf_op jit(solution)/shard_map/ppermute | solution.py:53
  74.9 4.1 %bitcast_multiply_fusion.2 = f32[1024,1024]{1,0:T(8,128)S(1)} fusion(bf16[8,640,128]{2,1,0:T(8,128)(2,1)S(1)} %bitcast.119, bf16[8,384,128]{2,1,0:T(8,128)(2,1)} %bitcast.35, bf16[8,512,128]{2,1,0:T(8,128)(2,1)S(1)} %bitcast.123, bf16[8,512,128]{2,1,0:T(8,128)(2,1)S(1)} %bitcast.125), kind=kOutput, calls=%fused_computation.2 | convolution fusion | flops 2156920832 | bytes 8388608 | tf_op jit(solution)/shard_map/dot_general | solution.py:166
  79.0 4.9 %fusion.7 = f32[1024,128]{1,0:T(8,128)S(1)} fusion(f32[1024,1024]{1,0:T(8,128)S(1)} %bitcast_multiply_fusion.2, f32[4096,128]{1,0:T(8,128)} %param.10, s32[]{:T(128)S(6)} %select_n.138), kind=kOutput, calls=%fused_computation.15 | convolution fusion | flops 1610612736 | bytes 5242884 | tf_op jit(solution)/shard_map/dot_general | solution.py:175
  84.0 1.9 %collective-permute-done.16 = f32[1024,128]{1,0:T(8,128)S(1)} collective-permute-done((f32[1024,128]{1,0:T(8,128)S(1)}, f32[1024,128]{1,0:T(8,128)S(1)}, u32[]{:S(2)}, u32[]{:S(2)}) %collective-permute-start.16) | collective-permute-done | bytes 524320 | tf_op jit(solution)/shard_map/ppermute | solution.py:93
  86.0 1.8 %collective-permute-start.17 = (f32[512,128]{1,0:T(8,128)S(1)}, f32[512,128]{1,0:T(8,128)S(1)}, u32[]{:S(2)}, u32[]{:S(2)}) collective-permute-start(f32[512,128]{1,0:T(8,128)S(1)} %slice_select_fusion), channel_id=1, source_target_pairs={{0,8},{4,12},{8,0},{12,4},{1,9},{5,13},{9,1},{13,5},{2,10},{6,14},... | collective-permute-start | bytes 786440 | tf_op jit(solution)/shard_map/ppermute | solution.py:96
  87.8 6.6 %collective-permute-done.17 = f32[512,128]{1,0:T(8,128)S(1)} collective-permute-done((f32[512,128]{1,0:T(8,128)S(1)}, f32[512,128]{1,0:T(8,128)S(1)}, u32[]{:S(2)}, u32[]{:S(2)}) %collective-permute-start.17) | collective-permute-done | bytes 262176 | tf_op jit(solution)/shard_map/ppermute | solution.py:96
  94.6 4.5 %fusion.2 = f32[1024,1024,1]{1,0,2:T(8,128)S(1)} fusion(bf16[8,640,128]{2,1,0:T(8,128)(2,1)} %bitcast.120, bf16[8,384,128]{2,1,0:T(8,128)(2,1)} %bitcast.35, bf16[8,512,128]{2,1,0:T(8,128)(2,1)} %bitcast.124, bf16[8,512,128]{2,1,0:T(8,128)(2,1)} %bitcast.126), kind=kOutput, calls=%fused_computation.6 | convolution fusion | flops 2155872256 | bytes 8388608 | tf_op jit(solution)/shard_map/dot_general | solution.py:169
  99.2 1.0 fusion.22
  100.5 2.0 %collective-permute-start.20 = (f32[128,128]{0,1:T(8,128)S(1)}, f32[128,128]{0,1:T(8,128)S(1)}, u32[]{:S(2)}, u32[]{:S(2)}) collective-permute-start(f32[128,128]{0,1:T(8,128)S(1)} %fusion.22), channel_id=1, source_target_pairs={{0,2},{1,3},{2,0},{3,1},{4,6},{5,7},{6,4},{7,5},{8,10},{9,11},{10,... | collective-permute-start | bytes 196616 | tf_op jit(solution)/shard_map/ppermute | solution.py:44
  102.6 2.0 %collective-permute-start.21 = (f32[128,128]{0,1:T(8,128)S(1)}, f32[128,128]{0,1:T(8,128)S(1)}, u32[]{:S(2)}, u32[]{:S(2)}) collective-permute-start(f32[128,128]{0,1:T(8,128)S(1)} %fusion.22), channel_id=1, source_target_pairs={{0,3},{1,2},{2,1},{3,0},{4,7},{5,6},{6,5},{7,4},{8,11},{9,10},{10,... | collective-permute-start | bytes 196616 | tf_op jit(solution)/shard_map/ppermute | solution.py:44
  104.6 3.6 %fusion = f32[1024,128]{1,0:T(8,128)S(1)} fusion(f32[1024,128]{1,0:T(8,128)S(1)} %constant_dynamic-update-slice_fusion.4, f32[1024,1024,1]{1,0,2:T(8,128)S(1)} %fusion.2), kind=kOutput, calls=%fused_computation.1 | convolution fusion | flops 1611661312 | bytes 5242880 | tf_op jit(solution)/shard_map/dot_general | solution.py:180
  108.4 0.8 collective-permute-done.20
  109.3 6.9 %collective-permute-done.22 = f32[512,128]{1,0:T(8,128)S(1)} collective-permute-done((f32[512,128]{1,0:T(8,128)S(1)}, f32[512,128]{1,0:T(8,128)S(1)}, u32[]{:S(2)}, u32[]{:S(2)}) %collective-permute-start.22) | collective-permute-done | bytes 262176 | tf_op jit(solution)/shard_map/ppermute | solution.py:76
  116.9 11.7 %cholesky.44 = f32[128,128]{1,0:T(8,128)S(1)} custom-call(f32[128,128]{1,0:T(8,128)S(1)} %fusion.15), custom_call_target="Cholesky" | custom-call | tf_op jit(solution)/shard_map/jit(cholesky)/cholesky | solution.py:108
  128.7 2.4 %collective-permute-start.24 = (f32[256,128]{1,0:T(8,128)S(1)}, f32[256,128]{1,0:T(8,128)S(1)}, u32[]{:S(2)}, u32[]{:S(2)}) collective-permute-start(f32[256,128]{1,0:T(8,128)S(1)} %get-tuple-element.9), channel_id=1, source_target_pairs={{0,2},{1,3},{2,0},{3,1},{4,6},{5,7},{6,4},{7,5},{8,10},{9,11},{10,... | collective-permute-start | bytes 393224 | tf_op jit(solution)/shard_map/ppermute | solution.py:79
  131.8 4.9 %collective-permute-done.24 = f32[256,128]{1,0:T(8,128)S(1)} collective-permute-done((f32[256,128]{1,0:T(8,128)S(1)}, f32[256,128]{1,0:T(8,128)S(1)}, u32[]{:S(2)}, u32[]{:S(2)}) %collective-permute-start.24) | collective-permute-done | bytes 131104 | tf_op jit(solution)/shard_map/ppermute | solution.py:79
  137.4 9.8 %custom-call.6 = f32[1,128,128]{1,2,0:T(8,128)S(1)} custom-call(f32[1,128,128]{2,1,0:T(8,128)S(1)} %fusion.9), custom_call_target="InvertDiagBlocksLowerTriangular" | custom-call | tf_op jit(solution)/shard_map/jit(_solve_triangular)/triangular_solve | solution.py:112
  148.7 1.2 collective-permute-start.27
  150.5 2.9 %collective-permute-done.27 = f32[128,128]{0,1:T(8,128)S(1)} collective-permute-done((f32[128,128]{0,1:T(8,128)S(1)}, f32[128,128]{0,1:T(8,128)S(1)}, u32[]{:S(2)}, u32[]{:S(2)}) %collective-permute-start.27) | collective-permute-done | bytes 65568 | tf_op jit(solution)/shard_map/ppermute | solution.py:44
  153.5 0.8 collective-permute-done.28
  154.4 11.9 %cholesky.55 = f32[128,128]{1,0:T(8,128)S(1)} custom-call(f32[128,128]{1,0:T(8,128)S(1)} %fusion.13), custom_call_target="Cholesky" | custom-call | tf_op jit(solution)/shard_map/jit(cholesky)/cholesky | solution.py:108
  167.7 9.8 %custom-call.7 = f32[1,128,128]{1,2,0:T(8,128)S(1)} custom-call(f32[1,128,128]{2,1,0:T(8,128)S(1)} %fusion.10), custom_call_target="InvertDiagBlocksLowerTriangular" | custom-call | tf_op jit(solution)/shard_map/jit(_solve_triangular)/triangular_solve | solution.py:112
  (116 shorter events, 17.9 us)
Async XLA Ops:
  0.6 9.4 %copy-start = (bf16[8,1024,128]{2,1,0:T(8,128)(2,1)S(1)}, bf16[8,1024,128]{2,1,0:T(8,128)(2,1)}, u32[]{:S(2)}) copy-start(bf16[8,1024,128]{2,1,0:T(8,128)(2,1)} %param.9) | copy-start | bytes 6291460
  0.6 9.4 %copy-start.6 = (bf16[1024,8,16]{0,2,1:T(8,128)(2,1)S(1)}, bf16[1024,8,16]{0,2,1:T(8,128)(2,1)}, u32[]{:S(2)}) copy-start(bf16[1024,8,16]{0,2,1:T(8,128)(2,1)} %param.7) | copy-start | bytes 786436
  2.9 3.2 %collective-permute-start = (f32[8,128,16]{1,2,0:T(8,128)S(1)}, f32[8,128,16]{1,2,0:T(8,128)S(1)}, u32[]{:S(2)}, u32[]{:S(2)}) collective-permute-start(f32[8,128,16]{1,2,0:T(8,128)S(1)} %fusion.24), channel_id=1, source_target_pairs={{0,4},{4,0},{8,12},{12,8},{1,5},{5,1},{9,13},{13,9},{2,6},{6,2},{1... | collective-permute-start | bytes 196616 | tf_op jit(solution)/shard_map/ppermute | solution.py:44
  3.4 5.2 %collective-permute-start.1 = (f32[8,128,16]{1,2,0:T(8,128)S(1)}, f32[8,128,16]{1,2,0:T(8,128)S(1)}, u32[]{:S(2)}, u32[]{:S(2)}) collective-permute-start(f32[8,128,16]{1,2,0:T(8,128)S(1)} %fusion.24), channel_id=1, source_target_pairs={{0,8},{4,12},{8,0},{12,4},{1,9},{5,13},{9,1},{13,5},{2,10},{6,14},... | collective-permute-start | bytes 196616 | tf_op jit(solution)/shard_map/ppermute | solution.py:44
  6.0 4.1 %collective-permute-start.2 = (f32[8,128,16]{1,2,0:T(8,128)S(1)}, f32[8,128,16]{1,2,0:T(8,128)S(1)}, u32[]{:S(2)}, u32[]{:S(2)}) collective-permute-start(f32[8,128,16]{1,2,0:T(8,128)S(1)} %fusion.24), channel_id=1, source_target_pairs={{0,12},{4,8},{8,4},{12,0},{1,13},{5,9},{9,5},{13,1},{2,14},{6,10},... | collective-permute-start | bytes 196616 | tf_op jit(solution)/shard_map/ppermute | solution.py:44
  10.7 27.2 %collective-permute-start.3 = (bf16[1024,128]{0,1:T(8,128)(2,1)S(1)}, bf16[1024,128]{0,1:T(8,128)(2,1)S(1)}, u32[]{:S(2)}, u32[]{:S(2)}) collective-permute-start(bf16[1024,128]{0,1:T(8,128)(2,1)S(1)} %bitcast.116), channel_id=1, source_target_pairs={{1,4},{2,8},{3,12},{4,1},{6,9},{7,13},{8,2},{9,6},{11,14},{12,3},{... | collective-permute-start | bytes 786440 | tf_op jit(solution)/shard_map/ppermute | solution.py:136
  11.7 21.1 %collective-permute-start.10 = (bf16[1,384,128]{2,1,0:T(8,128)(2,1)S(1)}, bf16[1,384,128]{2,1,0:T(8,128)(2,1)S(1)}, u32[]{:S(2)}, u32[]{:S(2)}) collective-permute-start(bf16[1,384,128]{2,1,0:T(8,128)(2,1)S(1)} %copy.37), channel_id=1, source_target_pairs={{0,2},{1,3},{2,0},{3,1},{4,6},{5,7},{6,4},{7,5},{8,10},{9,11},{10,... | collective-permute-start | bytes 294920 | tf_op jit(solution)/shard_map/ppermute | solution.py:53
  16.7 17.6 %collective-permute-start.13 = (bf16[1,640,128]{1,2,0:T(8,128)(2,1)S(1)}, bf16[1,640,128]{1,2,0:T(8,128)(2,1)S(1)}, u32[]{:S(2)}, u32[]{:S(2)}) collective-permute-start(bf16[1,640,128]{1,2,0:T(8,128)(2,1)S(1)} %bitcast.132), channel_id=1, source_target_pairs={{0,16},{16,0},{1,17},{17,1},{2,18},{18,2},{3,19},{19,3},{4,20},{20... | collective-permute-start | bytes 491528 | tf_op jit(solution)/shard_map/ppermute | solution.py:53
  32.8 10.0 %collective-permute-start.11 = (bf16[2,384,128]{2,1,0:T(8,128)(2,1)S(1)}, bf16[2,384,128]{2,1,0:T(8,128)(2,1)}, u32[]{:S(2)}, u32[]{:S(2)}) collective-permute-start(bf16[2,384,128]{2,1,0:T(8,128)(2,1)S(1)} %bitcast.129), channel_id=1, source_target_pairs={{0,1},{1,0},{2,3},{3,2},{4,5},{5,4},{6,7},{7,6},{8,9},{9,8},{10,11... | collective-permute-start | bytes 589832 | tf_op jit(solution)/shard_map/ppermute | solution.py:53
  34.3 0.7 copy-start.7
  36.8 21.2 %collective-permute-start.14 = (bf16[2,640,128]{2,1,0:T(8,128)(2,1)}, bf16[2,640,128]{2,1,0:T(8,128)(2,1)}, u32[]{:S(2)}, u32[]{:S(2)}) collective-permute-start(bf16[2,640,128]{2,1,0:T(8,128)(2,1)} %bitcast.41), channel_id=1, source_target_pairs={{0,2},{1,3},{2,0},{3,1},{4,6},{5,7},{6,4},{7,5},{8,10},{9,11},{10,... | collective-permute-start | bytes 983048 | tf_op jit(solution)/shard_map/ppermute | solution.py:53
  38.8 9.9 %collective-permute-start.4 = (bf16[1,512,128]{1,2,0:T(8,128)(2,1)}, bf16[1,512,128]{1,2,0:T(8,128)(2,1)}, u32[]{:S(2)}, u32[]{:S(2)}) collective-permute-start(bf16[1,512,128]{1,2,0:T(8,128)(2,1)} %get-tuple-element.12), channel_id=1, source_target_pairs={{0,16},{16,0},{1,17},{17,1},{2,18},{18,2},{3,19},{19,3},{4,20},{20... | collective-permute-start | bytes 393224 | tf_op jit(solution)/shard_map/ppermute | solution.py:53
  41.2 12.5 %collective-permute-start.7 = (bf16[1,512,128]{1,2,0:T(8,128)(2,1)}, bf16[1,512,128]{1,2,0:T(8,128)(2,1)}, u32[]{:S(2)}, u32[]{:S(2)}) collective-permute-start(bf16[1,512,128]{1,2,0:T(8,128)(2,1)} %get-tuple-element.13), channel_id=1, source_target_pairs={{0,16},{16,0},{1,17},{17,1},{2,18},{18,2},{3,19},{19,3},{4,20},{20... | collective-permute-start | bytes 393224 | tf_op jit(solution)/shard_map/ppermute | solution.py:53
  42.7 7.0 %copy-start.3 = (bf16[1,2,1,512,128]{4,3,1,2,0:T(8,128)(2,1)}, bf16[1,2,1,512,128]{4,3,1,2,0:T(8,128)(2,1)S(1)}, u32[]{:S(2)}) copy-start(bf16[1,2,1,512,128]{4,3,1,2,0:T(8,128)(2,1)S(1)} %constant_dynamic-update-slice_fusion.12) | copy-start | bytes 786436
  44.5 20.6 %collective-permute-start.12 = (bf16[4,384,128]{2,1,0:T(8,128)(2,1)}, bf16[4,384,128]{2,1,0:T(8,128)(2,1)}, u32[]{:S(2)}, u32[]{:S(2)}) collective-permute-start(bf16[4,384,128]{2,1,0:T(8,128)(2,1)} %bitcast.33), channel_id=1, source_target_pairs={{0,16},{16,0},{1,17},{17,1},{2,18},{18,2},{3,19},{19,3},{4,20},{20... | collective-permute-start | bytes 1179656 | tf_op jit(solution)/shard_map/ppermute | solution.py:53
  49.8 10.4 %collective-permute-start.5 = (bf16[2,512,128]{2,1,0:T(8,128)(2,1)S(1)}, bf16[2,512,128]{2,1,0:T(8,128)(2,1)}, u32[]{:S(2)}, u32[]{:S(2)}) collective-permute-start(bf16[2,512,128]{2,1,0:T(8,128)(2,1)S(1)} %bitcast.121), channel_id=1, source_target_pairs={{0,8},{4,12},{8,0},{12,4},{1,9},{5,13},{9,1},{13,5},{2,10},{6,14},... | collective-permute-start | bytes 786440 | tf_op jit(solution)/shard_map/ppermute | solution.py:53
  56.9 7.6 %collective-permute-start.8 = (bf16[2,512,128]{2,1,0:T(8,128)(2,1)}, bf16[2,512,128]{2,1,0:T(8,128)(2,1)S(1)}, u32[]{:S(2)}, u32[]{:S(2)}) collective-permute-start(bf16[2,512,128]{2,1,0:T(8,128)(2,1)} %bitcast.122), channel_id=1, source_target_pairs={{0,8},{4,12},{8,0},{12,4},{1,9},{5,13},{9,1},{13,5},{2,10},{6,14},... | collective-permute-start | bytes 786440 | tf_op jit(solution)/shard_map/ppermute | solution.py:53
  59.3 15.3 %collective-permute-start.15 = (bf16[4,640,128]{2,1,0:T(8,128)(2,1)S(1)}, bf16[4,640,128]{2,1,0:T(8,128)(2,1)S(1)}, u32[]{:S(2)}, u32[]{:S(2)}) collective-permute-start(bf16[4,640,128]{2,1,0:T(8,128)(2,1)S(1)} %bitcast.115), channel_id=1, source_target_pairs={{0,1},{1,0},{2,3},{3,2},{4,5},{5,4},{6,7},{7,6},{8,9},{9,8},{10,11... | collective-permute-start | bytes 1966088 | tf_op jit(solution)/shard_map/ppermute | solution.py:53
  61.2 13.5 %collective-permute-start.6 = (bf16[4,512,128]{2,1,0:T(8,128)(2,1)S(1)}, bf16[4,512,128]{2,1,0:T(8,128)(2,1)S(1)}, u32[]{:S(2)}, u32[]{:S(2)}) collective-permute-start(bf16[4,512,128]{2,1,0:T(8,128)(2,1)S(1)} %bitcast.118), channel_id=1, source_target_pairs={{0,4},{4,0},{8,12},{12,8},{1,5},{5,1},{9,13},{13,9},{2,6},{6,2},{1... | collective-permute-start | bytes 1572872 | tf_op jit(solution)/shard_map/ppermute | solution.py:53
  64.5 10.3 %collective-permute-start.9 = (bf16[4,512,128]{2,1,0:T(8,128)(2,1)S(1)}, bf16[4,512,128]{2,1,0:T(8,128)(2,1)S(1)}, u32[]{:S(2)}, u32[]{:S(2)}) collective-permute-start(bf16[4,512,128]{2,1,0:T(8,128)(2,1)S(1)} %bitcast.117), channel_id=1, source_target_pairs={{0,4},{4,0},{8,12},{12,8},{1,5},{5,1},{9,13},{13,9},{2,6},{6,2},{1... | collective-permute-start | bytes 1572872 | tf_op jit(solution)/shard_map/ppermute | solution.py:53
  74.7 4.3 %copy-start.2 = (bf16[2,2,2,640,128]{4,3,2,1,0:T(8,128)(2,1)}, bf16[2,2,2,640,128]{4,3,2,1,0:T(8,128)(2,1)S(1)}, u32[]{:S(2)}) copy-start(bf16[2,2,2,640,128]{4,3,2,1,0:T(8,128)(2,1)S(1)} %constant_dynamic-update-slice_fusion.6) | copy-start | bytes 3932164
  74.8 4.2 %copy-start.5 = (bf16[2,2,2,512,128]{4,3,2,1,0:T(8,128)(2,1)}, bf16[2,2,2,512,128]{4,3,2,1,0:T(8,128)(2,1)S(1)}, u32[]{:S(2)}) copy-start(bf16[2,2,2,512,128]{4,3,2,1,0:T(8,128)(2,1)S(1)} %constant_dynamic-update-slice_fusion.13) | copy-start | bytes 3145732
  74.9 4.1 %copy-start.4 = (bf16[2,2,2,512,128]{4,3,2,1,0:T(8,128)(2,1)}, bf16[2,2,2,512,128]{4,3,2,1,0:T(8,128)(2,1)S(1)}, u32[]{:S(2)}) copy-start(bf16[2,2,2,512,128]{4,3,2,1,0:T(8,128)(2,1)S(1)} %constant_dynamic-update-slice_fusion.10) | copy-start | bytes 3145732
  79.0 4.9 %copy-start.1 = (f32[1024,1024]{1,0:T(8,128)}, f32[1024,1024]{1,0:T(8,128)S(1)}, u32[]{:S(2)}) copy-start(f32[1024,1024]{1,0:T(8,128)S(1)} %bitcast_multiply_fusion.2) | copy-start | bytes 12582916
  83.9 2.0 %collective-permute-start.16 = (f32[1024,128]{1,0:T(8,128)S(1)}, f32[1024,128]{1,0:T(8,128)S(1)}, u32[]{:S(2)}, u32[]{:S(2)}) collective-permute-start(f32[1024,128]{1,0:T(8,128)S(1)} %fusion.7), channel_id=1, source_target_pairs={{0,4},{4,0},{8,12},{12,8},{1,5},{5,1},{9,13},{13,9},{2,6},{6,2},{1... | collective-permute-start | bytes 1572872 | tf_op jit(solution)/shard_map/ppermute | solution.py:93
  86.0 8.4 %collective-permute-start.17 = (f32[512,128]{1,0:T(8,128)S(1)}, f32[512,128]{1,0:T(8,128)S(1)}, u32[]{:S(2)}, u32[]{:S(2)}) collective-permute-start(f32[512,128]{1,0:T(8,128)S(1)} %slice_select_fusion), channel_id=1, source_target_pairs={{0,8},{4,12},{8,0},{12,4},{1,9},{5,13},{9,1},{13,5},{2,10},{6,14},... | collective-permute-start | bytes 786440 | tf_op jit(solution)/shard_map/ppermute | solution.py:96
  94.5 4.6 %collective-permute-start.18 = (f32[512,128]{1,0:T(8,128)S(1)}, f32[512,128]{1,0:T(8,128)S(1)}, u32[]{:S(2)}, u32[]{:S(2)}) collective-permute-start(f32[512,128]{1,0:T(8,128)S(1)} %get-tuple-element.11), channel_id=1, source_target_pairs={{0,4},{4,0},{8,12},{12,8},{1,5},{5,1},{9,13},{13,9},{2,6},{6,2},{1... | collective-permute-start | bytes 786440 | tf_op jit(solution)/shard_map/ppermute | solution.py:97
  100.2 8.2 %collective-permute-start.19 = (f32[128,128]{0,1:T(8,128)S(1)}, f32[128,128]{0,1:T(8,128)S(1)}, u32[]{:S(2)}, u32[]{:S(2)}) collective-permute-start(f32[128,128]{0,1:T(8,128)S(1)} %fusion.22), channel_id=1, source_target_pairs={{0,1},{1,0},{2,3},{3,2},{4,5},{5,4},{6,7},{7,6},{8,9},{9,8},{10,11... | collective-permute-start | bytes 196616 | tf_op jit(solution)/shard_map/ppermute | solution.py:44
  100.5 8.7 %collective-permute-start.20 = (f32[128,128]{0,1:T(8,128)S(1)}, f32[128,128]{0,1:T(8,128)S(1)}, u32[]{:S(2)}, u32[]{:S(2)}) collective-permute-start(f32[128,128]{0,1:T(8,128)S(1)} %fusion.22), channel_id=1, source_target_pairs={{0,2},{1,3},{2,0},{3,1},{4,6},{5,7},{6,4},{7,5},{8,10},{9,11},{10,... | collective-permute-start | bytes 196616 | tf_op jit(solution)/shard_map/ppermute | solution.py:44
  102.6 6.6 %collective-permute-start.21 = (f32[128,128]{0,1:T(8,128)S(1)}, f32[128,128]{0,1:T(8,128)S(1)}, u32[]{:S(2)}, u32[]{:S(2)}) collective-permute-start(f32[128,128]{0,1:T(8,128)S(1)} %fusion.22), channel_id=1, source_target_pairs={{0,3},{1,2},{2,1},{3,0},{4,7},{5,6},{6,5},{7,4},{8,11},{9,10},{10,... | collective-permute-start | bytes 196616 | tf_op jit(solution)/shard_map/ppermute | solution.py:44
  108.3 7.9 %collective-permute-start.22 = (f32[512,128]{1,0:T(8,128)S(1)}, f32[512,128]{1,0:T(8,128)S(1)}, u32[]{:S(2)}, u32[]{:S(2)}) collective-permute-start(f32[512,128]{1,0:T(8,128)S(1)} %slice_select_fusion.1), channel_id=1, source_target_pairs={{0,1},{1,0},{2,3},{3,2},{4,5},{5,4},{6,7},{7,6},{8,9},{9,8},{10,11... | collective-permute-start | bytes 786440 | tf_op jit(solution)/shard_map/ppermute | solution.py:76
  116.3 12.4 %collective-permute-start.23 = (f32[256,128]{1,0:T(8,128)S(1)}, f32[256,128]{1,0:T(8,128)S(1)}, u32[]{:S(2)}, u32[]{:S(2)}) collective-permute-start(f32[256,128]{1,0:T(8,128)S(1)} %slice_select_fusion.2), channel_id=1, source_target_pairs={{0,2},{1,3},{2,0},{3,1},{4,6},{5,7},{6,4},{7,5},{8,10},{9,11},{10,... | collective-permute-start | bytes 393224 | tf_op jit(solution)/shard_map/ppermute | solution.py:76
  128.7 8.0 %collective-permute-start.24 = (f32[256,128]{1,0:T(8,128)S(1)}, f32[256,128]{1,0:T(8,128)S(1)}, u32[]{:S(2)}, u32[]{:S(2)}) collective-permute-start(f32[256,128]{1,0:T(8,128)S(1)} %get-tuple-element.9), channel_id=1, source_target_pairs={{0,2},{1,3},{2,0},{3,1},{4,6},{5,7},{6,4},{7,5},{8,10},{9,11},{10,... | collective-permute-start | bytes 393224 | tf_op jit(solution)/shard_map/ppermute | solution.py:79
  136.7 10.6 %collective-permute-start.25 = (f32[512,128]{1,0:T(8,128)S(1)}, f32[512,128]{1,0:T(8,128)S(1)}, u32[]{:S(2)}, u32[]{:S(2)}) collective-permute-start(f32[512,128]{1,0:T(8,128)S(1)} %constant_dynamic-update-slice_fusion.2), channel_id=1, source_target_pairs={{0,1},{1,0},{2,3},{3,2},{4,5},{5,4},{6,7},{7,6},{8,9},{9,8},{10,11... | collective-permute-start | bytes 786440 | tf_op jit(solution)/shard_map/ppermute | solution.py:79
  148.6 1.9 %collective-permute-start.26 = (f32[128,128]{0,1:T(8,128)S(1)}, f32[128,128]{0,1:T(8,128)S(1)}, u32[]{:S(2)}, u32[]{:S(2)}) collective-permute-start(f32[128,128]{0,1:T(8,128)S(1)} %fusion.23), channel_id=1, source_target_pairs={{0,4},{4,0},{8,12},{12,8},{1,5},{5,1},{9,13},{13,9},{2,6},{6,2},{1... | collective-permute-start | bytes 196616 | tf_op jit(solution)/shard_map/ppermute | solution.py:44
  148.7 4.8 %collective-permute-start.27 = (f32[128,128]{0,1:T(8,128)S(1)}, f32[128,128]{0,1:T(8,128)S(1)}, u32[]{:S(2)}, u32[]{:S(2)}) collective-permute-start(f32[128,128]{0,1:T(8,128)S(1)} %fusion.23), channel_id=1, source_target_pairs={{0,8},{4,12},{8,0},{12,4},{1,9},{5,13},{9,1},{13,5},{2,10},{6,14},... | collective-permute-start | bytes 196616 | tf_op jit(solution)/shard_map/ppermute | solution.py:44
  149.9 4.4 %collective-permute-start.28 = (f32[128,128]{0,1:T(8,128)S(1)}, f32[128,128]{0,1:T(8,128)S(1)}, u32[]{:S(2)}, u32[]{:S(2)}) collective-permute-start(f32[128,128]{0,1:T(8,128)S(1)} %fusion.23), channel_id=1, source_target_pairs={{0,12},{4,8},{8,4},{12,0},{1,13},{5,9},{9,5},{13,1},{2,14},{6,10},... | collective-permute-start | bytes 196616 | tf_op jit(solution)/shard_map/ppermute | solution.py:44

commit v20 on v15

--- a/solution.py
+++ b/solution.py
@@ -105,7 +105,7 @@
     gram_part = jnp.dot(
         image.T, image, precision=lax.Precision.HIGHEST, preferred_element_type=jnp.float32
     )
-    return jnp.linalg.cholesky(_direct_sum(gram_part, gram_axis))
+    return lax.linalg.cholesky(_direct_sum(gram_part, gram_axis), symmetrize_input=False)
 
 
 def _right_solve(lower_factor, image):

time: 172 us -> 173 us (level)
  starting transfers between devices: 29.6 us -> 27.2 us
  waiting for transfers between devices: 54.1 us -> 56.5 us
    ppermute x9, waiting for transfers between devices: 8.33 us -> 11.1 us  [_direct_sum(): lax.ppermute(x, axis, [(i, i ^ k) for i in range(count)])]
    ppermute x2, starting transfers between devices: 2.47 us -> 0.14 us  [_halving_sum(): other = lax.ppermute(x, axis, [(i, i ^ step) for i in range(count)])]
    ppermute x2, waiting for transfers between devices: 6.9 us -> 4.77 us  [_halving_sum(): x = keep + lax.ppermute(give, axis, [(i, i ^ step) for i in range(count)])]
  transfers between devices with their start and end apart: 29 -> 29, of which waited for: 13 -> 14; matrix products, arithmetic and copies ran while one was open for 29% -> 27% of each run, Pallas kernels for 0% -> 0%
where the time goes in v20:
time: 173 us; the launch traced here: 172 us
  waiting for transfers between devices  56.5 us (33%)
  other arithmetic  47 us (27%)
  starting transfers between devices  27.2 us (16%)
  matrix products  21.1 us (12%)
  local copies, waits for them, and re-layouts  19.2 us (11%)
    another operation x6, other arithmetic, _lower_factor(): lax.linalg.cholesky(_direct_sum(gram_part, gram_axis), symmetrize_input=F...  25 us
    ppermute x12, waiting for transfers between devices, _butterfly_gather(): other = lax.ppermute(x, axis, [(i, i ^ step) for i in range(count)])  24.3 us
    another operation x4, other arithmetic, _right_solve(): jax.scipy.linalg.solve_triangular(lower_factor, image.T, lower=True)  20.9 us
    ppermute x12, starting transfers between devices, _butterfly_gather(): other = lax.ppermute(x, axis, [(i, i ^ step) for i in range(count)])  15 us
    ppermute x9, waiting for transfers between devices, _direct_sum(): lax.ppermute(x, axis, [(i, i ^ k) for i in range(count)])  11.1 us
    ppermute x9, starting transfers between devices, _direct_sum(): lax.ppermute(x, axis, [(i, i ^ k) for i in range(count)])  9.52 us
    ppermute x1, waiting for transfers between devices, _pair_split_sum(): mine = mine + lax.ppermute(mine, axis, [(i, i ^ 2) for i in range(count)])  8.06 us
    ppermute x2, waiting for transfers between devices, _halving_sum(): other = lax.ppermute(x, axis, [(i, i ^ step) for i in range(count)])  6.26 us
  transfers between devices with their start and end apart: 29, of which 14 were waited for; matrix products, arithmetic and copies ran while one was open for 27% of the time, Pallas kernels for 0%

profile of v20, /device:TPU:0, one launch (start us, length us, event | category | flops | bytes accessed | tf_op | source)
XLA Modules:
  0.0 172.2 jit_solution(16563182140806185497)
XLA Ops:
  0.7 2.2 %fusion.23 = f32[8,128,16]{1,2,0:T(8,128)S(1)} fusion(bf16[1024,8,16]{0,2,1:T(8,128)(2,1)} %param.7, bf16[8,1024,128]{2,1,0:T(8,128)(2,1)} %param.8), kind=kOutput, calls=%fused_computation.79 | convolution fusion | flops 33554432 | bytes 2424832 | tf_op jit(solution)/shard_map/mbs,bmr->brs/dot_general | solution.py:122
  3.4 2.6 %collective-permute-start.1 = (f32[8,128,16]{1,2,0:T(8,128)S(1)}, f32[8,128,16]{1,2,0:T(8,128)S(1)}, u32[]{:S(2)}, u32[]{:S(2)}) collective-permute-start(f32[8,128,16]{1,2,0:T(8,128)S(1)} %fusion.23), channel_id=1, source_target_pairs={{0,8},{4,12},{8,0},{12,4},{1,9},{5,13},{9,1},{13,5},{2,10},{6,14},... | collective-permute-start | bytes 196616 | tf_op jit(solution)/shard_map/ppermute | solution.py:44
  6.0 2.6 %collective-permute-done.1 = f32[8,128,16]{1,2,0:T(8,128)S(1)} collective-permute-done((f32[8,128,16]{1,2,0:T(8,128)S(1)}, f32[8,128,16]{1,2,0:T(8,128)S(1)}, u32[]{:S(2)}, u32[]{:S(2)}) %collective-permute-start.1) | collective-permute-done | bytes 65568 | tf_op jit(solution)/shard_map/ppermute | solution.py:44
  8.7 1.4 collective-permute-done.2
  10.7 1.4 collective-permute-start.3
  12.2 4.2 %collective-permute-start.10 = (bf16[1,512,128]{1,2,0:T(8,128)(2,1)S(1)}, bf16[1,512,128]{1,2,0:T(8,128)(2,1)S(1)}, u32[]{:S(2)}, u32[]{:S(2)}) collective-permute-start(bf16[1,512,128]{1,2,0:T(8,128)(2,1)S(1)} %bitcast.131), channel_id=1, source_target_pairs={{0,2},{1,3},{2,0},{3,1},{4,6},{5,7},{6,4},{7,5},{8,10},{9,11},{10,... | collective-permute-start | bytes 393224 | tf_op jit(solution)/shard_map/ppermute | solution.py:53
  16.4 1.5 collective-permute-start.13
  17.9 0.8 broadcast.52.clone.1
  19.5 0.7 broadcast.52.clone
  20.9 13.3 %collective-permute-done.10 = bf16[1,512,128]{1,2,0:T(8,128)(2,1)S(1)} collective-permute-done((bf16[1,512,128]{1,2,0:T(8,128)(2,1)S(1)}, bf16[1,512,128]{1,2,0:T(8,128)(2,1)S(1)}, u32[]{:S(2)}, u32[]{:S(2)}) %collective-permute-start.10) | collective-permute-done | bytes 131104 | tf_op jit(solution)/shard_map/ppermute | solution.py:53
  35.0 1.0 bitcast_dynamic-update-slice_fusion.12
  36.9 1.0 bitcast_dynamic-update-slice_fusion.5
  38.0 0.8 slice_bitcast_fusion.2
  38.8 1.6 collective-permute-start.4
  41.0 1.0 copy.11
  42.0 0.7 broadcast.52.clone.2
  43.4 2.2 %collective-permute-done.4 = bf16[1,512,128]{1,2,0:T(8,128)(2,1)} collective-permute-done((bf16[1,512,128]{1,2,0:T(8,128)(2,1)}, bf16[1,512,128]{1,2,0:T(8,128)(2,1)}, u32[]{:S(2)}, u32[]{:S(2)}) %collective-permute-start.4) | collective-permute-done | bytes 131104 | tf_op jit(solution)/shard_map/ppermute | solution.py:53
  45.6 1.0 copy.7
  46.7 4.7 %collective-permute-start.5 = (bf16[2,512,128]{2,1,0:T(8,128)(2,1)S(1)}, bf16[2,512,128]{2,1,0:T(8,128)(2,1)}, u32[]{:S(2)}, u32[]{:S(2)}) collective-permute-start(bf16[2,512,128]{2,1,0:T(8,128)(2,1)S(1)} %bitcast.116), channel_id=1, source_target_pairs={{0,8},{4,12},{8,0},{12,4},{1,9},{5,13},{9,1},{13,5},{2,10},{6,14},... | collective-permute-start | bytes 786440 | tf_op jit(solution)/shard_map/ppermute | solution.py:53
  51.4 1.0 copy.12
  53.5 1.0 bitcast_dynamic-update-slice_fusion.11
  54.5 1.6 collective-permute-start.12
  56.2 1.0 bitcast_dynamic-update-slice_fusion.10
  57.8 1.0 bitcast_dynamic-update-slice_fusion.7
  59.1 1.0 bitcast_dynamic-update-slice_fusion.8
  60.1 1.2 collective-permute-done.8
  61.9 7.7 %collective-permute-done.15 = bf16[4,512,128]{2,1,0:T(8,128)(2,1)S(1)} collective-permute-done((bf16[4,512,128]{2,1,0:T(8,128)(2,1)S(1)}, bf16[4,512,128]{2,1,0:T(8,128)(2,1)S(1)}, u32[]{:S(2)}, u32[]{:S(2)}) %collective-permute-start.15) | collective-permute-done | bytes 524320 | tf_op jit(solution)/shard_map/ppermute | solution.py:53
  70.0 2.4 %bitcast_multiply_fusion.2 = f32[1024,1024]{1,0:T(8,128)S(1)} fusion(bf16[8,512,128]{2,1,0:T(8,128)(2,1)S(1)} %bitcast.119, bf16[8,512,128]{2,1,0:T(8,128)(2,1)S(1)} %bitcast.121, bf16[8,512,128]{2,1,0:T(8,128)(2,1)S(1)} %bitcast.117, bf16[8,512,128]{2,1,0:T(8,128)(2,1)S(1)} %bitcast.123), kind=kOutput, calls=%fused_computation.2 | convolution fusion | flops 2156920832 | bytes 8388608 | tf_op jit(solution)/shard_map/dot_general | solution.py:165
  72.4 4.9 %fusion.7 = f32[1024,128]{1,0:T(8,128)S(1)} fusion(f32[1024,1024]{1,0:T(8,128)S(1)} %bitcast_multiply_fusion.2, f32[4096,128]{1,0:T(8,128)} %param.10, s32[]{:T(128)S(6)} %select_n.141), kind=kOutput, calls=%fused_computation.17 | convolution fusion | flops 1610612736 | bytes 5242884 | tf_op jit(solution)/shard_map/dot_general | solution.py:174
  77.4 1.9 %collective-permute-done.16 = f32[1024,128]{1,0:T(8,128)S(1)} collective-permute-done((f32[1024,128]{1,0:T(8,128)S(1)}, f32[1024,128]{1,0:T(8,128)S(1)}, u32[]{:S(2)}, u32[]{:S(2)}) %collective-permute-start.16) | collective-permute-done | bytes 524320 | tf_op jit(solution)/shard_map/ppermute | solution.py:93
  79.7 8.1 %collective-permute-done.17 = f32[512,128]{1,0:T(8,128)S(1)} collective-permute-done((f32[512,128]{1,0:T(8,128)S(1)}, f32[512,128]{1,0:T(8,128)S(1)}, u32[]{:S(2)}, u32[]{:S(2)}) %collective-permute-start.17) | collective-permute-done | bytes 262176 | tf_op jit(solution)/shard_map/ppermute | solution.py:96
  87.9 4.5 %fusion.2 = f32[1024,1024,1]{1,0,2:T(8,128)S(1)} fusion(bf16[8,512,128]{2,1,0:T(8,128)(2,1)} %bitcast.120, bf16[8,512,128]{2,1,0:T(8,128)(2,1)} %bitcast.122, bf16[8,512,128]{2,1,0:T(8,128)(2,1)} %bitcast.118, bf16[8,512,128]{2,1,0:T(8,128)(2,1)} %bitcast.124), kind=kOutput, calls=%fused_computation.6 | convolution fusion | flops 2155872256 | bytes 8388608 | tf_op jit(solution)/shard_map/dot_general | solution.py:168
  92.5 3.6 %fusion = f32[1024,128]{1,0:T(8,128)S(1)} fusion(f32[1024,128]{1,0:T(8,128)S(1)} %constant_dynamic-update-slice_fusion.4, f32[1024,1024,1]{1,0,2:T(8,128)S(1)} %fusion.2), kind=kOutput, calls=%fused_computation.1 | convolution fusion | flops 1611661312 | bytes 5242880 | tf_op jit(solution)/shard_map/dot_general | solution.py:179
  96.2 0.7 slice_select_fusion.1
  97.5 1.0 fusion.21
  98.5 1.5 collective-permute-start.19
  100.0 1.5 collective-permute-start.20
  101.5 1.4 collective-permute-start.21
  102.9 4.8 %collective-permute-done.22 = f32[512,128]{1,0:T(8,128)S(1)} collective-permute-done((f32[512,128]{1,0:T(8,128)}, f32[512,128]{1,0:T(8,128)S(1)}, u32[]{:S(2)}, u32[]{:S(2)}) %collective-permute-start.22) | collective-permute-done | bytes 262176 | tf_op jit(solution)/shard_map/ppermute | solution.py:76
  108.6 2.9 %collective-permute-done.21 = f32[128,128]{1,0:T(8,128)S(1)} collective-permute-done((f32[128,128]{1,0:T(8,128)S(1)}, f32[128,128]{1,0:T(8,128)S(1)}, u32[]{:S(2)}, u32[]{:S(2)}) %collective-permute-start.21) | collective-permute-done | bytes 65568 | tf_op jit(solution)/shard_map/ppermute | solution.py:44
  111.5 11.7 %custom-call.8 = f32[128,128]{1,0:T(8,128)S(1)} custom-call(f32[128,128]{1,0:T(8,128)S(1)} %add_add_fusion.1), custom_call_target="Cholesky" | custom-call | tf_op jit(solution)/shard_map/cholesky/custom-call.1 | solution.py:108
  124.1 6.3 %collective-permute-done.24 = f32[256,128]{1,0:T(8,128)S(1)} collective-permute-done((f32[256,128]{1,0:T(8,128)S(1)}, f32[256,128]{1,0:T(8,128)S(1)}, u32[]{:S(2)}, u32[]{:S(2)}) %collective-permute-start.24) | collective-permute-done | bytes 131104 | tf_op jit(solution)/shard_map/ppermute | solution.py:79
  131.1 9.8 %custom-call.9 = f32[1,128,128]{1,2,0:T(8,128)S(1)} custom-call(f32[1,128,128]{2,1,0:T(8,128)S(1)} %fusion.9), custom_call_target="InvertDiagBlocksLowerTriangular" | custom-call | tf_op jit(solution)/shard_map/jit(_solve_triangular)/triangular_solve | solution.py:112
  142.7 1.5 collective-permute-start.28
  144.2 3.2 %collective-permute-done.27 = f32[128,128]{1,0:T(8,128)S(1)} collective-permute-done((f32[128,128]{1,0:T(8,128)S(1)}, f32[128,128]{1,0:T(8,128)S(1)}, u32[]{:S(2)}, u32[]{:S(2)}) %collective-permute-start.27) | collective-permute-done | bytes 65568 | tf_op jit(solution)/shard_map/ppermute | solution.py:44
  147.7 11.9 %custom-call.10 = f32[128,128]{1,0:T(8,128)S(1)} custom-call(f32[128,128]{1,0:T(8,128)S(1)} %add_add_fusion), custom_call_target="Cholesky" | custom-call | tf_op jit(solution)/shard_map/cholesky/custom-call.1 | solution.py:108
  161.0 9.8 %custom-call.11 = f32[1,128,128]{1,2,0:T(8,128)S(1)} custom-call(f32[1,128,128]{2,1,0:T(8,128)S(1)} %fusion.10), custom_call_target="InvertDiagBlocksLowerTriangular" | custom-call | tf_op jit(solution)/shard_map/jit(_solve_triangular)/triangular_solve | solution.py:112
  171.5 0.8 copy.21
  (109 shorter events, 16.7 us)
Async XLA Ops:
  0.6 9.4 %copy-start = (bf16[8,1024,128]{2,1,0:T(8,128)(2,1)S(1)}, bf16[8,1024,128]{2,1,0:T(8,128)(2,1)}, u32[]{:S(2)}) copy-start(bf16[8,1024,128]{2,1,0:T(8,128)(2,1)} %param.9) | copy-start | bytes 6291460
  0.6 9.4 %copy-start.6 = (bf16[1024,8,16]{0,2,1:T(8,128)(2,1)S(1)}, bf16[1024,8,16]{0,2,1:T(8,128)(2,1)}, u32[]{:S(2)}) copy-start(bf16[1024,8,16]{0,2,1:T(8,128)(2,1)} %param.7) | copy-start | bytes 786436
  2.9 3.2 %collective-permute-start = (f32[8,128,16]{1,2,0:T(8,128)S(1)}, f32[8,128,16]{1,2,0:T(8,128)S(1)}, u32[]{:S(2)}, u32[]{:S(2)}) collective-permute-start(f32[8,128,16]{1,2,0:T(8,128)S(1)} %fusion.23), channel_id=1, source_target_pairs={{0,4},{4,0},{8,12},{12,8},{1,5},{5,1},{9,13},{13,9},{2,6},{6,2},{1... | collective-permute-start | bytes 196616 | tf_op jit(solution)/shard_map/ppermute | solution.py:44
  3.4 5.2 %collective-permute-start.1 = (f32[8,128,16]{1,2,0:T(8,128)S(1)}, f32[8,128,16]{1,2,0:T(8,128)S(1)}, u32[]{:S(2)}, u32[]{:S(2)}) collective-permute-start(f32[8,128,16]{1,2,0:T(8,128)S(1)} %fusion.23), channel_id=1, source_target_pairs={{0,8},{4,12},{8,0},{12,4},{1,9},{5,13},{9,1},{13,5},{2,10},{6,14},... | collective-permute-start | bytes 196616 | tf_op jit(solution)/shard_map/ppermute | solution.py:44
  6.0 4.1 %collective-permute-start.2 = (f32[8,128,16]{1,2,0:T(8,128)S(1)}, f32[8,128,16]{1,2,0:T(8,128)S(1)}, u32[]{:S(2)}, u32[]{:S(2)}) collective-permute-start(f32[8,128,16]{1,2,0:T(8,128)S(1)} %fusion.23), channel_id=1, source_target_pairs={{0,12},{4,8},{8,4},{12,0},{1,13},{5,9},{9,5},{13,1},{2,14},{6,10},... | collective-permute-start | bytes 196616 | tf_op jit(solution)/shard_map/ppermute | solution.py:44
  10.7 27.2 %collective-permute-start.3 = (bf16[1024,128]{0,1:T(8,128)(2,1)S(1)}, bf16[1024,128]{0,1:T(8,128)(2,1)}, u32[]{:S(2)}, u32[]{:S(2)}) collective-permute-start(bf16[1024,128]{0,1:T(8,128)(2,1)S(1)} %bitcast.110), channel_id=1, source_target_pairs={{1,4},{2,8},{3,12},{4,1},{6,9},{7,13},{8,2},{9,6},{11,14},{12,3},{... | collective-permute-start | bytes 786440 | tf_op jit(solution)/shard_map/ppermute | solution.py:136
  12.2 21.9 %collective-permute-start.10 = (bf16[1,512,128]{1,2,0:T(8,128)(2,1)S(1)}, bf16[1,512,128]{1,2,0:T(8,128)(2,1)S(1)}, u32[]{:S(2)}, u32[]{:S(2)}) collective-permute-start(bf16[1,512,128]{1,2,0:T(8,128)(2,1)S(1)} %bitcast.131), channel_id=1, source_target_pairs={{0,2},{1,3},{2,0},{3,1},{4,6},{5,7},{6,4},{7,5},{8,10},{9,11},{10,... | collective-permute-start | bytes 393224 | tf_op jit(solution)/shard_map/ppermute | solution.py:53
  16.4 19.6 %collective-permute-start.13 = (bf16[1,512,128]{1,2,0:T(8,128)(2,1)S(1)}, bf16[1,512,128]{1,2,0:T(8,128)(2,1)S(1)}, u32[]{:S(2)}, u32[]{:S(2)}) collective-permute-start(bf16[1,512,128]{1,2,0:T(8,128)(2,1)S(1)} %bitcast.128), channel_id=1, source_target_pairs={{0,16},{16,0},{1,17},{17,1},{2,18},{18,2},{3,19},{19,3},{4,20},{20... | collective-permute-start | bytes 393224 | tf_op jit(solution)/shard_map/ppermute | solution.py:53
  34.9 18.5 %collective-permute-start.11 = (bf16[2,512,128]{2,1,0:T(8,128)(2,1)}, bf16[2,512,128]{2,1,0:T(8,128)(2,1)}, u32[]{:S(2)}, u32[]{:S(2)}) collective-permute-start(bf16[2,512,128]{2,1,0:T(8,128)(2,1)} %bitcast.32), channel_id=1, source_target_pairs={{0,1},{1,0},{2,3},{3,2},{4,5},{5,4},{6,7},{7,6},{8,9},{9,8},{10,11... | collective-permute-start | bytes 786440 | tf_op jit(solution)/shard_map/ppermute | solution.py:53
  36.8 19.4 %collective-permute-start.14 = (bf16[2,512,128]{2,1,0:T(8,128)(2,1)}, bf16[2,512,128]{2,1,0:T(8,128)(2,1)}, u32[]{:S(2)}, u32[]{:S(2)}) collective-permute-start(bf16[2,512,128]{2,1,0:T(8,128)(2,1)} %bitcast.43), channel_id=1, source_target_pairs={{0,2},{1,3},{2,0},{3,1},{4,6},{5,7},{6,4},{7,5},{8,10},{9,11},{10,... | collective-permute-start | bytes 786440 | tf_op jit(solution)/shard_map/ppermute | solution.py:53
  38.8 6.7 %collective-permute-start.4 = (bf16[1,512,128]{1,2,0:T(8,128)(2,1)}, bf16[1,512,128]{1,2,0:T(8,128)(2,1)}, u32[]{:S(2)}, u32[]{:S(2)}) collective-permute-start(bf16[1,512,128]{1,2,0:T(8,128)(2,1)} %get-tuple-element.10), channel_id=1, source_target_pairs={{0,16},{16,0},{1,17},{17,1},{2,18},{18,2},{3,19},{19,3},{4,20},{20... | collective-permute-start | bytes 393224 | tf_op jit(solution)/shard_map/ppermute | solution.py:53
  40.4 10.9 %collective-permute-start.7 = (bf16[1,512,128]{1,2,0:T(8,128)(2,1)}, bf16[1,512,128]{1,2,0:T(8,128)(2,1)}, u32[]{:S(2)}, u32[]{:S(2)}) collective-permute-start(bf16[1,512,128]{1,2,0:T(8,128)(2,1)} %get-tuple-element.11), channel_id=1, source_target_pairs={{0,16},{16,0},{1,17},{17,1},{2,18},{18,2},{3,19},{19,3},{4,20},{20... | collective-permute-start | bytes 393224 | tf_op jit(solution)/shard_map/ppermute | solution.py:53
  46.7 12.4 %collective-permute-start.5 = (bf16[2,512,128]{2,1,0:T(8,128)(2,1)S(1)}, bf16[2,512,128]{2,1,0:T(8,128)(2,1)}, u32[]{:S(2)}, u32[]{:S(2)}) collective-permute-start(bf16[2,512,128]{2,1,0:T(8,128)(2,1)S(1)} %bitcast.116), channel_id=1, source_target_pairs={{0,8},{4,12},{8,0},{12,4},{1,9},{5,13},{9,1},{13,5},{2,10},{6,14},... | collective-permute-start | bytes 786440 | tf_op jit(solution)/shard_map/ppermute | solution.py:53
  53.1 8.3 %collective-permute-start.8 = (bf16[2,512,128]{2,1,0:T(8,128)(2,1)}, bf16[2,512,128]{2,1,0:T(8,128)(2,1)S(1)}, u32[]{:S(2)}, u32[]{:S(2)}) collective-permute-start(bf16[2,512,128]{2,1,0:T(8,128)(2,1)} %bitcast.20), channel_id=1, source_target_pairs={{0,8},{4,12},{8,0},{12,4},{1,9},{5,13},{9,1},{13,5},{2,10},{6,14},... | collective-permute-start | bytes 786440 | tf_op jit(solution)/shard_map/ppermute | solution.py:53
  54.5 15.2 %collective-permute-start.12 = (bf16[4,512,128]{2,1,0:T(8,128)(2,1)S(1)}, bf16[4,512,128]{2,1,0:T(8,128)(2,1)S(1)}, u32[]{:S(2)}, u32[]{:S(2)}) collective-permute-start(bf16[4,512,128]{2,1,0:T(8,128)(2,1)S(1)} %bitcast.113), channel_id=1, source_target_pairs={{0,16},{16,0},{1,17},{17,1},{2,18},{18,2},{3,19},{19,3},{4,20},{20... | collective-permute-start | bytes 1572872 | tf_op jit(solution)/shard_map/ppermute | solution.py:53
  57.4 12.2 %collective-permute-start.15 = (bf16[4,512,128]{2,1,0:T(8,128)(2,1)S(1)}, bf16[4,512,128]{2,1,0:T(8,128)(2,1)S(1)}, u32[]{:S(2)}, u32[]{:S(2)}) collective-permute-start(bf16[4,512,128]{2,1,0:T(8,128)(2,1)S(1)} %bitcast.111), channel_id=1, source_target_pairs={{0,1},{1,0},{2,3},{3,2},{4,5},{5,4},{6,7},{7,6},{8,9},{9,8},{10,11... | collective-permute-start | bytes 1572872 | tf_op jit(solution)/shard_map/ppermute | solution.py:53
  60.1 9.7 %collective-permute-start.6 = (bf16[4,512,128]{2,1,0:T(8,128)(2,1)S(1)}, bf16[4,512,128]{2,1,0:T(8,128)(2,1)S(1)}, u32[]{:S(2)}, u32[]{:S(2)}) collective-permute-start(bf16[4,512,128]{2,1,0:T(8,128)(2,1)S(1)} %bitcast.115), channel_id=1, source_target_pairs={{0,4},{4,0},{8,12},{12,8},{1,5},{5,1},{9,13},{13,9},{2,6},{6,2},{1... | collective-permute-start | bytes 1572872 | tf_op jit(solution)/shard_map/ppermute | solution.py:53
  61.4 8.5 %collective-permute-start.9 = (bf16[4,512,128]{2,1,0:T(8,128)(2,1)S(1)}, bf16[4,512,128]{2,1,0:T(8,128)(2,1)S(1)}, u32[]{:S(2)}, u32[]{:S(2)}) collective-permute-start(bf16[4,512,128]{2,1,0:T(8,128)(2,1)S(1)} %bitcast.112), channel_id=1, source_target_pairs={{0,4},{4,0},{8,12},{12,8},{1,5},{5,1},{9,13},{13,9},{2,6},{6,2},{1... | collective-permute-start | bytes 1572872 | tf_op jit(solution)/shard_map/ppermute | solution.py:53
  69.7 2.7 %copy-start.3 = (bf16[2,2,2,512,128]{4,3,2,1,0:T(8,128)(2,1)}, bf16[2,2,2,512,128]{4,3,2,1,0:T(8,128)(2,1)S(1)}, u32[]{:S(2)}) copy-start(bf16[2,2,2,512,128]{4,3,2,1,0:T(8,128)(2,1)S(1)} %constant_dynamic-update-slice_fusion.6) | copy-start | bytes 3145732
  69.8 2.6 %copy-start.4 = (bf16[1,2,4,512,128]{4,3,2,1,0:T(8,128)(2,1)}, bf16[1,2,4,512,128]{4,3,2,1,0:T(8,128)(2,1)S(1)}, u32[]{:S(2)}) copy-start(bf16[1,2,4,512,128]{4,3,2,1,0:T(8,128)(2,1)S(1)} %bitcast_dynamic-update-slice_fusion.3) | copy-start | bytes 3145732
  69.9 2.5 %copy-start.5 = (bf16[2,2,2,512,128]{4,3,2,1,0:T(8,128)(2,1)}, bf16[2,2,2,512,128]{4,3,2,1,0:T(8,128)(2,1)S(1)}, u32[]{:S(2)}) copy-start(bf16[2,2,2,512,128]{4,3,2,1,0:T(8,128)(2,1)S(1)} %constant_dynamic-update-slice_fusion.14) | copy-start | bytes 3145732
  70.0 2.4 %copy-start.2 = (bf16[2,2,2,512,128]{4,3,2,1,0:T(8,128)(2,1)}, bf16[2,2,2,512,128]{4,3,2,1,0:T(8,128)(2,1)S(1)}, u32[]{:S(2)}) copy-start(bf16[2,2,2,512,128]{4,3,2,1,0:T(8,128)(2,1)S(1)} %constant_dynamic-update-slice_fusion.11) | copy-start | bytes 3145732
  72.4 4.9 %copy-start.1 = (f32[1024,1024]{1,0:T(8,128)}, f32[1024,1024]{1,0:T(8,128)S(1)}, u32[]{:S(2)}) copy-start(f32[1024,1024]{1,0:T(8,128)S(1)} %bitcast_multiply_fusion.2) | copy-start | bytes 12582916
  77.3 2.0 %collective-permute-start.16 = (f32[1024,128]{1,0:T(8,128)S(1)}, f32[1024,128]{1,0:T(8,128)S(1)}, u32[]{:S(2)}, u32[]{:S(2)}) collective-permute-start(f32[1024,128]{1,0:T(8,128)S(1)} %fusion.7), channel_id=1, source_target_pairs={{0,4},{4,0},{8,12},{12,8},{1,5},{5,1},{9,13},{13,9},{2,6},{6,2},{1... | collective-permute-start | bytes 1572872 | tf_op jit(solution)/shard_map/ppermute | solution.py:93
  79.4 8.4 %collective-permute-start.17 = (f32[512,128]{1,0:T(8,128)S(1)}, f32[512,128]{1,0:T(8,128)S(1)}, u32[]{:S(2)}, u32[]{:S(2)}) collective-permute-start(f32[512,128]{1,0:T(8,128)S(1)} %slice_select_fusion), channel_id=1, source_target_pairs={{0,8},{4,12},{8,0},{12,4},{1,9},{5,13},{9,1},{13,5},{2,10},{6,14},... | collective-permute-start | bytes 786440 | tf_op jit(solution)/shard_map/ppermute | solution.py:96
  87.9 4.6 %collective-permute-start.18 = (f32[512,128]{1,0:T(8,128)S(1)}, f32[512,128]{1,0:T(8,128)S(1)}, u32[]{:S(2)}, u32[]{:S(2)}) collective-permute-start(f32[512,128]{1,0:T(8,128)S(1)} %get-tuple-element.9), channel_id=1, source_target_pairs={{0,4},{4,0},{8,12},{12,8},{1,5},{5,1},{9,13},{13,9},{2,6},{6,2},{1... | collective-permute-start | bytes 786440 | tf_op jit(solution)/shard_map/ppermute | solution.py:97
  96.9 10.8 %collective-permute-start.22 = (f32[512,128]{1,0:T(8,128)}, f32[512,128]{1,0:T(8,128)S(1)}, u32[]{:S(2)}, u32[]{:S(2)}) collective-permute-start(f32[512,128]{1,0:T(8,128)} %slice_select_fusion.1), channel_id=1, source_target_pairs={{0,1},{1,0},{2,3},{3,2},{4,5},{5,4},{6,7},{7,6},{8,9},{9,8},{10,11... | collective-permute-start | bytes 786440 | tf_op jit(solution)/shard_map/ppermute | solution.py:76
  98.5 10.1 %collective-permute-start.19 = (f32[128,128]{1,0:T(8,128)S(1)}, f32[128,128]{1,0:T(8,128)S(1)}, u32[]{:S(2)}, u32[]{:S(2)}) collective-permute-start(f32[128,128]{1,0:T(8,128)S(1)} %fusion.21), channel_id=1, source_target_pairs={{0,1},{1,0},{2,3},{3,2},{4,5},{5,4},{6,7},{7,6},{8,9},{9,8},{10,11... | collective-permute-start | bytes 196616 | tf_op jit(solution)/shard_map/ppermute | solution.py:44
  100.0 8.6 %collective-permute-start.20 = (f32[128,128]{1,0:T(8,128)S(1)}, f32[128,128]{1,0:T(8,128)S(1)}, u32[]{:S(2)}, u32[]{:S(2)}) collective-permute-start(f32[128,128]{1,0:T(8,128)S(1)} %fusion.21), channel_id=1, source_target_pairs={{0,2},{1,3},{2,0},{3,1},{4,6},{5,7},{6,4},{7,5},{8,10},{9,11},{10,... | collective-permute-start | bytes 196616 | tf_op jit(solution)/shard_map/ppermute | solution.py:44
  101.5 10.0 %collective-permute-start.21 = (f32[128,128]{1,0:T(8,128)S(1)}, f32[128,128]{1,0:T(8,128)S(1)}, u32[]{:S(2)}, u32[]{:S(2)}) collective-permute-start(f32[128,128]{1,0:T(8,128)S(1)} %fusion.21), channel_id=1, source_target_pairs={{0,3},{1,2},{2,1},{3,0},{4,7},{5,6},{6,5},{7,4},{8,11},{9,10},{10,... | collective-permute-start | bytes 196616 | tf_op jit(solution)/shard_map/ppermute | solution.py:44
  107.8 15.5 %collective-permute-start.23 = (f32[256,128]{1,0:T(8,128)S(1)}, f32[256,128]{1,0:T(8,128)S(1)}, u32[]{:S(2)}, u32[]{:S(2)}) collective-permute-start(f32[256,128]{1,0:T(8,128)S(1)} %slice_select_fusion.2), channel_id=1, source_target_pairs={{0,2},{1,3},{2,0},{3,1},{4,6},{5,7},{6,4},{7,5},{8,10},{9,11},{10,... | collective-permute-start | bytes 393224 | tf_op jit(solution)/shard_map/ppermute | solution.py:76
  123.3 7.0 %collective-permute-start.24 = (f32[256,128]{1,0:T(8,128)S(1)}, f32[256,128]{1,0:T(8,128)S(1)}, u32[]{:S(2)}, u32[]{:S(2)}) collective-permute-start(f32[256,128]{1,0:T(8,128)S(1)} %get-tuple-element.7), channel_id=1, source_target_pairs={{0,2},{1,3},{2,0},{3,1},{4,6},{5,7},{6,4},{7,5},{8,10},{9,11},{10,... | collective-permute-start | bytes 393224 | tf_op jit(solution)/shard_map/ppermute | solution.py:79
  130.4 10.6 %collective-permute-start.25 = (f32[512,128]{1,0:T(8,128)S(1)}, f32[512,128]{1,0:T(8,128)S(1)}, u32[]{:S(2)}, u32[]{:S(2)}) collective-permute-start(f32[512,128]{1,0:T(8,128)S(1)} %constant_dynamic-update-slice_fusion.2), channel_id=1, source_target_pairs={{0,1},{1,0},{2,3},{3,2},{4,5},{5,4},{6,7},{7,6},{8,9},{9,8},{10,11... | collective-permute-start | bytes 786440 | tf_op jit(solution)/shard_map/ppermute | solution.py:79
  142.3 1.9 %collective-permute-start.26 = (f32[128,128]{1,0:T(8,128)S(1)}, f32[128,128]{1,0:T(8,128)S(1)}, u32[]{:S(2)}, u32[]{:S(2)}) collective-permute-start(f32[128,128]{1,0:T(8,128)S(1)} %fusion.22), channel_id=1, source_target_pairs={{0,4},{4,0},{8,12},{12,8},{1,5},{5,1},{9,13},{13,9},{2,6},{6,2},{1... | collective-permute-start | bytes 196616 | tf_op jit(solution)/shard_map/ppermute | solution.py:44
  142.4 5.0 %collective-permute-start.27 = (f32[128,128]{1,0:T(8,128)S(1)}, f32[128,128]{1,0:T(8,128)S(1)}, u32[]{:S(2)}, u32[]{:S(2)}) collective-permute-start(f32[128,128]{1,0:T(8,128)S(1)} %fusion.22), channel_id=1, source_target_pairs={{0,8},{4,12},{8,0},{12,4},{1,9},{5,13},{9,1},{13,5},{2,10},{6,14},... | collective-permute-start | bytes 196616 | tf_op jit(solution)/shard_map/ppermute | solution.py:44
  142.7 5.0 %collective-permute-start.28 = (f32[128,128]{1,0:T(8,128)S(1)}, f32[128,128]{1,0:T(8,128)S(1)}, u32[]{:S(2)}, u32[]{:S(2)}) collective-permute-start(f32[128,128]{1,0:T(8,128)S(1)} %fusion.22), channel_id=1, source_target_pairs={{0,12},{4,8},{8,4},{12,0},{1,13},{5,9},{9,5},{13,1},{2,14},{6,10},... | collective-permute-start | bytes 196616 | tf_op jit(solution)/shard_map/ppermute | solution.py:44

commit v21 on v15

--- a/solution.py
+++ b/solution.py
@@ -165,9 +165,7 @@
     covariance = lax.dot_general(
         left_rows, right_rows, (((0, 2), (0, 2)), ((), ())), preferred_element_type=jnp.float32
     ) * scaling
-    covariance_t = lax.dot_general(
-        right_rows, left_rows, (((0, 2), (0, 2)), ((), ())), preferred_element_type=jnp.float32
-    ) * scaling
+    covariance_t = covariance.T
 
     def cov_times(block, on_rows):
         if on_rows:

time: 172 us -> 177 us (1.029)
  waiting for transfers between devices: 54.1 us -> 47 us
  local copies, waits for them, and re-layouts: 19.3 us -> 24.9 us
  starting transfers between devices: 29.6 us -> 33.7 us
    ppermute x12, waiting for transfers between devices: 24.3 us -> 16.4 us  [_butterfly_gather(): other = lax.ppermute(x, axis, [(i, i ^ step) for i in range(count)])]
    dot_general x1, matrix products: 3.6 us -> 8.46 us  [cov_times(): jnp.dot(covariance_t, block, precision=lax.Precision.HIGHEST, preferred_e...]
    dot_general x1 -> x0, matrix products: 4.54 us -> none  [shards(): lax.dot_general(right_rows, left_rows, (((0, 2), (0, 2)), ((), ())), pref...]
    dynamic_update_slice x12, local copies, waits for them, and re-layouts: 5.33 us -> 8.13 us  [_butterfly_gather(): both = lax.dynamic_update_slice_in_dim(both, theirs, 1 - first, 1)]
    ppermute x2, starting transfers between devices: 0.73 us -> 3.06 us  [_halving_sum(): x = keep + lax.ppermute(give, axis, [(i, i ^ step) for i in range(count)])]
    ppermute x9, starting transfers between devices: 9.52 us -> 11.8 us  [_direct_sum(): lax.ppermute(x, axis, [(i, i ^ k) for i in range(count)])]
    dynamic_update_slice x12, local copies, waits for them, and re-layouts: 5.3 us -> 7.37 us  [_butterfly_gather(): both = lax.dynamic_update_slice_in_dim(both, mine, first, 1)]
  transfers between devices with their start and end apart: 29 -> 29, of which waited for: 13 -> 12; matrix products, arithmetic and copies ran while one was open for 29% -> 31% of each run, Pallas kernels for 0% -> 0%
where the time goes in v21:
time: 177 us; the launch traced here: 176 us
  other arithmetic  47.9 us (27%)
  waiting for transfers between devices  47 us (27%)
  starting transfers between devices  33.7 us (19%)
  local copies, waits for them, and re-layouts  24.9 us (14%)
  matrix products  21.4 us (12%)
    another operation x6, other arithmetic, _lower_factor(): return jnp.linalg.cholesky(_direct_sum(gram_part, gram_axis))  24.8 us
    another operation x4, other arithmetic, _right_solve(): jax.scipy.linalg.solve_triangular(lower_factor, image.T, lower=True)  20.9 us
    ppermute x12, waiting for transfers between devices, _butterfly_gather(): other = lax.ppermute(x, axis, [(i, i ^ step) for i in range(count)])  16.4 us
    ppermute x12, starting transfers between devices, _butterfly_gather(): other = lax.ppermute(x, axis, [(i, i ^ step) for i in range(count)])  14.2 us
    ppermute x9, starting transfers between devices, _direct_sum(): lax.ppermute(x, axis, [(i, i ^ k) for i in range(count)])  11.8 us
    dot_general x1, matrix products, cov_times(): jnp.dot(covariance_t, block, precision=lax.Precision.HIGHEST, preferred_e...  8.46 us
    dynamic_update_slice x12, local copies, waits for them, and re-layouts, _butterfly_gather(): both = lax.dynamic_update_slice_in_dim(both, theirs, 1 - first, 1)  8.13 us
    ppermute x9, waiting for transfers between devices, _direct_sum(): lax.ppermute(x, axis, [(i, i ^ k) for i in range(count)])  8.03 us
  transfers between devices with their start and end apart: 29, of which 12 were waited for; matrix products, arithmetic and copies ran while one was open for 31% of the time, Pallas kernels for 0%

profile of v21, /device:TPU:0, one launch (start us, length us, event | category | flops | bytes accessed | tf_op | source)
XLA Modules:
  0.0 176.1 jit_solution(2468142397263956228)
XLA Ops:
  0.7 2.2 %fusion.27 = f32[8,128,16]{1,2,0:T(8,128)S(1)} fusion(bf16[1024,8,16]{0,2,1:T(8,128)(2,1)} %param.7, bf16[8,1024,128]{2,1,0:T(8,128)(2,1)} %param.8), kind=kOutput, calls=%fused_computation.82 | convolution fusion | flops 33554432 | bytes 2424832 | tf_op jit(solution)/shard_map/mbs,bmr->brs/dot_general | solution.py:122
  3.4 2.6 %collective-permute-start.1 = (f32[8,128,16]{1,2,0:T(8,128)S(1)}, f32[8,128,16]{1,2,0:T(8,128)S(1)}, u32[]{:S(2)}, u32[]{:S(2)}) collective-permute-start(f32[8,128,16]{1,2,0:T(8,128)S(1)} %fusion.27), channel_id=1, source_target_pairs={{0,8},{4,12},{8,0},{12,4},{1,9},{5,13},{9,1},{13,5},{2,10},{6,14},... | collective-permute-start | bytes 196616 | tf_op jit(solution)/shard_map/ppermute | solution.py:44
  6.0 2.6 %collective-permute-done.1 = f32[8,128,16]{1,2,0:T(8,128)S(1)} collective-permute-done((f32[8,128,16]{1,2,0:T(8,128)S(1)}, f32[8,128,16]{1,2,0:T(8,128)S(1)}, u32[]{:S(2)}, u32[]{:S(2)}) %collective-permute-start.1) | collective-permute-done | bytes 65568 | tf_op jit(solution)/shard_map/ppermute | solution.py:44
  8.7 1.4 collective-permute-done.2
  10.9 1.6 collective-permute-start.13
  12.4 2.6 %collective-permute-start.10 = (bf16[1,512,128]{1,2,0:T(8,128)(2,1)S(1)}, bf16[1,512,128]{1,2,0:T(8,128)(2,1)S(1)}, u32[]{:S(2)}, u32[]{:S(2)}) collective-permute-start(bf16[1,512,128]{1,2,0:T(8,128)(2,1)S(1)} %bitcast.129), channel_id=1, source_target_pairs={{0,2},{1,3},{2,0},{3,1},{4,6},{5,7},{6,4},{7,5},{8,10},{9,11},{10,... | collective-permute-start | bytes 393224 | tf_op jit(solution)/shard_map/ppermute | solution.py:53
  15.0 1.4 collective-permute-start.3
  20.1 4.2 %collective-permute-start.14 = (bf16[2,512,128]{2,1,0:T(8,128)(2,1)}, bf16[2,512,128]{2,1,0:T(8,128)(2,1)}, u32[]{:S(2)}, u32[]{:S(2)}) collective-permute-start(bf16[2,512,128]{2,1,0:T(8,128)(2,1)} %bitcast.43), channel_id=1, source_target_pairs={{0,2},{1,3},{2,0},{3,1},{4,6},{5,7},{6,4},{7,5},{8,10},{9,11},{10,... | collective-permute-start | bytes 786440 | tf_op jit(solution)/shard_map/ppermute | solution.py:53
  24.3 1.0 bitcast_dynamic-update-slice_fusion.5
  27.1 1.0 bitcast_dynamic-update-slice_fusion.12
  30.3 1.5 collective-permute-start.7
  32.0 0.9 constant_dynamic-update-slice_fusion.13
  32.9 11.3 %collective-permute-done.14 = bf16[2,512,128]{2,1,0:T(8,128)(2,1)} collective-permute-done((bf16[2,512,128]{2,1,0:T(8,128)(2,1)}, bf16[2,512,128]{2,1,0:T(8,128)(2,1)}, u32[]{:S(2)}, u32[]{:S(2)}) %collective-permute-start.14) | collective-permute-done | bytes 262176 | tf_op jit(solution)/shard_map/ppermute | solution.py:53
  44.2 1.0 bitcast_dynamic-update-slice_fusion.10
  45.2 1.0 bitcast_dynamic-update-slice_fusion.11
  47.1 1.0 copy-done.3
  48.0 1.0 copy.7
  49.1 2.2 %collective-permute-start.5 = (bf16[2,512,128]{2,1,0:T(8,128)(2,1)S(1)}, bf16[2,512,128]{2,1,0:T(8,128)(2,1)}, u32[]{:S(2)}, u32[]{:S(2)}) collective-permute-start(bf16[2,512,128]{2,1,0:T(8,128)(2,1)S(1)} %bitcast.121), channel_id=1, source_target_pairs={{0,8},{4,12},{8,0},{12,4},{1,9},{5,13},{9,1},{13,5},{2,10},{6,14},... | collective-permute-start | bytes 786440 | tf_op jit(solution)/shard_map/ppermute | solution.py:53
  52.9 1.0 copy.12
  54.6 1.0 bitcast_dynamic-update-slice_fusion.7
  55.9 2.1 %collective-permute-done.5 = bf16[2,512,128]{2,1,0:T(8,128)(2,1)} collective-permute-done((bf16[2,512,128]{2,1,0:T(8,128)(2,1)S(1)}, bf16[2,512,128]{2,1,0:T(8,128)(2,1)}, u32[]{:S(2)}, u32[]{:S(2)}) %collective-permute-start.5) | collective-permute-done | bytes 262176 | tf_op jit(solution)/shard_map/ppermute | solution.py:53
  58.0 1.7 bitcast_dynamic-update-slice_fusion.8
  59.7 3.0 %collective-permute-done.8 = bf16[2,512,128]{2,1,0:T(8,128)(2,1)S(1)} collective-permute-done((bf16[2,512,128]{2,1,0:T(8,128)(2,1)}, bf16[2,512,128]{2,1,0:T(8,128)(2,1)S(1)}, u32[]{:S(2)}, u32[]{:S(2)}) %collective-permute-start.8) | collective-permute-done | bytes 262176 | tf_op jit(solution)/shard_map/ppermute | solution.py:53
  62.9 1.2 bitcast_dynamic-update-slice_fusion.1
  64.4 1.1 constant_dynamic-update-slice_fusion.6
  65.5 1.1 bitcast_dynamic-update-slice_fusion.3
  66.8 2.4 %bitcast_multiply_fusion = f32[1024,1024]{1,0:T(8,128)S(1)} fusion(bf16[8,512,128]{2,1,0:T(8,128)(2,1)S(1)} %bitcast.123, bf16[8,512,128]{2,1,0:T(8,128)(2,1)S(1)} %bitcast.126, bf16[8,512,128]{2,1,0:T(8,128)(2,1)S(1)} %bitcast.124, bf16[8,512,128]{2,1,0:T(8,128)(2,1)S(1)} %bitcast.125), kind=kOutput, calls=%fused_computation | convolution fusion | flops 2156920832 | bytes 8388608 | tf_op jit(solution)/shard_map/dot_general | solution.py:165
  69.2 4.9 %fusion.10 = f32[1024,128]{1,0:T(8,128)S(1)} fusion(f32[1024,1024]{1,0:T(8,128)S(1)} %bitcast_multiply_fusion, f32[4096,128]{1,0:T(8,128)} %param.10, s32[]{:T(128)S(6)} %select_n.138), kind=kOutput, calls=%fused_computation.17 | convolution fusion | flops 1610612736 | bytes 5242884 | tf_op jit(solution)/shard_map/dot_general | solution.py:172
  74.6 1.5 collective-permute-done.16
  76.2 1.8 %collective-permute-start.17 = (f32[512,128]{1,0:T(8,128)S(1)}, f32[512,128]{1,0:T(8,128)}, u32[]{:S(2)}, u32[]{:S(2)}) collective-permute-start(f32[512,128]{1,0:T(8,128)S(1)} %slice_select_fusion), channel_id=1, source_target_pairs={{0,8},{4,12},{8,0},{12,4},{1,9},{5,13},{9,1},{13,5},{2,10},{6,14},... | collective-permute-start | bytes 786440 | tf_op jit(solution)/shard_map/ppermute | solution.py:96
  78.0 7.0 %collective-permute-done.17 = f32[512,128]{1,0:T(8,128)} collective-permute-done((f32[512,128]{1,0:T(8,128)S(1)}, f32[512,128]{1,0:T(8,128)}, u32[]{:S(2)}, u32[]{:S(2)}) %collective-permute-start.17) | collective-permute-done | bytes 262176 | tf_op jit(solution)/shard_map/ppermute | solution.py:96
  85.0 1.0 constant_dynamic-update-slice_fusion.5
  86.1 1.5 collective-permute-done.18
  87.6 1.0 fusion.24
  88.6 1.5 collective-permute-start.19
  90.1 5.3 %collective-permute-start.20 = (f32[128,128]{0,1:T(8,128)S(1)}, f32[128,128]{0,1:T(8,128)}, u32[]{:S(2)}, u32[]{:S(2)}) collective-permute-start(f32[128,128]{0,1:T(8,128)S(1)} %fusion.24), channel_id=1, source_target_pairs={{0,2},{1,3},{2,0},{3,1},{4,6},{5,7},{6,4},{7,5},{8,10},{9,11},{10,... | collective-permute-start | bytes 196616 | tf_op jit(solution)/shard_map/ppermute | solution.py:44
  95.4 8.5 %fusion.25 = f32[1024,128]{1,0:T(8,128)S(1)} fusion(f32[1024,1024]{1,0:T(8,128)} %copy-done.1, f32[1024,128]{1,0:T(8,128)S(1)} %constant_dynamic-update-slice_fusion.4), kind=kOutput, calls=%fused_computation.80 | convolution fusion | flops 1610612736 | bytes 5242880 | tf_op jit(solution)/shard_map/dot_general | solution.py:177
  104.6 0.9 add_add_fusion.1
  105.5 6.2 %collective-permute-done.22 = f32[512,128]{1,0:T(8,128)S(1)} collective-permute-done((f32[512,128]{1,0:T(8,128)S(1)}, f32[512,128]{1,0:T(8,128)S(1)}, u32[]{:S(2)}, u32[]{:S(2)}) %collective-permute-start.22) | collective-permute-done | bytes 262176 | tf_op jit(solution)/shard_map/ppermute | solution.py:76
  111.8 2.4 %collective-permute-start.23 = (f32[256,128]{1,0:T(8,128)S(1)}, f32[256,128]{1,0:T(8,128)S(1)}, u32[]{:S(2)}, u32[]{:S(2)}) collective-permute-start(f32[256,128]{1,0:T(8,128)S(1)} %slice_select_fusion.2), channel_id=1, source_target_pairs={{0,2},{1,3},{2,0},{3,1},{4,6},{5,7},{6,4},{7,5},{8,10},{9,11},{10,... | collective-permute-start | bytes 393224 | tf_op jit(solution)/shard_map/ppermute | solution.py:76
  114.3 11.7 %cholesky.44 = f32[128,128]{1,0:T(8,128)S(1)} custom-call(f32[128,128]{1,0:T(8,128)S(1)} %fusion.18), custom_call_target="Cholesky" | custom-call | tf_op jit(solution)/shard_map/jit(cholesky)/cholesky | solution.py:108
  127.4 6.3 %collective-permute-done.24 = f32[256,128]{1,0:T(8,128)S(1)} collective-permute-done((f32[256,128]{1,0:T(8,128)S(1)}, f32[256,128]{1,0:T(8,128)S(1)}, u32[]{:S(2)}, u32[]{:S(2)}) %collective-permute-start.24) | collective-permute-done | bytes 131104 | tf_op jit(solution)/shard_map/ppermute | solution.py:79
  134.6 9.8 %custom-call.6 = f32[1,128,128]{1,2,0:T(8,128)S(1)} custom-call(f32[1,128,128]{2,1,0:T(8,128)S(1)} %fusion.12), custom_call_target="InvertDiagBlocksLowerTriangular" | custom-call | tf_op jit(solution)/shard_map/jit(_solve_triangular)/triangular_solve | solution.py:112
  145.8 1.8 %collective-permute-start.27 = (f32[128,128]{0,1:T(8,128)S(1)}, f32[128,128]{0,1:T(8,128)S(1)}, u32[]{:S(2)}, u32[]{:S(2)}) collective-permute-start(f32[128,128]{0,1:T(8,128)S(1)} %fusion.26), channel_id=1, source_target_pairs={{0,8},{4,12},{8,0},{12,4},{1,9},{5,13},{9,1},{13,5},{2,10},{6,14},... | collective-permute-start | bytes 196616 | tf_op jit(solution)/shard_map/ppermute | solution.py:44
  147.7 2.6 %collective-permute-done.27 = f32[128,128]{0,1:T(8,128)S(1)} collective-permute-done((f32[128,128]{0,1:T(8,128)S(1)}, f32[128,128]{0,1:T(8,128)S(1)}, u32[]{:S(2)}, u32[]{:S(2)}) %collective-permute-start.27) | collective-permute-done | bytes 65568 | tf_op jit(solution)/shard_map/ppermute | solution.py:44
  150.3 1.4 collective-permute-done.28
  151.8 11.7 %cholesky.55 = f32[128,128]{1,0:T(8,128)S(1)} custom-call(f32[128,128]{1,0:T(8,128)S(1)} %fusion.16), custom_call_target="Cholesky" | custom-call | tf_op jit(solution)/shard_map/jit(cholesky)/cholesky | solution.py:108
  164.9 9.8 %custom-call.7 = f32[1,128,128]{1,2,0:T(8,128)S(1)} custom-call(f32[1,128,128]{2,1,0:T(8,128)S(1)} %fusion.13), custom_call_target="InvertDiagBlocksLowerTriangular" | custom-call | tf_op jit(solution)/shard_map/jit(_solve_triangular)/triangular_solve | solution.py:112
  (110 shorter events, 21.4 us)
Async XLA Ops:
  0.6 9.4 %copy-start = (bf16[8,1024,128]{2,1,0:T(8,128)(2,1)S(1)}, bf16[8,1024,128]{2,1,0:T(8,128)(2,1)}, u32[]{:S(2)}) copy-start(bf16[8,1024,128]{2,1,0:T(8,128)(2,1)} %param.9) | copy-start | bytes 6291460
  0.6 9.4 %copy-start.5 = (bf16[1024,8,16]{0,2,1:T(8,128)(2,1)S(1)}, bf16[1024,8,16]{0,2,1:T(8,128)(2,1)}, u32[]{:S(2)}) copy-start(bf16[1024,8,16]{0,2,1:T(8,128)(2,1)} %param.7) | copy-start | bytes 786436
  2.9 3.2 %collective-permute-start = (f32[8,128,16]{1,2,0:T(8,128)S(1)}, f32[8,128,16]{1,2,0:T(8,128)S(1)}, u32[]{:S(2)}, u32[]{:S(2)}) collective-permute-start(f32[8,128,16]{1,2,0:T(8,128)S(1)} %fusion.27), channel_id=1, source_target_pairs={{0,4},{4,0},{8,12},{12,8},{1,5},{5,1},{9,13},{13,9},{2,6},{6,2},{1... | collective-permute-start | bytes 196616 | tf_op jit(solution)/shard_map/ppermute | solution.py:44
  3.4 5.2 %collective-permute-start.1 = (f32[8,128,16]{1,2,0:T(8,128)S(1)}, f32[8,128,16]{1,2,0:T(8,128)S(1)}, u32[]{:S(2)}, u32[]{:S(2)}) collective-permute-start(f32[8,128,16]{1,2,0:T(8,128)S(1)} %fusion.27), channel_id=1, source_target_pairs={{0,8},{4,12},{8,0},{12,4},{1,9},{5,13},{9,1},{13,5},{2,10},{6,14},... | collective-permute-start | bytes 196616 | tf_op jit(solution)/shard_map/ppermute | solution.py:44
  6.0 4.1 %collective-permute-start.2 = (f32[8,128,16]{1,2,0:T(8,128)S(1)}, f32[8,128,16]{1,2,0:T(8,128)S(1)}, u32[]{:S(2)}, u32[]{:S(2)}) collective-permute-start(f32[8,128,16]{1,2,0:T(8,128)S(1)} %fusion.27), channel_id=1, source_target_pairs={{0,12},{4,8},{8,4},{12,0},{1,13},{5,9},{9,5},{13,1},{2,14},{6,10},... | collective-permute-start | bytes 196616 | tf_op jit(solution)/shard_map/ppermute | solution.py:44
  10.9 8.5 %collective-permute-start.13 = (bf16[1,512,128]{1,2,0:T(8,128)(2,1)S(1)}, bf16[1,512,128]{1,2,0:T(8,128)(2,1)S(1)}, u32[]{:S(2)}, u32[]{:S(2)}) collective-permute-start(bf16[1,512,128]{1,2,0:T(8,128)(2,1)S(1)} %bitcast.132), channel_id=1, source_target_pairs={{0,16},{16,0},{1,17},{17,1},{2,18},{18,2},{3,19},{19,3},{4,20},{20... | collective-permute-start | bytes 393224 | tf_op jit(solution)/shard_map/ppermute | solution.py:53
  12.4 12.9 %collective-permute-start.10 = (bf16[1,512,128]{1,2,0:T(8,128)(2,1)S(1)}, bf16[1,512,128]{1,2,0:T(8,128)(2,1)S(1)}, u32[]{:S(2)}, u32[]{:S(2)}) collective-permute-start(bf16[1,512,128]{1,2,0:T(8,128)(2,1)S(1)} %bitcast.129), channel_id=1, source_target_pairs={{0,2},{1,3},{2,0},{3,1},{4,6},{5,7},{6,4},{7,5},{8,10},{9,11},{10,... | collective-permute-start | bytes 393224 | tf_op jit(solution)/shard_map/ppermute | solution.py:53
  15.0 13.0 %collective-permute-start.3 = (bf16[1024,128]{0,1:T(8,128)(2,1)S(1)}, bf16[1024,128]{0,1:T(8,128)(2,1)}, u32[]{:S(2)}, u32[]{:S(2)}) collective-permute-start(bf16[1024,128]{0,1:T(8,128)(2,1)S(1)} %bitcast.116), channel_id=1, source_target_pairs={{1,4},{2,8},{3,12},{4,1},{6,9},{7,13},{8,2},{9,6},{11,14},{12,3},{... | collective-permute-start | bytes 786440 | tf_op jit(solution)/shard_map/ppermute | solution.py:136
  20.1 24.1 %collective-permute-start.14 = (bf16[2,512,128]{2,1,0:T(8,128)(2,1)}, bf16[2,512,128]{2,1,0:T(8,128)(2,1)}, u32[]{:S(2)}, u32[]{:S(2)}) collective-permute-start(bf16[2,512,128]{2,1,0:T(8,128)(2,1)} %bitcast.43), channel_id=1, source_target_pairs={{0,2},{1,3},{2,0},{3,1},{4,6},{5,7},{6,4},{7,5},{8,10},{9,11},{10,... | collective-permute-start | bytes 786440 | tf_op jit(solution)/shard_map/ppermute | solution.py:53
  26.1 19.1 %collective-permute-start.11 = (bf16[2,512,128]{2,1,0:T(8,128)(2,1)}, bf16[2,512,128]{2,1,0:T(8,128)(2,1)}, u32[]{:S(2)}, u32[]{:S(2)}) collective-permute-start(bf16[2,512,128]{2,1,0:T(8,128)(2,1)} %bitcast.32), channel_id=1, source_target_pairs={{0,1},{1,0},{2,3},{3,2},{4,5},{5,4},{6,7},{7,6},{8,9},{9,8},{10,11... | collective-permute-start | bytes 786440 | tf_op jit(solution)/shard_map/ppermute | solution.py:53
  29.0 19.0 %collective-permute-start.4 = (bf16[1,512,128]{1,2,0:T(8,128)(2,1)}, bf16[1,512,128]{1,2,0:T(8,128)(2,1)}, u32[]{:S(2)}, u32[]{:S(2)}) collective-permute-start(bf16[1,512,128]{1,2,0:T(8,128)(2,1)} %get-tuple-element.12), channel_id=1, source_target_pairs={{0,16},{16,0},{1,17},{17,1},{2,18},{18,2},{3,19},{19,3},{4,20},{20... | collective-permute-start | bytes 393224 | tf_op jit(solution)/shard_map/ppermute | solution.py:53
  30.3 22.5 %collective-permute-start.7 = (bf16[1,512,128]{1,2,0:T(8,128)(2,1)}, bf16[1,512,128]{1,2,0:T(8,128)(2,1)}, u32[]{:S(2)}, u32[]{:S(2)}) collective-permute-start(bf16[1,512,128]{1,2,0:T(8,128)(2,1)} %get-tuple-element.13), channel_id=1, source_target_pairs={{0,16},{16,0},{1,17},{17,1},{2,18},{18,2},{3,19},{19,3},{4,20},{20... | collective-permute-start | bytes 393224 | tf_op jit(solution)/shard_map/ppermute | solution.py:53
  32.9 13.4 %copy-start.2 = (bf16[1,2,1,512,128]{4,3,1,2,0:T(8,128)(2,1)}, bf16[1,2,1,512,128]{4,3,1,2,0:T(8,128)(2,1)S(1)}, u32[]{:S(2)}) copy-start(bf16[1,2,1,512,128]{4,3,1,2,0:T(8,128)(2,1)S(1)} %constant_dynamic-update-slice_fusion.13) | copy-start | bytes 786436
  45.1 19.2 %collective-permute-start.15 = (bf16[4,512,128]{2,1,0:T(8,128)(2,1)S(1)}, bf16[4,512,128]{2,1,0:T(8,128)(2,1)}, u32[]{:S(2)}, u32[]{:S(2)}) collective-permute-start(bf16[4,512,128]{2,1,0:T(8,128)(2,1)S(1)} %bitcast.117), channel_id=1, source_target_pairs={{0,1},{1,0},{2,3},{3,2},{4,5},{5,4},{6,7},{7,6},{8,9},{9,8},{10,11... | collective-permute-start | bytes 1572872 | tf_op jit(solution)/shard_map/ppermute | solution.py:53
  46.2 19.3 %collective-permute-start.12 = (bf16[4,512,128]{2,1,0:T(8,128)(2,1)S(1)}, bf16[4,512,128]{2,1,0:T(8,128)(2,1)}, u32[]{:S(2)}, u32[]{:S(2)}) collective-permute-start(bf16[4,512,128]{2,1,0:T(8,128)(2,1)S(1)} %bitcast.119), channel_id=1, source_target_pairs={{0,16},{16,0},{1,17},{17,1},{2,18},{18,2},{3,19},{19,3},{4,20},{20... | collective-permute-start | bytes 1572872 | tf_op jit(solution)/shard_map/ppermute | solution.py:53
  47.0 1.0 copy-start.3
  49.1 8.9 %collective-permute-start.5 = (bf16[2,512,128]{2,1,0:T(8,128)(2,1)S(1)}, bf16[2,512,128]{2,1,0:T(8,128)(2,1)}, u32[]{:S(2)}, u32[]{:S(2)}) collective-permute-start(bf16[2,512,128]{2,1,0:T(8,128)(2,1)S(1)} %bitcast.121), channel_id=1, source_target_pairs={{0,8},{4,12},{8,0},{12,4},{1,9},{5,13},{9,1},{13,5},{2,10},{6,14},... | collective-permute-start | bytes 786440 | tf_op jit(solution)/shard_map/ppermute | solution.py:53
  54.5 8.1 %collective-permute-start.8 = (bf16[2,512,128]{2,1,0:T(8,128)(2,1)}, bf16[2,512,128]{2,1,0:T(8,128)(2,1)S(1)}, u32[]{:S(2)}, u32[]{:S(2)}) collective-permute-start(bf16[2,512,128]{2,1,0:T(8,128)(2,1)} %bitcast.122), channel_id=1, source_target_pairs={{0,8},{4,12},{8,0},{12,4},{1,9},{5,13},{9,1},{13,5},{2,10},{6,14},... | collective-permute-start | bytes 786440 | tf_op jit(solution)/shard_map/ppermute | solution.py:53
  59.7 7.0 %collective-permute-start.6 = (bf16[4,512,128]{2,1,0:T(8,128)(2,1)}, bf16[4,512,128]{2,1,0:T(8,128)(2,1)S(1)}, u32[]{:S(2)}, u32[]{:S(2)}) collective-permute-start(bf16[4,512,128]{2,1,0:T(8,128)(2,1)} %bitcast.12), channel_id=1, source_target_pairs={{0,4},{4,0},{8,12},{12,8},{1,5},{5,1},{9,13},{13,9},{2,6},{6,2},{1... | collective-permute-start | bytes 1572872 | tf_op jit(solution)/shard_map/ppermute | solution.py:53
  62.7 1.7 copy-start.4
  62.7 4.0 %collective-permute-start.9 = (bf16[4,512,128]{2,1,0:T(8,128)(2,1)S(1)}, bf16[4,512,128]{2,1,0:T(8,128)(2,1)S(1)}, u32[]{:S(2)}, u32[]{:S(2)}) collective-permute-start(bf16[4,512,128]{2,1,0:T(8,128)(2,1)S(1)} %bitcast.118), channel_id=1, source_target_pairs={{0,4},{4,0},{8,12},{12,8},{1,5},{5,1},{9,13},{13,9},{2,6},{6,2},{1... | collective-permute-start | bytes 1572872 | tf_op jit(solution)/shard_map/ppermute | solution.py:53
  69.2 4.9 %copy-start.1 = (f32[1024,1024]{1,0:T(8,128)}, f32[1024,1024]{1,0:T(8,128)S(1)}, u32[]{:S(2)}) copy-start(f32[1024,1024]{1,0:T(8,128)S(1)} %bitcast_multiply_fusion) | copy-start | bytes 12582916
  74.1 2.0 %collective-permute-start.16 = (f32[1024,128]{1,0:T(8,128)S(1)}, f32[1024,128]{1,0:T(8,128)S(1)}, u32[]{:S(2)}, u32[]{:S(2)}) collective-permute-start(f32[1024,128]{1,0:T(8,128)S(1)} %fusion.10), channel_id=1, source_target_pairs={{0,4},{4,0},{8,12},{12,8},{1,5},{5,1},{9,13},{13,9},{2,6},{6,2},{1... | collective-permute-start | bytes 1572872 | tf_op jit(solution)/shard_map/ppermute | solution.py:93
  76.2 8.8 %collective-permute-start.17 = (f32[512,128]{1,0:T(8,128)S(1)}, f32[512,128]{1,0:T(8,128)}, u32[]{:S(2)}, u32[]{:S(2)}) collective-permute-start(f32[512,128]{1,0:T(8,128)S(1)} %slice_select_fusion), channel_id=1, source_target_pairs={{0,8},{4,12},{8,0},{12,4},{1,9},{5,13},{9,1},{13,5},{2,10},{6,14},... | collective-permute-start | bytes 786440 | tf_op jit(solution)/shard_map/ppermute | solution.py:96
  86.0 1.6 collective-permute-start.18
  88.6 15.9 %collective-permute-start.19 = (f32[128,128]{0,1:T(8,128)S(1)}, f32[128,128]{0,1:T(8,128)S(1)}, u32[]{:S(2)}, u32[]{:S(2)}) collective-permute-start(f32[128,128]{0,1:T(8,128)S(1)} %fusion.24), channel_id=1, source_target_pairs={{0,1},{1,0},{2,3},{3,2},{4,5},{5,4},{6,7},{7,6},{8,9},{9,8},{10,11... | collective-permute-start | bytes 196616 | tf_op jit(solution)/shard_map/ppermute | solution.py:44
  90.1 14.4 %collective-permute-start.20 = (f32[128,128]{0,1:T(8,128)S(1)}, f32[128,128]{0,1:T(8,128)}, u32[]{:S(2)}, u32[]{:S(2)}) collective-permute-start(f32[128,128]{0,1:T(8,128)S(1)} %fusion.24), channel_id=1, source_target_pairs={{0,2},{1,3},{2,0},{3,1},{4,6},{5,7},{6,4},{7,5},{8,10},{9,11},{10,... | collective-permute-start | bytes 196616 | tf_op jit(solution)/shard_map/ppermute | solution.py:44
  95.4 9.2 %collective-permute-start.21 = (f32[128,128]{0,1:T(8,128)S(1)}, f32[128,128]{0,1:T(8,128)}, u32[]{:S(2)}, u32[]{:S(2)}) collective-permute-start(f32[128,128]{0,1:T(8,128)S(1)} %fusion.24), channel_id=1, source_target_pairs={{0,3},{1,2},{2,1},{3,0},{4,7},{5,6},{6,5},{7,4},{8,11},{9,10},{10,... | collective-permute-start | bytes 196616 | tf_op jit(solution)/shard_map/ppermute | solution.py:44
  103.9 7.9 %collective-permute-start.22 = (f32[512,128]{1,0:T(8,128)S(1)}, f32[512,128]{1,0:T(8,128)S(1)}, u32[]{:S(2)}, u32[]{:S(2)}) collective-permute-start(f32[512,128]{1,0:T(8,128)S(1)} %slice_select_fusion.1), channel_id=1, source_target_pairs={{0,1},{1,0},{2,3},{3,2},{4,5},{5,4},{6,7},{7,6},{8,9},{9,8},{10,11... | collective-permute-start | bytes 786440 | tf_op jit(solution)/shard_map/ppermute | solution.py:76
  111.8 14.2 %collective-permute-start.23 = (f32[256,128]{1,0:T(8,128)S(1)}, f32[256,128]{1,0:T(8,128)S(1)}, u32[]{:S(2)}, u32[]{:S(2)}) collective-permute-start(f32[256,128]{1,0:T(8,128)S(1)} %slice_select_fusion.2), channel_id=1, source_target_pairs={{0,2},{1,3},{2,0},{3,1},{4,6},{5,7},{6,4},{7,5},{8,10},{9,11},{10,... | collective-permute-start | bytes 393224 | tf_op jit(solution)/shard_map/ppermute | solution.py:76
  126.1 7.6 %collective-permute-start.24 = (f32[256,128]{1,0:T(8,128)S(1)}, f32[256,128]{1,0:T(8,128)S(1)}, u32[]{:S(2)}, u32[]{:S(2)}) collective-permute-start(f32[256,128]{1,0:T(8,128)S(1)} %get-tuple-element.7), channel_id=1, source_target_pairs={{0,2},{1,3},{2,0},{3,1},{4,6},{5,7},{6,4},{7,5},{8,10},{9,11},{10,... | collective-permute-start | bytes 393224 | tf_op jit(solution)/shard_map/ppermute | solution.py:79
  133.7 10.8 %collective-permute-start.25 = (f32[512,128]{1,0:T(8,128)S(1)}, f32[512,128]{1,0:T(8,128)S(1)}, u32[]{:S(2)}, u32[]{:S(2)}) collective-permute-start(f32[512,128]{1,0:T(8,128)S(1)} %constant_dynamic-update-slice_fusion.2), channel_id=1, source_target_pairs={{0,1},{1,0},{2,3},{3,2},{4,5},{5,4},{6,7},{7,6},{8,9},{9,8},{10,11... | collective-permute-start | bytes 786440 | tf_op jit(solution)/shard_map/ppermute | solution.py:79
  145.8 1.9 %collective-permute-start.26 = (f32[128,128]{0,1:T(8,128)S(1)}, f32[128,128]{0,1:T(8,128)S(1)}, u32[]{:S(2)}, u32[]{:S(2)}) collective-permute-start(f32[128,128]{0,1:T(8,128)S(1)} %fusion.26), channel_id=1, source_target_pairs={{0,4},{4,0},{8,12},{12,8},{1,5},{5,1},{9,13},{13,9},{2,6},{6,2},{1... | collective-permute-start | bytes 196616 | tf_op jit(solution)/shard_map/ppermute | solution.py:44
  145.8 4.5 %collective-permute-start.27 = (f32[128,128]{0,1:T(8,128)S(1)}, f32[128,128]{0,1:T(8,128)S(1)}, u32[]{:S(2)}, u32[]{:S(2)}) collective-permute-start(f32[128,128]{0,1:T(8,128)S(1)} %fusion.26), channel_id=1, source_target_pairs={{0,8},{4,12},{8,0},{12,4},{1,9},{5,13},{9,1},{13,5},{2,10},{6,14},... | collective-permute-start | bytes 196616 | tf_op jit(solution)/shard_map/ppermute | solution.py:44
  147.6 4.1 %collective-permute-start.28 = (f32[128,128]{0,1:T(8,128)S(1)}, f32[128,128]{0,1:T(8,128)S(1)}, u32[]{:S(2)}, u32[]{:S(2)}) collective-permute-start(f32[128,128]{0,1:T(8,128)S(1)} %fusion.26), channel_id=1, source_target_pairs={{0,12},{4,8},{8,4},{12,0},{1,13},{5,9},{9,5},{13,1},{2,14},{6,10},... | collective-permute-start | bytes 196616 | tf_op jit(solution)/shard_map/ppermute | solution.py:44
